TPU v7x, 32 devices: a whole 2x2x4 slice. The times are simulated.
32 devices in a mesh: dp: 8 (over y, x, core), mp: 4 (over z).
Axes of the slice: x: 2, y: 2, z: 4, core: 2. Of those that a mesh axis runs over, the one named last changes fastest.
Arguments:
- activations: bfloat16 [4, 16, 1024, 4096], P(None, 'dp', 'mp'), may hold values from -6 to 6
- cotangents: bfloat16 [4, 16, 1024, 4096], P(None, 'dp', 'mp'), may hold values from -0.1875 to 0.1875
- lengths: int32 [16], P('dp'), may hold values from 128 to 1024, as said below
- project_in: bfloat16 [4, 64, 4096], replicated, may hold values from -0.09375 to 0.09375
- project_out: bfloat16 [4, 64, 4096], replicated, may hold values from -0.09375 to 0.09375
- preconditioner: bfloat16 [16384, 4096], P('mp', 'dp'), as said below
- queries: bfloat16 [8192, 16384], P('dp', 'mp'), may hold values from -0.0625 to 0.0625
Outputs:
- scores: float32 [16, 8192], P(None, ('dp', 'mp'))
Inputs may be any that keep to these rules, and one draw needn't show every extreme that they name: `lengths`: positions at or past an example's length are padding; some example has all 1024 positions live. `preconditioner`: each layer's 4096 x 4096 block is symmetric.
All inputs are finite; a program needn't handle non-finite values.
Results may differ from a plain program's by a relative error of at most 0.005.
Values may be sent and summed in bfloat16 or wider, within the bound.
No kernel may reach another device: no remote copies, remote signals or barrier semaphores. Data moves between devices by JAX's collectives and lax.ppermute only.
A program may use at most 128 MiB of HBM per device.

v0:
```python
import jax
import jax.numpy as jnp
from jax import lax
from jax.sharding import PartitionSpec as P


def split_parts(dense):
    upper = dense.astype(jnp.bfloat16)
    kept = lax.optimization_barrier(upper)
    lower = (dense - kept.astype(jnp.float32)).astype(jnp.bfloat16)
    return (upper, lower)


def body(activations, cotangents, lengths, project_in, project_out, preconditioner, queries):
    width_mp = lax.axis_size("mp")
    layer_count = activations.shape[0]
    tokens_here = activations.shape[2]
    factor_size = project_in.shape[1]
    block_size = factor_size * factor_size
    group_size = width_mp // layer_count
    mp_place = lax.axis_index("mp")
    contract = (((1,), (1,)), ((), ()))
    positions = mp_place * tokens_here + jnp.arange(tokens_here, dtype=jnp.int32)
    live_mask = positions[None, :] < lengths[:, None]
    left_factor = jnp.einsum(
        "lesd,lkd->lesk", activations, project_in, preferred_element_type=jnp.float32
    ).astype(jnp.bfloat16)
    right_factor = jnp.einsum(
        "lesd,lkd->lesk", cotangents, project_out, preferred_element_type=jnp.float32
    )
    right_factor = jnp.where(live_mask[None, :, :, None], right_factor, 0.0).astype(jnp.bfloat16)
    partial_grad = jnp.einsum(
        "lesj,lesc->eljc", right_factor, left_factor, preferred_element_type=jnp.float32
    )
    partial_grad = partial_grad.reshape(partial_grad.shape[0], layer_count * block_size)
    grad_total = lax.psum(partial_grad, "mp")
    layer_place = mp_place // group_size
    grad_layer = lax.dynamic_slice_in_dim(
        grad_total, layer_place * block_size, block_size, 1
    ).astype(jnp.bfloat16)
    spread = lax.all_to_all(grad_layer, "dp", split_axis=1, concat_axis=0, tiled=True)
    partial_pre = lax.dot_general(
        spread, preconditioner, contract, preferred_element_type=jnp.float32
    )
    precond_grad = lax.psum(partial_pre, "dp")
    upper_grad, lower_grad = split_parts(precond_grad)
    scores = lax.psum_scatter(
        lax.dot_general(queries, upper_grad, contract, preferred_element_type=jnp.float32)
        + lax.dot_general(queries, lower_grad, contract, preferred_element_type=jnp.float32),
        "mp",
        scatter_dimension=0,
        tiled=True,
    )
    return scores.T


def solution(mesh):
    return jax.shard_map(
        body,
        mesh=mesh,
        in_specs=(
            P(None, "dp", "mp", None),
            P(None, "dp", "mp", None),
            P("dp"),
            P(),
            P(),
            P("mp", "dp"),
            P("dp", "mp"),
        ),
        out_specs=P(None, ("dp", "mp")),
        check_vma=False,
    )
```

profile of v0, /device:TPU:0, one launch (start us, length us, event | category | flops | bytes accessed | tf_op | source)
XLA Modules:
  0.0 151.0 jit_solution(13580495785346025847)
XLA Ops:
  6.5 0.0 copy-start
  6.5 0.0 all-reduce.3.cloned.1.call-start
  6.5 0.9 broadcast_compare_fusion
  7.4 0.7 copy-done
  8.1 8.8 %fusion.16 = bf16[4,2,256,64]{2,3,0,1:T(8,128)(2,1)S(1)} fusion(bf16[4,64,4096]{2,1,0:T(8,128)(2,1)S(1)} %copy-done, bf16[4,2,256,4096]{3,2,1,0:T(8,128)(2,1)} %param.8, pred[2,256]{1,0:T(4,128)(4,1)S(1)} %broadcast_compare_fusion), kind=kOutput, calls=%fused_computation.8 | convolution fusion | flops 1074003968 | bytes 19137024 | tf_op jit(solution)/shard_map/lesd,lkd->lesk/dot_general | solution.py:28
  16.9 9.3 %fusion.24 = f32[2,4,64,64]{3,2,1,0:T(8,128)S(1)} fusion(bf16[4,2,256,64]{2,3,0,1:T(8,128)(2,1)S(1)} %fusion.16, bf16[4,64,4096]{2,1,0:T(8,128)(2,1)} %param.10, bf16[4,2,256,4096]{3,2,1,0:T(8,128)(2,1)} %param.7), kind=kOutput, calls=%fused_computation.11 | convolution fusion | flops 1090650112 | bytes 19267584 | tf_op jit(solution)/shard_map/lesj,lesc->eljc/dot_general | solution.py:32
  26.2 0.1 reshape.40
  26.3 23.0 %all-reduce.4 = bf16[2,16384]{1,0:T(2,128)(2,1)S(1)} all-reduce(f32[2,16384]{1,0:T(2,128)S(1)} %reshape.40), channel_id=1, replica_groups=mesh['dp'=8,'mp'=4] {'mp'}, use_global_device_ids=true, to_apply=%region_0.1 | all-reduce | flops 32768 | bytes 196608 | tf_op jit(solution)/shard_map/psum | solution.py:36
  49.4 8.3 %all_to_all.19 = bf16[2,8,512]{2,0,1:T(2,128)(2,1)S(1)} all-to-all(bf16[2,8,512]{2,0,1:T(2,128)(2,1)S(1)} %bitcast.27), channel_id=1, replica_groups=mesh['dp'=8,'mp'=4] {'dp'}, dimensions={1} | all-to-all | bytes 32768 | tf_op jit(solution)/shard_map/all_to_all | solution.py:41
  57.7 4.1 %fusion.27 = f32[16,4096]{1,0:T(8,128)} fusion(bf16[16,512]{1,0:T(8,128)(2,1)S(1)} %all_to_all.17, bf16[4096,512]{1,0:T(8,128)(2,1)} %param.12), kind=kOutput, calls=%fused_computation.16 | convolution fusion | flops 67108864 | bytes 4472832 | tf_op jit(solution)/shard_map/dot_general | solution.py:42
  61.7 0.0 all-reduce.3.cloned.1.call-update
  61.8 0.0 reduce-scatter.2.cloned.1.call-start
  61.8 50.5 %all-reduce.3.cloned.1.call-done = f32[16,4096]{1,0:T(8,128)} async-done(((f32[16,4096]{1,0:T(8,128)}), f32[16,4096]{1,0:T(8,128)}) %all-reduce.3.cloned.1.call-update) | async-done | bytes 262160 | tf_op jit(solution)/shard_map/psum | solution.py:45
  112.3 0.0 copy-start.1
  112.3 1.0 convert_element_type.21
  113.3 5.6 %fusion.28 = f32[16,1024]{1,0:T(8,128)S(1)} fusion(bf16[16,4096]{1,0:T(8,128)(2,1)S(1)} %convert_element_type.21, bf16[1024,4096]{1,0:T(8,128)(2,1)} %param.13), kind=kOutput, calls=%fused_computation.17 | convolution fusion | flops 134217728 | bytes 8585216 | tf_op jit(solution)/shard_map/dot_general | solution.py:48
  119.0 0.0 copy-done.1
  119.0 6.3 %fusion.21 = f32[1024,16]{0,1:T(8,128)} fusion(f32[16,1024]{1,0:T(8,128)S(1)} %fusion.28, bf16[1024,4096]{1,0:T(8,128)(2,1)} %param.13, f32[16,4096]{1,0:T(8,128)S(1)} %copy-done.1, bf16[16,4096]{1,0:T(8,128)(2,1)S(1)} %convert_element_type.21), kind=kOutput, calls=%fused_computation.10 | convolution fusion | flops 134430720 | bytes 8912896 | tf_op jit(solution)/shard_map/dot_general | solution.py:49
  125.3 0.0 reduce-scatter.2.cloned.1.call-update
  125.3 18.9 %reduce-scatter.2.cloned.1.call-done = f32[256,16]{0,1:T(8,128)} async-done(((f32[1024,16]{0,1:T(8,128)}), f32[256,16]{0,1:T(8,128)}) %reduce-scatter.2.cloned.1.call-update) | async-done | bytes 16400 | tf_op jit(solution)/shard_map/reduce_scatter | solution.py:47
  (3 shorter events, 0.0 us)
Async XLA Ops:
  6.5 1.6 %copy-start = (bf16[4,64,4096]{2,1,0:T(8,128)(2,1)S(1)}, bf16[4,64,4096]{2,1,0:T(8,128)(2,1)}, u32[]{:S(2)}) copy-start(bf16[4,64,4096]{2,1,0:T(8,128)(2,1)} %param.11) | copy-start | bytes 6291460
  6.5 105.8 %all-reduce.3.cloned.1.call-start = ((), (), s32[]{:S(2)}) async-start(), calls=%async_computation.2 | async-start | bytes 524288 | tf_op jit(solution)/shard_map/psum | solution.py:45
  61.8 82.4 %reduce-scatter.2.cloned.1.call-start = ((), (), s32[]{:S(2)}) async-start(), calls=%async_computation.3 | async-start | bytes 81920 | tf_op jit(solution)/shard_map/reduce_scatter | solution.py:47
  112.3 6.7 %copy-start.1 = (f32[16,4096]{1,0:T(8,128)S(1)}, f32[16,4096]{1,0:T(8,128)}, u32[]{:S(2)}) copy-start(f32[16,4096]{1,0:T(8,128)} %all-reduce.3.cloned.1.call-done) | copy-start | bytes 786436
Sparse Core Ops, SparseCore 0:
  61.9 50.3 all-reduce.2
  125.4 18.6 reduce-scatter.1
where the time goes:
time: 151 us
  waiting for transfers between devices  69.4 us (46%)
  matrix products  34.1 us (23%)
  blocking collectives  31.3 us (21%)
  between operations  13.4 us (9%)
  other arithmetic  1.91 us (1%)
    psum x1, waiting for transfers between devices, body(): precond_grad = lax.psum(partial_pre, 'dp')  50.5 us
    psum x1, blocking collectives, body(): grad_total = lax.psum(partial_grad, 'mp')  23 us
    reduce_scatter x1, waiting for transfers between devices, body(): lax.psum_scatter(lax.dot_general(queries, upper_grad, contract, preferred...  18.9 us
    dot_general x1, matrix products, body(): jnp.einsum('lesj,lesc->eljc', right_factor, left_factor, preferred_elemen...  9.26 us
    dot_general x1, matrix products, body(): jnp.einsum('lesd,lkd->lesk', cotangents, project_out, preferred_element_t...  8.75 us
    all_to_all x1, blocking collectives, body(): lax.all_to_all(grad_layer, 'dp', split_axis=1, concat_axis=0, tiled=True)  8.27 us
    dot_general x1, matrix products, body(): lax.dot_general(queries, lower_grad, contract, preferred_element_type=jnp...  6.3 us
    dot_general x1, matrix products, body(): lax.dot_general(queries, upper_grad, contract, preferred_element_type=jnp...  5.65 us
  transfers between devices with their start and end apart: 2, of which 2 were waited for; matrix products, arithmetic and copies ran while one was open for 0% of the time, Pallas kernels for 0%

commit v1 on v0

--- a/solution.py
+++ b/solution.py
@@ -11,7 +11,32 @@
     return (upper, lower)
 
 
-def body(activations, cotangents, lengths, project_in, project_out, preconditioner, queries):
+def shifted(x, axis, shift):
+    n = lax.axis_size(axis)
+    return lax.ppermute(x, axis, [(i, (i + shift) % n) for i in range(n)])
+
+
+def reduce_scatter_direct(x, axis, dim):
+    n = lax.axis_size(axis)
+    me = lax.axis_index(axis)
+    width = x.shape[dim] // n
+    total = lax.dynamic_slice_in_dim(x, me * width, width, dim)
+    for shift in range(1, n):
+        piece = lax.dynamic_slice_in_dim(x, ((me + shift) % n) * width, width, dim)
+        total = total + shifted(piece, axis, shift)
+    return total
+
+
+def all_gather_direct(x, axis):
+    n = lax.axis_size(axis)
+    me = lax.axis_index(axis)
+    got = [x] + [shifted(x, axis, shift) for shift in range(1, n)]
+    order = jnp.stack([got[(-k) % n] for k in range(n)])
+    doubled = jnp.concatenate([order, order], axis=0)
+    return lax.dynamic_slice_in_dim(doubled, (n - me) % n, n, 0)
+
+
+def body_start(activations, cotangents, lengths, project_in, project_out, preconditioner, queries):
     width_mp = lax.axis_size("mp")
     layer_count = activations.shape[0]
     tokens_here = activations.shape[2]
@@ -54,6 +79,49 @@
     return scores.T
 
 
+def body_direct(activations, cotangents, lengths, project_in, project_out, preconditioner, queries):
+    layer_count = activations.shape[0]
+    tokens_here = activations.shape[2]
+    factor_size = project_in.shape[1]
+    block_size = factor_size * factor_size
+    width_dp = lax.axis_size("dp")
+    mp_place = lax.axis_index("mp")
+    positions = mp_place * tokens_here + jnp.arange(tokens_here, dtype=jnp.int32)
+    live_mask = positions[None, :] < lengths[:, None]
+    left_factor = jnp.einsum(
+        "lesd,lkd->lesk", activations, project_in, preferred_element_type=jnp.float32
+    ).astype(jnp.bfloat16)
+    right_factor = jnp.einsum(
+        "lesd,lkd->lesk", cotangents, project_out, preferred_element_type=jnp.float32
+    )
+    right_factor = jnp.where(live_mask[None, :, :, None], right_factor, 0.0).astype(jnp.bfloat16)
+    partial_grad = jnp.einsum(
+        "lesj,lesc->eljc", right_factor, left_factor, preferred_element_type=jnp.float32
+    )
+    partial_grad = partial_grad.reshape(partial_grad.shape[0], layer_count * block_size)
+    grad_mine = reduce_scatter_direct(partial_grad, "mp", 1).astype(jnp.bfloat16)
+    grad_all = all_gather_direct(grad_mine, "dp")
+    grad_all = grad_all.reshape(-1, grad_all.shape[-1])
+    pre_part = jnp.dot(grad_all, preconditioner, preferred_element_type=jnp.float32)
+    pre_all = all_gather_direct(pre_part, "dp")
+    pre_all = jnp.transpose(pre_all, (1, 0, 2)).reshape(pre_all.shape[1], -1)
+    upper_grad, lower_grad = split_parts(pre_all)
+    both = jnp.concatenate([upper_grad, lower_grad], axis=0)
+    products = lax.dot_general(
+        both, queries, (((1,), (1,)), ((), ())), preferred_element_type=jnp.float32
+    )
+    examples = upper_grad.shape[0]
+    partial_scores = products[:examples] + products[examples:]
+    return reduce_scatter_direct(partial_scores, "mp", 1)
+
+
+def body(*args):
+    layer_count = args[0].shape[0]
+    if lax.axis_size("mp") == layer_count:
+        return body_direct(*args)
+    return body_start(*args)
+
+
 def solution(mesh):
     return jax.shard_map(
         body,

time: 151 us -> 74.1 us (0.49)
  waiting for transfers between devices: 69.4 us -> 19.5 us
  blocking collectives: 31.3 us -> 0 us
  starting transfers between devices: 0.04 us -> 24.2 us
  between operations: 13.4 us -> 0.32 us
  matrix products: 34.1 us -> 26.8 us
    psum x1 -> x0, waiting for transfers between devices: 50.5 us -> none  [body(): precond_grad = lax.psum(partial_pre, 'dp')]
    ppermute x0 -> x20, starting transfers between devices: none -> 24.2 us  [shifted(): return lax.ppermute(x, axis, [(i, (i + shift) % n) for i in range(n)])]
    psum x1 -> x0, blocking collectives: 23 us -> none  [body(): grad_total = lax.psum(partial_grad, 'mp')]
    ppermute x0 -> x20, waiting for transfers between devices: none -> 19.5 us  [shifted(): return lax.ppermute(x, axis, [(i, (i + shift) % n) for i in range(n)])]
    reduce_scatter x1 -> x0, waiting for transfers between devices: 18.9 us -> none  [body(): lax.psum_scatter(lax.dot_general(queries, upper_grad, contract, preferred...]
    all_to_all x1 -> x0, blocking collectives: 8.27 us -> none  [body(): lax.all_to_all(grad_layer, 'dp', split_axis=1, concat_axis=0, tiled=True)]
    dot_general x5 -> x4, matrix products: 34.1 us -> 26.8 us  [the longest x1 9.26 us: body_direct(): jnp.einsum('lesj,lesc->eljc', right_factor, left_factor, preferred_elemen...]
  transfers between devices with their start and end apart: 2 -> 20, of which waited for: 2 -> 9; matrix products, arithmetic and copies ran while one was open for 0% -> 0% of each run, Pallas kernels for 0% -> 0%
where the time goes in v1:
time: 74.1 us; the launch traced here: 73.9 us
  matrix products  26.8 us (36%)
  starting transfers between devices  24.2 us (33%)
  waiting for transfers between devices  19.5 us (26%)
  other arithmetic  1.59 us (2%)
  local copies, waits for them, and re-layouts  1.5 us (2%)
    ppermute x20, starting transfers between devices, shifted(): return lax.ppermute(x, axis, [(i, (i + shift) % n) for i in range(n)])  24.2 us
    ppermute x20, waiting for transfers between devices, shifted(): return lax.ppermute(x, axis, [(i, (i + shift) % n) for i in range(n)])  19.5 us
    dot_general x1, matrix products, body_direct(): jnp.einsum('lesj,lesc->eljc', right_factor, left_factor, preferred_elemen...  9.26 us
    dot_general x1, matrix products, body_direct(): jnp.einsum('lesd,lkd->lesk', cotangents, project_out, preferred_element_t...  8.75 us
    dot_general x1, matrix products, body_direct(): lax.dot_general(both, queries, (((1,), (1,)), ((), ())), preferred_elemen...  5.96 us
    dot_general x1, matrix products, body_direct(): jnp.dot(grad_all, preconditioner, preferred_element_type=jnp.float32)  2.83 us
  transfers between devices with their start and end apart: 20, of which 9 were waited for; matrix products, arithmetic and copies ran while one was open for 0% of the time, Pallas kernels for 0%

profile of v1, /device:TPU:0, one launch (start us, length us, event | category | flops | bytes accessed | tf_op | source)
XLA Modules:
  0.0 73.9 jit_solution(13347493090399087877)
XLA Ops:
  0.0 0.9 %broadcast_compare_fusion = pred[2,256]{1,0:T(4,128)(4,1)S(1)} fusion(s32[256]{0:T(256)S(1)} %iota_add_fusion, s32[2]{0:T(128)} %param.9), kind=kLoop, calls=%fused_computation.58 | loop fusion | flops 512 | bytes 1544 | tf_op jit(solution)/shard_map/lt | solution.py:90
  0.9 0.7 copy-done
  1.6 8.8 %fusion.16 = bf16[4,2,256,64]{2,3,0,1:T(8,128)(2,1)S(1)} fusion(bf16[4,64,4096]{2,1,0:T(8,128)(2,1)S(1)} %copy-done, bf16[4,2,256,4096]{3,2,1,0:T(8,128)(2,1)} %param.8, pred[2,256]{1,0:T(4,128)(4,1)S(1)} %broadcast_compare_fusion), kind=kOutput, calls=%fused_computation.8 | convolution fusion | flops 1074003968 | bytes 19137024 | tf_op jit(solution)/shard_map/lesd,lkd->lesk/dot_general | solution.py:94
  10.4 9.3 %fusion.23 = f32[2,4,64,64]{3,2,1,0:T(8,128)S(1)} fusion(bf16[4,2,256,64]{2,3,0,1:T(8,128)(2,1)S(1)} %fusion.16, bf16[4,64,4096]{2,1,0:T(8,128)(2,1)} %param.10, bf16[4,2,256,4096]{3,2,1,0:T(8,128)(2,1)} %param.7), kind=kOutput, calls=%fused_computation.9 | convolution fusion | flops 1090650112 | bytes 19267584 | tf_op jit(solution)/shard_map/lesj,lesc->eljc/dot_general | solution.py:98
  19.6 0.1 reshape.43
  19.8 3.1 %collective-permute-start = (f32[2,4096]{1,0:T(2,128)S(1)}, f32[2,4096]{1,0:T(2,128)S(1)}, u32[]{:S(2)}, u32[]{:S(2)}) collective-permute-start(f32[2,4096]{1,0:T(2,128)S(1)} %get-tuple-element.7), channel_id=1, source_target_pairs={{0,1},{1,2},{2,3},{3,0},{4,5},{5,6},{6,7},{7,4},{8,9},{9,10},{10,1... | collective-permute-start | bytes 98312 | tf_op jit(solution)/shard_map/ppermute | solution.py:16
  22.9 2.1 %collective-permute-start.2 = (f32[2,4096]{1,0:T(2,128)S(1)}, f32[2,4096]{1,0:T(2,128)S(1)}, u32[]{:S(2)}, u32[]{:S(2)}) collective-permute-start(f32[2,4096]{1,0:T(2,128)S(1)} %get-tuple-element.8), channel_id=1, source_target_pairs={{0,3},{1,0},{2,1},{3,2},{4,7},{5,4},{6,5},{7,6},{8,11},{9,8},{10,9... | collective-permute-start | bytes 98312 | tf_op jit(solution)/shard_map/ppermute | solution.py:16
  25.0 1.0 %collective-permute-start.1 = (f32[2,4096]{1,0:T(2,128)S(1)}, f32[2,4096]{1,0:T(2,128)S(1)}, u32[]{:S(2)}, u32[]{:S(2)}) collective-permute-start(f32[2,4096]{1,0:T(2,128)S(1)} %get-tuple-element.9), channel_id=1, source_target_pairs={{0,2},{1,3},{2,0},{3,1},{4,6},{5,7},{6,4},{7,5},{8,10},{9,11},{10,... | collective-permute-start | bytes 98312 | tf_op jit(solution)/shard_map/ppermute | solution.py:16
  26.0 0.9 %collective-permute-done = f32[2,4096]{1,0:T(2,128)S(1)} collective-permute-done((f32[2,4096]{1,0:T(2,128)S(1)}, f32[2,4096]{1,0:T(2,128)S(1)}, u32[]{:S(2)}, u32[]{:S(2)}) %collective-permute-start) | collective-permute-done | bytes 32800 | tf_op jit(solution)/shard_map/ppermute | solution.py:16
  26.9 0.3 collective-permute-done.2
  27.2 2.6 %collective-permute-done.1 = f32[2,4096]{1,0:T(2,128)S(1)} collective-permute-done((f32[2,4096]{1,0:T(2,128)S(1)}, f32[2,4096]{1,0:T(2,128)S(1)}, u32[]{:S(2)}, u32[]{:S(2)}) %collective-permute-start.1) | collective-permute-done | bytes 32800 | tf_op jit(solution)/shard_map/ppermute | solution.py:16
  29.9 0.6 collective-permute-start.3
  30.5 0.0 collective-permute-start.9
  30.5 1.6 %collective-permute-start.8 = (bf16[2,4096]{1,0:T(2,128)(2,1)S(1)}, bf16[2,4096]{1,0:T(2,128)(2,1)S(1)}, u32[]{:S(2)}, u32[]{:S(2)}) collective-permute-start(bf16[2,4096]{1,0:T(2,128)(2,1)S(1)} %get-tuple-element.6), channel_id=1, source_target_pairs={{0,8},{4,12},{8,16},{12,20},{16,24},{20,28},{24,0},{28,4},{1,9},{5... | collective-permute-start | bytes 49160 | tf_op jit(solution)/shard_map/ppermute | solution.py:16
  32.1 2.0 %collective-permute-start.7 = (bf16[2,4096]{1,0:T(2,128)(2,1)S(1)}, bf16[2,4096]{1,0:T(2,128)(2,1)S(1)}, u32[]{:S(2)}, u32[]{:S(2)}) collective-permute-start(bf16[2,4096]{1,0:T(2,128)(2,1)S(1)} %get-tuple-element.6), channel_id=1, source_target_pairs={{0,12},{4,16},{8,20},{12,24},{16,28},{20,0},{24,4},{28,8},{1,13},{... | collective-permute-start | bytes 49160 | tf_op jit(solution)/shard_map/ppermute | solution.py:16
  34.1 0.5 collective-permute-start.6
  34.6 0.0 collective-permute-done.3
  34.6 1.7 %collective-permute-start.4 = (bf16[2,4096]{1,0:T(2,128)(2,1)S(1)}, bf16[2,4096]{1,0:T(2,128)(2,1)S(1)}, u32[]{:S(2)}, u32[]{:S(2)}) collective-permute-start(bf16[2,4096]{1,0:T(2,128)(2,1)S(1)} %get-tuple-element.6), channel_id=1, source_target_pairs={{0,24},{4,28},{8,0},{12,4},{16,8},{20,12},{24,16},{28,20},{1,25},{... | collective-permute-start | bytes 49160 | tf_op jit(solution)/shard_map/ppermute | solution.py:16
  36.4 2.0 %collective-permute-done.4 = bf16[2,4096]{1,0:T(2,128)(2,1)S(1)} collective-permute-done((bf16[2,4096]{1,0:T(2,128)(2,1)S(1)}, bf16[2,4096]{1,0:T(2,128)(2,1)S(1)}, u32[]{:S(2)}, u32[]{:S(2)}) %collective-permute-start.4) | collective-permute-done | bytes 16416 | tf_op jit(solution)/shard_map/ppermute | solution.py:16
  38.3 0.0 collective-permute-start.5
  38.4 3.1 %collective-permute-done.5 = bf16[2,4096]{1,0:T(2,128)(2,1)S(1)} collective-permute-done((bf16[2,4096]{1,0:T(2,128)(2,1)S(1)}, bf16[2,4096]{1,0:T(2,128)(2,1)S(1)}, u32[]{:S(2)}, u32[]{:S(2)}) %collective-permute-start.5) | collective-permute-done | bytes 16416 | tf_op jit(solution)/shard_map/ppermute | solution.py:16
  41.5 0.0 collective-permute-done.6
  41.6 0.0 collective-permute-done.7
  41.6 0.0 collective-permute-done.8
  41.6 0.0 collective-permute-done.9
  41.9 0.1 constant_dynamic-slice_fusion.3
  42.0 0.1 reshape.44
  42.0 2.8 %constant_dynamic-update-slice_fusion.31 = (f32[16,16,512]{2,1,0:T(8,128)S(1)}, f32[16,512]{1,0:T(8,128)S(1)}) fusion(bf16[16,4096]{1,0:T(8,128)(2,1)S(1)} %reshape.44, bf16[4096,512]{1,0:T(8,128)(2,1)} %param.12), kind=kOutput, calls=%fused_computation.47 | convolution fusion | flops 67108864 | bytes 4390912 | tf_op jit(solution)/shard_map/dot_general | solution.py:105
  44.9 1.8 %collective-permute-start.10 = (f32[16,512]{1,0:T(8,128)S(1)}, f32[16,512]{1,0:T(8,128)S(1)}, u32[]{:S(2)}, u32[]{:S(2)}) collective-permute-start(f32[16,512]{1,0:T(8,128)S(1)} %get-tuple-element.14), channel_id=1, source_target_pairs={{0,28},{4,0},{8,4},{12,8},{16,12},{20,16},{24,20},{28,24},{1,29},{... | collective-permute-start | bytes 98312 | tf_op jit(solution)/shard_map/ppermute | solution.py:16
  46.7 0.0 collective-permute-start.16
  46.7 2.0 %collective-permute-start.15 = (f32[16,512]{1,0:T(8,128)S(1)}, f32[16,512]{1,0:T(8,128)S(1)}, u32[]{:S(2)}, u32[]{:S(2)}) collective-permute-start(f32[16,512]{1,0:T(8,128)S(1)} %get-tuple-element.14), channel_id=1, source_target_pairs={{0,8},{4,12},{8,16},{12,20},{16,24},{20,28},{24,0},{28,4},{1,9},{5... | collective-permute-start | bytes 98312 | tf_op jit(solution)/shard_map/ppermute | solution.py:16
  48.7 1.2 %collective-permute-start.14 = (f32[16,512]{1,0:T(8,128)S(1)}, f32[16,512]{1,0:T(8,128)S(1)}, u32[]{:S(2)}, u32[]{:S(2)}) collective-permute-start(f32[16,512]{1,0:T(8,128)S(1)} %get-tuple-element.14), channel_id=1, source_target_pairs={{0,12},{4,16},{8,20},{12,24},{16,28},{20,0},{24,4},{28,8},{1,13},{... | collective-permute-start | bytes 98312 | tf_op jit(solution)/shard_map/ppermute | solution.py:16
  49.9 1.2 %collective-permute-start.13 = (f32[16,512]{1,0:T(8,128)S(1)}, f32[16,512]{1,0:T(8,128)S(1)}, u32[]{:S(2)}, u32[]{:S(2)}) collective-permute-start(f32[16,512]{1,0:T(8,128)S(1)} %get-tuple-element.14), channel_id=1, source_target_pairs={{0,16},{4,20},{8,24},{12,28},{16,0},{20,4},{24,8},{28,12},{1,17},{... | collective-permute-start | bytes 98312 | tf_op jit(solution)/shard_map/ppermute | solution.py:16
  51.1 0.0 collective-permute-done.10
  51.1 1.4 %collective-permute-start.11 = (f32[16,512]{1,0:T(8,128)S(1)}, f32[16,512]{1,0:T(8,128)S(1)}, u32[]{:S(2)}, u32[]{:S(2)}) collective-permute-start(f32[16,512]{1,0:T(8,128)S(1)} %get-tuple-element.14), channel_id=1, source_target_pairs={{0,24},{4,28},{8,0},{12,4},{16,8},{20,12},{24,16},{28,20},{1,25},{... | collective-permute-start | bytes 98312 | tf_op jit(solution)/shard_map/ppermute | solution.py:16
  52.6 2.5 %collective-permute-done.11 = f32[16,512]{1,0:T(8,128)S(1)} collective-permute-done((f32[16,512]{1,0:T(8,128)S(1)}, f32[16,512]{1,0:T(8,128)S(1)}, u32[]{:S(2)}, u32[]{:S(2)}) %collective-permute-start.11) | collective-permute-done | bytes 32800 | tf_op jit(solution)/shard_map/ppermute | solution.py:16
  55.1 0.0 collective-permute-start.12
  55.1 3.3 %collective-permute-done.12 = f32[16,512]{1,0:T(8,128)S(1)} collective-permute-done((f32[16,512]{1,0:T(8,128)S(1)}, f32[16,512]{1,0:T(8,128)S(1)}, u32[]{:S(2)}, u32[]{:S(2)}) %collective-permute-start.12) | collective-permute-done | bytes 32800 | tf_op jit(solution)/shard_map/ppermute | solution.py:16
  58.4 0.0 collective-permute-done.13
  58.4 0.0 collective-permute-done.14
  58.4 0.0 collective-permute-done.15
  58.7 6.0 %fusion.26 = f32[32,1024]{1,0:T(8,128)S(1)} fusion(bf16[1024,4096]{1,0:T(8,128)(2,1)} %param.13, bf16[16,4096]{1,0:T(8,128)(2,1)S(1)} %subtract_convert_fusion, bf16[16,4096]{1,0:T(8,128)(2,1)S(1)} %convert_element_type.21), kind=kOutput, calls=%fused_computation.10 | convolution fusion | flops 268959744 | bytes 8781824 | tf_op jit(solution)/shard_map/dot_general | solution.py:110
  64.7 0.1 collective-permute-start.17
  64.8 3.8 %collective-permute-start.19 = (f32[16,256]{1,0:T(8,128)S(1)}, f32[16,256]{1,0:T(8,128)S(1)}, u32[]{:S(2)}, u32[]{:S(2)}) collective-permute-start(f32[16,256]{1,0:T(8,128)S(1)} %get-tuple-element.11), channel_id=1, source_target_pairs={{0,3},{1,0},{2,1},{3,2},{4,7},{5,4},{6,5},{7,6},{8,11},{9,8},{10,9... | collective-permute-start | bytes 49160 | tf_op jit(solution)/shard_map/ppermute | solution.py:16
  68.6 1.7 %collective-permute-done.17 = f32[16,256]{1,0:T(8,128)S(1)} collective-permute-done((f32[16,256]{1,0:T(8,128)S(1)}, f32[16,256]{1,0:T(8,128)S(1)}, u32[]{:S(2)}, u32[]{:S(2)}) %collective-permute-start.17) | collective-permute-done | bytes 16416 | tf_op jit(solution)/shard_map/ppermute | solution.py:16
  70.3 0.0 collective-permute-done.19
  70.3 2.9 %collective-permute-done.18 = f32[16,256]{1,0:T(8,128)S(1)} collective-permute-done((f32[16,256]{1,0:T(8,128)S(1)}, f32[16,256]{1,0:T(8,128)S(1)}, u32[]{:S(2)}, u32[]{:S(2)}) %collective-permute-start.18) | collective-permute-done | bytes 16416 | tf_op jit(solution)/shard_map/ppermute | solution.py:16
  73.2 0.6 add_add_fusion
  (42 shorter events, 0.6 us)
Async XLA Ops:
  0.0 1.6 %copy-start = (bf16[4,64,4096]{2,1,0:T(8,128)(2,1)S(1)}, bf16[4,64,4096]{2,1,0:T(8,128)(2,1)}, u32[]{:S(2)}) copy-start(bf16[4,64,4096]{2,1,0:T(8,128)(2,1)} %param.11) | copy-start | bytes 6291460
  19.8 7.1 %collective-permute-start = (f32[2,4096]{1,0:T(2,128)S(1)}, f32[2,4096]{1,0:T(2,128)S(1)}, u32[]{:S(2)}, u32[]{:S(2)}) collective-permute-start(f32[2,4096]{1,0:T(2,128)S(1)} %get-tuple-element.7), channel_id=1, source_target_pairs={{0,1},{1,2},{2,3},{3,0},{4,5},{5,6},{6,7},{7,4},{8,9},{9,10},{10,1... | collective-permute-start | bytes 98312 | tf_op jit(solution)/shard_map/ppermute | solution.py:16
  22.9 4.3 %collective-permute-start.2 = (f32[2,4096]{1,0:T(2,128)S(1)}, f32[2,4096]{1,0:T(2,128)S(1)}, u32[]{:S(2)}, u32[]{:S(2)}) collective-permute-start(f32[2,4096]{1,0:T(2,128)S(1)} %get-tuple-element.8), channel_id=1, source_target_pairs={{0,3},{1,0},{2,1},{3,2},{4,7},{5,4},{6,5},{7,6},{8,11},{9,8},{10,9... | collective-permute-start | bytes 98312 | tf_op jit(solution)/shard_map/ppermute | solution.py:16
  25.0 4.8 %collective-permute-start.1 = (f32[2,4096]{1,0:T(2,128)S(1)}, f32[2,4096]{1,0:T(2,128)S(1)}, u32[]{:S(2)}, u32[]{:S(2)}) collective-permute-start(f32[2,4096]{1,0:T(2,128)S(1)} %get-tuple-element.9), channel_id=1, source_target_pairs={{0,2},{1,3},{2,0},{3,1},{4,6},{5,7},{6,4},{7,5},{8,10},{9,11},{10,... | collective-permute-start | bytes 98312 | tf_op jit(solution)/shard_map/ppermute | solution.py:16
  29.9 4.7 %collective-permute-start.3 = (bf16[2,4096]{1,0:T(2,128)(2,1)S(1)}, bf16[2,4096]{1,0:T(2,128)(2,1)S(1)}, u32[]{:S(2)}, u32[]{:S(2)}) collective-permute-start(bf16[2,4096]{1,0:T(2,128)(2,1)S(1)} %get-tuple-element.6), channel_id=1, source_target_pairs={{0,28},{4,0},{8,4},{12,8},{16,12},{20,16},{24,20},{28,24},{1,29},{... | collective-permute-start | bytes 49160 | tf_op jit(solution)/shard_map/ppermute | solution.py:16
  30.5 11.2 %collective-permute-start.9 = (bf16[2,4096]{1,0:T(2,128)(2,1)S(1)}, bf16[2,4096]{1,0:T(2,128)(2,1)S(1)}, u32[]{:S(2)}, u32[]{:S(2)}) collective-permute-start(bf16[2,4096]{1,0:T(2,128)(2,1)S(1)} %get-tuple-element.6), channel_id=1, source_target_pairs={{0,4},{4,8},{8,12},{12,16},{16,20},{20,24},{24,28},{28,0},{1,5},{5... | collective-permute-start | bytes 49160 | tf_op jit(solution)/shard_map/ppermute | solution.py:16
  30.5 11.1 %collective-permute-start.8 = (bf16[2,4096]{1,0:T(2,128)(2,1)S(1)}, bf16[2,4096]{1,0:T(2,128)(2,1)S(1)}, u32[]{:S(2)}, u32[]{:S(2)}) collective-permute-start(bf16[2,4096]{1,0:T(2,128)(2,1)S(1)} %get-tuple-element.6), channel_id=1, source_target_pairs={{0,8},{4,12},{8,16},{12,20},{16,24},{20,28},{24,0},{28,4},{1,9},{5... | collective-permute-start | bytes 49160 | tf_op jit(solution)/shard_map/ppermute | solution.py:16
  32.1 9.5 %collective-permute-start.7 = (bf16[2,4096]{1,0:T(2,128)(2,1)S(1)}, bf16[2,4096]{1,0:T(2,128)(2,1)S(1)}, u32[]{:S(2)}, u32[]{:S(2)}) collective-permute-start(bf16[2,4096]{1,0:T(2,128)(2,1)S(1)} %get-tuple-element.6), channel_id=1, source_target_pairs={{0,12},{4,16},{8,20},{12,24},{16,28},{20,0},{24,4},{28,8},{1,13},{... | collective-permute-start | bytes 49160 | tf_op jit(solution)/shard_map/ppermute | solution.py:16
  34.1 7.4 %collective-permute-start.6 = (bf16[2,4096]{1,0:T(2,128)(2,1)S(1)}, bf16[2,4096]{1,0:T(2,128)(2,1)S(1)}, u32[]{:S(2)}, u32[]{:S(2)}) collective-permute-start(bf16[2,4096]{1,0:T(2,128)(2,1)S(1)} %get-tuple-element.6), channel_id=1, source_target_pairs={{0,16},{4,20},{8,24},{12,28},{16,0},{20,4},{24,8},{28,12},{1,17},{... | collective-permute-start | bytes 49160 | tf_op jit(solution)/shard_map/ppermute | solution.py:16
  34.6 3.7 %collective-permute-start.4 = (bf16[2,4096]{1,0:T(2,128)(2,1)S(1)}, bf16[2,4096]{1,0:T(2,128)(2,1)S(1)}, u32[]{:S(2)}, u32[]{:S(2)}) collective-permute-start(bf16[2,4096]{1,0:T(2,128)(2,1)S(1)} %get-tuple-element.6), channel_id=1, source_target_pairs={{0,24},{4,28},{8,0},{12,4},{16,8},{20,12},{24,16},{28,20},{1,25},{... | collective-permute-start | bytes 49160 | tf_op jit(solution)/shard_map/ppermute | solution.py:16
  38.3 3.2 %collective-permute-start.5 = (bf16[2,4096]{1,0:T(2,128)(2,1)S(1)}, bf16[2,4096]{1,0:T(2,128)(2,1)S(1)}, u32[]{:S(2)}, u32[]{:S(2)}) collective-permute-start(bf16[2,4096]{1,0:T(2,128)(2,1)S(1)} %get-tuple-element.6), channel_id=1, source_target_pairs={{0,20},{4,24},{8,28},{12,0},{16,4},{20,8},{24,12},{28,16},{1,21},{... | collective-permute-start | bytes 49160 | tf_op jit(solution)/shard_map/ppermute | solution.py:16
  44.9 6.3 %collective-permute-start.10 = (f32[16,512]{1,0:T(8,128)S(1)}, f32[16,512]{1,0:T(8,128)S(1)}, u32[]{:S(2)}, u32[]{:S(2)}) collective-permute-start(f32[16,512]{1,0:T(8,128)S(1)} %get-tuple-element.14), channel_id=1, source_target_pairs={{0,28},{4,0},{8,4},{12,8},{16,12},{20,16},{24,20},{28,24},{1,29},{... | collective-permute-start | bytes 98312 | tf_op jit(solution)/shard_map/ppermute | solution.py:16
  46.7 11.8 %collective-permute-start.16 = (f32[16,512]{1,0:T(8,128)S(1)}, f32[16,512]{1,0:T(8,128)S(1)}, u32[]{:S(2)}, u32[]{:S(2)}) collective-permute-start(f32[16,512]{1,0:T(8,128)S(1)} %get-tuple-element.14), channel_id=1, source_target_pairs={{0,4},{4,8},{8,12},{12,16},{16,20},{20,24},{24,28},{28,0},{1,5},{5... | collective-permute-start | bytes 98312 | tf_op jit(solution)/shard_map/ppermute | solution.py:16
  46.7 11.7 %collective-permute-start.15 = (f32[16,512]{1,0:T(8,128)S(1)}, f32[16,512]{1,0:T(8,128)S(1)}, u32[]{:S(2)}, u32[]{:S(2)}) collective-permute-start(f32[16,512]{1,0:T(8,128)S(1)} %get-tuple-element.14), channel_id=1, source_target_pairs={{0,8},{4,12},{8,16},{12,20},{16,24},{20,28},{24,0},{28,4},{1,9},{5... | collective-permute-start | bytes 98312 | tf_op jit(solution)/shard_map/ppermute | solution.py:16
  48.7 9.7 %collective-permute-start.14 = (f32[16,512]{1,0:T(8,128)S(1)}, f32[16,512]{1,0:T(8,128)S(1)}, u32[]{:S(2)}, u32[]{:S(2)}) collective-permute-start(f32[16,512]{1,0:T(8,128)S(1)} %get-tuple-element.14), channel_id=1, source_target_pairs={{0,12},{4,16},{8,20},{12,24},{16,28},{20,0},{24,4},{28,8},{1,13},{... | collective-permute-start | bytes 98312 | tf_op jit(solution)/shard_map/ppermute | solution.py:16
  49.9 8.5 %collective-permute-start.13 = (f32[16,512]{1,0:T(8,128)S(1)}, f32[16,512]{1,0:T(8,128)S(1)}, u32[]{:S(2)}, u32[]{:S(2)}) collective-permute-start(f32[16,512]{1,0:T(8,128)S(1)} %get-tuple-element.14), channel_id=1, source_target_pairs={{0,16},{4,20},{8,24},{12,28},{16,0},{20,4},{24,8},{28,12},{1,17},{... | collective-permute-start | bytes 98312 | tf_op jit(solution)/shard_map/ppermute | solution.py:16
  51.1 3.9 %collective-permute-start.11 = (f32[16,512]{1,0:T(8,128)S(1)}, f32[16,512]{1,0:T(8,128)S(1)}, u32[]{:S(2)}, u32[]{:S(2)}) collective-permute-start(f32[16,512]{1,0:T(8,128)S(1)} %get-tuple-element.14), channel_id=1, source_target_pairs={{0,24},{4,28},{8,0},{12,4},{16,8},{20,12},{24,16},{28,20},{1,25},{... | collective-permute-start | bytes 98312 | tf_op jit(solution)/shard_map/ppermute | solution.py:16
  55.1 3.3 %collective-permute-start.12 = (f32[16,512]{1,0:T(8,128)S(1)}, f32[16,512]{1,0:T(8,128)S(1)}, u32[]{:S(2)}, u32[]{:S(2)}) collective-permute-start(f32[16,512]{1,0:T(8,128)S(1)} %get-tuple-element.14), channel_id=1, source_target_pairs={{0,20},{4,24},{8,28},{12,0},{16,4},{20,8},{24,12},{28,16},{1,21},{... | collective-permute-start | bytes 98312 | tf_op jit(solution)/shard_map/ppermute | solution.py:16
  64.7 5.6 %collective-permute-start.17 = (f32[16,256]{1,0:T(8,128)S(1)}, f32[16,256]{1,0:T(8,128)S(1)}, u32[]{:S(2)}, u32[]{:S(2)}) collective-permute-start(f32[16,256]{1,0:T(8,128)S(1)} %get-tuple-element.10), channel_id=1, source_target_pairs={{0,1},{1,2},{2,3},{3,0},{4,5},{5,6},{6,7},{7,4},{8,9},{9,10},{10,1... | collective-permute-start | bytes 49160 | tf_op jit(solution)/shard_map/ppermute | solution.py:16
  64.8 5.5 %collective-permute-start.19 = (f32[16,256]{1,0:T(8,128)S(1)}, f32[16,256]{1,0:T(8,128)S(1)}, u32[]{:S(2)}, u32[]{:S(2)}) collective-permute-start(f32[16,256]{1,0:T(8,128)S(1)} %get-tuple-element.11), channel_id=1, source_target_pairs={{0,3},{1,0},{2,1},{3,2},{4,7},{5,4},{6,5},{7,6},{8,11},{9,8},{10,9... | collective-permute-start | bytes 49160 | tf_op jit(solution)/shard_map/ppermute | solution.py:16
  68.6 4.6 %collective-permute-start.18 = (f32[16,256]{1,0:T(8,128)S(1)}, f32[16,256]{1,0:T(8,128)S(1)}, u32[]{:S(2)}, u32[]{:S(2)}) collective-permute-start(f32[16,256]{1,0:T(8,128)S(1)} %get-tuple-element.12), channel_id=1, source_target_pairs={{0,2},{1,3},{2,0},{3,1},{4,6},{5,7},{6,4},{7,5},{8,10},{9,11},{10,... | collective-permute-start | bytes 49160 | tf_op jit(solution)/shard_map/ppermute | solution.py:16

commit v2 on v1

--- a/solution.py
+++ b/solution.py
@@ -79,37 +79,55 @@
     return scores.T
 
 
+def layer_gradient(activations, cotangents, live_mask, project_in, project_out, layer):
+    acts = lax.dynamic_index_in_dim(activations, layer, 0, keepdims=False)
+    cots = lax.dynamic_index_in_dim(cotangents, layer, 0, keepdims=False)
+    w_in = lax.dynamic_index_in_dim(project_in, layer, 0, keepdims=False)
+    w_out = lax.dynamic_index_in_dim(project_out, layer, 0, keepdims=False)
+    left_factor = jnp.einsum(
+        "esd,kd->esk", acts, w_in, preferred_element_type=jnp.float32
+    ).astype(jnp.bfloat16)
+    right_factor = jnp.einsum(
+        "esd,kd->esk", cots, w_out, preferred_element_type=jnp.float32
+    )
+    right_factor = jnp.where(live_mask[:, :, None], right_factor, 0.0).astype(jnp.bfloat16)
+    grad = jnp.einsum(
+        "esj,esc->ejc", right_factor, left_factor, preferred_element_type=jnp.float32
+    )
+    return grad.reshape(grad.shape[0], -1)
+
+
 def body_direct(activations, cotangents, lengths, project_in, project_out, preconditioner, queries):
     layer_count = activations.shape[0]
     tokens_here = activations.shape[2]
-    factor_size = project_in.shape[1]
-    block_size = factor_size * factor_size
     width_dp = lax.axis_size("dp")
+    dp_place = lax.axis_index("dp")
     mp_place = lax.axis_index("mp")
     positions = mp_place * tokens_here + jnp.arange(tokens_here, dtype=jnp.int32)
     live_mask = positions[None, :] < lengths[:, None]
-    left_factor = jnp.einsum(
-        "lesd,lkd->lesk", activations, project_in, preferred_element_type=jnp.float32
-    ).astype(jnp.bfloat16)
-    right_factor = jnp.einsum(
-        "lesd,lkd->lesk", cotangents, project_out, preferred_element_type=jnp.float32
-    )
-    right_factor = jnp.where(live_mask[None, :, :, None], right_factor, 0.0).astype(jnp.bfloat16)
-    partial_grad = jnp.einsum(
-        "lesj,lesc->eljc", right_factor, left_factor, preferred_element_type=jnp.float32
-    )
-    partial_grad = partial_grad.reshape(partial_grad.shape[0], layer_count * block_size)
-    grad_mine = reduce_scatter_direct(partial_grad, "mp", 1).astype(jnp.bfloat16)
-    grad_all = all_gather_direct(grad_mine, "dp")
+    grad_args = (activations, cotangents, live_mask, project_in, project_out)
+    received = []
+    for shift in range(1, layer_count):
+        grad = layer_gradient(*grad_args, (mp_place + shift) % layer_count)
+        received.append(shifted(grad, "mp", shift))
+    grad_mine = layer_gradient(*grad_args, mp_place)
+    for grad in received:
+        grad_mine = grad_mine + grad
+    grad_all = all_gather_direct(grad_mine.astype(jnp.bfloat16), "dp")
     grad_all = grad_all.reshape(-1, grad_all.shape[-1])
     pre_part = jnp.dot(grad_all, preconditioner, preferred_element_type=jnp.float32)
-    pre_all = all_gather_direct(pre_part, "dp")
-    pre_all = jnp.transpose(pre_all, (1, 0, 2)).reshape(pre_all.shape[1], -1)
-    upper_grad, lower_grad = split_parts(pre_all)
+    upper_grad, lower_grad = split_parts(pre_part)
     both = jnp.concatenate([upper_grad, lower_grad], axis=0)
-    products = lax.dot_general(
-        both, queries, (((1,), (1,)), ((), ())), preferred_element_type=jnp.float32
-    )
+    block = both.shape[1]
+    products = None
+    for shift in range(width_dp):
+        got = both if shift == 0 else shifted(both, "dp", shift)
+        source = (dp_place - shift) % width_dp
+        columns = lax.dynamic_slice_in_dim(queries, source * block, block, 1)
+        term = lax.dot_general(
+            got, columns, (((1,), (1,)), ((), ())), preferred_element_type=jnp.float32
+        )
+        products = term if products is None else products + term
     examples = upper_grad.shape[0]
     partial_scores = products[:examples] + products[examples:]
     return reduce_scatter_direct(partial_scores, "mp", 1)

time: 74.1 us -> 80.7 us (1.089)
  matrix products: 26.8 us -> 45.4 us
  waiting for transfers between devices: 19.5 us -> 6.31 us
    dot_general x3 -> x16, matrix products: 24 us -> 42.6 us  [the longest x4 15.3 us: layer_gradient(): jnp.einsum('esj,esc->ejc', right_factor, left_factor, preferred_element_t...]
    ppermute x20, waiting for transfers between devices: 19.5 us -> 6.31 us  [shifted(): return lax.ppermute(x, axis, [(i, (i + shift) % n) for i in range(n)])]
  transfers between devices with their start and end apart: 20 -> 20, of which waited for: 9 -> 6; matrix products, arithmetic and copies ran while one was open for 0% -> 42% of each run, Pallas kernels for 0% -> 0%
where the time goes in v2:
time: 80.7 us; the launch traced here: 80.1 us
  matrix products  45.4 us (56%)
  starting transfers between devices  24.9 us (31%)
  waiting for transfers between devices  6.31 us (8%)
  local copies, waits for them, and re-layouts  1.62 us (2%)
  other arithmetic  1.56 us (2%)
    ppermute x20, starting transfers between devices, shifted(): return lax.ppermute(x, axis, [(i, (i + shift) % n) for i in range(n)])  24.9 us
    dot_general x4, matrix products, layer_gradient(): jnp.einsum('esj,esc->ejc', right_factor, left_factor, preferred_element_t...  15.3 us
    dot_general x4, matrix products, layer_gradient(): jnp.einsum('esd,kd->esk', acts, w_in, preferred_element_type=jnp.float32)  14.3 us
    dot_general x8, matrix products, body_direct(): lax.dot_general(got, columns, (((1,), (1,)), ((), ())), preferred_element...  13 us
    ppermute x20, waiting for transfers between devices, shifted(): return lax.ppermute(x, axis, [(i, (i + shift) % n) for i in range(n)])  6.31 us
    dot_general x1, matrix products, body_direct(): jnp.dot(grad_all, preconditioner, preferred_element_type=jnp.float32)  2.83 us
  transfers between devices with their start and end apart: 20, of which 6 were waited for; matrix products, arithmetic and copies ran while one was open for 42% of the time, Pallas kernels for 0%

profile of v2, /device:TPU:0, one launch (start us, length us, event | category | flops | bytes accessed | tf_op | source)
XLA Modules:
  0.0 80.1 jit_solution(18347008098822261588)
XLA Ops:
  0.0 0.9 %broadcast_compare_fusion = pred[2,256]{1,0:T(4,128)(4,1)S(1)} fusion(s32[256]{0:T(256)S(1)} %iota_add_fusion, s32[2]{0:T(128)} %param.9), kind=kLoop, calls=%fused_computation.126 | loop fusion | flops 512 | bytes 1544 | tf_op jit(solution)/shard_map/lt | solution.py:107
  0.9 0.7 copy-done
  1.6 3.6 %fusion.56 = bf16[2,256,64]{1,2,0:T(8,128)(2,1)S(1)} fusion(bf16[4,2,256,4096]{3,2,1,0:T(8,128)(2,1)} %param.7, s32[]{:T(128)S(6)} %select_n.138, bf16[4,64,4096]{2,1,0:T(8,128)(2,1)S(1)} %copy-done), kind=kOutput, calls=%fused_computation.40 | convolution fusion | flops 268468224 | bytes 4785152 | tf_op jit(solution)/shard_map/esd,kd->esk/dot_general | solution.py:87
  5.2 3.8 %fusion.69 = f32[2,64,64]{2,1,0:T(8,128)S(1)} fusion(bf16[2,256,64]{1,2,0:T(8,128)(2,1)S(1)} %fusion.56, bf16[4,2,256,4096]{3,2,1,0:T(8,128)(2,1)} %param.8, s32[]{:T(128)S(6)} %select_n.138, bf16[4,64,4096]{2,1,0:T(8,128)(2,1)} %param.11, pred[2,256]{1,0:T(4,128)(4,1)S(1)} %broadcast_compare_fusion), kind=kOutput, calls=%fused_computation.44 | convolution fusion | flops 272695296 | bytes 4818432 | tf_op jit(solution)/shard_map/esj,esc->ejc/dot_general | solution.py:94
  9.0 0.1 reshape.48
  9.1 3.1 %collective-permute-start = (f32[2,4096]{1,0:T(2,128)S(1)}, f32[2,4096]{1,0:T(2,128)S(1)}, u32[]{:S(2)}, u32[]{:S(2)}) collective-permute-start(f32[2,4096]{1,0:T(2,128)S(1)} %reshape.48), channel_id=1, source_target_pairs={{0,1},{1,2},{2,3},{3,0},{4,5},{5,6},{6,7},{7,4},{8,9},{9,10},{10,1... | collective-permute-start | bytes 98312 | tf_op jit(solution)/shard_map/ppermute | solution.py:16
  12.2 3.6 %fusion.59 = bf16[2,256,64]{1,2,0:T(8,128)(2,1)S(1)} fusion(bf16[4,2,256,4096]{3,2,1,0:T(8,128)(2,1)} %param.7, s32[]{:T(128)S(6)} %select_n.141, bf16[4,64,4096]{2,1,0:T(8,128)(2,1)S(1)} %copy-done), kind=kOutput, calls=%fused_computation.41 | convolution fusion | flops 268468224 | bytes 4785152 | tf_op jit(solution)/shard_map/esd,kd->esk/dot_general | solution.py:87
  15.8 3.8 %fusion.72 = f32[2,64,64]{2,1,0:T(8,128)S(1)} fusion(bf16[2,256,64]{1,2,0:T(8,128)(2,1)S(1)} %fusion.59, bf16[4,2,256,4096]{3,2,1,0:T(8,128)(2,1)} %param.8, s32[]{:T(128)S(6)} %select_n.141, bf16[4,64,4096]{2,1,0:T(8,128)(2,1)} %param.11, pred[2,256]{1,0:T(4,128)(4,1)S(1)} %broadcast_compare_fusion), kind=kOutput, calls=%fused_computation.45 | convolution fusion | flops 272695296 | bytes 4818432 | tf_op jit(solution)/shard_map/esj,esc->ejc/dot_general | solution.py:94
  19.6 0.1 reshape.49
  19.7 2.7 %collective-permute-start.1 = (f32[2,4096]{1,0:T(2,128)S(1)}, f32[2,4096]{1,0:T(2,128)S(1)}, u32[]{:S(2)}, u32[]{:S(2)}) collective-permute-start(f32[2,4096]{1,0:T(2,128)S(1)} %reshape.49), channel_id=1, source_target_pairs={{0,2},{1,3},{2,0},{3,1},{4,6},{5,7},{6,4},{7,5},{8,10},{9,11},{10,... | collective-permute-start | bytes 98312 | tf_op jit(solution)/shard_map/ppermute | solution.py:16
  22.4 3.6 %fusion.62 = bf16[2,256,64]{1,2,0:T(8,128)(2,1)S(1)} fusion(bf16[4,2,256,4096]{3,2,1,0:T(8,128)(2,1)} %param.7, s32[]{:T(128)S(6)} %select_n.144, bf16[4,64,4096]{2,1,0:T(8,128)(2,1)S(1)} %copy-done), kind=kOutput, calls=%fused_computation.42 | convolution fusion | flops 268468224 | bytes 4785152 | tf_op jit(solution)/shard_map/esd,kd->esk/dot_general | solution.py:87
  25.9 3.8 %fusion.75 = f32[2,64,64]{2,1,0:T(8,128)S(1)} fusion(bf16[2,256,64]{1,2,0:T(8,128)(2,1)S(1)} %fusion.62, bf16[4,2,256,4096]{3,2,1,0:T(8,128)(2,1)} %param.8, s32[]{:T(128)S(6)} %select_n.144, bf16[4,64,4096]{2,1,0:T(8,128)(2,1)} %param.11, pred[2,256]{1,0:T(4,128)(4,1)S(1)} %broadcast_compare_fusion), kind=kOutput, calls=%fused_computation.46 | convolution fusion | flops 272695296 | bytes 4818432 | tf_op jit(solution)/shard_map/esj,esc->ejc/dot_general | solution.py:94
  29.8 0.1 reshape.50
  29.9 1.4 %collective-permute-start.2 = (f32[2,4096]{1,0:T(2,128)S(1)}, f32[2,4096]{1,0:T(2,128)S(1)}, u32[]{:S(2)}, u32[]{:S(2)}) collective-permute-start(f32[2,4096]{1,0:T(2,128)S(1)} %reshape.50), channel_id=1, source_target_pairs={{0,3},{1,0},{2,1},{3,2},{4,7},{5,4},{6,5},{7,6},{8,11},{9,8},{10,9... | collective-permute-start | bytes 98312 | tf_op jit(solution)/shard_map/ppermute | solution.py:16
  31.3 3.6 %fusion.53 = bf16[2,256,64]{1,2,0:T(8,128)(2,1)S(1)} fusion(bf16[4,2,256,4096]{3,2,1,0:T(8,128)(2,1)} %param.7, s32[]{:T(128)S(6)} %select_n.135, bf16[4,64,4096]{2,1,0:T(8,128)(2,1)S(1)} %copy-done), kind=kOutput, calls=%fused_computation.39 | convolution fusion | flops 268468224 | bytes 4785152 | tf_op jit(solution)/shard_map/esd,kd->esk/dot_general | solution.py:87
  34.8 3.8 %fusion.66 = f32[2,64,64]{2,1,0:T(8,128)S(1)} fusion(bf16[2,256,64]{1,2,0:T(8,128)(2,1)S(1)} %fusion.53, bf16[4,2,256,4096]{3,2,1,0:T(8,128)(2,1)} %param.8, s32[]{:T(128)S(6)} %select_n.135, bf16[4,64,4096]{2,1,0:T(8,128)(2,1)} %param.11, pred[2,256]{1,0:T(4,128)(4,1)S(1)} %broadcast_compare_fusion), kind=kOutput, calls=%fused_computation.43 | convolution fusion | flops 272695296 | bytes 4818432 | tf_op jit(solution)/shard_map/esj,esc->ejc/dot_general | solution.py:94
  38.7 0.1 reshape.47
  38.8 1.1 %collective-permute-start.3 = (bf16[2,4096]{1,0:T(2,128)(2,1)S(1)}, bf16[2,4096]{1,0:T(2,128)(2,1)S(1)}, u32[]{:S(2)}, u32[]{:S(2)}) collective-permute-start(bf16[2,4096]{1,0:T(2,128)(2,1)S(1)} %get-tuple-element.6), channel_id=1, source_target_pairs={{0,28},{4,0},{8,4},{12,8},{16,12},{20,16},{24,20},{28,24},{1,29},{... | collective-permute-start | bytes 49160 | tf_op jit(solution)/shard_map/ppermute | solution.py:16
  39.9 1.7 %collective-permute-start.4 = (bf16[2,4096]{1,0:T(2,128)(2,1)S(1)}, bf16[2,4096]{1,0:T(2,128)(2,1)S(1)}, u32[]{:S(2)}, u32[]{:S(2)}) collective-permute-start(bf16[2,4096]{1,0:T(2,128)(2,1)S(1)} %get-tuple-element.6), channel_id=1, source_target_pairs={{0,24},{4,28},{8,0},{12,4},{16,8},{20,12},{24,16},{28,20},{1,25},{... | collective-permute-start | bytes 49160 | tf_op jit(solution)/shard_map/ppermute | solution.py:16
  41.7 1.5 %collective-permute-start.6 = (bf16[2,4096]{1,0:T(2,128)(2,1)S(1)}, bf16[2,4096]{1,0:T(2,128)(2,1)S(1)}, u32[]{:S(2)}, u32[]{:S(2)}) collective-permute-start(bf16[2,4096]{1,0:T(2,128)(2,1)S(1)} %get-tuple-element.6), channel_id=1, source_target_pairs={{0,16},{4,20},{8,24},{12,28},{16,0},{20,4},{24,8},{28,12},{1,17},{... | collective-permute-start | bytes 49160 | tf_op jit(solution)/shard_map/ppermute | solution.py:16
  43.2 0.4 collective-permute-start.7
  43.6 1.5 %collective-permute-start.8 = (bf16[2,4096]{1,0:T(2,128)(2,1)S(1)}, bf16[2,4096]{1,0:T(2,128)(2,1)S(1)}, u32[]{:S(2)}, u32[]{:S(2)}) collective-permute-start(bf16[2,4096]{1,0:T(2,128)(2,1)S(1)} %get-tuple-element.6), channel_id=1, source_target_pairs={{0,8},{4,12},{8,16},{12,20},{16,24},{20,28},{24,0},{28,4},{1,9},{5... | collective-permute-start | bytes 49160 | tf_op jit(solution)/shard_map/ppermute | solution.py:16
  45.2 0.2 collective-permute-done.6
  45.4 0.9 %collective-permute-done.7 = bf16[2,4096]{1,0:T(2,128)(2,1)S(1)} collective-permute-done((bf16[2,4096]{1,0:T(2,128)(2,1)S(1)}, bf16[2,4096]{1,0:T(2,128)(2,1)S(1)}, u32[]{:S(2)}, u32[]{:S(2)}) %collective-permute-start.7) | collective-permute-done | bytes 16416 | tf_op jit(solution)/shard_map/ppermute | solution.py:16
  46.4 1.8 %collective-permute-done.8 = bf16[2,4096]{1,0:T(2,128)(2,1)S(1)} collective-permute-done((bf16[2,4096]{1,0:T(2,128)(2,1)S(1)}, bf16[2,4096]{1,0:T(2,128)(2,1)S(1)}, u32[]{:S(2)}, u32[]{:S(2)}) %collective-permute-start.8) | collective-permute-done | bytes 16416 | tf_op jit(solution)/shard_map/ppermute | solution.py:16
  48.2 1.0 %collective-permute-done.9 = bf16[2,4096]{1,0:T(2,128)(2,1)S(1)} collective-permute-done((bf16[2,4096]{1,0:T(2,128)(2,1)S(1)}, bf16[2,4096]{1,0:T(2,128)(2,1)S(1)}, u32[]{:S(2)}, u32[]{:S(2)}) %collective-permute-start.9) | collective-permute-done | bytes 16416 | tf_op jit(solution)/shard_map/ppermute | solution.py:16
  49.4 0.1 constant_dynamic-slice_fusion
  49.6 2.8 %fusion.147 = (bf16[16,512]{1,0:T(8,128)(2,1)S(1)}, f32[16,512]{1,0:T(8,128)S(1)}) fusion(bf16[16,4096]{1,0:T(8,128)(2,1)S(1)} %reshape.51, bf16[4096,512]{1,0:T(8,128)(2,1)} %param.12), kind=kOutput, calls=%fused_computation.132 | convolution fusion | flops 67117056 | bytes 4374528 | tf_op jit(solution)/shard_map/dot_general | solution.py:118
  52.5 0.8 %collective-permute-start.14 = (bf16[32,512]{1,0:T(8,128)(2,1)S(1)}, bf16[32,512]{1,0:T(8,128)(2,1)S(1)}, u32[]{:S(2)}, u32[]{:S(2)}) collective-permute-start(bf16[32,512]{1,0:T(8,128)(2,1)S(1)} %pad_maximum_fusion), channel_id=1, source_target_pairs={{0,20},{4,24},{8,28},{12,0},{16,4},{20,8},{24,12},{28,16},{1,21},{... | collective-permute-start | bytes 98312 | tf_op jit(solution)/shard_map/ppermute | solution.py:16
  53.4 1.5 %collective-permute-start.13 = (bf16[32,512]{1,0:T(8,128)(2,1)S(1)}, bf16[32,512]{1,0:T(8,128)(2,1)S(1)}, u32[]{:S(2)}, u32[]{:S(2)}) collective-permute-start(bf16[32,512]{1,0:T(8,128)(2,1)S(1)} %pad_maximum_fusion), channel_id=1, source_target_pairs={{0,16},{4,20},{8,24},{12,28},{16,0},{20,4},{24,8},{28,12},{1,17},{... | collective-permute-start | bytes 98312 | tf_op jit(solution)/shard_map/ppermute | solution.py:16
  54.9 0.6 collective-permute-start.12
  55.5 1.7 %collective-permute-start.15 = (bf16[32,512]{1,0:T(8,128)(2,1)S(1)}, bf16[32,512]{1,0:T(8,128)(2,1)S(1)}, u32[]{:S(2)}, u32[]{:S(2)}) collective-permute-start(bf16[32,512]{1,0:T(8,128)(2,1)S(1)} %pad_maximum_fusion), channel_id=1, source_target_pairs={{0,24},{4,28},{8,0},{12,4},{16,8},{20,12},{24,16},{28,20},{1,25},{... | collective-permute-start | bytes 98312 | tf_op jit(solution)/shard_map/ppermute | solution.py:16
  57.2 1.6 %fusion.89 = f32[32,1024]{1,0:T(8,128)S(1)} fusion(bf16[1024,4096]{1,0:T(8,128)(2,1)} %param.13, s32[]{:T(128)S(6)} %select_n.149, bf16[16,512]{1,0:T(8,128)(2,1)S(1)} %subtract_convert_fusion, bf16[16,512]{1,0:T(8,128)(2,1)S(1)} %get-tuple-element.10), kind=kOutput, calls=%fused_computation.59 | convolution fusion | flops 33619968 | bytes 1212420 | tf_op jit(solution)/shard_map/dot_general | solution.py:127
  58.9 1.1 %collective-permute-start.16 = (bf16[32,512]{1,0:T(8,128)(2,1)S(1)}, bf16[32,512]{1,0:T(8,128)(2,1)S(1)}, u32[]{:S(2)}, u32[]{:S(2)}) collective-permute-start(bf16[32,512]{1,0:T(8,128)(2,1)S(1)} %pad_maximum_fusion), channel_id=1, source_target_pairs={{0,28},{4,0},{8,4},{12,8},{16,12},{20,16},{24,20},{28,24},{1,29},{... | collective-permute-start | bytes 98312 | tf_op jit(solution)/shard_map/ppermute | solution.py:16
  59.9 1.6 %convolution_add_fusion.1 = f32[32,1024]{1,0:T(8,128)S(1)} fusion(f32[32,1024]{1,0:T(8,128)S(1)} %fusion.89, bf16[32,512]{1,0:T(8,128)(2,1)S(1)} %collective-permute-done.10, bf16[1024,4096]{1,0:T(8,128)(2,1)} %param.13, s32[]{:T(128)S(6)} %select_n.151), kind=kOutput, calls=%fused_computation.29 | convolution fusion | flops 33587200 | bytes 1343492 | tf_op jit(solution)/shard_map/dot_general | solution.py:127
  61.6 1.8 %collective-permute-start.11 = (bf16[32,512]{1,0:T(8,128)(2,1)S(1)}, bf16[32,512]{1,0:T(8,128)(2,1)S(1)}, u32[]{:S(2)}, u32[]{:S(2)}) collective-permute-start(bf16[32,512]{1,0:T(8,128)(2,1)S(1)} %pad_maximum_fusion), channel_id=1, source_target_pairs={{0,8},{4,12},{8,16},{12,20},{16,24},{20,28},{24,0},{28,4},{1,9},{5... | collective-permute-start | bytes 98312 | tf_op jit(solution)/shard_map/ppermute | solution.py:16
  63.4 1.6 %fusion.81 = f32[32,1024]{1,0:T(8,128)S(1)} fusion(bf16[32,512]{1,0:T(8,128)(2,1)S(1)} %collective-permute-done.14, bf16[1024,4096]{1,0:T(8,128)(2,1)} %param.13, s32[]{:T(128)S(6)} %select_n.159), kind=kOutput, calls=%fused_computation.51 | convolution fusion | flops 33554432 | bytes 1212420 | tf_op jit(solution)/shard_map/dot_general | solution.py:127
  65.0 1.6 %fusion.83 = f32[32,1024]{1,0:T(8,128)S(1)} fusion(bf16[32,512]{1,0:T(8,128)(2,1)S(1)} %collective-permute-done.13, bf16[1024,4096]{1,0:T(8,128)(2,1)} %param.13, s32[]{:T(128)S(6)} %select_n.157), kind=kOutput, calls=%fused_computation.53 | convolution fusion | flops 33554432 | bytes 1212420 | tf_op jit(solution)/shard_map/dot_general | solution.py:127
  66.7 1.6 %fusion.85 = f32[32,1024]{1,0:T(8,128)S(1)} fusion(bf16[32,512]{1,0:T(8,128)(2,1)S(1)} %collective-permute-done.12, bf16[1024,4096]{1,0:T(8,128)(2,1)} %param.13, s32[]{:T(128)S(6)} %select_n.155), kind=kOutput, calls=%fused_computation.55 | convolution fusion | flops 33554432 | bytes 1212420 | tf_op jit(solution)/shard_map/dot_general | solution.py:127
  68.3 1.6 %fusion.79 = f32[32,1024]{1,0:T(8,128)S(1)} fusion(bf16[32,512]{1,0:T(8,128)(2,1)S(1)} %collective-permute-done.15, bf16[1024,4096]{1,0:T(8,128)(2,1)} %param.13, s32[]{:T(128)S(6)} %select_n.161), kind=kOutput, calls=%fused_computation.49 | convolution fusion | flops 33554432 | bytes 1212420 | tf_op jit(solution)/shard_map/dot_general | solution.py:127
  70.0 1.6 %fusion.77 = f32[32,1024]{1,0:T(8,128)S(1)} fusion(bf16[32,512]{1,0:T(8,128)(2,1)S(1)} %collective-permute-done.16, bf16[1024,4096]{1,0:T(8,128)(2,1)} %param.13, s32[]{:T(128)S(6)} %select_n.163), kind=kOutput, calls=%fused_computation.47 | convolution fusion | flops 33554432 | bytes 1212420 | tf_op jit(solution)/shard_map/dot_general | solution.py:127
  71.6 1.7 %fusion.40 = f32[32,1024]{1,0:T(8,128)S(1)} fusion(f32[32,1024]{1,0:T(8,128)S(1)} %fusion.77, f32[32,1024]{1,0:T(8,128)S(1)} %fusion.79, f32[32,1024]{1,0:T(8,128)S(1)} %fusion.81, f32[32,1024]{1,0:T(8,128)S(1)} %fusion.83, f32[32,1024]{1,0:T(8,128)S(1)} %fusion.85, f32[32,1024]{1,0:T(8,128)S(1)} %convolution_add_fusion.1, ...), kind=kOutput, calls=%fused_computation.34 | convolution fusion | flops 33751040 | bytes 1998852 | tf_op jit(solution)/shard_map/dot_general | solution.py:127
  73.3 0.7 collective-permute-start.17
  74.0 0.3 collective-permute-start.18
  74.4 2.8 %collective-permute-start.19 = (f32[16,256]{1,0:T(8,128)S(1)}, f32[16,256]{1,0:T(8,128)S(1)}, u32[]{:S(2)}, u32[]{:S(2)}) collective-permute-start(f32[16,256]{1,0:T(8,128)S(1)} %get-tuple-element.8), channel_id=1, source_target_pairs={{0,3},{1,0},{2,1},{3,2},{4,7},{5,4},{6,5},{7,6},{8,11},{9,8},{10,9... | collective-permute-start | bytes 49160 | tf_op jit(solution)/shard_map/ppermute | solution.py:16
  77.2 1.7 %collective-permute-done.17 = f32[16,256]{1,0:T(8,128)S(1)} collective-permute-done((f32[16,256]{1,0:T(8,128)S(1)}, f32[16,256]{1,0:T(8,128)S(1)}, u32[]{:S(2)}, u32[]{:S(2)}) %collective-permute-start.17) | collective-permute-done | bytes 16416 | tf_op jit(solution)/shard_map/ppermute | solution.py:16
  78.9 0.6 collective-permute-done.19
  79.5 0.6 add_add_fusion
  (40 shorter events, 0.8 us)
Async XLA Ops:
  0.0 1.6 %copy-start = (bf16[4,64,4096]{2,1,0:T(8,128)(2,1)S(1)}, bf16[4,64,4096]{2,1,0:T(8,128)(2,1)}, u32[]{:S(2)}) copy-start(bf16[4,64,4096]{2,1,0:T(8,128)(2,1)} %param.10) | copy-start | bytes 6291460
  9.1 29.7 %collective-permute-start = (f32[2,4096]{1,0:T(2,128)S(1)}, f32[2,4096]{1,0:T(2,128)S(1)}, u32[]{:S(2)}, u32[]{:S(2)}) collective-permute-start(f32[2,4096]{1,0:T(2,128)S(1)} %reshape.48), channel_id=1, source_target_pairs={{0,1},{1,2},{2,3},{3,0},{4,5},{5,6},{6,7},{7,4},{8,9},{9,10},{10,1... | collective-permute-start | bytes 98312 | tf_op jit(solution)/shard_map/ppermute | solution.py:16
  19.7 19.1 %collective-permute-start.1 = (f32[2,4096]{1,0:T(2,128)S(1)}, f32[2,4096]{1,0:T(2,128)S(1)}, u32[]{:S(2)}, u32[]{:S(2)}) collective-permute-start(f32[2,4096]{1,0:T(2,128)S(1)} %reshape.49), channel_id=1, source_target_pairs={{0,2},{1,3},{2,0},{3,1},{4,6},{5,7},{6,4},{7,5},{8,10},{9,11},{10,... | collective-permute-start | bytes 98312 | tf_op jit(solution)/shard_map/ppermute | solution.py:16
  29.9 8.9 %collective-permute-start.2 = (f32[2,4096]{1,0:T(2,128)S(1)}, f32[2,4096]{1,0:T(2,128)S(1)}, u32[]{:S(2)}, u32[]{:S(2)}) collective-permute-start(f32[2,4096]{1,0:T(2,128)S(1)} %reshape.50), channel_id=1, source_target_pairs={{0,3},{1,0},{2,1},{3,2},{4,7},{5,4},{6,5},{7,6},{8,11},{9,8},{10,9... | collective-permute-start | bytes 98312 | tf_op jit(solution)/shard_map/ppermute | solution.py:16
  38.8 4.7 %collective-permute-start.3 = (bf16[2,4096]{1,0:T(2,128)(2,1)S(1)}, bf16[2,4096]{1,0:T(2,128)(2,1)S(1)}, u32[]{:S(2)}, u32[]{:S(2)}) collective-permute-start(bf16[2,4096]{1,0:T(2,128)(2,1)S(1)} %get-tuple-element.6), channel_id=1, source_target_pairs={{0,28},{4,0},{8,4},{12,8},{16,12},{20,16},{24,20},{28,24},{1,29},{... | collective-permute-start | bytes 49160 | tf_op jit(solution)/shard_map/ppermute | solution.py:16
  39.9 5.2 %collective-permute-start.4 = (bf16[2,4096]{1,0:T(2,128)(2,1)S(1)}, bf16[2,4096]{1,0:T(2,128)(2,1)S(1)}, u32[]{:S(2)}, u32[]{:S(2)}) collective-permute-start(bf16[2,4096]{1,0:T(2,128)(2,1)S(1)} %get-tuple-element.6), channel_id=1, source_target_pairs={{0,24},{4,28},{8,0},{12,4},{16,8},{20,12},{24,16},{28,20},{1,25},{... | collective-permute-start | bytes 49160 | tf_op jit(solution)/shard_map/ppermute | solution.py:16
  41.6 3.6 %collective-permute-start.5 = (bf16[2,4096]{1,0:T(2,128)(2,1)S(1)}, bf16[2,4096]{1,0:T(2,128)(2,1)S(1)}, u32[]{:S(2)}, u32[]{:S(2)}) collective-permute-start(bf16[2,4096]{1,0:T(2,128)(2,1)S(1)} %get-tuple-element.6), channel_id=1, source_target_pairs={{0,20},{4,24},{8,28},{12,0},{16,4},{20,8},{24,12},{28,16},{1,21},{... | collective-permute-start | bytes 49160 | tf_op jit(solution)/shard_map/ppermute | solution.py:16
  41.7 3.7 %collective-permute-start.6 = (bf16[2,4096]{1,0:T(2,128)(2,1)S(1)}, bf16[2,4096]{1,0:T(2,128)(2,1)S(1)}, u32[]{:S(2)}, u32[]{:S(2)}) collective-permute-start(bf16[2,4096]{1,0:T(2,128)(2,1)S(1)} %get-tuple-element.6), channel_id=1, source_target_pairs={{0,16},{4,20},{8,24},{12,28},{16,0},{20,4},{24,8},{28,12},{1,17},{... | collective-permute-start | bytes 49160 | tf_op jit(solution)/shard_map/ppermute | solution.py:16
  43.2 3.2 %collective-permute-start.7 = (bf16[2,4096]{1,0:T(2,128)(2,1)S(1)}, bf16[2,4096]{1,0:T(2,128)(2,1)S(1)}, u32[]{:S(2)}, u32[]{:S(2)}) collective-permute-start(bf16[2,4096]{1,0:T(2,128)(2,1)S(1)} %get-tuple-element.6), channel_id=1, source_target_pairs={{0,12},{4,16},{8,20},{12,24},{16,28},{20,0},{24,4},{28,8},{1,13},{... | collective-permute-start | bytes 49160 | tf_op jit(solution)/shard_map/ppermute | solution.py:16
  43.6 4.6 %collective-permute-start.8 = (bf16[2,4096]{1,0:T(2,128)(2,1)S(1)}, bf16[2,4096]{1,0:T(2,128)(2,1)S(1)}, u32[]{:S(2)}, u32[]{:S(2)}) collective-permute-start(bf16[2,4096]{1,0:T(2,128)(2,1)S(1)} %get-tuple-element.6), channel_id=1, source_target_pairs={{0,8},{4,12},{8,16},{12,20},{16,24},{20,28},{24,0},{28,4},{1,9},{5... | collective-permute-start | bytes 49160 | tf_op jit(solution)/shard_map/ppermute | solution.py:16
  45.1 4.1 %collective-permute-start.9 = (bf16[2,4096]{1,0:T(2,128)(2,1)S(1)}, bf16[2,4096]{1,0:T(2,128)(2,1)S(1)}, u32[]{:S(2)}, u32[]{:S(2)}) collective-permute-start(bf16[2,4096]{1,0:T(2,128)(2,1)S(1)} %get-tuple-element.6), channel_id=1, source_target_pairs={{0,4},{4,8},{8,12},{12,16},{16,20},{20,24},{24,28},{28,0},{1,5},{5... | collective-permute-start | bytes 49160 | tf_op jit(solution)/shard_map/ppermute | solution.py:16
  52.5 6.4 %collective-permute-start.10 = (bf16[32,512]{1,0:T(8,128)(2,1)S(1)}, bf16[32,512]{1,0:T(8,128)(2,1)S(1)}, u32[]{:S(2)}, u32[]{:S(2)}) collective-permute-start(bf16[32,512]{1,0:T(8,128)(2,1)S(1)} %pad_maximum_fusion), channel_id=1, source_target_pairs={{0,4},{4,8},{8,12},{12,16},{16,20},{20,24},{24,28},{28,0},{1,5},{5... | collective-permute-start | bytes 98312 | tf_op jit(solution)/shard_map/ppermute | solution.py:16
  52.5 9.0 %collective-permute-start.14 = (bf16[32,512]{1,0:T(8,128)(2,1)S(1)}, bf16[32,512]{1,0:T(8,128)(2,1)S(1)}, u32[]{:S(2)}, u32[]{:S(2)}) collective-permute-start(bf16[32,512]{1,0:T(8,128)(2,1)S(1)} %pad_maximum_fusion), channel_id=1, source_target_pairs={{0,20},{4,24},{8,28},{12,0},{16,4},{20,8},{24,12},{28,16},{1,21},{... | collective-permute-start | bytes 98312 | tf_op jit(solution)/shard_map/ppermute | solution.py:16
  53.4 11.6 %collective-permute-start.13 = (bf16[32,512]{1,0:T(8,128)(2,1)S(1)}, bf16[32,512]{1,0:T(8,128)(2,1)S(1)}, u32[]{:S(2)}, u32[]{:S(2)}) collective-permute-start(bf16[32,512]{1,0:T(8,128)(2,1)S(1)} %pad_maximum_fusion), channel_id=1, source_target_pairs={{0,16},{4,20},{8,24},{12,28},{16,0},{20,4},{24,8},{28,12},{1,17},{... | collective-permute-start | bytes 98312 | tf_op jit(solution)/shard_map/ppermute | solution.py:16
  54.9 11.8 %collective-permute-start.12 = (bf16[32,512]{1,0:T(8,128)(2,1)S(1)}, bf16[32,512]{1,0:T(8,128)(2,1)S(1)}, u32[]{:S(2)}, u32[]{:S(2)}) collective-permute-start(bf16[32,512]{1,0:T(8,128)(2,1)S(1)} %pad_maximum_fusion), channel_id=1, source_target_pairs={{0,12},{4,16},{8,20},{12,24},{16,28},{20,0},{24,4},{28,8},{1,13},{... | collective-permute-start | bytes 98312 | tf_op jit(solution)/shard_map/ppermute | solution.py:16
  55.5 12.8 %collective-permute-start.15 = (bf16[32,512]{1,0:T(8,128)(2,1)S(1)}, bf16[32,512]{1,0:T(8,128)(2,1)S(1)}, u32[]{:S(2)}, u32[]{:S(2)}) collective-permute-start(bf16[32,512]{1,0:T(8,128)(2,1)S(1)} %pad_maximum_fusion), channel_id=1, source_target_pairs={{0,24},{4,28},{8,0},{12,4},{16,8},{20,12},{24,16},{28,20},{1,25},{... | collective-permute-start | bytes 98312 | tf_op jit(solution)/shard_map/ppermute | solution.py:16
  58.9 11.1 %collective-permute-start.16 = (bf16[32,512]{1,0:T(8,128)(2,1)S(1)}, bf16[32,512]{1,0:T(8,128)(2,1)S(1)}, u32[]{:S(2)}, u32[]{:S(2)}) collective-permute-start(bf16[32,512]{1,0:T(8,128)(2,1)S(1)} %pad_maximum_fusion), channel_id=1, source_target_pairs={{0,28},{4,0},{8,4},{12,8},{16,12},{20,16},{24,20},{28,24},{1,29},{... | collective-permute-start | bytes 98312 | tf_op jit(solution)/shard_map/ppermute | solution.py:16
  61.6 10.0 %collective-permute-start.11 = (bf16[32,512]{1,0:T(8,128)(2,1)S(1)}, bf16[32,512]{1,0:T(8,128)(2,1)S(1)}, u32[]{:S(2)}, u32[]{:S(2)}) collective-permute-start(bf16[32,512]{1,0:T(8,128)(2,1)S(1)} %pad_maximum_fusion), channel_id=1, source_target_pairs={{0,8},{4,12},{8,16},{12,20},{16,24},{20,28},{24,0},{28,4},{1,9},{5... | collective-permute-start | bytes 98312 | tf_op jit(solution)/shard_map/ppermute | solution.py:16
  73.3 5.6 %collective-permute-start.17 = (f32[16,256]{1,0:T(8,128)S(1)}, f32[16,256]{1,0:T(8,128)S(1)}, u32[]{:S(2)}, u32[]{:S(2)}) collective-permute-start(f32[16,256]{1,0:T(8,128)S(1)} %get-tuple-element.7), channel_id=1, source_target_pairs={{0,1},{1,2},{2,3},{3,0},{4,5},{5,6},{6,7},{7,4},{8,9},{9,10},{10,1... | collective-permute-start | bytes 49160 | tf_op jit(solution)/shard_map/ppermute | solution.py:16
  74.0 4.9 %collective-permute-start.18 = (f32[16,256]{1,0:T(8,128)S(1)}, f32[16,256]{1,0:T(8,128)S(1)}, u32[]{:S(2)}, u32[]{:S(2)}) collective-permute-start(f32[16,256]{1,0:T(8,128)S(1)} %get-tuple-element.9), channel_id=1, source_target_pairs={{0,2},{1,3},{2,0},{3,1},{4,6},{5,7},{6,4},{7,5},{8,10},{9,11},{10,... | collective-permute-start | bytes 49160 | tf_op jit(solution)/shard_map/ppermute | solution.py:16
  74.4 5.1 %collective-permute-start.19 = (f32[16,256]{1,0:T(8,128)S(1)}, f32[16,256]{1,0:T(8,128)S(1)}, u32[]{:S(2)}, u32[]{:S(2)}) collective-permute-start(f32[16,256]{1,0:T(8,128)S(1)} %get-tuple-element.8), channel_id=1, source_target_pairs={{0,3},{1,0},{2,1},{3,2},{4,7},{5,4},{6,5},{7,6},{8,11},{9,8},{10,9... | collective-permute-start | bytes 49160 | tf_op jit(solution)/shard_map/ppermute | solution.py:16

commit v3 on v1

--- a/solution.py
+++ b/solution.py
@@ -34,6 +34,12 @@
     order = jnp.stack([got[(-k) % n] for k in range(n)])
     doubled = jnp.concatenate([order, order], axis=0)
     return lax.dynamic_slice_in_dim(doubled, (n - me) % n, n, 0)
+
+
+def all_gather_a2a(x, axis):
+    n = lax.axis_size(axis)
+    copies = jnp.broadcast_to(x[None], (n,) + x.shape)
+    return lax.all_to_all(copies, axis, 0, 0, tiled=True)
 
 
 def body_start(activations, cotangents, lengths, project_in, project_out, preconditioner, queries):
@@ -100,15 +106,16 @@
     )
     partial_grad = partial_grad.reshape(partial_grad.shape[0], layer_count * block_size)
     grad_mine = reduce_scatter_direct(partial_grad, "mp", 1).astype(jnp.bfloat16)
-    grad_all = all_gather_direct(grad_mine, "dp")
+    grad_all = all_gather_a2a(grad_mine, "dp")
     grad_all = grad_all.reshape(-1, grad_all.shape[-1])
     pre_part = jnp.dot(grad_all, preconditioner, preferred_element_type=jnp.float32)
-    pre_all = all_gather_direct(pre_part, "dp")
-    pre_all = jnp.transpose(pre_all, (1, 0, 2)).reshape(pre_all.shape[1], -1)
-    upper_grad, lower_grad = split_parts(pre_all)
+    upper_grad, lower_grad = split_parts(pre_part)
     both = jnp.concatenate([upper_grad, lower_grad], axis=0)
+    both_all = all_gather_a2a(both, "dp")
+    blocks, block = both_all.shape[0], both_all.shape[2]
+    query_blocks = queries.reshape(queries.shape[0], blocks, block)
     products = lax.dot_general(
-        both, queries, (((1,), (1,)), ((), ())), preferred_element_type=jnp.float32
+        both_all, query_blocks, (((0, 2), (1, 2)), ((), ())), preferred_element_type=jnp.float32
     )
     examples = upper_grad.shape[0]
     partial_scores = products[:examples] + products[examples:]

time: 74.1 us -> 68.6 us (0.926)
  starting transfers between devices: 24.2 us -> 13.4 us
  blocking collectives: 0 us -> 9.18 us
  waiting for transfers between devices: 19.5 us -> 15.3 us
    ppermute x20 -> x6, starting transfers between devices: 24.2 us -> 10 us  [shifted(): return lax.ppermute(x, axis, [(i, (i + shift) % n) for i in range(n)])]
    ppermute x20 -> x6, waiting for transfers between devices: 19.5 us -> 8.49 us  [shifted(): return lax.ppermute(x, axis, [(i, (i + shift) % n) for i in range(n)])]
    all_to_all x0 -> x1, blocking collectives: none -> 9.18 us  [all_gather_a2a(): return lax.all_to_all(copies, axis, 0, 0, tiled=True)]
    all_to_all x0 -> x1, waiting for transfers between devices: none -> 6.81 us  [all_gather_a2a(): return lax.all_to_all(copies, axis, 0, 0, tiled=True)]
    all_to_all x0 -> x1, starting transfers between devices: none -> 3.41 us  [all_gather_a2a(): return lax.all_to_all(copies, axis, 0, 0, tiled=True)]
    broadcast_in_dim x0 -> x2, local copies, waits for them, and re-layouts: none -> 0.8 us  [all_gather_a2a(): copies = jnp.broadcast_to(x[None], (n,) + x.shape)]
  transfers between devices with their start and end apart: 20 -> 7, of which waited for: 9 -> 6; matrix products, arithmetic and copies ran while one was open for 0% -> 0% of each run, Pallas kernels for 0% -> 0%
where the time goes in v3:
time: 68.6 us; the launch traced here: 68.2 us
  matrix products  26.8 us (39%)
  waiting for transfers between devices  15.3 us (22%)
  starting transfers between devices  13.4 us (20%)
  blocking collectives  9.18 us (13%)
  local copies, waits for them, and re-layouts  1.75 us (3%)
  other arithmetic  1.56 us (2%)
    ppermute x6, starting transfers between devices, shifted(): return lax.ppermute(x, axis, [(i, (i + shift) % n) for i in range(n)])  10 us
    dot_general x1, matrix products, body_direct(): jnp.einsum('lesj,lesc->eljc', right_factor, left_factor, preferred_elemen...  9.26 us
    all_to_all x1, blocking collectives, all_gather_a2a(): return lax.all_to_all(copies, axis, 0, 0, tiled=True)  9.18 us
    dot_general x1, matrix products, body_direct(): jnp.einsum('lesd,lkd->lesk', cotangents, project_out, preferred_element_t...  8.75 us
    ppermute x6, waiting for transfers between devices, shifted(): return lax.ppermute(x, axis, [(i, (i + shift) % n) for i in range(n)])  8.49 us
    all_to_all x1, waiting for transfers between devices, all_gather_a2a(): return lax.all_to_all(copies, axis, 0, 0, tiled=True)  6.81 us
    dot_general x1, matrix products, body_direct(): lax.dot_general(both_all, query_blocks, (((0, 2), (1, 2)), ((), ())), pre...  5.98 us
    all_to_all x1, starting transfers between devices, all_gather_a2a(): return lax.all_to_all(copies, axis, 0, 0, tiled=True)  3.41 us
  transfers between devices with their start and end apart: 7, of which 6 were waited for; matrix products, arithmetic and copies ran while one was open for 0% of the time, Pallas kernels for 0%

profile of v3, /device:TPU:0, one launch (start us, length us, event | category | flops | bytes accessed | tf_op | source)
XLA Modules:
  0.0 68.2 jit_solution(10341963617420715268)
XLA Ops:
  0.0 0.0 copy-start
  0.0 0.9 %broadcast_compare_fusion = pred[2,256]{1,0:T(4,128)(4,1)S(1)} fusion(s32[256]{0:T(256)S(1)} %iota_add_fusion, s32[2]{0:T(128)} %param.9), kind=kLoop, calls=%fused_computation.25 | loop fusion | flops 512 | bytes 1544 | tf_op jit(solution)/shard_map/lt | solution.py:96
  0.9 0.7 %copy-done = bf16[4,64,4096]{2,1,0:T(8,128)(2,1)S(1)} copy-done((bf16[4,64,4096]{2,1,0:T(8,128)(2,1)S(1)}, bf16[4,64,4096]{2,1,0:T(8,128)(2,1)}, u32[]{:S(2)}) %copy-start) | copy-done | bytes 2097176
  1.6 8.8 %fusion.19 = bf16[4,2,256,64]{2,3,0,1:T(8,128)(2,1)S(1)} fusion(bf16[4,64,4096]{2,1,0:T(8,128)(2,1)S(1)} %copy-done, bf16[4,2,256,4096]{3,2,1,0:T(8,128)(2,1)} %param.8, pred[2,256]{1,0:T(4,128)(4,1)S(1)} %broadcast_compare_fusion), kind=kOutput, calls=%fused_computation.11 | convolution fusion | flops 1074003968 | bytes 19137024 | tf_op jit(solution)/shard_map/lesd,lkd->lesk/dot_general | solution.py:100
  10.4 9.3 %fusion.29 = f32[2,4,64,64]{3,2,1,0:T(8,128)S(1)} fusion(bf16[4,2,256,64]{2,3,0,1:T(8,128)(2,1)S(1)} %fusion.19, bf16[4,64,4096]{2,1,0:T(8,128)(2,1)} %param.10, bf16[4,2,256,4096]{3,2,1,0:T(8,128)(2,1)} %param.7), kind=kOutput, calls=%fused_computation.13 | convolution fusion | flops 1090650112 | bytes 19267584 | tf_op jit(solution)/shard_map/lesj,lesc->eljc/dot_general | solution.py:104
  19.6 0.1 reshape.45
  19.8 3.1 %collective-permute-start = (f32[2,4096]{1,0:T(2,128)S(1)}, f32[2,4096]{1,0:T(2,128)S(1)}, u32[]{:S(2)}, u32[]{:S(2)}) collective-permute-start(f32[2,4096]{1,0:T(2,128)S(1)} %get-tuple-element.5), channel_id=1, source_target_pairs={{0,1},{1,2},{2,3},{3,0},{4,5},{5,6},{6,7},{7,4},{8,9},{9,10},{10,1... | collective-permute-start | bytes 98312 | tf_op jit(solution)/shard_map/ppermute | solution.py:16
  22.9 2.1 %collective-permute-start.2 = (f32[2,4096]{1,0:T(2,128)S(1)}, f32[2,4096]{1,0:T(2,128)S(1)}, u32[]{:S(2)}, u32[]{:S(2)}) collective-permute-start(f32[2,4096]{1,0:T(2,128)S(1)} %get-tuple-element.6), channel_id=1, source_target_pairs={{0,3},{1,0},{2,1},{3,2},{4,7},{5,4},{6,5},{7,6},{8,11},{9,8},{10,9... | collective-permute-start | bytes 98312 | tf_op jit(solution)/shard_map/ppermute | solution.py:16
  25.0 1.0 %collective-permute-start.1 = (f32[2,4096]{1,0:T(2,128)S(1)}, f32[2,4096]{1,0:T(2,128)S(1)}, u32[]{:S(2)}, u32[]{:S(2)}) collective-permute-start(f32[2,4096]{1,0:T(2,128)S(1)} %get-tuple-element.7), channel_id=1, source_target_pairs={{0,2},{1,3},{2,0},{3,1},{4,6},{5,7},{6,4},{7,5},{8,10},{9,11},{10,... | collective-permute-start | bytes 98312 | tf_op jit(solution)/shard_map/ppermute | solution.py:16
  26.0 0.9 %collective-permute-done = f32[2,4096]{1,0:T(2,128)S(1)} collective-permute-done((f32[2,4096]{1,0:T(2,128)S(1)}, f32[2,4096]{1,0:T(2,128)S(1)}, u32[]{:S(2)}, u32[]{:S(2)}) %collective-permute-start) | collective-permute-done | bytes 32800 | tf_op jit(solution)/shard_map/ppermute | solution.py:16
  26.9 0.3 collective-permute-done.2
  27.2 2.6 %collective-permute-done.1 = f32[2,4096]{1,0:T(2,128)S(1)} collective-permute-done((f32[2,4096]{1,0:T(2,128)S(1)}, f32[2,4096]{1,0:T(2,128)S(1)}, u32[]{:S(2)}, u32[]{:S(2)}) %collective-permute-start.1) | collective-permute-done | bytes 32800 | tf_op jit(solution)/shard_map/ppermute | solution.py:16
  29.9 0.1 broadcast_in_dim.18
  30.0 9.2 %all_to_all.10 = bf16[8,2,4096]{2,1,0:T(2,128)(2,1)S(1)} all-to-all(bf16[8,2,4096]{2,1,0:T(2,128)(2,1)S(1)} %broadcast_in_dim.18), channel_id=1, replica_groups=mesh['dp'=8,'mp'=4] {'dp'}, dimensions={0} | all-to-all | bytes 262144 | tf_op jit(solution)/shard_map/all_to_all | solution.py:42
  39.1 0.1 reshape.46
  39.2 2.8 %fusion.32 = (bf16[16,512]{1,0:T(8,128)(2,1)S(1)}, f32[16,512]{1,0:T(8,128)S(1)}) fusion(bf16[16,4096]{1,0:T(8,128)(2,1)S(1)} %reshape.46, bf16[4096,512]{1,0:T(8,128)(2,1)} %param.12), kind=kOutput, calls=%fused_computation.27 | convolution fusion | flops 67117056 | bytes 4374528 | tf_op jit(solution)/shard_map/dot_general | solution.py:111
  42.1 0.7 %broadcast_in_dim.30 = bf16[8,32,512]{2,1,0:T(8,128)(2,1)} broadcast(bf16[32,512]{1,0:T(8,128)(2,1)S(1)} %pad_maximum_fusion), dimensions={1,2} | broadcast | bytes 294912 | tf_op jit(solution)/shard_map/broadcast_in_dim | solution.py:41
  42.8 3.4 %all-to-all-start.1 = ((bf16[8,32,512]{2,1,0:T(8,128)(2,1)}), bf16[8,32,512]{2,1,0:T(8,128)(2,1)S(1)}, u32[]{:S(2)}, u32[]{:S(2)}) async-start(bf16[8,32,512]{2,1,0:T(8,128)(2,1)} %broadcast_in_dim.30), calls=%async_computation.1 | async-start | bytes 524288 | tf_op jit(solution)/shard_map/all_to_all | solution.py:42
  46.2 6.8 %all-to-all-done.1 = bf16[8,32,512]{2,1,0:T(8,128)(2,1)S(1)} async-done(((bf16[8,32,512]{2,1,0:T(8,128)(2,1)}), bf16[8,32,512]{2,1,0:T(8,128)(2,1)S(1)}, u32[]{:S(2)}, u32[]{:S(2)}) %all-to-all-start.1) | async-done | bytes 262176 | tf_op jit(solution)/shard_map/all_to_all | solution.py:42
  53.0 6.0 %fusion.24 = f32[32,1024]{1,0:T(8,128)S(1)} fusion(bf16[8,32,512]{2,1,0:T(8,128)(2,1)S(1)} %all-to-all-done.1, bf16[128,8,8,512]{3,2,1,0:T(8,128)(2,1)} %bitcast.28), kind=kOutput, calls=%fused_computation.12 | convolution fusion | flops 268435456 | bytes 8781824 | tf_op jit(solution)/shard_map/dot_general | solution.py:117
  59.1 0.1 collective-permute-start.3
  59.1 3.8 %collective-permute-start.5 = (f32[16,256]{1,0:T(8,128)S(1)}, f32[16,256]{1,0:T(8,128)S(1)}, u32[]{:S(2)}, u32[]{:S(2)}) collective-permute-start(f32[16,256]{1,0:T(8,128)S(1)} %get-tuple-element.9), channel_id=1, source_target_pairs={{0,3},{1,0},{2,1},{3,2},{4,7},{5,4},{6,5},{7,6},{8,11},{9,8},{10,9... | collective-permute-start | bytes 49160 | tf_op jit(solution)/shard_map/ppermute | solution.py:16
  62.9 0.0 collective-permute-start.4
  62.9 1.7 %collective-permute-done.3 = f32[16,256]{1,0:T(8,128)S(1)} collective-permute-done((f32[16,256]{1,0:T(8,128)S(1)}, f32[16,256]{1,0:T(8,128)S(1)}, u32[]{:S(2)}, u32[]{:S(2)}) %collective-permute-start.3) | collective-permute-done | bytes 16416 | tf_op jit(solution)/shard_map/ppermute | solution.py:16
  64.7 0.0 collective-permute-done.5
  64.7 2.9 %collective-permute-done.4 = f32[16,256]{1,0:T(8,128)S(1)} collective-permute-done((f32[16,256]{1,0:T(8,128)S(1)}, f32[16,256]{1,0:T(8,128)S(1)}, u32[]{:S(2)}, u32[]{:S(2)}) %collective-permute-start.4) | collective-permute-done | bytes 16416 | tf_op jit(solution)/shard_map/ppermute | solution.py:16
  67.6 0.6 add_add_fusion
  (7 shorter events, 0.1 us)
Async XLA Ops:
  0.0 1.6 %copy-start = (bf16[4,64,4096]{2,1,0:T(8,128)(2,1)S(1)}, bf16[4,64,4096]{2,1,0:T(8,128)(2,1)}, u32[]{:S(2)}) copy-start(bf16[4,64,4096]{2,1,0:T(8,128)(2,1)} %param.11) | copy-start | bytes 6291460
  19.8 7.1 %collective-permute-start = (f32[2,4096]{1,0:T(2,128)S(1)}, f32[2,4096]{1,0:T(2,128)S(1)}, u32[]{:S(2)}, u32[]{:S(2)}) collective-permute-start(f32[2,4096]{1,0:T(2,128)S(1)} %get-tuple-element.5), channel_id=1, source_target_pairs={{0,1},{1,2},{2,3},{3,0},{4,5},{5,6},{6,7},{7,4},{8,9},{9,10},{10,1... | collective-permute-start | bytes 98312 | tf_op jit(solution)/shard_map/ppermute | solution.py:16
  22.9 4.3 %collective-permute-start.2 = (f32[2,4096]{1,0:T(2,128)S(1)}, f32[2,4096]{1,0:T(2,128)S(1)}, u32[]{:S(2)}, u32[]{:S(2)}) collective-permute-start(f32[2,4096]{1,0:T(2,128)S(1)} %get-tuple-element.6), channel_id=1, source_target_pairs={{0,3},{1,0},{2,1},{3,2},{4,7},{5,4},{6,5},{7,6},{8,11},{9,8},{10,9... | collective-permute-start | bytes 98312 | tf_op jit(solution)/shard_map/ppermute | solution.py:16
  25.0 4.8 %collective-permute-start.1 = (f32[2,4096]{1,0:T(2,128)S(1)}, f32[2,4096]{1,0:T(2,128)S(1)}, u32[]{:S(2)}, u32[]{:S(2)}) collective-permute-start(f32[2,4096]{1,0:T(2,128)S(1)} %get-tuple-element.7), channel_id=1, source_target_pairs={{0,2},{1,3},{2,0},{3,1},{4,6},{5,7},{6,4},{7,5},{8,10},{9,11},{10,... | collective-permute-start | bytes 98312 | tf_op jit(solution)/shard_map/ppermute | solution.py:16
  42.8 10.3 %all-to-all-start.1 = ((bf16[8,32,512]{2,1,0:T(8,128)(2,1)}), bf16[8,32,512]{2,1,0:T(8,128)(2,1)S(1)}, u32[]{:S(2)}, u32[]{:S(2)}) async-start(bf16[8,32,512]{2,1,0:T(8,128)(2,1)} %broadcast_in_dim.30), calls=%async_computation.1 | async-start | bytes 524288 | tf_op jit(solution)/shard_map/all_to_all | solution.py:42
  59.1 5.6 %collective-permute-start.3 = (f32[16,256]{1,0:T(8,128)S(1)}, f32[16,256]{1,0:T(8,128)S(1)}, u32[]{:S(2)}, u32[]{:S(2)}) collective-permute-start(f32[16,256]{1,0:T(8,128)S(1)} %get-tuple-element.8), channel_id=1, source_target_pairs={{0,1},{1,2},{2,3},{3,0},{4,5},{5,6},{6,7},{7,4},{8,9},{9,10},{10,1... | collective-permute-start | bytes 49160 | tf_op jit(solution)/shard_map/ppermute | solution.py:16
  59.1 5.5 %collective-permute-start.5 = (f32[16,256]{1,0:T(8,128)S(1)}, f32[16,256]{1,0:T(8,128)S(1)}, u32[]{:S(2)}, u32[]{:S(2)}) collective-permute-start(f32[16,256]{1,0:T(8,128)S(1)} %get-tuple-element.9), channel_id=1, source_target_pairs={{0,3},{1,0},{2,1},{3,2},{4,7},{5,4},{6,5},{7,6},{8,11},{9,8},{10,9... | collective-permute-start | bytes 49160 | tf_op jit(solution)/shard_map/ppermute | solution.py:16
  62.9 4.6 %collective-permute-start.4 = (f32[16,256]{1,0:T(8,128)S(1)}, f32[16,256]{1,0:T(8,128)S(1)}, u32[]{:S(2)}, u32[]{:S(2)}) collective-permute-start(f32[16,256]{1,0:T(8,128)S(1)} %get-tuple-element.10), channel_id=1, source_target_pairs={{0,2},{1,3},{2,0},{3,1},{4,6},{5,7},{6,4},{7,5},{8,10},{9,11},{10,... | collective-permute-start | bytes 49160 | tf_op jit(solution)/shard_map/ppermute | solution.py:16

commit v4 on v3

--- a/solution.py
+++ b/solution.py
@@ -1,6 +1,8 @@
 import jax
 import jax.numpy as jnp
 from jax import lax
+from jax.experimental import pallas as pl
+from jax.experimental.pallas import tpu as pltpu
 from jax.sharding import PartitionSpec as P
 
 
@@ -40,6 +42,43 @@
     n = lax.axis_size(axis)
     copies = jnp.broadcast_to(x[None], (n,) + x.shape)
     return lax.all_to_all(copies, axis, 0, 0, tiled=True)
+
+
+def gradient_kernel(limits_ref, act_ref, cot_ref, win_ref, wout_ref, out_ref):
+    example = pl.program_id(1)
+    nt = (((1,), (1,)), ((), ()))
+    left = lax.dot_general(
+        act_ref[...], win_ref[...], nt, preferred_element_type=jnp.float32
+    ).astype(jnp.bfloat16)
+    right = lax.dot_general(cot_ref[...], wout_ref[...], nt, preferred_element_type=jnp.float32)
+    rows = lax.broadcasted_iota(jnp.int32, right.shape, 0)
+    right = jnp.where(rows < limits_ref[example], right, 0.0).astype(jnp.bfloat16)
+    out_ref[...] = lax.dot_general(
+        right, left, (((0,), (0,)), ((), ())), preferred_element_type=jnp.float32
+    )
+
+
+def layer_gradients(activations, cotangents, limits, project_in, project_out):
+    layers, examples, tokens, width = activations.shape
+    factor = project_in.shape[1]
+    data = pl.BlockSpec((None, None, tokens, width), lambda l, e, lim: (l, e, 0, 0))
+    weights = pl.BlockSpec((None, factor, width), lambda l, e, lim: (l, 0, 0))
+    flops = 4 * layers * examples * tokens * width * factor
+    moved = 2 * (activations.size + cotangents.size + project_in.size + project_out.size)
+    return pl.pallas_call(
+        gradient_kernel,
+        out_shape=jax.ShapeDtypeStruct((examples, layers, factor, factor), jnp.float32),
+        grid_spec=pltpu.PrefetchScalarGridSpec(
+            num_scalar_prefetch=1,
+            grid=(layers, examples),
+            in_specs=[data, data, weights, weights],
+            out_specs=pl.BlockSpec(
+                (None, None, factor, factor), lambda l, e, lim: (e, l, 0, 0)
+            ),
+        ),
+        compiler_params=pltpu.CompilerParams(vmem_limit_bytes=48 << 20),
+        cost_estimate=pl.CostEstimate(flops=flops, transcendentals=0, bytes_accessed=moved),
+    )(limits, activations, cotangents, project_in, project_out)
 
 
 def body_start(activations, cotangents, lengths, project_in, project_out, preconditioner, queries):
@@ -92,18 +131,8 @@
     block_size = factor_size * factor_size
     width_dp = lax.axis_size("dp")
     mp_place = lax.axis_index("mp")
-    positions = mp_place * tokens_here + jnp.arange(tokens_here, dtype=jnp.int32)
-    live_mask = positions[None, :] < lengths[:, None]
-    left_factor = jnp.einsum(
-        "lesd,lkd->lesk", activations, project_in, preferred_element_type=jnp.float32
-    ).astype(jnp.bfloat16)
-    right_factor = jnp.einsum(
-        "lesd,lkd->lesk", cotangents, project_out, preferred_element_type=jnp.float32
-    )
-    right_factor = jnp.where(live_mask[None, :, :, None], right_factor, 0.0).astype(jnp.bfloat16)
-    partial_grad = jnp.einsum(
-        "lesj,lesc->eljc", right_factor, left_factor, preferred_element_type=jnp.float32
-    )
+    limits = lengths - mp_place * tokens_here
+    partial_grad = layer_gradients(activations, cotangents, limits, project_in, project_out)
     partial_grad = partial_grad.reshape(partial_grad.shape[0], layer_count * block_size)
     grad_mine = reduce_scatter_direct(partial_grad, "mp", 1).astype(jnp.bfloat16)
     grad_all = all_gather_a2a(grad_mine, "dp")

time: 68.6 us -> 69.7 us (1.016)
  matrix products: 26.8 us -> 8.81 us
  Pallas kernels: 0 us -> 16.9 us
  local copies, waits for them, and re-layouts: 1.75 us -> 4.21 us
    dot_general x2 -> x0, matrix products: 18 us -> none  [the longest x1 9.26 us: body_direct(): jnp.einsum('lesj,lesc->eljc', right_factor, left_factor, preferred_elemen...]
    pallas_call x0 -> x1, Pallas kernels: none -> 16.9 us  [layer_gradients(): pl.pallas_call(gradient_kernel, out_shape=jax.ShapeDtypeStruct((examples,...]
    unnamed x2 -> x4, local copies, waits for them, and re-layouts: 0.73 us -> 3.18 us
    lt x1 -> x0, other arithmetic: 0.88 us -> none  [body_direct(): live_mask = positions[None, :] < lengths[:, None]]
where the time goes in v4:
time: 69.7 us; the launch traced here: 69.3 us
  Pallas kernels  16.9 us (24%)
  waiting for transfers between devices  15.3 us (22%)
  starting transfers between devices  13.4 us (19%)
  blocking collectives  9.18 us (13%)
  matrix products  8.81 us (13%)
  local copies, waits for them, and re-layouts  4.21 us (6%)
  other arithmetic  1.34 us (2%)
    pallas_call x1, Pallas kernels, layer_gradients(): pl.pallas_call(gradient_kernel, out_shape=jax.ShapeDtypeStruct((examples,...  16.9 us
    ppermute x6, starting transfers between devices, shifted(): return lax.ppermute(x, axis, [(i, (i + shift) % n) for i in range(n)])  10 us
    all_to_all x1, blocking collectives, all_gather_a2a(): return lax.all_to_all(copies, axis, 0, 0, tiled=True)  9.18 us
    ppermute x6, waiting for transfers between devices, shifted(): return lax.ppermute(x, axis, [(i, (i + shift) % n) for i in range(n)])  8.5 us
    all_to_all x1, waiting for transfers between devices, all_gather_a2a(): return lax.all_to_all(copies, axis, 0, 0, tiled=True)  6.81 us
    dot_general x1, matrix products, body_direct(): lax.dot_general(both_all, query_blocks, (((0, 2), (1, 2)), ((), ())), pre...  5.98 us
    all_to_all x1, starting transfers between devices, all_gather_a2a(): return lax.all_to_all(copies, axis, 0, 0, tiled=True)  3.41 us
    unnamed x4, local copies, waits for them, and re-layouts  3.18 us
  transfers between devices with their start and end apart: 7, of which 6 were waited for; matrix products, arithmetic and copies ran while one was open for 0% of the time, Pallas kernels for 0%

profile of v4, /device:TPU:0, one launch (start us, length us, event | category | flops | bytes accessed | tf_op | source)
XLA Modules:
  0.0 69.3 jit_solution(8780084307414747324)
XLA Ops:
  0.0 0.7 broadcast_subtract_fusion.limits_ref
  0.7 0.0 copy-start
  0.7 1.6 %copy-done = bf16[4,64,4096]{2,1,0:T(8,128)(2,1)S(1)} copy-done((bf16[4,64,4096]{2,1,0:T(8,128)(2,1)S(1)}, bf16[4,64,4096]{2,1,0:T(8,128)(2,1)}, u32[]{:S(2)}) %copy-start) | copy-done | bytes 2097176
  2.2 0.0 copy-start.1
  2.3 1.6 %copy-done.1 = bf16[4,64,4096]{2,1,0:T(8,128)(2,1)S(1)} copy-done((bf16[4,64,4096]{2,1,0:T(8,128)(2,1)S(1)}, bf16[4,64,4096]{2,1,0:T(8,128)(2,1)}, u32[]{:S(2)}) %copy-start.1) | copy-done | bytes 2097176
  3.8 16.9 %shard_map.73 = f32[2,4,64,64]{3,2,1,0:T(8,128)S(1)} custom-call(s32[2]{0:T(128)S(1)} %broadcast_subtract_fusion.limits_ref, bf16[4,2,256,4096]{3,2,1,0:T(8,128)(2,1)} %act_ref.1, bf16[4,2,256,4096]{3,2,1,0:T(8,128)(2,1)} %cot_ref.1, bf16[4,64,4096]{2,1,0:T(8,128)(2,1)S(1)} %copy-done, bf16[4,64,4096]{2,1,0:T(8,128)(2,1)S(1)} %copy-done.1), custom_call_target="tpu_custom_call" | custom-call | flops 2147483648 | bytes 37748736 | tf_op jit(solution)/shard_map/pallas_call | solution.py:68
  20.7 0.1 reshape.11
  20.9 3.1 %collective-permute-start = (f32[2,4096]{1,0:T(2,128)S(1)}, f32[2,4096]{1,0:T(2,128)S(1)}, u32[]{:S(2)}, u32[]{:S(2)}) collective-permute-start(f32[2,4096]{1,0:T(2,128)S(1)} %get-tuple-element.5), channel_id=1, source_target_pairs={{0,1},{1,2},{2,3},{3,0},{4,5},{5,6},{6,7},{7,4},{8,9},{9,10},{10,1... | collective-permute-start | bytes 98312 | tf_op jit(solution)/shard_map/ppermute | solution.py:18
  24.0 2.1 %collective-permute-start.2 = (f32[2,4096]{1,0:T(2,128)S(1)}, f32[2,4096]{1,0:T(2,128)S(1)}, u32[]{:S(2)}, u32[]{:S(2)}) collective-permute-start(f32[2,4096]{1,0:T(2,128)S(1)} %get-tuple-element.6), channel_id=1, source_target_pairs={{0,3},{1,0},{2,1},{3,2},{4,7},{5,4},{6,5},{7,6},{8,11},{9,8},{10,9... | collective-permute-start | bytes 98312 | tf_op jit(solution)/shard_map/ppermute | solution.py:18
  26.1 0.9 %collective-permute-start.1 = (f32[2,4096]{1,0:T(2,128)S(1)}, f32[2,4096]{1,0:T(2,128)S(1)}, u32[]{:S(2)}, u32[]{:S(2)}) collective-permute-start(f32[2,4096]{1,0:T(2,128)S(1)} %get-tuple-element.7), channel_id=1, source_target_pairs={{0,2},{1,3},{2,0},{3,1},{4,6},{5,7},{6,4},{7,5},{8,10},{9,11},{10,... | collective-permute-start | bytes 98312 | tf_op jit(solution)/shard_map/ppermute | solution.py:18
  27.1 1.0 %collective-permute-done = f32[2,4096]{1,0:T(2,128)S(1)} collective-permute-done((f32[2,4096]{1,0:T(2,128)S(1)}, f32[2,4096]{1,0:T(2,128)S(1)}, u32[]{:S(2)}, u32[]{:S(2)}) %collective-permute-start) | collective-permute-done | bytes 32800 | tf_op jit(solution)/shard_map/ppermute | solution.py:18
  28.0 0.2 collective-permute-done.2
  28.3 2.6 %collective-permute-done.1 = f32[2,4096]{1,0:T(2,128)S(1)} collective-permute-done((f32[2,4096]{1,0:T(2,128)S(1)}, f32[2,4096]{1,0:T(2,128)S(1)}, u32[]{:S(2)}, u32[]{:S(2)}) %collective-permute-start.1) | collective-permute-done | bytes 32800 | tf_op jit(solution)/shard_map/ppermute | solution.py:18
  31.0 0.1 broadcast_in_dim.4
  31.0 9.2 %all_to_all.10 = bf16[8,2,4096]{2,1,0:T(2,128)(2,1)S(1)} all-to-all(bf16[8,2,4096]{2,1,0:T(2,128)(2,1)S(1)} %broadcast_in_dim.4), channel_id=1, replica_groups=mesh['dp'=8,'mp'=4] {'dp'}, dimensions={0} | all-to-all | bytes 262144 | tf_op jit(solution)/shard_map/all_to_all | solution.py:44
  40.2 0.1 reshape.12
  40.3 2.8 %fusion.6 = (bf16[16,512]{1,0:T(8,128)(2,1)S(1)}, f32[16,512]{1,0:T(8,128)S(1)}) fusion(bf16[16,4096]{1,0:T(8,128)(2,1)S(1)} %reshape.12, bf16[4096,512]{1,0:T(8,128)(2,1)} %param.12), kind=kOutput, calls=%fused_computation.16 | convolution fusion | flops 67117056 | bytes 4374528 | tf_op jit(solution)/shard_map/dot_general | solution.py:140
  43.1 0.7 %broadcast_in_dim.5 = bf16[8,32,512]{2,1,0:T(8,128)(2,1)} broadcast(bf16[32,512]{1,0:T(8,128)(2,1)S(1)} %pad_maximum_fusion), dimensions={1,2} | broadcast | bytes 294912 | tf_op jit(solution)/shard_map/broadcast_in_dim | solution.py:43
  43.9 3.4 %all-to-all-start.1 = ((bf16[8,32,512]{2,1,0:T(8,128)(2,1)}), bf16[8,32,512]{2,1,0:T(8,128)(2,1)S(1)}, u32[]{:S(2)}, u32[]{:S(2)}) async-start(bf16[8,32,512]{2,1,0:T(8,128)(2,1)} %broadcast_in_dim.5), calls=%async_computation.1 | async-start | bytes 524288 | tf_op jit(solution)/shard_map/all_to_all | solution.py:44
  47.3 6.8 %all-to-all-done.1 = bf16[8,32,512]{2,1,0:T(8,128)(2,1)S(1)} async-done(((bf16[8,32,512]{2,1,0:T(8,128)(2,1)}), bf16[8,32,512]{2,1,0:T(8,128)(2,1)S(1)}, u32[]{:S(2)}, u32[]{:S(2)}) %all-to-all-start.1) | async-done | bytes 262176 | tf_op jit(solution)/shard_map/all_to_all | solution.py:44
  54.1 6.0 %fusion.3 = f32[32,1024]{1,0:T(8,128)S(1)} fusion(bf16[8,32,512]{2,1,0:T(8,128)(2,1)S(1)} %all-to-all-done.1, bf16[128,8,8,512]{3,2,1,0:T(8,128)(2,1)} %bitcast.13), kind=kOutput, calls=%fused_computation.3 | convolution fusion | flops 268435456 | bytes 8781824 | tf_op jit(solution)/shard_map/dot_general | solution.py:146
  60.2 0.1 collective-permute-start.3
  60.2 3.8 %collective-permute-start.5 = (f32[16,256]{1,0:T(8,128)S(1)}, f32[16,256]{1,0:T(8,128)S(1)}, u32[]{:S(2)}, u32[]{:S(2)}) collective-permute-start(f32[16,256]{1,0:T(8,128)S(1)} %get-tuple-element.9), channel_id=1, source_target_pairs={{0,3},{1,0},{2,1},{3,2},{4,7},{5,4},{6,5},{7,6},{8,11},{9,8},{10,9... | collective-permute-start | bytes 49160 | tf_op jit(solution)/shard_map/ppermute | solution.py:18
  64.0 0.0 collective-permute-start.4
  64.0 1.7 %collective-permute-done.3 = f32[16,256]{1,0:T(8,128)S(1)} collective-permute-done((f32[16,256]{1,0:T(8,128)S(1)}, f32[16,256]{1,0:T(8,128)S(1)}, u32[]{:S(2)}, u32[]{:S(2)}) %collective-permute-start.3) | collective-permute-done | bytes 16416 | tf_op jit(solution)/shard_map/ppermute | solution.py:18
  65.8 0.0 collective-permute-done.5
  65.8 2.9 %collective-permute-done.4 = f32[16,256]{1,0:T(8,128)S(1)} collective-permute-done((f32[16,256]{1,0:T(8,128)S(1)}, f32[16,256]{1,0:T(8,128)S(1)}, u32[]{:S(2)}, u32[]{:S(2)}) %collective-permute-start.4) | collective-permute-done | bytes 16416 | tf_op jit(solution)/shard_map/ppermute | solution.py:18
  68.7 0.6 add_add_fusion
  (6 shorter events, 0.1 us)
Async XLA Ops:
  0.7 1.6 %copy-start = (bf16[4,64,4096]{2,1,0:T(8,128)(2,1)S(1)}, bf16[4,64,4096]{2,1,0:T(8,128)(2,1)}, u32[]{:S(2)}) copy-start(bf16[4,64,4096]{2,1,0:T(8,128)(2,1)} %win_ref.1) | copy-start | bytes 6291460
  2.2 1.6 %copy-start.1 = (bf16[4,64,4096]{2,1,0:T(8,128)(2,1)S(1)}, bf16[4,64,4096]{2,1,0:T(8,128)(2,1)}, u32[]{:S(2)}) copy-start(bf16[4,64,4096]{2,1,0:T(8,128)(2,1)} %wout_ref.1) | copy-start | bytes 6291460
  20.9 7.1 %collective-permute-start = (f32[2,4096]{1,0:T(2,128)S(1)}, f32[2,4096]{1,0:T(2,128)S(1)}, u32[]{:S(2)}, u32[]{:S(2)}) collective-permute-start(f32[2,4096]{1,0:T(2,128)S(1)} %get-tuple-element.5), channel_id=1, source_target_pairs={{0,1},{1,2},{2,3},{3,0},{4,5},{5,6},{6,7},{7,4},{8,9},{9,10},{10,1... | collective-permute-start | bytes 98312 | tf_op jit(solution)/shard_map/ppermute | solution.py:18
  24.0 4.3 %collective-permute-start.2 = (f32[2,4096]{1,0:T(2,128)S(1)}, f32[2,4096]{1,0:T(2,128)S(1)}, u32[]{:S(2)}, u32[]{:S(2)}) collective-permute-start(f32[2,4096]{1,0:T(2,128)S(1)} %get-tuple-element.6), channel_id=1, source_target_pairs={{0,3},{1,0},{2,1},{3,2},{4,7},{5,4},{6,5},{7,6},{8,11},{9,8},{10,9... | collective-permute-start | bytes 98312 | tf_op jit(solution)/shard_map/ppermute | solution.py:18
  26.1 4.8 %collective-permute-start.1 = (f32[2,4096]{1,0:T(2,128)S(1)}, f32[2,4096]{1,0:T(2,128)S(1)}, u32[]{:S(2)}, u32[]{:S(2)}) collective-permute-start(f32[2,4096]{1,0:T(2,128)S(1)} %get-tuple-element.7), channel_id=1, source_target_pairs={{0,2},{1,3},{2,0},{3,1},{4,6},{5,7},{6,4},{7,5},{8,10},{9,11},{10,... | collective-permute-start | bytes 98312 | tf_op jit(solution)/shard_map/ppermute | solution.py:18
  43.9 10.3 %all-to-all-start.1 = ((bf16[8,32,512]{2,1,0:T(8,128)(2,1)}), bf16[8,32,512]{2,1,0:T(8,128)(2,1)S(1)}, u32[]{:S(2)}, u32[]{:S(2)}) async-start(bf16[8,32,512]{2,1,0:T(8,128)(2,1)} %broadcast_in_dim.5), calls=%async_computation.1 | async-start | bytes 524288 | tf_op jit(solution)/shard_map/all_to_all | solution.py:44
  60.2 5.6 %collective-permute-start.3 = (f32[16,256]{1,0:T(8,128)S(1)}, f32[16,256]{1,0:T(8,128)S(1)}, u32[]{:S(2)}, u32[]{:S(2)}) collective-permute-start(f32[16,256]{1,0:T(8,128)S(1)} %get-tuple-element.8), channel_id=1, source_target_pairs={{0,1},{1,2},{2,3},{3,0},{4,5},{5,6},{6,7},{7,4},{8,9},{9,10},{10,1... | collective-permute-start | bytes 49160 | tf_op jit(solution)/shard_map/ppermute | solution.py:18
  60.2 5.5 %collective-permute-start.5 = (f32[16,256]{1,0:T(8,128)S(1)}, f32[16,256]{1,0:T(8,128)S(1)}, u32[]{:S(2)}, u32[]{:S(2)}) collective-permute-start(f32[16,256]{1,0:T(8,128)S(1)} %get-tuple-element.9), channel_id=1, source_target_pairs={{0,3},{1,0},{2,1},{3,2},{4,7},{5,4},{6,5},{7,6},{8,11},{9,8},{10,9... | collective-permute-start | bytes 49160 | tf_op jit(solution)/shard_map/ppermute | solution.py:18
  64.0 4.6 %collective-permute-start.4 = (f32[16,256]{1,0:T(8,128)S(1)}, f32[16,256]{1,0:T(8,128)S(1)}, u32[]{:S(2)}, u32[]{:S(2)}) collective-permute-start(f32[16,256]{1,0:T(8,128)S(1)} %get-tuple-element.10), channel_id=1, source_target_pairs={{0,2},{1,3},{2,0},{3,1},{4,6},{5,7},{6,4},{7,5},{8,10},{9,11},{10,... | collective-permute-start | bytes 49160 | tf_op jit(solution)/shard_map/ppermute | solution.py:18

commit v5 on v4

--- a/solution.py
+++ b/solution.py
@@ -44,21 +44,23 @@
     return lax.all_to_all(copies, axis, 0, 0, tiled=True)
 
 
-def gradient_kernel(limits_ref, act_ref, cot_ref, win_ref, wout_ref, out_ref):
+def gradient_kernel(lengths_ref, act_ref, cot_ref, win_ref, wout_ref, out_ref):
     example = pl.program_id(1)
+    tokens = act_ref.shape[0]
+    limit = lengths_ref[example] - lax.axis_index("mp") * tokens
     nt = (((1,), (1,)), ((), ()))
     left = lax.dot_general(
         act_ref[...], win_ref[...], nt, preferred_element_type=jnp.float32
     ).astype(jnp.bfloat16)
     right = lax.dot_general(cot_ref[...], wout_ref[...], nt, preferred_element_type=jnp.float32)
     rows = lax.broadcasted_iota(jnp.int32, right.shape, 0)
-    right = jnp.where(rows < limits_ref[example], right, 0.0).astype(jnp.bfloat16)
+    right = jnp.where(rows < limit, right, 0.0).astype(jnp.bfloat16)
     out_ref[...] = lax.dot_general(
         right, left, (((0,), (0,)), ((), ())), preferred_element_type=jnp.float32
     )
 
 
-def layer_gradients(activations, cotangents, limits, project_in, project_out):
+def layer_gradients(activations, cotangents, lengths, project_in, project_out):
     layers, examples, tokens, width = activations.shape
     factor = project_in.shape[1]
     data = pl.BlockSpec((None, None, tokens, width), lambda l, e, lim: (l, e, 0, 0))
@@ -76,9 +78,8 @@
                 (None, None, factor, factor), lambda l, e, lim: (e, l, 0, 0)
             ),
         ),
-        compiler_params=pltpu.CompilerParams(vmem_limit_bytes=48 << 20),
         cost_estimate=pl.CostEstimate(flops=flops, transcendentals=0, bytes_accessed=moved),
-    )(limits, activations, cotangents, project_in, project_out)
+    )(lengths, activations, cotangents, project_in, project_out)
 
 
 def body_start(activations, cotangents, lengths, project_in, project_out, preconditioner, queries):
@@ -131,8 +132,7 @@
     block_size = factor_size * factor_size
     width_dp = lax.axis_size("dp")
     mp_place = lax.axis_index("mp")
-    limits = lengths - mp_place * tokens_here
-    partial_grad = layer_gradients(activations, cotangents, limits, project_in, project_out)
+    partial_grad = layer_gradients(activations, cotangents, lengths, project_in, project_out)
     partial_grad = partial_grad.reshape(partial_grad.shape[0], layer_count * block_size)
     grad_mine = reduce_scatter_direct(partial_grad, "mp", 1).astype(jnp.bfloat16)
     grad_all = all_gather_a2a(grad_mine, "dp")

time: 69.7 us -> 68.2 us (0.978)
  local copies, waits for them, and re-layouts: 4.21 us -> 1.98 us
  Pallas kernels: 16.9 us -> 18.3 us
    unnamed x4 -> x0, local copies, waits for them, and re-layouts: 3.18 us -> none
    pallas_call x1, Pallas kernels: 16.9 us -> 18.3 us  [layer_gradients(): pl.pallas_call(gradient_kernel, out_shape=jax.ShapeDtypeStruct((examples,...]
    reshape x1, local copies, waits for them, and re-layouts: 0.14 us -> 1.09 us  [body_direct(): partial_grad.reshape(partial_grad.shape[0], layer_count * block_size)]
where the time goes in v5:
time: 68.2 us; the launch traced here: 67.8 us
  Pallas kernels  18.3 us (27%)
  waiting for transfers between devices  15.3 us (22%)
  starting transfers between devices  13.4 us (20%)
  blocking collectives  9.17 us (13%)
  matrix products  8.81 us (13%)
  local copies, waits for them, and re-layouts  1.98 us (3%)
  other arithmetic  0.69 us (1%)
    pallas_call x1, Pallas kernels, layer_gradients(): pl.pallas_call(gradient_kernel, out_shape=jax.ShapeDtypeStruct((examples,...  18.3 us
    ppermute x6, starting transfers between devices, shifted(): return lax.ppermute(x, axis, [(i, (i + shift) % n) for i in range(n)])  10 us
    all_to_all x1, blocking collectives, all_gather_a2a(): return lax.all_to_all(copies, axis, 0, 0, tiled=True)  9.17 us
    ppermute x6, waiting for transfers between devices, shifted(): return lax.ppermute(x, axis, [(i, (i + shift) % n) for i in range(n)])  8.5 us
    all_to_all x1, waiting for transfers between devices, all_gather_a2a(): return lax.all_to_all(copies, axis, 0, 0, tiled=True)  6.81 us
    dot_general x1, matrix products, body_direct(): lax.dot_general(both_all, query_blocks, (((0, 2), (1, 2)), ((), ())), pre...  5.98 us
    all_to_all x1, starting transfers between devices, all_gather_a2a(): return lax.all_to_all(copies, axis, 0, 0, tiled=True)  3.41 us
    dot_general x1, matrix products, body_direct(): jnp.dot(grad_all, preconditioner, preferred_element_type=jnp.float32)  2.83 us
  transfers between devices with their start and end apart: 7, of which 6 were waited for; matrix products, arithmetic and copies ran while one was open for 0% of the time, Pallas kernels for 0%

profile of v5, /device:TPU:0, one launch (start us, length us, event | category | flops | bytes accessed | tf_op | source)
XLA Modules:
  0.0 67.8 jit_solution(12356166428322090115)
XLA Ops:
  0.0 18.3 %shard_map.73 = f32[2,4,64,64]{3,2,1,0:T(8,128)} custom-call(s32[2]{0:T(128)} %lengths_ref.1, bf16[4,2,256,4096]{3,2,1,0:T(8,128)(2,1)} %act_ref.1, bf16[4,2,256,4096]{3,2,1,0:T(8,128)(2,1)} %cot_ref.1, bf16[4,64,4096]{2,1,0:T(8,128)(2,1)} %win_ref.1, bf16[4,64,4096]{2,1,0:T(8,128)(2,1)} %wout_ref.1), custom_call_target="tpu_custom_call" | custom-call | flops 2147483648 | bytes 37748736 | tf_op jit(solution)/shard_map/pallas_call | solution.py:70
  18.3 1.1 %reshape.11 = f32[2,16384]{1,0:T(2,128)S(1)} reshape(f32[2,4,64,64]{3,2,1,0:T(8,128)} %shard_map.73) | data formatting | bytes 262144 | tf_op jit(solution)/shard_map/reshape | solution.py:136
  19.4 3.1 %collective-permute-start = (f32[2,4096]{1,0:T(2,128)S(1)}, f32[2,4096]{1,0:T(2,128)S(1)}, u32[]{:S(2)}, u32[]{:S(2)}) collective-permute-start(f32[2,4096]{1,0:T(2,128)S(1)} %get-tuple-element.5), channel_id=1, source_target_pairs={{0,1},{1,2},{2,3},{3,0},{4,5},{5,6},{6,7},{7,4},{8,9},{9,10},{10,1... | collective-permute-start | bytes 98312 | tf_op jit(solution)/shard_map/ppermute | solution.py:18
  22.5 2.1 %collective-permute-start.2 = (f32[2,4096]{1,0:T(2,128)S(1)}, f32[2,4096]{1,0:T(2,128)S(1)}, u32[]{:S(2)}, u32[]{:S(2)}) collective-permute-start(f32[2,4096]{1,0:T(2,128)S(1)} %get-tuple-element.6), channel_id=1, source_target_pairs={{0,3},{1,0},{2,1},{3,2},{4,7},{5,4},{6,5},{7,6},{8,11},{9,8},{10,9... | collective-permute-start | bytes 98312 | tf_op jit(solution)/shard_map/ppermute | solution.py:18
  24.6 0.9 %collective-permute-start.1 = (f32[2,4096]{1,0:T(2,128)S(1)}, f32[2,4096]{1,0:T(2,128)S(1)}, u32[]{:S(2)}, u32[]{:S(2)}) collective-permute-start(f32[2,4096]{1,0:T(2,128)S(1)} %get-tuple-element.7), channel_id=1, source_target_pairs={{0,2},{1,3},{2,0},{3,1},{4,6},{5,7},{6,4},{7,5},{8,10},{9,11},{10,... | collective-permute-start | bytes 98312 | tf_op jit(solution)/shard_map/ppermute | solution.py:18
  25.6 1.0 %collective-permute-done = f32[2,4096]{1,0:T(2,128)S(1)} collective-permute-done((f32[2,4096]{1,0:T(2,128)S(1)}, f32[2,4096]{1,0:T(2,128)S(1)}, u32[]{:S(2)}, u32[]{:S(2)}) %collective-permute-start) | collective-permute-done | bytes 32800 | tf_op jit(solution)/shard_map/ppermute | solution.py:18
  26.6 0.2 collective-permute-done.2
  26.8 2.6 %collective-permute-done.1 = f32[2,4096]{1,0:T(2,128)S(1)} collective-permute-done((f32[2,4096]{1,0:T(2,128)S(1)}, f32[2,4096]{1,0:T(2,128)S(1)}, u32[]{:S(2)}, u32[]{:S(2)}) %collective-permute-start.1) | collective-permute-done | bytes 32800 | tf_op jit(solution)/shard_map/ppermute | solution.py:18
  29.5 0.1 broadcast_in_dim.4
  29.6 9.2 %all_to_all.10 = bf16[8,2,4096]{2,1,0:T(2,128)(2,1)S(1)} all-to-all(bf16[8,2,4096]{2,1,0:T(2,128)(2,1)S(1)} %broadcast_in_dim.4), channel_id=1, replica_groups=mesh['dp'=8,'mp'=4] {'dp'}, dimensions={0} | all-to-all | bytes 262144 | tf_op jit(solution)/shard_map/all_to_all | solution.py:44
  38.7 0.1 reshape.12
  38.8 2.8 %fusion.6 = (bf16[16,512]{1,0:T(8,128)(2,1)S(1)}, f32[16,512]{1,0:T(8,128)S(1)}) fusion(bf16[16,4096]{1,0:T(8,128)(2,1)S(1)} %reshape.12, bf16[4096,512]{1,0:T(8,128)(2,1)} %param.12), kind=kOutput, calls=%fused_computation.15 | convolution fusion | flops 67117056 | bytes 4374528 | tf_op jit(solution)/shard_map/dot_general | solution.py:140
  41.7 0.7 %broadcast_in_dim.5 = bf16[8,32,512]{2,1,0:T(8,128)(2,1)} broadcast(bf16[32,512]{1,0:T(8,128)(2,1)S(1)} %pad_maximum_fusion), dimensions={1,2} | broadcast | bytes 294912 | tf_op jit(solution)/shard_map/broadcast_in_dim | solution.py:43
  42.4 3.4 %all-to-all-start.1 = ((bf16[8,32,512]{2,1,0:T(8,128)(2,1)}), bf16[8,32,512]{2,1,0:T(8,128)(2,1)S(1)}, u32[]{:S(2)}, u32[]{:S(2)}) async-start(bf16[8,32,512]{2,1,0:T(8,128)(2,1)} %broadcast_in_dim.5), calls=%async_computation.1 | async-start | bytes 524288 | tf_op jit(solution)/shard_map/all_to_all | solution.py:44
  45.8 6.8 %all-to-all-done.1 = bf16[8,32,512]{2,1,0:T(8,128)(2,1)S(1)} async-done(((bf16[8,32,512]{2,1,0:T(8,128)(2,1)}), bf16[8,32,512]{2,1,0:T(8,128)(2,1)S(1)}, u32[]{:S(2)}, u32[]{:S(2)}) %all-to-all-start.1) | async-done | bytes 262176 | tf_op jit(solution)/shard_map/all_to_all | solution.py:44
  52.7 6.0 %fusion.3 = f32[32,1024]{1,0:T(8,128)S(1)} fusion(bf16[8,32,512]{2,1,0:T(8,128)(2,1)S(1)} %all-to-all-done.1, bf16[128,8,8,512]{3,2,1,0:T(8,128)(2,1)} %bitcast.13), kind=kOutput, calls=%fused_computation.3 | convolution fusion | flops 268435456 | bytes 8781824 | tf_op jit(solution)/shard_map/dot_general | solution.py:146
  58.7 0.1 collective-permute-start.3
  58.8 3.8 %collective-permute-start.5 = (f32[16,256]{1,0:T(8,128)S(1)}, f32[16,256]{1,0:T(8,128)S(1)}, u32[]{:S(2)}, u32[]{:S(2)}) collective-permute-start(f32[16,256]{1,0:T(8,128)S(1)} %get-tuple-element.9), channel_id=1, source_target_pairs={{0,3},{1,0},{2,1},{3,2},{4,7},{5,4},{6,5},{7,6},{8,11},{9,8},{10,9... | collective-permute-start | bytes 49160 | tf_op jit(solution)/shard_map/ppermute | solution.py:18
  62.6 0.0 collective-permute-start.4
  62.6 1.7 %collective-permute-done.3 = f32[16,256]{1,0:T(8,128)S(1)} collective-permute-done((f32[16,256]{1,0:T(8,128)S(1)}, f32[16,256]{1,0:T(8,128)S(1)}, u32[]{:S(2)}, u32[]{:S(2)}) %collective-permute-start.3) | collective-permute-done | bytes 16416 | tf_op jit(solution)/shard_map/ppermute | solution.py:18
  64.3 0.0 collective-permute-done.5
  64.3 2.9 %collective-permute-done.4 = f32[16,256]{1,0:T(8,128)S(1)} collective-permute-done((f32[16,256]{1,0:T(8,128)S(1)}, f32[16,256]{1,0:T(8,128)S(1)}, u32[]{:S(2)}, u32[]{:S(2)}) %collective-permute-start.4) | collective-permute-done | bytes 16416 | tf_op jit(solution)/shard_map/ppermute | solution.py:18
  67.2 0.6 add_add_fusion
  (6 shorter events, 0.1 us)
Async XLA Ops:
  19.4 7.1 %collective-permute-start = (f32[2,4096]{1,0:T(2,128)S(1)}, f32[2,4096]{1,0:T(2,128)S(1)}, u32[]{:S(2)}, u32[]{:S(2)}) collective-permute-start(f32[2,4096]{1,0:T(2,128)S(1)} %get-tuple-element.5), channel_id=1, source_target_pairs={{0,1},{1,2},{2,3},{3,0},{4,5},{5,6},{6,7},{7,4},{8,9},{9,10},{10,1... | collective-permute-start | bytes 98312 | tf_op jit(solution)/shard_map/ppermute | solution.py:18
  22.5 4.3 %collective-permute-start.2 = (f32[2,4096]{1,0:T(2,128)S(1)}, f32[2,4096]{1,0:T(2,128)S(1)}, u32[]{:S(2)}, u32[]{:S(2)}) collective-permute-start(f32[2,4096]{1,0:T(2,128)S(1)} %get-tuple-element.6), channel_id=1, source_target_pairs={{0,3},{1,0},{2,1},{3,2},{4,7},{5,4},{6,5},{7,6},{8,11},{9,8},{10,9... | collective-permute-start | bytes 98312 | tf_op jit(solution)/shard_map/ppermute | solution.py:18
  24.6 4.8 %collective-permute-start.1 = (f32[2,4096]{1,0:T(2,128)S(1)}, f32[2,4096]{1,0:T(2,128)S(1)}, u32[]{:S(2)}, u32[]{:S(2)}) collective-permute-start(f32[2,4096]{1,0:T(2,128)S(1)} %get-tuple-element.7), channel_id=1, source_target_pairs={{0,2},{1,3},{2,0},{3,1},{4,6},{5,7},{6,4},{7,5},{8,10},{9,11},{10,... | collective-permute-start | bytes 98312 | tf_op jit(solution)/shard_map/ppermute | solution.py:18
  42.4 10.3 %all-to-all-start.1 = ((bf16[8,32,512]{2,1,0:T(8,128)(2,1)}), bf16[8,32,512]{2,1,0:T(8,128)(2,1)S(1)}, u32[]{:S(2)}, u32[]{:S(2)}) async-start(bf16[8,32,512]{2,1,0:T(8,128)(2,1)} %broadcast_in_dim.5), calls=%async_computation.1 | async-start | bytes 524288 | tf_op jit(solution)/shard_map/all_to_all | solution.py:44
  58.7 5.6 %collective-permute-start.3 = (f32[16,256]{1,0:T(8,128)S(1)}, f32[16,256]{1,0:T(8,128)S(1)}, u32[]{:S(2)}, u32[]{:S(2)}) collective-permute-start(f32[16,256]{1,0:T(8,128)S(1)} %get-tuple-element.8), channel_id=1, source_target_pairs={{0,1},{1,2},{2,3},{3,0},{4,5},{5,6},{6,7},{7,4},{8,9},{9,10},{10,1... | collective-permute-start | bytes 49160 | tf_op jit(solution)/shard_map/ppermute | solution.py:18
  58.8 5.5 %collective-permute-start.5 = (f32[16,256]{1,0:T(8,128)S(1)}, f32[16,256]{1,0:T(8,128)S(1)}, u32[]{:S(2)}, u32[]{:S(2)}) collective-permute-start(f32[16,256]{1,0:T(8,128)S(1)} %get-tuple-element.9), channel_id=1, source_target_pairs={{0,3},{1,0},{2,1},{3,2},{4,7},{5,4},{6,5},{7,6},{8,11},{9,8},{10,9... | collective-permute-start | bytes 49160 | tf_op jit(solution)/shard_map/ppermute | solution.py:18
  62.6 4.6 %collective-permute-start.4 = (f32[16,256]{1,0:T(8,128)S(1)}, f32[16,256]{1,0:T(8,128)S(1)}, u32[]{:S(2)}, u32[]{:S(2)}) collective-permute-start(f32[16,256]{1,0:T(8,128)S(1)} %get-tuple-element.10), channel_id=1, source_target_pairs={{0,2},{1,3},{2,0},{3,1},{4,6},{5,7},{6,4},{7,5},{8,10},{9,11},{10,... | collective-permute-start | bytes 49160 | tf_op jit(solution)/shard_map/ppermute | solution.py:18

commit v6 on v5

--- a/solution.py
+++ b/solution.py
@@ -44,7 +44,7 @@
     return lax.all_to_all(copies, axis, 0, 0, tiled=True)
 
 
-def gradient_kernel(lengths_ref, act_ref, cot_ref, win_ref, wout_ref, out_ref):
+def gradient_kernel(layers_ref, lengths_ref, act_ref, cot_ref, win_ref, wout_ref, out_ref):
     example = pl.program_id(1)
     tokens = act_ref.shape[0]
     limit = lengths_ref[example] - lax.axis_index("mp") * tokens
@@ -60,26 +60,27 @@
     )
 
 
-def layer_gradients(activations, cotangents, lengths, project_in, project_out):
-    layers, examples, tokens, width = activations.shape
+def layer_gradients(layers, activations, cotangents, lengths, project_in, project_out):
+    slots = layers.shape[0]
+    _, examples, tokens, width = activations.shape
     factor = project_in.shape[1]
-    data = pl.BlockSpec((None, None, tokens, width), lambda l, e, lim: (l, e, 0, 0))
-    weights = pl.BlockSpec((None, factor, width), lambda l, e, lim: (l, 0, 0))
-    flops = 4 * layers * examples * tokens * width * factor
-    moved = 2 * (activations.size + cotangents.size + project_in.size + project_out.size)
+    data = pl.BlockSpec((None, None, tokens, width), lambda t, e, lay, lens: (lay[t], e, 0, 0))
+    weights = pl.BlockSpec((None, factor, width), lambda t, e, lay, lens: (lay[t], 0, 0))
+    flops = 4 * slots * examples * tokens * width * factor
+    moved = 2 * slots * (examples * tokens * width + factor * width) * 2
     return pl.pallas_call(
         gradient_kernel,
-        out_shape=jax.ShapeDtypeStruct((examples, layers, factor, factor), jnp.float32),
+        out_shape=jax.ShapeDtypeStruct((slots, examples, factor, factor), jnp.float32),
         grid_spec=pltpu.PrefetchScalarGridSpec(
-            num_scalar_prefetch=1,
-            grid=(layers, examples),
+            num_scalar_prefetch=2,
+            grid=(slots, examples),
             in_specs=[data, data, weights, weights],
             out_specs=pl.BlockSpec(
-                (None, None, factor, factor), lambda l, e, lim: (e, l, 0, 0)
+                (None, None, factor, factor), lambda t, e, lay, lens: (t, e, 0, 0)
             ),
         ),
         cost_estimate=pl.CostEstimate(flops=flops, transcendentals=0, bytes_accessed=moved),
-    )(lengths, activations, cotangents, project_in, project_out)
+    )(layers, lengths, activations, cotangents, project_in, project_out)
 
 
 def body_start(activations, cotangents, lengths, project_in, project_out, preconditioner, queries):
@@ -132,9 +133,14 @@
     block_size = factor_size * factor_size
     width_dp = lax.axis_size("dp")
     mp_place = lax.axis_index("mp")
-    partial_grad = layer_gradients(activations, cotangents, lengths, project_in, project_out)
-    partial_grad = partial_grad.reshape(partial_grad.shape[0], layer_count * block_size)
-    grad_mine = reduce_scatter_direct(partial_grad, "mp", 1).astype(jnp.bfloat16)
+    others = (mp_place + jnp.arange(1, layer_count, dtype=jnp.int32)) % layer_count
+    grad_args = (activations, cotangents, lengths, project_in, project_out)
+    grad_others = layer_gradients(others, *grad_args)
+    received = [shifted(grad_others[shift - 1], "mp", shift) for shift in range(1, layer_count)]
+    grad_mine = layer_gradients(mp_place[None].astype(jnp.int32), *grad_args)[0]
+    for grad in received:
+        grad_mine = grad_mine + grad
+    grad_mine = grad_mine.reshape(grad_mine.shape[0], block_size).astype(jnp.bfloat16)
     grad_all = all_gather_a2a(grad_mine, "dp")
     grad_all = grad_all.reshape(-1, grad_all.shape[-1])
     pre_part = jnp.dot(grad_all, preconditioner, preferred_element_type=jnp.float32)

time: 68.2 us -> 69.2 us (1.015)
  waiting for transfers between devices: 15.3 us -> 12.3 us
  Pallas kernels: 18.3 us -> 21 us
  other arithmetic: 0.69 us -> 2.06 us
    ppermute x6, waiting for transfers between devices: 8.5 us -> 5.54 us  [shifted(): return lax.ppermute(x, axis, [(i, (i + shift) % n) for i in range(n)])]
    pallas_call x1 -> x2, Pallas kernels: 18.3 us -> 21 us  [layer_gradients(): pl.pallas_call(gradient_kernel, out_shape=jax.ShapeDtypeStruct((slots, ex...]
    reshape x1 -> x0, local copies, waits for them, and re-layouts: 1.09 us -> none  [body_direct(): partial_grad.reshape(partial_grad.shape[0], layer_count * block_size)]
    squeeze x0 -> x1, local copies, waits for them, and re-layouts: none -> 0.92 us  [body_direct(): grad_others[shift - 1]]
    convert_element_type x1, other arithmetic: 0.03 us -> 0.86 us  [body_direct(): grad_mine.reshape(grad_mine.shape[0], block_size).astype(jnp.bfloat16)]
  transfers between devices with their start and end apart: 7 -> 7, of which waited for: 6 -> 4; matrix products, arithmetic and copies ran while one was open for 0% -> 0% of each run, Pallas kernels for 0% -> 10%
where the time goes in v6:
time: 69.2 us; the launch traced here: 68.8 us
  Pallas kernels  21 us (30%)
  starting transfers between devices  13.5 us (20%)
  waiting for transfers between devices  12.3 us (18%)
  blocking collectives  9.02 us (13%)
  matrix products  8.81 us (13%)
  other arithmetic  2.06 us (3%)
  local copies, waits for them, and re-layouts  1.89 us (3%)
    pallas_call x2, Pallas kernels, layer_gradients(): pl.pallas_call(gradient_kernel, out_shape=jax.ShapeDtypeStruct((slots, ex...  21 us
    ppermute x6, starting transfers between devices, shifted(): return lax.ppermute(x, axis, [(i, (i + shift) % n) for i in range(n)])  10.1 us
    all_to_all x1, blocking collectives, all_gather_a2a(): return lax.all_to_all(copies, axis, 0, 0, tiled=True)  9.02 us
    all_to_all x1, waiting for transfers between devices, all_gather_a2a(): return lax.all_to_all(copies, axis, 0, 0, tiled=True)  6.8 us
    dot_general x1, matrix products, body_direct(): lax.dot_general(both_all, query_blocks, (((0, 2), (1, 2)), ((), ())), pre...  5.98 us
    ppermute x6, waiting for transfers between devices, shifted(): return lax.ppermute(x, axis, [(i, (i + shift) % n) for i in range(n)])  5.54 us
    all_to_all x1, starting transfers between devices, all_gather_a2a(): return lax.all_to_all(copies, axis, 0, 0, tiled=True)  3.41 us
    dot_general x1, matrix products, body_direct(): jnp.dot(grad_all, preconditioner, preferred_element_type=jnp.float32)  2.83 us
  transfers between devices with their start and end apart: 7, of which 4 were waited for; matrix products, arithmetic and copies ran while one was open for 0% of the time, Pallas kernels for 10%

profile of v6, /device:TPU:0, one launch (start us, length us, event | category | flops | bytes accessed | tf_op | source)
XLA Modules:
  0.0 68.8 jit_solution(4112299603861052221)
XLA Ops:
  0.0 0.6 and_select_fusion.layers_ref
  0.6 14.5 %shard_map.74 = f32[3,2,64,64]{3,2,1,0:T(8,128)} custom-call(s32[3]{0:T(128)} %and_select_fusion.layers_ref, s32[2]{0:T(128)} %lengths_ref.3, bf16[4,2,256,4096]{3,2,1,0:T(8,128)(2,1)} %act_ref.3, bf16[4,2,256,4096]{3,2,1,0:T(8,128)(2,1)} %cot_ref.3, bf16[4,64,4096]{2,1,0:T(8,128)(2,1)} %win_ref.3, bf16[4,64,4096]{2,1,0:T(8,128)(2,1)} %wout_ref.3), custom_call_target="tpu_custom_call" | custom-call | flops 1610612736 | bytes 28311552 | tf_op jit(solution)/shard_map/pallas_call | solution.py:71
  15.0 0.9 %slice_bitcast_fusion.2 = (f32[2,64,64]{2,1,0:T(8,128)S(1)}, f32[2,64,64]{2,1,0:T(8,128)S(1)}, f32[2,64,64]{2,1,0:T(8,128)S(1)}) fusion(f32[3,2,64,64]{3,2,1,0:T(8,128)} %shard_map.74), kind=kLoop, calls=%fused_computation.7 | loop fusion | bytes 196608 | tf_op jit(solution)/shard_map/squeeze | solution.py:139
  15.9 5.1 %collective-permute-start.2 = (f32[2,64,64]{2,1,0:T(8,128)S(1)}, f32[2,64,64]{2,1,0:T(8,128)S(1)}, u32[]{:S(2)}, u32[]{:S(2)}) collective-permute-start(f32[2,64,64]{2,1,0:T(8,128)S(1)} %get-tuple-element.6), channel_id=1, source_target_pairs={{0,3},{1,0},{2,1},{3,2},{4,7},{5,4},{6,5},{7,6},{8,11},{9,8},{10,9... | collective-permute-start | bytes 98312 | tf_op jit(solution)/shard_map/ppermute | solution.py:18
  21.1 0.0 collective-permute-start.1
  21.1 1.0 %collective-permute-start = (f32[2,64,64]{2,1,0:T(8,128)S(1)}, f32[2,64,64]{2,1,0:T(8,128)S(1)}, u32[]{:S(2)}, u32[]{:S(2)}) collective-permute-start(f32[2,64,64]{2,1,0:T(8,128)S(1)} %get-tuple-element.5), channel_id=1, source_target_pairs={{0,1},{1,2},{2,3},{3,0},{4,5},{5,6},{6,7},{7,4},{8,9},{9,10},{10,1... | collective-permute-start | bytes 98312 | tf_op jit(solution)/shard_map/ppermute | solution.py:18
  22.1 6.6 %shard_map.73 = f32[1,2,64,64]{3,2,1,0:T(8,128)} custom-call(s32[1]{0:T(128)} %bitcast.layers_ref, s32[2]{0:T(128)} %lengths_ref.3, bf16[4,2,256,4096]{3,2,1,0:T(8,128)(2,1)} %act_ref.3, bf16[4,2,256,4096]{3,2,1,0:T(8,128)(2,1)} %cot_ref.3, bf16[4,64,4096]{2,1,0:T(8,128)(2,1)} %win_ref.3, bf16[4,64,4096]{2,1,0:T(8,128)(2,1)} %wout_ref.3), custom_call_target="tpu_custom_call" | custom-call | flops 536870912 | bytes 9437184 | tf_op jit(solution)/shard_map/pallas_call | solution.py:71
  28.6 0.0 collective-permute-done.2
  28.6 0.0 collective-permute-done.1
  28.6 0.0 collective-permute-done
  28.7 0.9 %fusion.8 = bf16[2,64,64]{2,1,0:T(8,128)(2,1)S(1)} fusion(f32[2,64,64]{2,1,0:T(8,128)S(1)} %collective-permute-done.2, f32[2,64,64]{2,1,0:T(8,128)S(1)} %collective-permute-done.1, f32[2,64,64]{2,1,0:T(8,128)S(1)} %collective-permute-done, f32[1,2,64,64]{3,2,1,0:T(8,128)} %shard_map.73), kind=kLoop, calls=%fused_computation.11 | loop fusion | flops 32768 | bytes 147456 | tf_op jit(solution)/shard_map/convert_element_type | solution.py:143
  29.5 0.1 convert_element_type.20
  29.6 0.1 broadcast_in_dim.7
  29.7 9.0 %all_to_all.10 = bf16[8,2,4096]{2,1,0:T(2,128)(2,1)S(1)} all-to-all(bf16[8,2,4096]{2,1,0:T(2,128)(2,1)S(1)} %broadcast_in_dim.7), channel_id=1, replica_groups=mesh['dp'=8,'mp'=4] {'dp'}, dimensions={0} | all-to-all | bytes 262144 | tf_op jit(solution)/shard_map/all_to_all | solution.py:44
  38.7 0.1 reshape.14
  38.8 2.8 %fusion.10 = (bf16[16,512]{1,0:T(8,128)(2,1)S(1)}, f32[16,512]{1,0:T(8,128)S(1)}) fusion(bf16[16,4096]{1,0:T(8,128)(2,1)S(1)} %reshape.14, bf16[4096,512]{1,0:T(8,128)(2,1)} %param.12), kind=kOutput, calls=%fused_computation.22 | convolution fusion | flops 67117056 | bytes 4374528 | tf_op jit(solution)/shard_map/dot_general | solution.py:146
  41.6 0.7 %broadcast_in_dim.8 = bf16[8,32,512]{2,1,0:T(8,128)(2,1)} broadcast(bf16[32,512]{1,0:T(8,128)(2,1)S(1)} %pad_maximum_fusion), dimensions={1,2} | broadcast | bytes 294912 | tf_op jit(solution)/shard_map/broadcast_in_dim | solution.py:43
  42.4 3.4 %all-to-all-start.1 = ((bf16[8,32,512]{2,1,0:T(8,128)(2,1)}), bf16[8,32,512]{2,1,0:T(8,128)(2,1)S(1)}, u32[]{:S(2)}, u32[]{:S(2)}) async-start(bf16[8,32,512]{2,1,0:T(8,128)(2,1)} %broadcast_in_dim.8), calls=%async_computation.1 | async-start | bytes 524288 | tf_op jit(solution)/shard_map/all_to_all | solution.py:44
  45.8 6.8 %all-to-all-done.1 = bf16[8,32,512]{2,1,0:T(8,128)(2,1)S(1)} async-done(((bf16[8,32,512]{2,1,0:T(8,128)(2,1)}), bf16[8,32,512]{2,1,0:T(8,128)(2,1)S(1)}, u32[]{:S(2)}, u32[]{:S(2)}) %all-to-all-start.1) | async-done | bytes 262176 | tf_op jit(solution)/shard_map/all_to_all | solution.py:44
  52.6 6.0 %fusion.3 = f32[32,1024]{1,0:T(8,128)S(1)} fusion(bf16[8,32,512]{2,1,0:T(8,128)(2,1)S(1)} %all-to-all-done.1, bf16[128,8,8,512]{3,2,1,0:T(8,128)(2,1)} %bitcast.26), kind=kOutput, calls=%fused_computation.3 | convolution fusion | flops 268435456 | bytes 8781824 | tf_op jit(solution)/shard_map/dot_general | solution.py:152
  58.7 2.9 %collective-permute-start.5 = (f32[16,256]{1,0:T(8,128)S(1)}, f32[16,256]{1,0:T(8,128)S(1)}, u32[]{:S(2)}, u32[]{:S(2)}) collective-permute-start(f32[16,256]{1,0:T(8,128)S(1)} %get-tuple-element.9), channel_id=1, source_target_pairs={{0,3},{1,0},{2,1},{3,2},{4,7},{5,4},{6,5},{7,6},{8,11},{9,8},{10,9... | collective-permute-start | bytes 49160 | tf_op jit(solution)/shard_map/ppermute | solution.py:18
  61.5 1.1 %collective-permute-start.4 = (f32[16,256]{1,0:T(8,128)S(1)}, f32[16,256]{1,0:T(8,128)S(1)}, u32[]{:S(2)}, u32[]{:S(2)}) collective-permute-start(f32[16,256]{1,0:T(8,128)S(1)} %get-tuple-element.10), channel_id=1, source_target_pairs={{0,2},{1,3},{2,0},{3,1},{4,6},{5,7},{6,4},{7,5},{8,10},{9,11},{10,... | collective-permute-start | bytes 49160 | tf_op jit(solution)/shard_map/ppermute | solution.py:18
  62.6 0.0 collective-permute-start.3
  62.7 0.3 collective-permute-done.5
  63.0 3.2 %collective-permute-done.4 = f32[16,256]{1,0:T(8,128)S(1)} collective-permute-done((f32[16,256]{1,0:T(8,128)S(1)}, f32[16,256]{1,0:T(8,128)S(1)}, u32[]{:S(2)}, u32[]{:S(2)}) %collective-permute-start.4) | collective-permute-done | bytes 16416 | tf_op jit(solution)/shard_map/ppermute | solution.py:18
  66.2 2.0 %collective-permute-done.3 = f32[16,256]{1,0:T(8,128)S(1)} collective-permute-done((f32[16,256]{1,0:T(8,128)S(1)}, f32[16,256]{1,0:T(8,128)S(1)}, u32[]{:S(2)}, u32[]{:S(2)}) %collective-permute-start.3) | collective-permute-done | bytes 16416 | tf_op jit(solution)/shard_map/ppermute | solution.py:18
  68.2 0.6 add_add_fusion
  (4 shorter events, 0.1 us)
Async XLA Ops:
  15.9 12.7 %collective-permute-start.2 = (f32[2,64,64]{2,1,0:T(8,128)S(1)}, f32[2,64,64]{2,1,0:T(8,128)S(1)}, u32[]{:S(2)}, u32[]{:S(2)}) collective-permute-start(f32[2,64,64]{2,1,0:T(8,128)S(1)} %get-tuple-element.6), channel_id=1, source_target_pairs={{0,3},{1,0},{2,1},{3,2},{4,7},{5,4},{6,5},{7,6},{8,11},{9,8},{10,9... | collective-permute-start | bytes 98312 | tf_op jit(solution)/shard_map/ppermute | solution.py:18
  21.1 7.6 %collective-permute-start.1 = (f32[2,64,64]{2,1,0:T(8,128)S(1)}, f32[2,64,64]{2,1,0:T(8,128)S(1)}, u32[]{:S(2)}, u32[]{:S(2)}) collective-permute-start(f32[2,64,64]{2,1,0:T(8,128)S(1)} %get-tuple-element.7), channel_id=1, source_target_pairs={{0,2},{1,3},{2,0},{3,1},{4,6},{5,7},{6,4},{7,5},{8,10},{9,11},{10,... | collective-permute-start | bytes 98312 | tf_op jit(solution)/shard_map/ppermute | solution.py:18
  21.1 7.6 %collective-permute-start = (f32[2,64,64]{2,1,0:T(8,128)S(1)}, f32[2,64,64]{2,1,0:T(8,128)S(1)}, u32[]{:S(2)}, u32[]{:S(2)}) collective-permute-start(f32[2,64,64]{2,1,0:T(8,128)S(1)} %get-tuple-element.5), channel_id=1, source_target_pairs={{0,1},{1,2},{2,3},{3,0},{4,5},{5,6},{6,7},{7,4},{8,9},{9,10},{10,1... | collective-permute-start | bytes 98312 | tf_op jit(solution)/shard_map/ppermute | solution.py:18
  42.4 10.3 %all-to-all-start.1 = ((bf16[8,32,512]{2,1,0:T(8,128)(2,1)}), bf16[8,32,512]{2,1,0:T(8,128)(2,1)S(1)}, u32[]{:S(2)}, u32[]{:S(2)}) async-start(bf16[8,32,512]{2,1,0:T(8,128)(2,1)} %broadcast_in_dim.8), calls=%async_computation.1 | async-start | bytes 524288 | tf_op jit(solution)/shard_map/all_to_all | solution.py:44
  58.7 4.3 %collective-permute-start.5 = (f32[16,256]{1,0:T(8,128)S(1)}, f32[16,256]{1,0:T(8,128)S(1)}, u32[]{:S(2)}, u32[]{:S(2)}) collective-permute-start(f32[16,256]{1,0:T(8,128)S(1)} %get-tuple-element.9), channel_id=1, source_target_pairs={{0,3},{1,0},{2,1},{3,2},{4,7},{5,4},{6,5},{7,6},{8,11},{9,8},{10,9... | collective-permute-start | bytes 49160 | tf_op jit(solution)/shard_map/ppermute | solution.py:18
  61.5 4.6 %collective-permute-start.4 = (f32[16,256]{1,0:T(8,128)S(1)}, f32[16,256]{1,0:T(8,128)S(1)}, u32[]{:S(2)}, u32[]{:S(2)}) collective-permute-start(f32[16,256]{1,0:T(8,128)S(1)} %get-tuple-element.10), channel_id=1, source_target_pairs={{0,2},{1,3},{2,0},{3,1},{4,6},{5,7},{6,4},{7,5},{8,10},{9,11},{10,... | collective-permute-start | bytes 49160 | tf_op jit(solution)/shard_map/ppermute | solution.py:18
  62.6 5.5 %collective-permute-start.3 = (f32[16,256]{1,0:T(8,128)S(1)}, f32[16,256]{1,0:T(8,128)S(1)}, u32[]{:S(2)}, u32[]{:S(2)}) collective-permute-start(f32[16,256]{1,0:T(8,128)S(1)} %get-tuple-element.8), channel_id=1, source_target_pairs={{0,1},{1,2},{2,3},{3,0},{4,5},{5,6},{6,7},{7,4},{8,9},{9,10},{10,1... | collective-permute-start | bytes 49160 | tf_op jit(solution)/shard_map/ppermute | solution.py:18

commit v7 on v5

--- a/solution.py
+++ b/solution.py
@@ -69,13 +69,13 @@
     moved = 2 * (activations.size + cotangents.size + project_in.size + project_out.size)
     return pl.pallas_call(
         gradient_kernel,
-        out_shape=jax.ShapeDtypeStruct((examples, layers, factor, factor), jnp.float32),
+        out_shape=jax.ShapeDtypeStruct((layers, examples, factor, factor), jnp.float32),
         grid_spec=pltpu.PrefetchScalarGridSpec(
             num_scalar_prefetch=1,
             grid=(layers, examples),
             in_specs=[data, data, weights, weights],
             out_specs=pl.BlockSpec(
-                (None, None, factor, factor), lambda l, e, lim: (e, l, 0, 0)
+                (None, None, factor, factor), lambda l, e, lim: (l, e, 0, 0)
             ),
         ),
         cost_estimate=pl.CostEstimate(flops=flops, transcendentals=0, bytes_accessed=moved),
@@ -133,20 +133,19 @@
     width_dp = lax.axis_size("dp")
     mp_place = lax.axis_index("mp")
     partial_grad = layer_gradients(activations, cotangents, lengths, project_in, project_out)
-    partial_grad = partial_grad.reshape(partial_grad.shape[0], layer_count * block_size)
-    grad_mine = reduce_scatter_direct(partial_grad, "mp", 1).astype(jnp.bfloat16)
+    grad_mine = reduce_scatter_direct(partial_grad, "mp", 0)[0]
+    grad_mine = grad_mine.astype(jnp.bfloat16).reshape(grad_mine.shape[0], block_size)
     grad_all = all_gather_a2a(grad_mine, "dp")
     grad_all = grad_all.reshape(-1, grad_all.shape[-1])
     pre_part = jnp.dot(grad_all, preconditioner, preferred_element_type=jnp.float32)
-    upper_grad, lower_grad = split_parts(pre_part)
-    both = jnp.concatenate([upper_grad, lower_grad], axis=0)
-    both_all = all_gather_a2a(both, "dp")
+    upper_grad, lower_grad = split_parts(all_gather_a2a(pre_part, "dp"))
+    both_all = jnp.concatenate([upper_grad, lower_grad], axis=1)
     blocks, block = both_all.shape[0], both_all.shape[2]
     query_blocks = queries.reshape(queries.shape[0], blocks, block)
     products = lax.dot_general(
         both_all, query_blocks, (((0, 2), (1, 2)), ((), ())), preferred_element_type=jnp.float32
     )
-    examples = upper_grad.shape[0]
+    examples = upper_grad.shape[1]
     partial_scores = products[:examples] + products[examples:]
     return reduce_scatter_direct(partial_scores, "mp", 1)
 

time: 68.2 us -> 68.1 us (level)
  waiting for transfers between devices: 15.3 us -> 13.5 us
  starting transfers between devices: 13.4 us -> 14.5 us
  other arithmetic: 0.69 us -> 1.54 us
    ppermute x6, waiting for transfers between devices: 8.5 us -> 6.68 us  [shifted(): return lax.ppermute(x, axis, [(i, (i + shift) % n) for i in range(n)])]
    ppermute x6, starting transfers between devices: 10 us -> 11.1 us  [shifted(): return lax.ppermute(x, axis, [(i, (i + shift) % n) for i in range(n)])]
    reshape x1 -> x0, local copies, waits for them, and re-layouts: 1.09 us -> none  [body_direct(): partial_grad.reshape(partial_grad.shape[0], layer_count * block_size)]
    dynamic_slice x2, local copies, waits for them, and re-layouts: 0.03 us -> 0.93 us  [reduce_scatter_direct(): piece = lax.dynamic_slice_in_dim(x, (me + shift) % n * width, width, dim)]
    convert_element_type x1 -> x2, other arithmetic: 0.03 us -> 0.87 us  [the longest x1 0.86 us: body_direct(): grad_mine.astype(jnp.bfloat16).reshape(grad_mine.shape[0], block_size)]
  transfers between devices with their start and end apart: 7 -> 7, of which waited for: 6 -> 7; matrix products, arithmetic and copies ran while one was open for 0% -> 0% of each run, Pallas kernels for 0% -> 0%
where the time goes in v7:
time: 68.1 us; the launch traced here: 67.7 us
  Pallas kernels  18.3 us (27%)
  starting transfers between devices  14.5 us (21%)
  waiting for transfers between devices  13.5 us (20%)
  blocking collectives  9.02 us (13%)
  matrix products  8.81 us (13%)
  local copies, waits for them, and re-layouts  1.9 us (3%)
  other arithmetic  1.54 us (2%)
    pallas_call x1, Pallas kernels, layer_gradients(): pl.pallas_call(gradient_kernel, out_shape=jax.ShapeDtypeStruct((layers, e...  18.3 us
    ppermute x6, starting transfers between devices, shifted(): return lax.ppermute(x, axis, [(i, (i + shift) % n) for i in range(n)])  11.1 us
    all_to_all x1, blocking collectives, all_gather_a2a(): return lax.all_to_all(copies, axis, 0, 0, tiled=True)  9.02 us
    all_to_all x1, waiting for transfers between devices, all_gather_a2a(): return lax.all_to_all(copies, axis, 0, 0, tiled=True)  6.81 us
    ppermute x6, waiting for transfers between devices, shifted(): return lax.ppermute(x, axis, [(i, (i + shift) % n) for i in range(n)])  6.68 us
    dot_general x1, matrix products, body_direct(): lax.dot_general(both_all, query_blocks, (((0, 2), (1, 2)), ((), ())), pre...  5.98 us
    all_to_all x1, starting transfers between devices, all_gather_a2a(): return lax.all_to_all(copies, axis, 0, 0, tiled=True)  3.41 us
    dot_general x1, matrix products, body_direct(): jnp.dot(grad_all, preconditioner, preferred_element_type=jnp.float32)  2.83 us
  transfers between devices with their start and end apart: 7, of which 7 were waited for; matrix products, arithmetic and copies ran while one was open for 0% of the time, Pallas kernels for 0%

profile of v7, /device:TPU:0, one launch (start us, length us, event | category | flops | bytes accessed | tf_op | source)
XLA Modules:
  0.0 67.7 jit_solution(4672497787476369455)
XLA Ops:
  0.0 18.3 %shard_map.73 = f32[4,2,64,64]{3,2,1,0:T(8,128)} custom-call(s32[2]{0:T(128)} %lengths_ref.1, bf16[4,2,256,4096]{3,2,1,0:T(8,128)(2,1)} %act_ref.1, bf16[4,2,256,4096]{3,2,1,0:T(8,128)(2,1)} %cot_ref.1, bf16[4,64,4096]{2,1,0:T(8,128)(2,1)} %win_ref.1, bf16[4,64,4096]{2,1,0:T(8,128)(2,1)} %wout_ref.1), custom_call_target="tpu_custom_call" | custom-call | flops 2147483648 | bytes 37748736 | tf_op jit(solution)/shard_map/pallas_call | solution.py:70
  18.3 0.9 %constant_dynamic-slice_fusion.5 = (f32[1,2,64,64]{3,2,1,0:T(8,128)S(1)}, f32[1,2,64,64]{3,2,1,0:T(8,128)S(1)}, f32[1,2,64,64]{3,2,1,0:T(8,128)S(1)}) fusion(f32[4,2,64,64]{3,2,1,0:T(8,128)} %shard_map.73, s32[]{:T(128)S(6)} %select_n.47, s32[]{:T(128)S(6)} %select_n.51, s32[]{:T(128)S(6)} %select_n.49), kind=kLoop, calls=%fused_computation.16 | loop fusion | bytes 196620 | tf_op jit(solution)/shard_map/dynamic_slice | solution.py:27
  19.2 3.1 %collective-permute-start = (f32[1,2,64,64]{3,2,1,0:T(8,128)S(1)}, f32[1,2,64,64]{3,2,1,0:T(8,128)S(1)}, u32[]{:S(2)}, u32[]{:S(2)}) collective-permute-start(f32[1,2,64,64]{3,2,1,0:T(8,128)S(1)} %get-tuple-element.5), channel_id=1, source_target_pairs={{0,1},{1,2},{2,3},{3,0},{4,5},{5,6},{6,7},{7,4},{8,9},{9,10},{10,1... | collective-permute-start | bytes 98312 | tf_op jit(solution)/shard_map/ppermute | solution.py:18
  22.3 2.6 %collective-permute-start.1 = (f32[1,2,64,64]{3,2,1,0:T(8,128)S(1)}, f32[1,2,64,64]{3,2,1,0:T(8,128)S(1)}, u32[]{:S(2)}, u32[]{:S(2)}) collective-permute-start(f32[1,2,64,64]{3,2,1,0:T(8,128)S(1)} %get-tuple-element.7), channel_id=1, source_target_pairs={{0,2},{1,3},{2,0},{3,1},{4,6},{5,7},{6,4},{7,5},{8,10},{9,11},{10,... | collective-permute-start | bytes 98312 | tf_op jit(solution)/shard_map/ppermute | solution.py:18
  24.9 1.3 %collective-permute-start.2 = (f32[1,2,64,64]{3,2,1,0:T(8,128)S(1)}, f32[1,2,64,64]{3,2,1,0:T(8,128)S(1)}, u32[]{:S(2)}, u32[]{:S(2)}) collective-permute-start(f32[1,2,64,64]{3,2,1,0:T(8,128)S(1)} %get-tuple-element.6), channel_id=1, source_target_pairs={{0,3},{1,0},{2,1},{3,2},{4,7},{5,4},{6,5},{7,6},{8,11},{9,8},{10,9... | collective-permute-start | bytes 98312 | tf_op jit(solution)/shard_map/ppermute | solution.py:18
  26.2 0.5 collective-permute-done
  26.8 2.6 %collective-permute-done.1 = f32[1,2,64,64]{3,2,1,0:T(8,128)S(1)} collective-permute-done((f32[1,2,64,64]{3,2,1,0:T(8,128)S(1)}, f32[1,2,64,64]{3,2,1,0:T(8,128)S(1)}, u32[]{:S(2)}, u32[]{:S(2)}) %collective-permute-start.1) | collective-permute-done | bytes 32800 | tf_op jit(solution)/shard_map/ppermute | solution.py:18
  29.4 0.2 collective-permute-done.2
  29.6 0.9 %add_convert_fusion = bf16[1,2,64,64]{3,2,1,0:T(8,128)(2,1)S(1)} fusion(f32[1,2,64,64]{3,2,1,0:T(8,128)S(1)} %collective-permute-done.2, f32[1,2,64,64]{3,2,1,0:T(8,128)S(1)} %collective-permute-done.1, f32[1,2,64,64]{3,2,1,0:T(8,128)S(1)} %collective-permute-done, f32[4,2,64,64]{3,2,1,0:T(8,128)} %shard_map.73, s32[]{:T(128)S(6)} %select_n.45), kind=kLoop, calls=%fused_computation.9 | loop fusion | flops 32768 | bytes 147460 | tf_op jit(solution)/shard_map/convert_element_type | solution.py:137
  30.5 0.1 convert_element_type.20
  30.6 0.1 broadcast_in_dim.4
  30.6 9.0 %all_to_all.10 = bf16[8,2,4096]{2,1,0:T(2,128)(2,1)S(1)} all-to-all(bf16[8,2,4096]{2,1,0:T(2,128)(2,1)S(1)} %broadcast_in_dim.4), channel_id=1, replica_groups=mesh['dp'=8,'mp'=4] {'dp'}, dimensions={0} | all-to-all | bytes 262144 | tf_op jit(solution)/shard_map/all_to_all | solution.py:44
  39.7 0.1 reshape.13
  39.7 2.8 %fusion.10 = f32[16,512]{1,0:T(8,128)S(1)} fusion(bf16[16,4096]{1,0:T(8,128)(2,1)S(1)} %reshape.13, bf16[4096,512]{1,0:T(8,128)(2,1)} %param.12), kind=kOutput, calls=%fused_computation.18 | convolution fusion | flops 67108864 | bytes 4358144 | tf_op jit(solution)/shard_map/dot_general | solution.py:140
  42.6 0.7 %broadcast_in_dim.5 = f32[8,16,512]{2,1,0:T(8,128)} broadcast(f32[16,512]{1,0:T(8,128)S(1)} %fusion.10), dimensions={1,2} | broadcast | bytes 294912 | tf_op jit(solution)/shard_map/broadcast_in_dim | solution.py:43
  43.3 3.4 %all-to-all-start.1 = ((f32[8,16,512]{2,1,0:T(8,128)}), f32[8,16,512]{2,1,0:T(8,128)S(1)}, u32[]{:S(2)}, u32[]{:S(2)}) async-start(f32[8,16,512]{2,1,0:T(8,128)} %broadcast_in_dim.5), calls=%async_computation.1 | async-start | bytes 524288 | tf_op jit(solution)/shard_map/all_to_all | solution.py:44
  46.7 6.8 %all-to-all-done.1 = f32[8,16,512]{2,1,0:T(8,128)S(1)} async-done(((f32[8,16,512]{2,1,0:T(8,128)}), f32[8,16,512]{2,1,0:T(8,128)S(1)}, u32[]{:S(2)}, u32[]{:S(2)}) %all-to-all-start.1) | async-done | bytes 262176 | tf_op jit(solution)/shard_map/all_to_all | solution.py:44
  53.6 6.0 %fusion.3 = f32[32,1024]{1,0:T(8,128)S(1)} fusion(bf16[128,8,8,512]{3,2,1,0:T(8,128)(2,1)} %bitcast.12, bf16[8,16,512]{2,1,0:T(8,128)(2,1)S(1)} %subtract_convert_fusion, bf16[8,16,512]{2,1,0:T(8,128)(2,1)S(1)} %convert_element_type.21), kind=kOutput, calls=%fused_computation.3 | convolution fusion | flops 268959744 | bytes 8781824 | tf_op jit(solution)/shard_map/dot_general | solution.py:145
  59.6 1.6 %collective-permute-start.3 = (f32[16,256]{1,0:T(8,128)S(1)}, f32[16,256]{1,0:T(8,128)S(1)}, u32[]{:S(2)}, u32[]{:S(2)}) collective-permute-start(f32[16,256]{1,0:T(8,128)S(1)} %get-tuple-element.8), channel_id=1, source_target_pairs={{0,1},{1,2},{2,3},{3,0},{4,5},{5,6},{6,7},{7,4},{8,9},{9,10},{10,1... | collective-permute-start | bytes 49160 | tf_op jit(solution)/shard_map/ppermute | solution.py:18
  61.3 2.0 %collective-permute-start.4 = (f32[16,256]{1,0:T(8,128)S(1)}, f32[16,256]{1,0:T(8,128)S(1)}, u32[]{:S(2)}, u32[]{:S(2)}) collective-permute-start(f32[16,256]{1,0:T(8,128)S(1)} %get-tuple-element.10), channel_id=1, source_target_pairs={{0,2},{1,3},{2,0},{3,1},{4,6},{5,7},{6,4},{7,5},{8,10},{9,11},{10,... | collective-permute-start | bytes 49160 | tf_op jit(solution)/shard_map/ppermute | solution.py:18
  63.3 0.4 collective-permute-start.5
  63.7 1.6 %collective-permute-done.3 = f32[16,256]{1,0:T(8,128)S(1)} collective-permute-done((f32[16,256]{1,0:T(8,128)S(1)}, f32[16,256]{1,0:T(8,128)S(1)}, u32[]{:S(2)}, u32[]{:S(2)}) %collective-permute-start.3) | collective-permute-done | bytes 16416 | tf_op jit(solution)/shard_map/ppermute | solution.py:18
  65.3 0.6 collective-permute-done.4
  65.9 1.1 %collective-permute-done.5 = f32[16,256]{1,0:T(8,128)S(1)} collective-permute-done((f32[16,256]{1,0:T(8,128)S(1)}, f32[16,256]{1,0:T(8,128)S(1)}, u32[]{:S(2)}, u32[]{:S(2)}) %collective-permute-start.5) | collective-permute-done | bytes 16416 | tf_op jit(solution)/shard_map/ppermute | solution.py:18
  67.1 0.6 add_add_fusion
  (4 shorter events, 0.1 us)
Async XLA Ops:
  19.2 7.6 %collective-permute-start = (f32[1,2,64,64]{3,2,1,0:T(8,128)S(1)}, f32[1,2,64,64]{3,2,1,0:T(8,128)S(1)}, u32[]{:S(2)}, u32[]{:S(2)}) collective-permute-start(f32[1,2,64,64]{3,2,1,0:T(8,128)S(1)} %get-tuple-element.5), channel_id=1, source_target_pairs={{0,1},{1,2},{2,3},{3,0},{4,5},{5,6},{6,7},{7,4},{8,9},{9,10},{10,1... | collective-permute-start | bytes 98312 | tf_op jit(solution)/shard_map/ppermute | solution.py:18
  22.3 7.1 %collective-permute-start.1 = (f32[1,2,64,64]{3,2,1,0:T(8,128)S(1)}, f32[1,2,64,64]{3,2,1,0:T(8,128)S(1)}, u32[]{:S(2)}, u32[]{:S(2)}) collective-permute-start(f32[1,2,64,64]{3,2,1,0:T(8,128)S(1)} %get-tuple-element.7), channel_id=1, source_target_pairs={{0,2},{1,3},{2,0},{3,1},{4,6},{5,7},{6,4},{7,5},{8,10},{9,11},{10,... | collective-permute-start | bytes 98312 | tf_op jit(solution)/shard_map/ppermute | solution.py:18
  24.9 4.7 %collective-permute-start.2 = (f32[1,2,64,64]{3,2,1,0:T(8,128)S(1)}, f32[1,2,64,64]{3,2,1,0:T(8,128)S(1)}, u32[]{:S(2)}, u32[]{:S(2)}) collective-permute-start(f32[1,2,64,64]{3,2,1,0:T(8,128)S(1)} %get-tuple-element.6), channel_id=1, source_target_pairs={{0,3},{1,0},{2,1},{3,2},{4,7},{5,4},{6,5},{7,6},{8,11},{9,8},{10,9... | collective-permute-start | bytes 98312 | tf_op jit(solution)/shard_map/ppermute | solution.py:18
  43.3 10.3 %all-to-all-start.1 = ((f32[8,16,512]{2,1,0:T(8,128)}), f32[8,16,512]{2,1,0:T(8,128)S(1)}, u32[]{:S(2)}, u32[]{:S(2)}) async-start(f32[8,16,512]{2,1,0:T(8,128)} %broadcast_in_dim.5), calls=%async_computation.1 | async-start | bytes 524288 | tf_op jit(solution)/shard_map/all_to_all | solution.py:44
  59.6 5.7 %collective-permute-start.3 = (f32[16,256]{1,0:T(8,128)S(1)}, f32[16,256]{1,0:T(8,128)S(1)}, u32[]{:S(2)}, u32[]{:S(2)}) collective-permute-start(f32[16,256]{1,0:T(8,128)S(1)} %get-tuple-element.8), channel_id=1, source_target_pairs={{0,1},{1,2},{2,3},{3,0},{4,5},{5,6},{6,7},{7,4},{8,9},{9,10},{10,1... | collective-permute-start | bytes 49160 | tf_op jit(solution)/shard_map/ppermute | solution.py:18
  61.3 4.6 %collective-permute-start.4 = (f32[16,256]{1,0:T(8,128)S(1)}, f32[16,256]{1,0:T(8,128)S(1)}, u32[]{:S(2)}, u32[]{:S(2)}) collective-permute-start(f32[16,256]{1,0:T(8,128)S(1)} %get-tuple-element.10), channel_id=1, source_target_pairs={{0,2},{1,3},{2,0},{3,1},{4,6},{5,7},{6,4},{7,5},{8,10},{9,11},{10,... | collective-permute-start | bytes 49160 | tf_op jit(solution)/shard_map/ppermute | solution.py:18
  63.3 3.7 %collective-permute-start.5 = (f32[16,256]{1,0:T(8,128)S(1)}, f32[16,256]{1,0:T(8,128)S(1)}, u32[]{:S(2)}, u32[]{:S(2)}) collective-permute-start(f32[16,256]{1,0:T(8,128)S(1)} %get-tuple-element.9), channel_id=1, source_target_pairs={{0,3},{1,0},{2,1},{3,2},{4,7},{5,4},{6,5},{7,6},{8,11},{9,8},{10,9... | collective-permute-start | bytes 49160 | tf_op jit(solution)/shard_map/ppermute | solution.py:18

commit v8 on v7

--- a/solution.py
+++ b/solution.py
@@ -45,26 +45,28 @@
 
 
 def gradient_kernel(lengths_ref, act_ref, cot_ref, win_ref, wout_ref, out_ref):
-    example = pl.program_id(1)
-    tokens = act_ref.shape[0]
-    limit = lengths_ref[example] - lax.axis_index("mp") * tokens
+    tokens = act_ref.shape[1]
+    offset = lax.axis_index("mp") * tokens
     nt = (((1,), (1,)), ((), ()))
-    left = lax.dot_general(
-        act_ref[...], win_ref[...], nt, preferred_element_type=jnp.float32
-    ).astype(jnp.bfloat16)
-    right = lax.dot_general(cot_ref[...], wout_ref[...], nt, preferred_element_type=jnp.float32)
-    rows = lax.broadcasted_iota(jnp.int32, right.shape, 0)
-    right = jnp.where(rows < limit, right, 0.0).astype(jnp.bfloat16)
-    out_ref[...] = lax.dot_general(
-        right, left, (((0,), (0,)), ((), ())), preferred_element_type=jnp.float32
-    )
+    for example in range(act_ref.shape[0]):
+        left = lax.dot_general(
+            act_ref[example], win_ref[...], nt, preferred_element_type=jnp.float32
+        ).astype(jnp.bfloat16)
+        right = lax.dot_general(
+            cot_ref[example], wout_ref[...], nt, preferred_element_type=jnp.float32
+        )
+        rows = lax.broadcasted_iota(jnp.int32, right.shape, 0)
+        right = jnp.where(rows < lengths_ref[example] - offset, right, 0.0).astype(jnp.bfloat16)
+        out_ref[example] = lax.dot_general(
+            right, left, (((0,), (0,)), ((), ())), preferred_element_type=jnp.float32
+        )
 
 
 def layer_gradients(activations, cotangents, lengths, project_in, project_out):
     layers, examples, tokens, width = activations.shape
     factor = project_in.shape[1]
-    data = pl.BlockSpec((None, None, tokens, width), lambda l, e, lim: (l, e, 0, 0))
-    weights = pl.BlockSpec((None, factor, width), lambda l, e, lim: (l, 0, 0))
+    data = pl.BlockSpec((None, examples, tokens, width), lambda l, lens: (l, 0, 0, 0))
+    weights = pl.BlockSpec((None, factor, width), lambda l, lens: (l, 0, 0))
     flops = 4 * layers * examples * tokens * width * factor
     moved = 2 * (activations.size + cotangents.size + project_in.size + project_out.size)
     return pl.pallas_call(
@@ -72,11 +74,9 @@
         out_shape=jax.ShapeDtypeStruct((layers, examples, factor, factor), jnp.float32),
         grid_spec=pltpu.PrefetchScalarGridSpec(
             num_scalar_prefetch=1,
-            grid=(layers, examples),
+            grid=(layers,),
             in_specs=[data, data, weights, weights],
-            out_specs=pl.BlockSpec(
-                (None, None, factor, factor), lambda l, e, lim: (l, e, 0, 0)
-            ),
+            out_specs=pl.BlockSpec((None, examples, factor, factor), lambda l, lens: (l, 0, 0, 0)),
         ),
         cost_estimate=pl.CostEstimate(flops=flops, transcendentals=0, bytes_accessed=moved),
     )(lengths, activations, cotangents, project_in, project_out)

time: 68.1 us -> 66.7 us (0.979)
  Pallas kernels: 18.3 us -> 16.9 us
    pallas_call x1, Pallas kernels: 18.3 us -> 16.9 us  [layer_gradients(): pl.pallas_call(gradient_kernel, out_shape=jax.ShapeDtypeStruct((layers, e...]
where the time goes in v8:
time: 66.7 us; the launch traced here: 66.3 us
  Pallas kernels  16.9 us (25%)
  starting transfers between devices  14.5 us (22%)
  waiting for transfers between devices  13.5 us (20%)
  blocking collectives  9.01 us (14%)
  matrix products  8.81 us (13%)
  local copies, waits for them, and re-layouts  1.9 us (3%)
  other arithmetic  1.54 us (2%)
    pallas_call x1, Pallas kernels, layer_gradients(): pl.pallas_call(gradient_kernel, out_shape=jax.ShapeDtypeStruct((layers, e...  16.9 us
    ppermute x6, starting transfers between devices, shifted(): return lax.ppermute(x, axis, [(i, (i + shift) % n) for i in range(n)])  11.1 us
    all_to_all x1, blocking collectives, all_gather_a2a(): return lax.all_to_all(copies, axis, 0, 0, tiled=True)  9.01 us
    all_to_all x1, waiting for transfers between devices, all_gather_a2a(): return lax.all_to_all(copies, axis, 0, 0, tiled=True)  6.81 us
    ppermute x6, waiting for transfers between devices, shifted(): return lax.ppermute(x, axis, [(i, (i + shift) % n) for i in range(n)])  6.68 us
    dot_general x1, matrix products, body_direct(): lax.dot_general(both_all, query_blocks, (((0, 2), (1, 2)), ((), ())), pre...  5.98 us
    all_to_all x1, starting transfers between devices, all_gather_a2a(): return lax.all_to_all(copies, axis, 0, 0, tiled=True)  3.41 us
    dot_general x1, matrix products, body_direct(): jnp.dot(grad_all, preconditioner, preferred_element_type=jnp.float32)  2.83 us
  transfers between devices with their start and end apart: 7, of which 7 were waited for; matrix products, arithmetic and copies ran while one was open for 0% of the time, Pallas kernels for 0%

profile of v8, /device:TPU:0, one launch (start us, length us, event | category | flops | bytes accessed | tf_op | source)
XLA Modules:
  0.0 66.3 jit_solution(5761222658726616594)
XLA Ops:
  0.0 16.9 %shard_map.73 = f32[4,2,64,64]{3,2,1,0:T(8,128)} custom-call(s32[2]{0:T(128)} %lengths_ref.1, bf16[4,2,256,4096]{3,2,1,0:T(8,128)(2,1)} %act_ref.1, bf16[4,2,256,4096]{3,2,1,0:T(8,128)(2,1)} %cot_ref.1, bf16[4,64,4096]{2,1,0:T(8,128)(2,1)} %win_ref.1, bf16[4,64,4096]{2,1,0:T(8,128)(2,1)} %wout_ref.1), custom_call_target="tpu_custom_call" | custom-call | flops 2147483648 | bytes 37748736 | tf_op jit(solution)/shard_map/pallas_call | solution.py:72
  16.9 0.9 %constant_dynamic-slice_fusion.5 = (f32[1,2,64,64]{3,2,1,0:T(8,128)S(1)}, f32[1,2,64,64]{3,2,1,0:T(8,128)S(1)}, f32[1,2,64,64]{3,2,1,0:T(8,128)S(1)}) fusion(f32[4,2,64,64]{3,2,1,0:T(8,128)} %shard_map.73, s32[]{:T(128)S(6)} %select_n.47, s32[]{:T(128)S(6)} %select_n.51, s32[]{:T(128)S(6)} %select_n.49), kind=kLoop, calls=%fused_computation.16 | loop fusion | bytes 196620 | tf_op jit(solution)/shard_map/dynamic_slice | solution.py:27
  17.8 3.1 %collective-permute-start = (f32[1,2,64,64]{3,2,1,0:T(8,128)S(1)}, f32[1,2,64,64]{3,2,1,0:T(8,128)S(1)}, u32[]{:S(2)}, u32[]{:S(2)}) collective-permute-start(f32[1,2,64,64]{3,2,1,0:T(8,128)S(1)} %get-tuple-element.5), channel_id=1, source_target_pairs={{0,1},{1,2},{2,3},{3,0},{4,5},{5,6},{6,7},{7,4},{8,9},{9,10},{10,1... | collective-permute-start | bytes 98312 | tf_op jit(solution)/shard_map/ppermute | solution.py:18
  20.9 2.6 %collective-permute-start.1 = (f32[1,2,64,64]{3,2,1,0:T(8,128)S(1)}, f32[1,2,64,64]{3,2,1,0:T(8,128)S(1)}, u32[]{:S(2)}, u32[]{:S(2)}) collective-permute-start(f32[1,2,64,64]{3,2,1,0:T(8,128)S(1)} %get-tuple-element.7), channel_id=1, source_target_pairs={{0,2},{1,3},{2,0},{3,1},{4,6},{5,7},{6,4},{7,5},{8,10},{9,11},{10,... | collective-permute-start | bytes 98312 | tf_op jit(solution)/shard_map/ppermute | solution.py:18
  23.5 1.3 %collective-permute-start.2 = (f32[1,2,64,64]{3,2,1,0:T(8,128)S(1)}, f32[1,2,64,64]{3,2,1,0:T(8,128)S(1)}, u32[]{:S(2)}, u32[]{:S(2)}) collective-permute-start(f32[1,2,64,64]{3,2,1,0:T(8,128)S(1)} %get-tuple-element.6), channel_id=1, source_target_pairs={{0,3},{1,0},{2,1},{3,2},{4,7},{5,4},{6,5},{7,6},{8,11},{9,8},{10,9... | collective-permute-start | bytes 98312 | tf_op jit(solution)/shard_map/ppermute | solution.py:18
  24.9 0.5 collective-permute-done
  25.4 2.6 %collective-permute-done.1 = f32[1,2,64,64]{3,2,1,0:T(8,128)S(1)} collective-permute-done((f32[1,2,64,64]{3,2,1,0:T(8,128)S(1)}, f32[1,2,64,64]{3,2,1,0:T(8,128)S(1)}, u32[]{:S(2)}, u32[]{:S(2)}) %collective-permute-start.1) | collective-permute-done | bytes 32800 | tf_op jit(solution)/shard_map/ppermute | solution.py:18
  28.0 0.2 collective-permute-done.2
  28.2 0.9 %add_convert_fusion = bf16[1,2,64,64]{3,2,1,0:T(8,128)(2,1)S(1)} fusion(f32[1,2,64,64]{3,2,1,0:T(8,128)S(1)} %collective-permute-done.2, f32[1,2,64,64]{3,2,1,0:T(8,128)S(1)} %collective-permute-done.1, f32[1,2,64,64]{3,2,1,0:T(8,128)S(1)} %collective-permute-done, f32[4,2,64,64]{3,2,1,0:T(8,128)} %shard_map.73, s32[]{:T(128)S(6)} %select_n.45), kind=kLoop, calls=%fused_computation.9 | loop fusion | flops 32768 | bytes 147460 | tf_op jit(solution)/shard_map/convert_element_type | solution.py:137
  29.1 0.1 convert_element_type.20
  29.2 0.1 broadcast_in_dim.4
  29.3 9.0 %all_to_all.10 = bf16[8,2,4096]{2,1,0:T(2,128)(2,1)S(1)} all-to-all(bf16[8,2,4096]{2,1,0:T(2,128)(2,1)S(1)} %broadcast_in_dim.4), channel_id=1, replica_groups=mesh['dp'=8,'mp'=4] {'dp'}, dimensions={0} | all-to-all | bytes 262144 | tf_op jit(solution)/shard_map/all_to_all | solution.py:44
  38.3 0.1 reshape.13
  38.3 2.8 %fusion.10 = f32[16,512]{1,0:T(8,128)S(1)} fusion(bf16[16,4096]{1,0:T(8,128)(2,1)S(1)} %reshape.13, bf16[4096,512]{1,0:T(8,128)(2,1)} %param.12), kind=kOutput, calls=%fused_computation.18 | convolution fusion | flops 67108864 | bytes 4358144 | tf_op jit(solution)/shard_map/dot_general | solution.py:140
  41.2 0.7 %broadcast_in_dim.5 = f32[8,16,512]{2,1,0:T(8,128)} broadcast(f32[16,512]{1,0:T(8,128)S(1)} %fusion.10), dimensions={1,2} | broadcast | bytes 294912 | tf_op jit(solution)/shard_map/broadcast_in_dim | solution.py:43
  41.9 3.4 %all-to-all-start.1 = ((f32[8,16,512]{2,1,0:T(8,128)}), f32[8,16,512]{2,1,0:T(8,128)S(1)}, u32[]{:S(2)}, u32[]{:S(2)}) async-start(f32[8,16,512]{2,1,0:T(8,128)} %broadcast_in_dim.5), calls=%async_computation.1 | async-start | bytes 524288 | tf_op jit(solution)/shard_map/all_to_all | solution.py:44
  45.3 6.8 %all-to-all-done.1 = f32[8,16,512]{2,1,0:T(8,128)S(1)} async-done(((f32[8,16,512]{2,1,0:T(8,128)}), f32[8,16,512]{2,1,0:T(8,128)S(1)}, u32[]{:S(2)}, u32[]{:S(2)}) %all-to-all-start.1) | async-done | bytes 262176 | tf_op jit(solution)/shard_map/all_to_all | solution.py:44
  52.2 6.0 %fusion.3 = f32[32,1024]{1,0:T(8,128)S(1)} fusion(bf16[128,8,8,512]{3,2,1,0:T(8,128)(2,1)} %bitcast.12, bf16[8,16,512]{2,1,0:T(8,128)(2,1)S(1)} %subtract_convert_fusion, bf16[8,16,512]{2,1,0:T(8,128)(2,1)S(1)} %convert_element_type.21), kind=kOutput, calls=%fused_computation.3 | convolution fusion | flops 268959744 | bytes 8781824 | tf_op jit(solution)/shard_map/dot_general | solution.py:145
  58.3 1.6 %collective-permute-start.3 = (f32[16,256]{1,0:T(8,128)S(1)}, f32[16,256]{1,0:T(8,128)S(1)}, u32[]{:S(2)}, u32[]{:S(2)}) collective-permute-start(f32[16,256]{1,0:T(8,128)S(1)} %get-tuple-element.8), channel_id=1, source_target_pairs={{0,1},{1,2},{2,3},{3,0},{4,5},{5,6},{6,7},{7,4},{8,9},{9,10},{10,1... | collective-permute-start | bytes 49160 | tf_op jit(solution)/shard_map/ppermute | solution.py:18
  59.9 2.0 %collective-permute-start.4 = (f32[16,256]{1,0:T(8,128)S(1)}, f32[16,256]{1,0:T(8,128)S(1)}, u32[]{:S(2)}, u32[]{:S(2)}) collective-permute-start(f32[16,256]{1,0:T(8,128)S(1)} %get-tuple-element.10), channel_id=1, source_target_pairs={{0,2},{1,3},{2,0},{3,1},{4,6},{5,7},{6,4},{7,5},{8,10},{9,11},{10,... | collective-permute-start | bytes 49160 | tf_op jit(solution)/shard_map/ppermute | solution.py:18
  61.9 0.4 collective-permute-start.5
  62.3 1.6 %collective-permute-done.3 = f32[16,256]{1,0:T(8,128)S(1)} collective-permute-done((f32[16,256]{1,0:T(8,128)S(1)}, f32[16,256]{1,0:T(8,128)S(1)}, u32[]{:S(2)}, u32[]{:S(2)}) %collective-permute-start.3) | collective-permute-done | bytes 16416 | tf_op jit(solution)/shard_map/ppermute | solution.py:18
  63.9 0.6 collective-permute-done.4
  64.5 1.1 %collective-permute-done.5 = f32[16,256]{1,0:T(8,128)S(1)} collective-permute-done((f32[16,256]{1,0:T(8,128)S(1)}, f32[16,256]{1,0:T(8,128)S(1)}, u32[]{:S(2)}, u32[]{:S(2)}) %collective-permute-start.5) | collective-permute-done | bytes 16416 | tf_op jit(solution)/shard_map/ppermute | solution.py:18
  65.7 0.6 add_add_fusion
  (4 shorter events, 0.1 us)
Async XLA Ops:
  17.8 7.6 %collective-permute-start = (f32[1,2,64,64]{3,2,1,0:T(8,128)S(1)}, f32[1,2,64,64]{3,2,1,0:T(8,128)S(1)}, u32[]{:S(2)}, u32[]{:S(2)}) collective-permute-start(f32[1,2,64,64]{3,2,1,0:T(8,128)S(1)} %get-tuple-element.5), channel_id=1, source_target_pairs={{0,1},{1,2},{2,3},{3,0},{4,5},{5,6},{6,7},{7,4},{8,9},{9,10},{10,1... | collective-permute-start | bytes 98312 | tf_op jit(solution)/shard_map/ppermute | solution.py:18
  20.9 7.1 %collective-permute-start.1 = (f32[1,2,64,64]{3,2,1,0:T(8,128)S(1)}, f32[1,2,64,64]{3,2,1,0:T(8,128)S(1)}, u32[]{:S(2)}, u32[]{:S(2)}) collective-permute-start(f32[1,2,64,64]{3,2,1,0:T(8,128)S(1)} %get-tuple-element.7), channel_id=1, source_target_pairs={{0,2},{1,3},{2,0},{3,1},{4,6},{5,7},{6,4},{7,5},{8,10},{9,11},{10,... | collective-permute-start | bytes 98312 | tf_op jit(solution)/shard_map/ppermute | solution.py:18
  23.5 4.7 %collective-permute-start.2 = (f32[1,2,64,64]{3,2,1,0:T(8,128)S(1)}, f32[1,2,64,64]{3,2,1,0:T(8,128)S(1)}, u32[]{:S(2)}, u32[]{:S(2)}) collective-permute-start(f32[1,2,64,64]{3,2,1,0:T(8,128)S(1)} %get-tuple-element.6), channel_id=1, source_target_pairs={{0,3},{1,0},{2,1},{3,2},{4,7},{5,4},{6,5},{7,6},{8,11},{9,8},{10,9... | collective-permute-start | bytes 98312 | tf_op jit(solution)/shard_map/ppermute | solution.py:18
  41.9 10.3 %all-to-all-start.1 = ((f32[8,16,512]{2,1,0:T(8,128)}), f32[8,16,512]{2,1,0:T(8,128)S(1)}, u32[]{:S(2)}, u32[]{:S(2)}) async-start(f32[8,16,512]{2,1,0:T(8,128)} %broadcast_in_dim.5), calls=%async_computation.1 | async-start | bytes 524288 | tf_op jit(solution)/shard_map/all_to_all | solution.py:44
  58.3 5.7 %collective-permute-start.3 = (f32[16,256]{1,0:T(8,128)S(1)}, f32[16,256]{1,0:T(8,128)S(1)}, u32[]{:S(2)}, u32[]{:S(2)}) collective-permute-start(f32[16,256]{1,0:T(8,128)S(1)} %get-tuple-element.8), channel_id=1, source_target_pairs={{0,1},{1,2},{2,3},{3,0},{4,5},{5,6},{6,7},{7,4},{8,9},{9,10},{10,1... | collective-permute-start | bytes 49160 | tf_op jit(solution)/shard_map/ppermute | solution.py:18
  59.9 4.6 %collective-permute-start.4 = (f32[16,256]{1,0:T(8,128)S(1)}, f32[16,256]{1,0:T(8,128)S(1)}, u32[]{:S(2)}, u32[]{:S(2)}) collective-permute-start(f32[16,256]{1,0:T(8,128)S(1)} %get-tuple-element.10), channel_id=1, source_target_pairs={{0,2},{1,3},{2,0},{3,1},{4,6},{5,7},{6,4},{7,5},{8,10},{9,11},{10,... | collective-permute-start | bytes 49160 | tf_op jit(solution)/shard_map/ppermute | solution.py:18
  61.9 3.7 %collective-permute-start.5 = (f32[16,256]{1,0:T(8,128)S(1)}, f32[16,256]{1,0:T(8,128)S(1)}, u32[]{:S(2)}, u32[]{:S(2)}) collective-permute-start(f32[16,256]{1,0:T(8,128)S(1)} %get-tuple-element.9), channel_id=1, source_target_pairs={{0,3},{1,0},{2,1},{3,2},{4,7},{5,4},{6,5},{7,6},{8,11},{9,8},{10,9... | collective-permute-start | bytes 49160 | tf_op jit(solution)/shard_map/ppermute | solution.py:18

commit v9 on v8

--- a/solution.py
+++ b/solution.py
@@ -82,6 +82,40 @@
     )(lengths, activations, cotangents, project_in, project_out)
 
 
+def scores_kernel(parts_ref, query_ref, out_ref):
+    blocks, rows, block = parts_ref.shape
+    total = None
+    for index in range(blocks):
+        term = lax.dot_general(
+            parts_ref[index],
+            query_ref[:, index * block:(index + 1) * block],
+            (((1,), (1,)), ((), ())),
+            preferred_element_type=jnp.float32,
+        )
+        total = term if total is None else total + term
+    half = rows // 2
+    out_ref[...] = total[:half] + total[half:]
+
+
+def query_scores(parts, queries):
+    blocks, rows, block = parts.shape
+    count = queries.shape[0]
+    tile = 256 if count % 256 == 0 else count
+    flops = 2 * rows * count * blocks * block
+    moved = 2 * (parts.size + queries.size) + 4 * (rows // 2) * count
+    return pl.pallas_call(
+        scores_kernel,
+        out_shape=jax.ShapeDtypeStruct((rows // 2, count), jnp.float32),
+        grid=(count // tile,),
+        in_specs=[
+            pl.BlockSpec((blocks, rows, block), lambda i: (0, 0, 0)),
+            pl.BlockSpec((tile, queries.shape[1]), lambda i: (i, 0)),
+        ],
+        out_specs=pl.BlockSpec((rows // 2, tile), lambda i: (0, i)),
+        cost_estimate=pl.CostEstimate(flops=flops, transcendentals=0, bytes_accessed=moved),
+    )(parts, queries)
+
+
 def body_start(activations, cotangents, lengths, project_in, project_out, preconditioner, queries):
     width_mp = lax.axis_size("mp")
     layer_count = activations.shape[0]
@@ -140,13 +174,7 @@
     pre_part = jnp.dot(grad_all, preconditioner, preferred_element_type=jnp.float32)
     upper_grad, lower_grad = split_parts(all_gather_a2a(pre_part, "dp"))
     both_all = jnp.concatenate([upper_grad, lower_grad], axis=1)
-    blocks, block = both_all.shape[0], both_all.shape[2]
-    query_blocks = queries.reshape(queries.shape[0], blocks, block)
-    products = lax.dot_general(
-        both_all, query_blocks, (((0, 2), (1, 2)), ((), ())), preferred_element_type=jnp.float32
-    )
-    examples = upper_grad.shape[1]
-    partial_scores = products[:examples] + products[examples:]
+    partial_scores = query_scores(both_all, queries)
     return reduce_scatter_direct(partial_scores, "mp", 1)
 
 

time: 66.7 us -> 69 us (1.034)
  Pallas kernels: 16.9 us -> 23 us
  matrix products: 8.81 us -> 2.83 us
  other arithmetic: 1.54 us -> 2.96 us
  local copies, waits for them, and re-layouts: 1.9 us -> 2.64 us
    pallas_call x0 -> x1, Pallas kernels: none -> 6.09 us  [query_scores(): pl.pallas_call(scores_kernel, out_shape=jax.ShapeDtypeStruct((rows // 2,...]
    dot_general x1 -> x0, matrix products: 5.98 us -> none  [body_direct(): lax.dot_general(both_all, query_blocks, (((0, 2), (1, 2)), ((), ())), pre...]
    dynamic_slice x2, local copies, waits for them, and re-layouts: 0.93 us -> 1.67 us  [reduce_scatter_direct(): piece = lax.dynamic_slice_in_dim(x, (me + shift) % n * width, width, dim)]
    concatenate x0 -> x1, other arithmetic: none -> 0.72 us  [body_direct(): both_all = jnp.concatenate([upper_grad, lower_grad], axis=1)]
    add x1, other arithmetic: 0.61 us -> 1.33 us  [reduce_scatter_direct(): total = total + shifted(piece, axis, shift)]
where the time goes in v9:
time: 69 us; the launch traced here: 68.5 us
  Pallas kernels  23 us (33%)
  starting transfers between devices  14.5 us (21%)
  waiting for transfers between devices  13.5 us (20%)
  blocking collectives  9.01 us (13%)
  other arithmetic  2.96 us (4%)
  matrix products  2.83 us (4%)
  local copies, waits for them, and re-layouts  2.64 us (4%)
    pallas_call x1, Pallas kernels, layer_gradients(): pl.pallas_call(gradient_kernel, out_shape=jax.ShapeDtypeStruct((layers, e...  16.9 us
    ppermute x6, starting transfers between devices, shifted(): return lax.ppermute(x, axis, [(i, (i + shift) % n) for i in range(n)])  11.1 us
    all_to_all x1, blocking collectives, all_gather_a2a(): return lax.all_to_all(copies, axis, 0, 0, tiled=True)  9.01 us
    all_to_all x1, waiting for transfers between devices, all_gather_a2a(): return lax.all_to_all(copies, axis, 0, 0, tiled=True)  6.81 us
    ppermute x6, waiting for transfers between devices, shifted(): return lax.ppermute(x, axis, [(i, (i + shift) % n) for i in range(n)])  6.71 us
    pallas_call x1, Pallas kernels, query_scores(): pl.pallas_call(scores_kernel, out_shape=jax.ShapeDtypeStruct((rows // 2,...  6.09 us
    all_to_all x1, starting transfers between devices, all_gather_a2a(): return lax.all_to_all(copies, axis, 0, 0, tiled=True)  3.41 us
    dot_general x1, matrix products, body_direct(): jnp.dot(grad_all, preconditioner, preferred_element_type=jnp.float32)  2.83 us
  transfers between devices with their start and end apart: 7, of which 7 were waited for; matrix products, arithmetic and copies ran while one was open for 0% of the time, Pallas kernels for 0%

profile of v9, /device:TPU:0, one launch (start us, length us, event | category | flops | bytes accessed | tf_op | source)
XLA Modules:
  0.0 68.5 jit_solution(8140880035933709204)
XLA Ops:
  0.0 16.9 %shard_map.73 = f32[4,2,64,64]{3,2,1,0:T(8,128)} custom-call(s32[2]{0:T(128)} %lengths_ref.1, bf16[4,2,256,4096]{3,2,1,0:T(8,128)(2,1)} %act_ref.1, bf16[4,2,256,4096]{3,2,1,0:T(8,128)(2,1)} %cot_ref.1, bf16[4,64,4096]{2,1,0:T(8,128)(2,1)} %win_ref.1, bf16[4,64,4096]{2,1,0:T(8,128)(2,1)} %wout_ref.1), custom_call_target="tpu_custom_call" | custom-call | flops 2147483648 | bytes 37748736 | tf_op jit(solution)/shard_map/pallas_call | solution.py:72
  16.9 0.9 %constant_dynamic-slice_fusion.5 = (f32[1,2,64,64]{3,2,1,0:T(8,128)S(1)}, f32[1,2,64,64]{3,2,1,0:T(8,128)S(1)}, f32[1,2,64,64]{3,2,1,0:T(8,128)S(1)}) fusion(f32[4,2,64,64]{3,2,1,0:T(8,128)} %shard_map.73, s32[]{:T(128)S(6)} %select_n.47, s32[]{:T(128)S(6)} %select_n.51, s32[]{:T(128)S(6)} %select_n.49), kind=kLoop, calls=%fused_computation.9 | loop fusion | bytes 196620 | tf_op jit(solution)/shard_map/dynamic_slice | solution.py:27
  17.8 3.1 %collective-permute-start = (f32[1,2,64,64]{3,2,1,0:T(8,128)S(1)}, f32[1,2,64,64]{3,2,1,0:T(8,128)S(1)}, u32[]{:S(2)}, u32[]{:S(2)}) collective-permute-start(f32[1,2,64,64]{3,2,1,0:T(8,128)S(1)} %get-tuple-element.5), channel_id=1, source_target_pairs={{0,1},{1,2},{2,3},{3,0},{4,5},{5,6},{6,7},{7,4},{8,9},{9,10},{10,1... | collective-permute-start | bytes 98312 | tf_op jit(solution)/shard_map/ppermute | solution.py:18
  20.9 2.6 %collective-permute-start.1 = (f32[1,2,64,64]{3,2,1,0:T(8,128)S(1)}, f32[1,2,64,64]{3,2,1,0:T(8,128)S(1)}, u32[]{:S(2)}, u32[]{:S(2)}) collective-permute-start(f32[1,2,64,64]{3,2,1,0:T(8,128)S(1)} %get-tuple-element.7), channel_id=1, source_target_pairs={{0,2},{1,3},{2,0},{3,1},{4,6},{5,7},{6,4},{7,5},{8,10},{9,11},{10,... | collective-permute-start | bytes 98312 | tf_op jit(solution)/shard_map/ppermute | solution.py:18
  23.5 1.3 %collective-permute-start.2 = (f32[1,2,64,64]{3,2,1,0:T(8,128)S(1)}, f32[1,2,64,64]{3,2,1,0:T(8,128)S(1)}, u32[]{:S(2)}, u32[]{:S(2)}) collective-permute-start(f32[1,2,64,64]{3,2,1,0:T(8,128)S(1)} %get-tuple-element.6), channel_id=1, source_target_pairs={{0,3},{1,0},{2,1},{3,2},{4,7},{5,4},{6,5},{7,6},{8,11},{9,8},{10,9... | collective-permute-start | bytes 98312 | tf_op jit(solution)/shard_map/ppermute | solution.py:18
  24.9 0.5 collective-permute-done
  25.4 2.6 %collective-permute-done.1 = f32[1,2,64,64]{3,2,1,0:T(8,128)S(1)} collective-permute-done((f32[1,2,64,64]{3,2,1,0:T(8,128)S(1)}, f32[1,2,64,64]{3,2,1,0:T(8,128)S(1)}, u32[]{:S(2)}, u32[]{:S(2)}) %collective-permute-start.1) | collective-permute-done | bytes 32800 | tf_op jit(solution)/shard_map/ppermute | solution.py:18
  28.0 0.2 collective-permute-done.2
  28.2 0.9 %add_convert_fusion = bf16[1,2,64,64]{3,2,1,0:T(8,128)(2,1)S(1)} fusion(f32[1,2,64,64]{3,2,1,0:T(8,128)S(1)} %collective-permute-done.2, f32[1,2,64,64]{3,2,1,0:T(8,128)S(1)} %collective-permute-done.1, f32[1,2,64,64]{3,2,1,0:T(8,128)S(1)} %collective-permute-done, f32[4,2,64,64]{3,2,1,0:T(8,128)} %shard_map.73, s32[]{:T(128)S(6)} %select_n.45), kind=kLoop, calls=%fused_computation.2 | loop fusion | flops 32768 | bytes 147460 | tf_op jit(solution)/shard_map/convert_element_type | solution.py:171
  29.1 0.1 convert_element_type.20
  29.2 0.1 broadcast_in_dim.4
  29.3 9.0 %all_to_all.10 = bf16[8,2,4096]{2,1,0:T(2,128)(2,1)S(1)} all-to-all(bf16[8,2,4096]{2,1,0:T(2,128)(2,1)S(1)} %broadcast_in_dim.4), channel_id=1, replica_groups=mesh['dp'=8,'mp'=4] {'dp'}, dimensions={0} | all-to-all | bytes 262144 | tf_op jit(solution)/shard_map/all_to_all | solution.py:44
  38.3 0.1 reshape.10
  38.3 2.8 %fusion = f32[16,512]{1,0:T(8,128)S(1)} fusion(bf16[16,4096]{1,0:T(8,128)(2,1)S(1)} %reshape.10, bf16[4096,512]{1,0:T(8,128)(2,1)} %param.12), kind=kOutput, calls=%fused_computation.10 | convolution fusion | flops 67108864 | bytes 4358144 | tf_op jit(solution)/shard_map/dot_general | solution.py:174
  41.2 0.7 %broadcast_in_dim.5 = f32[8,16,512]{2,1,0:T(8,128)} broadcast(f32[16,512]{1,0:T(8,128)S(1)} %fusion), dimensions={1,2} | broadcast | bytes 294912 | tf_op jit(solution)/shard_map/broadcast_in_dim | solution.py:43
  41.9 3.4 %all-to-all-start.1 = ((f32[8,16,512]{2,1,0:T(8,128)}), f32[8,16,512]{2,1,0:T(8,128)S(1)}, u32[]{:S(2)}, u32[]{:S(2)}) async-start(f32[8,16,512]{2,1,0:T(8,128)} %broadcast_in_dim.5), calls=%async_computation.1 | async-start | bytes 524288 | tf_op jit(solution)/shard_map/all_to_all | solution.py:44
  45.3 6.8 %all-to-all-done.1 = f32[8,16,512]{2,1,0:T(8,128)S(1)} async-done(((f32[8,16,512]{2,1,0:T(8,128)}), f32[8,16,512]{2,1,0:T(8,128)S(1)}, u32[]{:S(2)}, u32[]{:S(2)}) %all-to-all-start.1) | async-done | bytes 262176 | tf_op jit(solution)/shard_map/all_to_all | solution.py:44
  52.2 0.7 %pad_maximum_fusion.parts_ref = bf16[8,32,512]{2,1,0:T(8,128)(2,1)} fusion(bf16[8,16,512]{2,1,0:T(8,128)(2,1)S(1)} %subtract_convert_fusion, bf16[8,16,512]{2,1,0:T(8,128)(2,1)S(1)} %convert_element_type.21), kind=kLoop, calls=%fused_computation | loop fusion | flops 524288 | bytes 524288 | tf_op jit(solution)/shard_map/concatenate | solution.py:176
  52.9 6.1 %shard_map.74 = f32[16,1024]{1,0:T(8,128)} custom-call(bf16[8,32,512]{2,1,0:T(8,128)(2,1)} %pad_maximum_fusion.parts_ref, bf16[1024,4096]{1,0:T(8,128)(2,1)} %query_ref.1), custom_call_target="tpu_custom_call" | custom-call | flops 268435456 | bytes 8716288 | tf_op jit(solution)/shard_map/pallas_call | solution.py:106
  59.0 0.8 %constant_dynamic-slice_fusion.2 = (f32[16,256]{1,0:T(8,128)S(1)}, f32[16,256]{1,0:T(8,128)S(1)}, f32[16,256]{1,0:T(8,128)S(1)}) fusion(f32[16,1024]{1,0:T(8,128)} %shard_map.74, s32[]{:T(128)S(6)} %select_n.53, s32[]{:T(128)S(6)} %select_n.55, s32[]{:T(128)S(6)} %select_n.54), kind=kLoop, calls=%fused_computation.6 | loop fusion | bytes 98316 | tf_op jit(solution)/shard_map/dynamic_slice | solution.py:27
  59.8 1.6 %collective-permute-start.3 = (f32[16,256]{1,0:T(8,128)S(1)}, f32[16,256]{1,0:T(8,128)S(1)}, u32[]{:S(2)}, u32[]{:S(2)}) collective-permute-start(f32[16,256]{1,0:T(8,128)S(1)} %get-tuple-element.8), channel_id=1, source_target_pairs={{0,1},{1,2},{2,3},{3,0},{4,5},{5,6},{6,7},{7,4},{8,9},{9,10},{10,1... | collective-permute-start | bytes 49160 | tf_op jit(solution)/shard_map/ppermute | solution.py:18
  61.4 2.0 %collective-permute-start.4 = (f32[16,256]{1,0:T(8,128)S(1)}, f32[16,256]{1,0:T(8,128)S(1)}, u32[]{:S(2)}, u32[]{:S(2)}) collective-permute-start(f32[16,256]{1,0:T(8,128)S(1)} %get-tuple-element.10), channel_id=1, source_target_pairs={{0,2},{1,3},{2,0},{3,1},{4,6},{5,7},{6,4},{7,5},{8,10},{9,11},{10,... | collective-permute-start | bytes 49160 | tf_op jit(solution)/shard_map/ppermute | solution.py:18
  63.4 0.4 collective-permute-start.5
  63.8 1.6 %collective-permute-done.3 = f32[16,256]{1,0:T(8,128)S(1)} collective-permute-done((f32[16,256]{1,0:T(8,128)S(1)}, f32[16,256]{1,0:T(8,128)S(1)}, u32[]{:S(2)}, u32[]{:S(2)}) %collective-permute-start.3) | collective-permute-done | bytes 16416 | tf_op jit(solution)/shard_map/ppermute | solution.py:18
  65.4 0.6 collective-permute-done.4
  66.0 1.1 %collective-permute-done.5 = f32[16,256]{1,0:T(8,128)S(1)} collective-permute-done((f32[16,256]{1,0:T(8,128)S(1)}, f32[16,256]{1,0:T(8,128)S(1)}, u32[]{:S(2)}, u32[]{:S(2)}) %collective-permute-start.5) | collective-permute-done | bytes 16416 | tf_op jit(solution)/shard_map/ppermute | solution.py:18
  67.1 1.3 %add_add_fusion = f32[16,256]{1,0:T(8,128)} fusion(f32[16,256]{1,0:T(8,128)S(1)} %collective-permute-done.5, f32[16,256]{1,0:T(8,128)S(1)} %collective-permute-done.4, f32[16,256]{1,0:T(8,128)S(1)} %collective-permute-done.3, f32[16,1024]{1,0:T(8,128)} %shard_map.74, s32[]{:T(128)S(6)} %select_n.52), kind=kLoop, calls=%fused_computation.3 | loop fusion | flops 12288 | bytes 81924 | tf_op jit(solution)/shard_map/add | solution.py:28
  (2 shorter events, 0.1 us)
Async XLA Ops:
  17.8 7.6 %collective-permute-start = (f32[1,2,64,64]{3,2,1,0:T(8,128)S(1)}, f32[1,2,64,64]{3,2,1,0:T(8,128)S(1)}, u32[]{:S(2)}, u32[]{:S(2)}) collective-permute-start(f32[1,2,64,64]{3,2,1,0:T(8,128)S(1)} %get-tuple-element.5), channel_id=1, source_target_pairs={{0,1},{1,2},{2,3},{3,0},{4,5},{5,6},{6,7},{7,4},{8,9},{9,10},{10,1... | collective-permute-start | bytes 98312 | tf_op jit(solution)/shard_map/ppermute | solution.py:18
  20.9 7.1 %collective-permute-start.1 = (f32[1,2,64,64]{3,2,1,0:T(8,128)S(1)}, f32[1,2,64,64]{3,2,1,0:T(8,128)S(1)}, u32[]{:S(2)}, u32[]{:S(2)}) collective-permute-start(f32[1,2,64,64]{3,2,1,0:T(8,128)S(1)} %get-tuple-element.7), channel_id=1, source_target_pairs={{0,2},{1,3},{2,0},{3,1},{4,6},{5,7},{6,4},{7,5},{8,10},{9,11},{10,... | collective-permute-start | bytes 98312 | tf_op jit(solution)/shard_map/ppermute | solution.py:18
  23.5 4.7 %collective-permute-start.2 = (f32[1,2,64,64]{3,2,1,0:T(8,128)S(1)}, f32[1,2,64,64]{3,2,1,0:T(8,128)S(1)}, u32[]{:S(2)}, u32[]{:S(2)}) collective-permute-start(f32[1,2,64,64]{3,2,1,0:T(8,128)S(1)} %get-tuple-element.6), channel_id=1, source_target_pairs={{0,3},{1,0},{2,1},{3,2},{4,7},{5,4},{6,5},{7,6},{8,11},{9,8},{10,9... | collective-permute-start | bytes 98312 | tf_op jit(solution)/shard_map/ppermute | solution.py:18
  41.9 10.3 %all-to-all-start.1 = ((f32[8,16,512]{2,1,0:T(8,128)}), f32[8,16,512]{2,1,0:T(8,128)S(1)}, u32[]{:S(2)}, u32[]{:S(2)}) async-start(f32[8,16,512]{2,1,0:T(8,128)} %broadcast_in_dim.5), calls=%async_computation.1 | async-start | bytes 524288 | tf_op jit(solution)/shard_map/all_to_all | solution.py:44
  59.8 5.6 %collective-permute-start.3 = (f32[16,256]{1,0:T(8,128)S(1)}, f32[16,256]{1,0:T(8,128)S(1)}, u32[]{:S(2)}, u32[]{:S(2)}) collective-permute-start(f32[16,256]{1,0:T(8,128)S(1)} %get-tuple-element.8), channel_id=1, source_target_pairs={{0,1},{1,2},{2,3},{3,0},{4,5},{5,6},{6,7},{7,4},{8,9},{9,10},{10,1... | collective-permute-start | bytes 49160 | tf_op jit(solution)/shard_map/ppermute | solution.py:18
  61.4 4.6 %collective-permute-start.4 = (f32[16,256]{1,0:T(8,128)S(1)}, f32[16,256]{1,0:T(8,128)S(1)}, u32[]{:S(2)}, u32[]{:S(2)}) collective-permute-start(f32[16,256]{1,0:T(8,128)S(1)} %get-tuple-element.10), channel_id=1, source_target_pairs={{0,2},{1,3},{2,0},{3,1},{4,6},{5,7},{6,4},{7,5},{8,10},{9,11},{10,... | collective-permute-start | bytes 49160 | tf_op jit(solution)/shard_map/ppermute | solution.py:18
  63.4 3.7 %collective-permute-start.5 = (f32[16,256]{1,0:T(8,128)S(1)}, f32[16,256]{1,0:T(8,128)S(1)}, u32[]{:S(2)}, u32[]{:S(2)}) collective-permute-start(f32[16,256]{1,0:T(8,128)S(1)} %get-tuple-element.9), channel_id=1, source_target_pairs={{0,3},{1,0},{2,1},{3,2},{4,7},{5,4},{6,5},{7,6},{8,11},{9,8},{10,9... | collective-permute-start | bytes 49160 | tf_op jit(solution)/shard_map/ppermute | solution.py:18

commit v10 on v9

--- a/solution.py
+++ b/solution.py
@@ -82,38 +82,42 @@
     )(lengths, activations, cotangents, project_in, project_out)
 
 
-def scores_kernel(parts_ref, query_ref, out_ref):
-    blocks, rows, block = parts_ref.shape
+def scores_kernel(pre_ref, query_ref, out_ref):
+    blocks, examples, block = pre_ref.shape
     total = None
     for index in range(blocks):
+        dense = pre_ref[index]
+        upper = dense.astype(jnp.bfloat16)
+        lower = (dense - upper.astype(jnp.float32)).astype(jnp.bfloat16)
+        parts = jnp.concatenate([upper, lower], axis=0)
         term = lax.dot_general(
-            parts_ref[index],
             query_ref[:, index * block:(index + 1) * block],
+            parts,
             (((1,), (1,)), ((), ())),
             preferred_element_type=jnp.float32,
         )
         total = term if total is None else total + term
-    half = rows // 2
-    out_ref[...] = total[:half] + total[half:]
-
-
-def query_scores(parts, queries):
-    blocks, rows, block = parts.shape
+    flipped = total.T
+    out_ref[...] = flipped[:examples] + flipped[examples:]
+
+
+def query_scores(pre_all, queries):
+    blocks, examples, block = pre_all.shape
     count = queries.shape[0]
     tile = 256 if count % 256 == 0 else count
-    flops = 2 * rows * count * blocks * block
-    moved = 2 * (parts.size + queries.size) + 4 * (rows // 2) * count
+    flops = 4 * examples * count * blocks * block
+    moved = 4 * pre_all.size + 2 * queries.size + 4 * examples * count
     return pl.pallas_call(
         scores_kernel,
-        out_shape=jax.ShapeDtypeStruct((rows // 2, count), jnp.float32),
+        out_shape=jax.ShapeDtypeStruct((examples, count), jnp.float32),
         grid=(count // tile,),
         in_specs=[
-            pl.BlockSpec((blocks, rows, block), lambda i: (0, 0, 0)),
+            pl.BlockSpec((blocks, examples, block), lambda i: (0, 0, 0)),
             pl.BlockSpec((tile, queries.shape[1]), lambda i: (i, 0)),
         ],
-        out_specs=pl.BlockSpec((rows // 2, tile), lambda i: (0, i)),
+        out_specs=pl.BlockSpec((examples, tile), lambda i: (0, i)),
         cost_estimate=pl.CostEstimate(flops=flops, transcendentals=0, bytes_accessed=moved),
-    )(parts, queries)
+    )(pre_all, queries)
 
 
 def body_start(activations, cotangents, lengths, project_in, project_out, preconditioner, queries):
@@ -172,9 +176,7 @@
     grad_all = all_gather_a2a(grad_mine, "dp")
     grad_all = grad_all.reshape(-1, grad_all.shape[-1])
     pre_part = jnp.dot(grad_all, preconditioner, preferred_element_type=jnp.float32)
-    upper_grad, lower_grad = split_parts(all_gather_a2a(pre_part, "dp"))
-    both_all = jnp.concatenate([upper_grad, lower_grad], axis=1)
-    partial_scores = query_scores(both_all, queries)
+    partial_scores = query_scores(all_gather_a2a(pre_part, "dp"), queries)
     return reduce_scatter_direct(partial_scores, "mp", 1)
 
 

time: 69 us -> 69 us (level)
  other arithmetic: 2.96 us -> 2.18 us
  local copies, waits for them, and re-layouts: 2.64 us -> 3.36 us
    concatenate x1 -> x0, other arithmetic: 0.72 us -> none  [body_direct(): both_all = jnp.concatenate([upper_grad, lower_grad], axis=1)]
    unnamed x0 -> x2, local copies, waits for them, and re-layouts: none -> 0.71 us
where the time goes in v10:
time: 69 us; the launch traced here: 68.4 us
  Pallas kernels  23 us (33%)
  starting transfers between devices  14.5 us (21%)
  waiting for transfers between devices  13.5 us (20%)
  blocking collectives  9.01 us (13%)
  local copies, waits for them, and re-layouts  3.36 us (5%)
  matrix products  2.83 us (4%)
  other arithmetic  2.18 us (3%)
    pallas_call x1, Pallas kernels, layer_gradients(): pl.pallas_call(gradient_kernel, out_shape=jax.ShapeDtypeStruct((layers, e...  16.9 us
    ppermute x6, starting transfers between devices, shifted(): return lax.ppermute(x, axis, [(i, (i + shift) % n) for i in range(n)])  11.1 us
    all_to_all x1, blocking collectives, all_gather_a2a(): return lax.all_to_all(copies, axis, 0, 0, tiled=True)  9.01 us
    all_to_all x1, waiting for transfers between devices, all_gather_a2a(): return lax.all_to_all(copies, axis, 0, 0, tiled=True)  6.81 us
    ppermute x6, waiting for transfers between devices, shifted(): return lax.ppermute(x, axis, [(i, (i + shift) % n) for i in range(n)])  6.71 us
    pallas_call x1, Pallas kernels, query_scores(): pl.pallas_call(scores_kernel, out_shape=jax.ShapeDtypeStruct((examples, c...  6.12 us
    all_to_all x1, starting transfers between devices, all_gather_a2a(): return lax.all_to_all(copies, axis, 0, 0, tiled=True)  3.41 us
    dot_general x1, matrix products, body_direct(): jnp.dot(grad_all, preconditioner, preferred_element_type=jnp.float32)  2.83 us
  transfers between devices with their start and end apart: 7, of which 7 were waited for; matrix products, arithmetic and copies ran while one was open for 0% of the time, Pallas kernels for 0%

profile of v10, /device:TPU:0, one launch (start us, length us, event | category | flops | bytes accessed | tf_op | source)
XLA Modules:
  0.0 68.4 jit_solution(438012056050391366)
XLA Ops:
  0.0 16.9 %shard_map.73 = f32[4,2,64,64]{3,2,1,0:T(8,128)} custom-call(s32[2]{0:T(128)} %lengths_ref.1, bf16[4,2,256,4096]{3,2,1,0:T(8,128)(2,1)} %act_ref.1, bf16[4,2,256,4096]{3,2,1,0:T(8,128)(2,1)} %cot_ref.1, bf16[4,64,4096]{2,1,0:T(8,128)(2,1)} %win_ref.1, bf16[4,64,4096]{2,1,0:T(8,128)(2,1)} %wout_ref.1), custom_call_target="tpu_custom_call" | custom-call | flops 2147483648 | bytes 37748736 | tf_op jit(solution)/shard_map/pallas_call | solution.py:72
  16.9 0.9 %constant_dynamic-slice_fusion.5 = (f32[1,2,64,64]{3,2,1,0:T(8,128)S(1)}, f32[1,2,64,64]{3,2,1,0:T(8,128)S(1)}, f32[1,2,64,64]{3,2,1,0:T(8,128)S(1)}) fusion(f32[4,2,64,64]{3,2,1,0:T(8,128)} %shard_map.73, s32[]{:T(128)S(6)} %select_n.47, s32[]{:T(128)S(6)} %select_n.51, s32[]{:T(128)S(6)} %select_n.49), kind=kLoop, calls=%fused_computation.7 | loop fusion | bytes 196620 | tf_op jit(solution)/shard_map/dynamic_slice | solution.py:27
  17.8 3.1 %collective-permute-start = (f32[1,2,64,64]{3,2,1,0:T(8,128)S(1)}, f32[1,2,64,64]{3,2,1,0:T(8,128)S(1)}, u32[]{:S(2)}, u32[]{:S(2)}) collective-permute-start(f32[1,2,64,64]{3,2,1,0:T(8,128)S(1)} %get-tuple-element.5), channel_id=1, source_target_pairs={{0,1},{1,2},{2,3},{3,0},{4,5},{5,6},{6,7},{7,4},{8,9},{9,10},{10,1... | collective-permute-start | bytes 98312 | tf_op jit(solution)/shard_map/ppermute | solution.py:18
  20.9 2.6 %collective-permute-start.1 = (f32[1,2,64,64]{3,2,1,0:T(8,128)S(1)}, f32[1,2,64,64]{3,2,1,0:T(8,128)S(1)}, u32[]{:S(2)}, u32[]{:S(2)}) collective-permute-start(f32[1,2,64,64]{3,2,1,0:T(8,128)S(1)} %get-tuple-element.7), channel_id=1, source_target_pairs={{0,2},{1,3},{2,0},{3,1},{4,6},{5,7},{6,4},{7,5},{8,10},{9,11},{10,... | collective-permute-start | bytes 98312 | tf_op jit(solution)/shard_map/ppermute | solution.py:18
  23.5 1.3 %collective-permute-start.2 = (f32[1,2,64,64]{3,2,1,0:T(8,128)S(1)}, f32[1,2,64,64]{3,2,1,0:T(8,128)S(1)}, u32[]{:S(2)}, u32[]{:S(2)}) collective-permute-start(f32[1,2,64,64]{3,2,1,0:T(8,128)S(1)} %get-tuple-element.6), channel_id=1, source_target_pairs={{0,3},{1,0},{2,1},{3,2},{4,7},{5,4},{6,5},{7,6},{8,11},{9,8},{10,9... | collective-permute-start | bytes 98312 | tf_op jit(solution)/shard_map/ppermute | solution.py:18
  24.9 0.5 collective-permute-done
  25.4 2.6 %collective-permute-done.1 = f32[1,2,64,64]{3,2,1,0:T(8,128)S(1)} collective-permute-done((f32[1,2,64,64]{3,2,1,0:T(8,128)S(1)}, f32[1,2,64,64]{3,2,1,0:T(8,128)S(1)}, u32[]{:S(2)}, u32[]{:S(2)}) %collective-permute-start.1) | collective-permute-done | bytes 32800 | tf_op jit(solution)/shard_map/ppermute | solution.py:18
  28.0 0.2 collective-permute-done.2
  28.2 0.9 %add_convert_fusion = bf16[1,2,64,64]{3,2,1,0:T(8,128)(2,1)S(1)} fusion(f32[1,2,64,64]{3,2,1,0:T(8,128)S(1)} %collective-permute-done.2, f32[1,2,64,64]{3,2,1,0:T(8,128)S(1)} %collective-permute-done.1, f32[1,2,64,64]{3,2,1,0:T(8,128)S(1)} %collective-permute-done, f32[4,2,64,64]{3,2,1,0:T(8,128)} %shard_map.73, s32[]{:T(128)S(6)} %select_n.45), kind=kLoop, calls=%fused_computation | loop fusion | flops 32768 | bytes 147460 | tf_op jit(solution)/shard_map/convert_element_type | solution.py:175
  29.1 0.1 convert_element_type.11
  29.2 0.1 broadcast_in_dim.4
  29.3 9.0 %all_to_all.10 = bf16[8,2,4096]{2,1,0:T(2,128)(2,1)S(1)} all-to-all(bf16[8,2,4096]{2,1,0:T(2,128)(2,1)S(1)} %broadcast_in_dim.4), channel_id=1, replica_groups=mesh['dp'=8,'mp'=4] {'dp'}, dimensions={0} | all-to-all | bytes 262144 | tf_op jit(solution)/shard_map/all_to_all | solution.py:44
  38.3 0.1 reshape.10
  38.3 2.8 %fusion = f32[16,512]{1,0:T(8,128)S(1)} fusion(bf16[16,4096]{1,0:T(8,128)(2,1)S(1)} %reshape.10, bf16[4096,512]{1,0:T(8,128)(2,1)} %param.12), kind=kOutput, calls=%fused_computation.8 | convolution fusion | flops 67108864 | bytes 4358144 | tf_op jit(solution)/shard_map/dot_general | solution.py:178
  41.2 0.8 %broadcast_in_dim.5 = f32[8,16,512]{2,1,0:T(8,128)} broadcast(f32[16,512]{1,0:T(8,128)S(1)} %fusion), dimensions={1,2} | broadcast | bytes 294912 | tf_op jit(solution)/shard_map/broadcast_in_dim | solution.py:43
  41.9 3.4 %all-to-all-start.1 = ((f32[8,16,512]{2,1,0:T(8,128)}), f32[8,16,512]{2,1,0:T(8,128)S(1)}, u32[]{:S(2)}, u32[]{:S(2)}) async-start(f32[8,16,512]{2,1,0:T(8,128)} %broadcast_in_dim.5), calls=%async_computation.1 | async-start | bytes 524288 | tf_op jit(solution)/shard_map/all_to_all | solution.py:44
  45.4 6.8 %all-to-all-done.1.pre_ref = f32[8,16,512]{2,1,0:T(8,128)S(1)} async-done(((f32[8,16,512]{2,1,0:T(8,128)}), f32[8,16,512]{2,1,0:T(8,128)S(1)}, u32[]{:S(2)}, u32[]{:S(2)}) %all-to-all-start.1) | async-done | bytes 262176 | tf_op jit(solution)/shard_map/all_to_all | solution.py:44
  52.2 0.0 copy-start
  52.2 0.7 %copy-done = f32[8,16,512]{2,1,0:T(8,128)} copy-done((f32[8,16,512]{2,1,0:T(8,128)}, f32[8,16,512]{2,1,0:T(8,128)S(1)}, u32[]{:S(2)}) %copy-start) | copy-done | bytes 262168
  52.9 6.1 %shard_map.74 = f32[16,1024]{1,0:T(8,128)} custom-call(f32[8,16,512]{2,1,0:T(8,128)} %copy-done, bf16[1024,4096]{1,0:T(8,128)(2,1)} %query_ref.1), custom_call_target="tpu_custom_call" | custom-call | flops 268435456 | bytes 8716288 | tf_op jit(solution)/shard_map/pallas_call | solution.py:110
  59.0 0.8 %constant_dynamic-slice_fusion.2 = (f32[16,256]{1,0:T(8,128)S(1)}, f32[16,256]{1,0:T(8,128)S(1)}, f32[16,256]{1,0:T(8,128)S(1)}) fusion(f32[16,1024]{1,0:T(8,128)} %shard_map.74, s32[]{:T(128)S(6)} %select_n.53, s32[]{:T(128)S(6)} %select_n.55, s32[]{:T(128)S(6)} %select_n.54), kind=kLoop, calls=%fused_computation.4 | loop fusion | bytes 98316 | tf_op jit(solution)/shard_map/dynamic_slice | solution.py:27
  59.8 1.6 %collective-permute-start.3 = (f32[16,256]{1,0:T(8,128)S(1)}, f32[16,256]{1,0:T(8,128)S(1)}, u32[]{:S(2)}, u32[]{:S(2)}) collective-permute-start(f32[16,256]{1,0:T(8,128)S(1)} %get-tuple-element.8), channel_id=1, source_target_pairs={{0,1},{1,2},{2,3},{3,0},{4,5},{5,6},{6,7},{7,4},{8,9},{9,10},{10,1... | collective-permute-start | bytes 49160 | tf_op jit(solution)/shard_map/ppermute | solution.py:18
  61.4 2.0 %collective-permute-start.4 = (f32[16,256]{1,0:T(8,128)S(1)}, f32[16,256]{1,0:T(8,128)S(1)}, u32[]{:S(2)}, u32[]{:S(2)}) collective-permute-start(f32[16,256]{1,0:T(8,128)S(1)} %get-tuple-element.10), channel_id=1, source_target_pairs={{0,2},{1,3},{2,0},{3,1},{4,6},{5,7},{6,4},{7,5},{8,10},{9,11},{10,... | collective-permute-start | bytes 49160 | tf_op jit(solution)/shard_map/ppermute | solution.py:18
  63.4 0.4 collective-permute-start.5
  63.8 1.6 %collective-permute-done.3 = f32[16,256]{1,0:T(8,128)S(1)} collective-permute-done((f32[16,256]{1,0:T(8,128)S(1)}, f32[16,256]{1,0:T(8,128)S(1)}, u32[]{:S(2)}, u32[]{:S(2)}) %collective-permute-start.3) | collective-permute-done | bytes 16416 | tf_op jit(solution)/shard_map/ppermute | solution.py:18
  65.4 0.6 collective-permute-done.4
  66.0 1.1 %collective-permute-done.5 = f32[16,256]{1,0:T(8,128)S(1)} collective-permute-done((f32[16,256]{1,0:T(8,128)S(1)}, f32[16,256]{1,0:T(8,128)S(1)}, u32[]{:S(2)}, u32[]{:S(2)}) %collective-permute-start.5) | collective-permute-done | bytes 16416 | tf_op jit(solution)/shard_map/ppermute | solution.py:18
  67.1 1.3 %add_add_fusion = f32[16,256]{1,0:T(8,128)} fusion(f32[16,256]{1,0:T(8,128)S(1)} %collective-permute-done.5, f32[16,256]{1,0:T(8,128)S(1)} %collective-permute-done.4, f32[16,256]{1,0:T(8,128)S(1)} %collective-permute-done.3, f32[16,1024]{1,0:T(8,128)} %shard_map.74, s32[]{:T(128)S(6)} %select_n.52), kind=kLoop, calls=%fused_computation.1 | loop fusion | flops 12288 | bytes 81924 | tf_op jit(solution)/shard_map/add | solution.py:28
Async XLA Ops:
  17.8 7.6 %collective-permute-start = (f32[1,2,64,64]{3,2,1,0:T(8,128)S(1)}, f32[1,2,64,64]{3,2,1,0:T(8,128)S(1)}, u32[]{:S(2)}, u32[]{:S(2)}) collective-permute-start(f32[1,2,64,64]{3,2,1,0:T(8,128)S(1)} %get-tuple-element.5), channel_id=1, source_target_pairs={{0,1},{1,2},{2,3},{3,0},{4,5},{5,6},{6,7},{7,4},{8,9},{9,10},{10,1... | collective-permute-start | bytes 98312 | tf_op jit(solution)/shard_map/ppermute | solution.py:18
  20.9 7.1 %collective-permute-start.1 = (f32[1,2,64,64]{3,2,1,0:T(8,128)S(1)}, f32[1,2,64,64]{3,2,1,0:T(8,128)S(1)}, u32[]{:S(2)}, u32[]{:S(2)}) collective-permute-start(f32[1,2,64,64]{3,2,1,0:T(8,128)S(1)} %get-tuple-element.7), channel_id=1, source_target_pairs={{0,2},{1,3},{2,0},{3,1},{4,6},{5,7},{6,4},{7,5},{8,10},{9,11},{10,... | collective-permute-start | bytes 98312 | tf_op jit(solution)/shard_map/ppermute | solution.py:18
  23.5 4.7 %collective-permute-start.2 = (f32[1,2,64,64]{3,2,1,0:T(8,128)S(1)}, f32[1,2,64,64]{3,2,1,0:T(8,128)S(1)}, u32[]{:S(2)}, u32[]{:S(2)}) collective-permute-start(f32[1,2,64,64]{3,2,1,0:T(8,128)S(1)} %get-tuple-element.6), channel_id=1, source_target_pairs={{0,3},{1,0},{2,1},{3,2},{4,7},{5,4},{6,5},{7,6},{8,11},{9,8},{10,9... | collective-permute-start | bytes 98312 | tf_op jit(solution)/shard_map/ppermute | solution.py:18
  41.9 10.3 %all-to-all-start.1 = ((f32[8,16,512]{2,1,0:T(8,128)}), f32[8,16,512]{2,1,0:T(8,128)S(1)}, u32[]{:S(2)}, u32[]{:S(2)}) async-start(f32[8,16,512]{2,1,0:T(8,128)} %broadcast_in_dim.5), calls=%async_computation.1 | async-start | bytes 524288 | tf_op jit(solution)/shard_map/all_to_all | solution.py:44
  52.2 0.7 %copy-start = (f32[8,16,512]{2,1,0:T(8,128)}, f32[8,16,512]{2,1,0:T(8,128)S(1)}, u32[]{:S(2)}) copy-start(f32[8,16,512]{2,1,0:T(8,128)S(1)} %all-to-all-done.1.pre_ref) | copy-start | bytes 786436
  59.8 5.6 %collective-permute-start.3 = (f32[16,256]{1,0:T(8,128)S(1)}, f32[16,256]{1,0:T(8,128)S(1)}, u32[]{:S(2)}, u32[]{:S(2)}) collective-permute-start(f32[16,256]{1,0:T(8,128)S(1)} %get-tuple-element.8), channel_id=1, source_target_pairs={{0,1},{1,2},{2,3},{3,0},{4,5},{5,6},{6,7},{7,4},{8,9},{9,10},{10,1... | collective-permute-start | bytes 49160 | tf_op jit(solution)/shard_map/ppermute | solution.py:18
  61.4 4.6 %collective-permute-start.4 = (f32[16,256]{1,0:T(8,128)S(1)}, f32[16,256]{1,0:T(8,128)S(1)}, u32[]{:S(2)}, u32[]{:S(2)}) collective-permute-start(f32[16,256]{1,0:T(8,128)S(1)} %get-tuple-element.10), channel_id=1, source_target_pairs={{0,2},{1,3},{2,0},{3,1},{4,6},{5,7},{6,4},{7,5},{8,10},{9,11},{10,... | collective-permute-start | bytes 49160 | tf_op jit(solution)/shard_map/ppermute | solution.py:18
  63.4 3.7 %collective-permute-start.5 = (f32[16,256]{1,0:T(8,128)S(1)}, f32[16,256]{1,0:T(8,128)S(1)}, u32[]{:S(2)}, u32[]{:S(2)}) collective-permute-start(f32[16,256]{1,0:T(8,128)S(1)} %get-tuple-element.9), channel_id=1, source_target_pairs={{0,3},{1,0},{2,1},{3,2},{4,7},{5,4},{6,5},{7,6},{8,11},{9,8},{10,9... | collective-permute-start | bytes 49160 | tf_op jit(solution)/shard_map/ppermute | solution.py:18

commit v11 on v8

--- a/solution.py
+++ b/solution.py
@@ -44,16 +44,23 @@
     return lax.all_to_all(copies, axis, 0, 0, tiled=True)
 
 
-def gradient_kernel(lengths_ref, act_ref, cot_ref, win_ref, wout_ref, out_ref):
+def gradient_kernel(lengths_ref, act_ref, cot_hbm, win_ref, wout_ref, out_ref, cot_buf, sem):
+    layer = pl.program_id(0)
+    fetch = pltpu.make_async_copy(cot_hbm.at[layer], cot_buf, sem)
+    fetch.start()
     tokens = act_ref.shape[1]
     offset = lax.axis_index("mp") * tokens
     nt = (((1,), (1,)), ((), ()))
-    for example in range(act_ref.shape[0]):
-        left = lax.dot_general(
+    lefts = [
+        lax.dot_general(
             act_ref[example], win_ref[...], nt, preferred_element_type=jnp.float32
         ).astype(jnp.bfloat16)
+        for example in range(act_ref.shape[0])
+    ]
+    fetch.wait()
+    for example, left in enumerate(lefts):
         right = lax.dot_general(
-            cot_ref[example], wout_ref[...], nt, preferred_element_type=jnp.float32
+            cot_buf[example], wout_ref[...], nt, preferred_element_type=jnp.float32
         )
         rows = lax.broadcasted_iota(jnp.int32, right.shape, 0)
         right = jnp.where(rows < lengths_ref[example] - offset, right, 0.0).astype(jnp.bfloat16)
@@ -75,8 +82,12 @@
         grid_spec=pltpu.PrefetchScalarGridSpec(
             num_scalar_prefetch=1,
             grid=(layers,),
-            in_specs=[data, data, weights, weights],
+            in_specs=[data, pl.BlockSpec(memory_space=pl.ANY), weights, weights],
             out_specs=pl.BlockSpec((None, examples, factor, factor), lambda l, lens: (l, 0, 0, 0)),
+            scratch_shapes=[
+                pltpu.VMEM((examples, tokens, width), cotangents.dtype),
+                pltpu.SemaphoreType.DMA(()),
+            ],
         ),
         cost_estimate=pl.CostEstimate(flops=flops, transcendentals=0, bytes_accessed=moved),
     )(lengths, activations, cotangents, project_in, project_out)

time: 66.7 us -> 77 us (1.15)
  Pallas kernels: 16.9 us -> 27.2 us
    pallas_call x1, Pallas kernels: 16.9 us -> 27.2 us  [layer_gradients(): pl.pallas_call(gradient_kernel, out_shape=jax.ShapeDtypeStruct((layers, e...]
where the time goes in v11:
time: 77 us; the launch traced here: 76.6 us
  Pallas kernels  27.2 us (35%)
  starting transfers between devices  14.5 us (19%)
  waiting for transfers between devices  13.5 us (18%)
  blocking collectives  9.01 us (12%)
  matrix products  8.81 us (11%)
  local copies, waits for them, and re-layouts  1.91 us (2%)
  other arithmetic  1.54 us (2%)
    pallas_call x1, Pallas kernels, layer_gradients(): pl.pallas_call(gradient_kernel, out_shape=jax.ShapeDtypeStruct((layers, e...  27.2 us
    ppermute x6, starting transfers between devices, shifted(): return lax.ppermute(x, axis, [(i, (i + shift) % n) for i in range(n)])  11.1 us
    all_to_all x1, blocking collectives, all_gather_a2a(): return lax.all_to_all(copies, axis, 0, 0, tiled=True)  9.01 us
    all_to_all x1, waiting for transfers between devices, all_gather_a2a(): return lax.all_to_all(copies, axis, 0, 0, tiled=True)  6.81 us
    ppermute x6, waiting for transfers between devices, shifted(): return lax.ppermute(x, axis, [(i, (i + shift) % n) for i in range(n)])  6.68 us
    dot_general x1, matrix products, body_direct(): lax.dot_general(both_all, query_blocks, (((0, 2), (1, 2)), ((), ())), pre...  5.98 us
    all_to_all x1, starting transfers between devices, all_gather_a2a(): return lax.all_to_all(copies, axis, 0, 0, tiled=True)  3.41 us
    dot_general x1, matrix products, body_direct(): jnp.dot(grad_all, preconditioner, preferred_element_type=jnp.float32)  2.83 us
  transfers between devices with their start and end apart: 7, of which 7 were waited for; matrix products, arithmetic and copies ran while one was open for 0% of the time, Pallas kernels for 0%

profile of v11, /device:TPU:0, one launch (start us, length us, event | category | flops | bytes accessed | tf_op | source)
XLA Modules:
  0.0 76.6 jit_solution(4967706828043494608)
XLA Ops:
  0.0 27.2 %shard_map.73 = f32[4,2,64,64]{3,2,1,0:T(8,128)} custom-call(s32[2]{0:T(128)} %lengths_ref.1, bf16[4,2,256,4096]{3,2,1,0:T(8,128)(2,1)} %act_ref.1, bf16[4,2,256,4096]{3,2,1,0:T(8,128)(2,1)} %cot_hbm.1, bf16[4,64,4096]{2,1,0:T(8,128)(2,1)} %win_ref.1, bf16[4,64,4096]{2,1,0:T(8,128)(2,1)} %wout_ref.1), custom_call_target="tpu_custom_call" | custom-call | flops 2147483648 | bytes 37748736 | tf_op jit(solution)/shard_map/pallas_call | solution.py:79
  27.2 0.9 %constant_dynamic-slice_fusion.5 = (f32[1,2,64,64]{3,2,1,0:T(8,128)S(1)}, f32[1,2,64,64]{3,2,1,0:T(8,128)S(1)}, f32[1,2,64,64]{3,2,1,0:T(8,128)S(1)}) fusion(f32[4,2,64,64]{3,2,1,0:T(8,128)} %shard_map.73, s32[]{:T(128)S(6)} %select_n.47, s32[]{:T(128)S(6)} %select_n.51, s32[]{:T(128)S(6)} %select_n.49), kind=kLoop, calls=%fused_computation.16 | loop fusion | bytes 196620 | tf_op jit(solution)/shard_map/dynamic_slice | solution.py:27
  28.1 3.1 %collective-permute-start = (f32[1,2,64,64]{3,2,1,0:T(8,128)S(1)}, f32[1,2,64,64]{3,2,1,0:T(8,128)S(1)}, u32[]{:S(2)}, u32[]{:S(2)}) collective-permute-start(f32[1,2,64,64]{3,2,1,0:T(8,128)S(1)} %get-tuple-element.5), channel_id=1, source_target_pairs={{0,1},{1,2},{2,3},{3,0},{4,5},{5,6},{6,7},{7,4},{8,9},{9,10},{10,1... | collective-permute-start | bytes 98312 | tf_op jit(solution)/shard_map/ppermute | solution.py:18
  31.2 2.6 %collective-permute-start.1 = (f32[1,2,64,64]{3,2,1,0:T(8,128)S(1)}, f32[1,2,64,64]{3,2,1,0:T(8,128)S(1)}, u32[]{:S(2)}, u32[]{:S(2)}) collective-permute-start(f32[1,2,64,64]{3,2,1,0:T(8,128)S(1)} %get-tuple-element.7), channel_id=1, source_target_pairs={{0,2},{1,3},{2,0},{3,1},{4,6},{5,7},{6,4},{7,5},{8,10},{9,11},{10,... | collective-permute-start | bytes 98312 | tf_op jit(solution)/shard_map/ppermute | solution.py:18
  33.8 1.3 %collective-permute-start.2 = (f32[1,2,64,64]{3,2,1,0:T(8,128)S(1)}, f32[1,2,64,64]{3,2,1,0:T(8,128)S(1)}, u32[]{:S(2)}, u32[]{:S(2)}) collective-permute-start(f32[1,2,64,64]{3,2,1,0:T(8,128)S(1)} %get-tuple-element.6), channel_id=1, source_target_pairs={{0,3},{1,0},{2,1},{3,2},{4,7},{5,4},{6,5},{7,6},{8,11},{9,8},{10,9... | collective-permute-start | bytes 98312 | tf_op jit(solution)/shard_map/ppermute | solution.py:18
  35.1 0.5 collective-permute-done
  35.7 2.6 %collective-permute-done.1 = f32[1,2,64,64]{3,2,1,0:T(8,128)S(1)} collective-permute-done((f32[1,2,64,64]{3,2,1,0:T(8,128)S(1)}, f32[1,2,64,64]{3,2,1,0:T(8,128)S(1)}, u32[]{:S(2)}, u32[]{:S(2)}) %collective-permute-start.1) | collective-permute-done | bytes 32800 | tf_op jit(solution)/shard_map/ppermute | solution.py:18
  38.3 0.2 collective-permute-done.2
  38.5 0.9 %add_convert_fusion = bf16[1,2,64,64]{3,2,1,0:T(8,128)(2,1)S(1)} fusion(f32[1,2,64,64]{3,2,1,0:T(8,128)S(1)} %collective-permute-done.2, f32[1,2,64,64]{3,2,1,0:T(8,128)S(1)} %collective-permute-done.1, f32[1,2,64,64]{3,2,1,0:T(8,128)S(1)} %collective-permute-done, f32[4,2,64,64]{3,2,1,0:T(8,128)} %shard_map.73, s32[]{:T(128)S(6)} %select_n.45), kind=kLoop, calls=%fused_computation.9 | loop fusion | flops 32768 | bytes 147460 | tf_op jit(solution)/shard_map/convert_element_type | solution.py:148
  39.4 0.1 convert_element_type.20
  39.5 0.1 broadcast_in_dim.4
  39.5 9.0 %all_to_all.10 = bf16[8,2,4096]{2,1,0:T(2,128)(2,1)S(1)} all-to-all(bf16[8,2,4096]{2,1,0:T(2,128)(2,1)S(1)} %broadcast_in_dim.4), channel_id=1, replica_groups=mesh['dp'=8,'mp'=4] {'dp'}, dimensions={0} | all-to-all | bytes 262144 | tf_op jit(solution)/shard_map/all_to_all | solution.py:44
  48.5 0.1 reshape.13
  48.6 2.8 %fusion.10 = f32[16,512]{1,0:T(8,128)S(1)} fusion(bf16[16,4096]{1,0:T(8,128)(2,1)S(1)} %reshape.13, bf16[4096,512]{1,0:T(8,128)(2,1)} %param.12), kind=kOutput, calls=%fused_computation.18 | convolution fusion | flops 67108864 | bytes 4358144 | tf_op jit(solution)/shard_map/dot_general | solution.py:151
  51.4 0.7 broadcast_in_dim.5
  52.2 3.4 %all-to-all-start.1 = ((f32[8,16,512]{2,1,0:T(8,128)}), f32[8,16,512]{2,1,0:T(8,128)S(1)}, u32[]{:S(2)}, u32[]{:S(2)}) async-start(f32[8,16,512]{2,1,0:T(8,128)} %broadcast_in_dim.5), calls=%async_computation.1 | async-start | bytes 524288 | tf_op jit(solution)/shard_map/all_to_all | solution.py:44
  55.6 6.8 %all-to-all-done.1 = f32[8,16,512]{2,1,0:T(8,128)S(1)} async-done(((f32[8,16,512]{2,1,0:T(8,128)}), f32[8,16,512]{2,1,0:T(8,128)S(1)}, u32[]{:S(2)}, u32[]{:S(2)}) %all-to-all-start.1) | async-done | bytes 262176 | tf_op jit(solution)/shard_map/all_to_all | solution.py:44
  62.5 6.0 %fusion.3 = f32[32,1024]{1,0:T(8,128)S(1)} fusion(bf16[128,8,8,512]{3,2,1,0:T(8,128)(2,1)} %bitcast.12, bf16[8,16,512]{2,1,0:T(8,128)(2,1)S(1)} %subtract_convert_fusion, bf16[8,16,512]{2,1,0:T(8,128)(2,1)S(1)} %convert_element_type.21), kind=kOutput, calls=%fused_computation.3 | convolution fusion | flops 268959744 | bytes 8781824 | tf_op jit(solution)/shard_map/dot_general | solution.py:156
  68.5 1.7 %collective-permute-start.3 = (f32[16,256]{1,0:T(8,128)S(1)}, f32[16,256]{1,0:T(8,128)S(1)}, u32[]{:S(2)}, u32[]{:S(2)}) collective-permute-start(f32[16,256]{1,0:T(8,128)S(1)} %get-tuple-element.8), channel_id=1, source_target_pairs={{0,1},{1,2},{2,3},{3,0},{4,5},{5,6},{6,7},{7,4},{8,9},{9,10},{10,1... | collective-permute-start | bytes 49160 | tf_op jit(solution)/shard_map/ppermute | solution.py:18
  70.2 2.0 %collective-permute-start.4 = (f32[16,256]{1,0:T(8,128)S(1)}, f32[16,256]{1,0:T(8,128)S(1)}, u32[]{:S(2)}, u32[]{:S(2)}) collective-permute-start(f32[16,256]{1,0:T(8,128)S(1)} %get-tuple-element.10), channel_id=1, source_target_pairs={{0,2},{1,3},{2,0},{3,1},{4,6},{5,7},{6,4},{7,5},{8,10},{9,11},{10,... | collective-permute-start | bytes 49160 | tf_op jit(solution)/shard_map/ppermute | solution.py:18
  72.2 0.4 collective-permute-start.5
  72.6 1.6 %collective-permute-done.3 = f32[16,256]{1,0:T(8,128)S(1)} collective-permute-done((f32[16,256]{1,0:T(8,128)S(1)}, f32[16,256]{1,0:T(8,128)S(1)}, u32[]{:S(2)}, u32[]{:S(2)}) %collective-permute-start.3) | collective-permute-done | bytes 16416 | tf_op jit(solution)/shard_map/ppermute | solution.py:18
  74.2 0.6 collective-permute-done.4
  74.8 1.1 %collective-permute-done.5 = f32[16,256]{1,0:T(8,128)S(1)} collective-permute-done((f32[16,256]{1,0:T(8,128)S(1)}, f32[16,256]{1,0:T(8,128)S(1)}, u32[]{:S(2)}, u32[]{:S(2)}) %collective-permute-start.5) | collective-permute-done | bytes 16416 | tf_op jit(solution)/shard_map/ppermute | solution.py:18
  75.9 0.6 add_add_fusion
  (4 shorter events, 0.1 us)
Async XLA Ops:
  28.1 7.6 %collective-permute-start = (f32[1,2,64,64]{3,2,1,0:T(8,128)S(1)}, f32[1,2,64,64]{3,2,1,0:T(8,128)S(1)}, u32[]{:S(2)}, u32[]{:S(2)}) collective-permute-start(f32[1,2,64,64]{3,2,1,0:T(8,128)S(1)} %get-tuple-element.5), channel_id=1, source_target_pairs={{0,1},{1,2},{2,3},{3,0},{4,5},{5,6},{6,7},{7,4},{8,9},{9,10},{10,1... | collective-permute-start | bytes 98312 | tf_op jit(solution)/shard_map/ppermute | solution.py:18
  31.2 7.1 %collective-permute-start.1 = (f32[1,2,64,64]{3,2,1,0:T(8,128)S(1)}, f32[1,2,64,64]{3,2,1,0:T(8,128)S(1)}, u32[]{:S(2)}, u32[]{:S(2)}) collective-permute-start(f32[1,2,64,64]{3,2,1,0:T(8,128)S(1)} %get-tuple-element.7), channel_id=1, source_target_pairs={{0,2},{1,3},{2,0},{3,1},{4,6},{5,7},{6,4},{7,5},{8,10},{9,11},{10,... | collective-permute-start | bytes 98312 | tf_op jit(solution)/shard_map/ppermute | solution.py:18
  33.8 4.7 %collective-permute-start.2 = (f32[1,2,64,64]{3,2,1,0:T(8,128)S(1)}, f32[1,2,64,64]{3,2,1,0:T(8,128)S(1)}, u32[]{:S(2)}, u32[]{:S(2)}) collective-permute-start(f32[1,2,64,64]{3,2,1,0:T(8,128)S(1)} %get-tuple-element.6), channel_id=1, source_target_pairs={{0,3},{1,0},{2,1},{3,2},{4,7},{5,4},{6,5},{7,6},{8,11},{9,8},{10,9... | collective-permute-start | bytes 98312 | tf_op jit(solution)/shard_map/ppermute | solution.py:18
  52.2 10.3 %all-to-all-start.1 = ((f32[8,16,512]{2,1,0:T(8,128)}), f32[8,16,512]{2,1,0:T(8,128)S(1)}, u32[]{:S(2)}, u32[]{:S(2)}) async-start(f32[8,16,512]{2,1,0:T(8,128)} %broadcast_in_dim.5), calls=%async_computation.1 | async-start | bytes 524288 | tf_op jit(solution)/shard_map/all_to_all | solution.py:44
  68.5 5.7 %collective-permute-start.3 = (f32[16,256]{1,0:T(8,128)S(1)}, f32[16,256]{1,0:T(8,128)S(1)}, u32[]{:S(2)}, u32[]{:S(2)}) collective-permute-start(f32[16,256]{1,0:T(8,128)S(1)} %get-tuple-element.8), channel_id=1, source_target_pairs={{0,1},{1,2},{2,3},{3,0},{4,5},{5,6},{6,7},{7,4},{8,9},{9,10},{10,1... | collective-permute-start | bytes 49160 | tf_op jit(solution)/shard_map/ppermute | solution.py:18
  70.2 4.6 %collective-permute-start.4 = (f32[16,256]{1,0:T(8,128)S(1)}, f32[16,256]{1,0:T(8,128)S(1)}, u32[]{:S(2)}, u32[]{:S(2)}) collective-permute-start(f32[16,256]{1,0:T(8,128)S(1)} %get-tuple-element.10), channel_id=1, source_target_pairs={{0,2},{1,3},{2,0},{3,1},{4,6},{5,7},{6,4},{7,5},{8,10},{9,11},{10,... | collective-permute-start | bytes 49160 | tf_op jit(solution)/shard_map/ppermute | solution.py:18
  72.2 3.7 %collective-permute-start.5 = (f32[16,256]{1,0:T(8,128)S(1)}, f32[16,256]{1,0:T(8,128)S(1)}, u32[]{:S(2)}, u32[]{:S(2)}) collective-permute-start(f32[16,256]{1,0:T(8,128)S(1)} %get-tuple-element.9), channel_id=1, source_target_pairs={{0,3},{1,0},{2,1},{3,2},{4,7},{5,4},{6,5},{7,6},{8,11},{9,8},{10,9... | collective-permute-start | bytes 49160 | tf_op jit(solution)/shard_map/ppermute | solution.py:18

commit v12 on v8

--- a/solution.py
+++ b/solution.py
@@ -44,10 +44,12 @@
     return lax.all_to_all(copies, axis, 0, 0, tiled=True)
 
 
-def gradient_kernel(lengths_ref, act_ref, cot_ref, win_ref, wout_ref, out_ref):
+def gradient_kernel(order_ref, lengths_ref, act_ref, cot_ref, win_ref, wout_ref, *out_refs):
+    step = pl.program_id(0)
     tokens = act_ref.shape[1]
     offset = lax.axis_index("mp") * tokens
     nt = (((1,), (1,)), ((), ()))
+    grads = []
     for example in range(act_ref.shape[0]):
         left = lax.dot_general(
             act_ref[example], win_ref[...], nt, preferred_element_type=jnp.float32
@@ -57,29 +59,35 @@
         )
         rows = lax.broadcasted_iota(jnp.int32, right.shape, 0)
         right = jnp.where(rows < lengths_ref[example] - offset, right, 0.0).astype(jnp.bfloat16)
-        out_ref[example] = lax.dot_general(
+        grads.append(lax.dot_general(
             right, left, (((0,), (0,)), ((), ())), preferred_element_type=jnp.float32
-        )
+        ))
+    for index, out_ref in enumerate(out_refs):
+        @pl.when(step == index)
+        def _():
+            for example, grad in enumerate(grads):
+                out_ref[example] = grad
 
 
-def layer_gradients(activations, cotangents, lengths, project_in, project_out):
+def layer_gradients(order, activations, cotangents, lengths, project_in, project_out):
     layers, examples, tokens, width = activations.shape
     factor = project_in.shape[1]
-    data = pl.BlockSpec((None, examples, tokens, width), lambda l, lens: (l, 0, 0, 0))
-    weights = pl.BlockSpec((None, factor, width), lambda l, lens: (l, 0, 0))
+    data = pl.BlockSpec((None, examples, tokens, width), lambda t, rank, lens: (rank[t], 0, 0, 0))
+    weights = pl.BlockSpec((None, factor, width), lambda t, rank, lens: (rank[t], 0, 0))
+    result = pl.BlockSpec((examples, factor, factor), lambda t, rank, lens: (0, 0, 0))
     flops = 4 * layers * examples * tokens * width * factor
     moved = 2 * (activations.size + cotangents.size + project_in.size + project_out.size)
     return pl.pallas_call(
         gradient_kernel,
-        out_shape=jax.ShapeDtypeStruct((layers, examples, factor, factor), jnp.float32),
+        out_shape=[jax.ShapeDtypeStruct((examples, factor, factor), jnp.float32)] * layers,
         grid_spec=pltpu.PrefetchScalarGridSpec(
-            num_scalar_prefetch=1,
+            num_scalar_prefetch=2,
             grid=(layers,),
             in_specs=[data, data, weights, weights],
-            out_specs=pl.BlockSpec((None, examples, factor, factor), lambda l, lens: (l, 0, 0, 0)),
+            out_specs=[result] * layers,
         ),
         cost_estimate=pl.CostEstimate(flops=flops, transcendentals=0, bytes_accessed=moved),
-    )(lengths, activations, cotangents, project_in, project_out)
+    )(order, lengths, activations, cotangents, project_in, project_out)
 
 
 def body_start(activations, cotangents, lengths, project_in, project_out, preconditioner, queries):
@@ -132,8 +140,11 @@
     block_size = factor_size * factor_size
     width_dp = lax.axis_size("dp")
     mp_place = lax.axis_index("mp")
-    partial_grad = layer_gradients(activations, cotangents, lengths, project_in, project_out)
-    grad_mine = reduce_scatter_direct(partial_grad, "mp", 0)[0]
+    order = (mp_place + jnp.arange(1, layer_count + 1, dtype=jnp.int32)) % layer_count
+    grads = layer_gradients(order, activations, cotangents, lengths, project_in, project_out)
+    grad_mine = grads[-1]
+    for shift in range(1, layer_count):
+        grad_mine = grad_mine + shifted(grads[shift - 1], "mp", shift)
     grad_mine = grad_mine.astype(jnp.bfloat16).reshape(grad_mine.shape[0], block_size)
     grad_all = all_gather_a2a(grad_mine, "dp")
     grad_all = grad_all.reshape(-1, grad_all.shape[-1])

time: 66.7 us -> 67.9 us (1.018)
  waiting for transfers between devices: 13.5 us -> 16.1 us
  starting transfers between devices: 14.5 us -> 13.4 us
  local copies, waits for them, and re-layouts: 1.9 us -> 0.98 us
    ppermute x6, waiting for transfers between devices: 6.68 us -> 9.33 us  [shifted(): return lax.ppermute(x, axis, [(i, (i + shift) % n) for i in range(n)])]
    ppermute x6, starting transfers between devices: 11.1 us -> 9.97 us  [shifted(): return lax.ppermute(x, axis, [(i, (i + shift) % n) for i in range(n)])]
    dynamic_slice x2 -> x1, local copies, waits for them, and re-layouts: 0.93 us -> 0.01 us  [reduce_scatter_direct(): piece = lax.dynamic_slice_in_dim(x, (me + shift) % n * width, width, dim)]
  transfers between devices with their start and end apart: 7 -> 7, of which waited for: 7 -> 5; matrix products, arithmetic and copies ran while one was open for 0% -> 0% of each run, Pallas kernels for 0% -> 0%
where the time goes in v12:
time: 67.9 us; the launch traced here: 67.5 us
  Pallas kernels  17 us (25%)
  waiting for transfers between devices  16.1 us (24%)
  starting transfers between devices  13.4 us (20%)
  blocking collectives  9.02 us (13%)
  matrix products  8.81 us (13%)
  other arithmetic  2.07 us (3%)
  local copies, waits for them, and re-layouts  0.98 us (1%)
    pallas_call x1, Pallas kernels, layer_gradients(): pl.pallas_call(gradient_kernel, out_shape=[jax.ShapeDtypeStruct((examples...  17 us
    ppermute x6, starting transfers between devices, shifted(): return lax.ppermute(x, axis, [(i, (i + shift) % n) for i in range(n)])  9.97 us
    ppermute x6, waiting for transfers between devices, shifted(): return lax.ppermute(x, axis, [(i, (i + shift) % n) for i in range(n)])  9.33 us
    all_to_all x1, blocking collectives, all_gather_a2a(): return lax.all_to_all(copies, axis, 0, 0, tiled=True)  9.02 us
    all_to_all x1, waiting for transfers between devices, all_gather_a2a(): return lax.all_to_all(copies, axis, 0, 0, tiled=True)  6.8 us
    dot_general x1, matrix products, body_direct(): lax.dot_general(both_all, query_blocks, (((0, 2), (1, 2)), ((), ())), pre...  5.98 us
    all_to_all x1, starting transfers between devices, all_gather_a2a(): return lax.all_to_all(copies, axis, 0, 0, tiled=True)  3.41 us
    dot_general x1, matrix products, body_direct(): jnp.dot(grad_all, preconditioner, preferred_element_type=jnp.float32)  2.83 us
  transfers between devices with their start and end apart: 7, of which 5 were waited for; matrix products, arithmetic and copies ran while one was open for 0% of the time, Pallas kernels for 0%

profile of v12, /device:TPU:0, one launch (start us, length us, event | category | flops | bytes accessed | tf_op | source)
XLA Modules:
  0.0 67.5 jit_solution(2431168003416578598)
XLA Ops:
  0.0 0.5 and_select_fusion.order_ref
  0.5 17.0 %shard_map.73 = (f32[2,64,64]{2,1,0:T(8,128)}, f32[2,64,64]{2,1,0:T(8,128)}, f32[2,64,64]{2,1,0:T(8,128)}, f32[2,64,64]{2,1,0:T(8,128)}) custom-call(s32[4]{0:T(128)} %and_select_fusion.order_ref, s32[2]{0:T(128)} %lengths_ref.1, bf16[4,2,256,4096]{3,2,1,0:T(8,128)(2,1)} %act_ref.1, bf16[4,2,256,4096]{3,2,1,0:T(8,128)(2,1)} %cot_ref.1, ...), custom_call_target="tpu_custom_call" | custom-call | flops 2147483648 | bytes 37748736 | tf_op jit(solution)/shard_map/pallas_call | solution.py:80
  17.5 5.1 %collective-permute-start.2 = (f32[2,64,64]{2,1,0:T(8,128)}, f32[2,64,64]{2,1,0:T(8,128)S(1)}, u32[]{:S(2)}, u32[]{:S(2)}) collective-permute-start(f32[2,64,64]{2,1,0:T(8,128)} %get-tuple-element.12), channel_id=1, source_target_pairs={{0,3},{1,0},{2,1},{3,2},{4,7},{5,4},{6,5},{7,6},{8,11},{9,8},{10,9... | collective-permute-start | bytes 98312 | tf_op jit(solution)/shard_map/ppermute | solution.py:18
  22.6 0.0 collective-permute-start.1
  22.6 1.1 %collective-permute-start = (f32[2,64,64]{2,1,0:T(8,128)}, f32[2,64,64]{2,1,0:T(8,128)S(1)}, u32[]{:S(2)}, u32[]{:S(2)}) collective-permute-start(f32[2,64,64]{2,1,0:T(8,128)} %get-tuple-element.10), channel_id=1, source_target_pairs={{0,1},{1,2},{2,3},{3,0},{4,5},{5,6},{6,7},{7,4},{8,9},{9,10},{10,1... | collective-permute-start | bytes 98312 | tf_op jit(solution)/shard_map/ppermute | solution.py:18
  23.7 1.7 %collective-permute-done.2 = f32[2,64,64]{2,1,0:T(8,128)S(1)} collective-permute-done((f32[2,64,64]{2,1,0:T(8,128)}, f32[2,64,64]{2,1,0:T(8,128)S(1)}, u32[]{:S(2)}, u32[]{:S(2)}) %collective-permute-start.2) | collective-permute-done | bytes 32800 | tf_op jit(solution)/shard_map/ppermute | solution.py:18
  25.4 4.0 %collective-permute-done.1 = f32[2,64,64]{2,1,0:T(8,128)S(1)} collective-permute-done((f32[2,64,64]{2,1,0:T(8,128)}, f32[2,64,64]{2,1,0:T(8,128)S(1)}, u32[]{:S(2)}, u32[]{:S(2)}) %collective-permute-start.1) | collective-permute-done | bytes 32800 | tf_op jit(solution)/shard_map/ppermute | solution.py:18
  29.3 0.0 collective-permute-done
  29.3 0.9 %add_convert_fusion = bf16[2,64,64]{2,1,0:T(8,128)(2,1)S(1)} fusion(f32[2,64,64]{2,1,0:T(8,128)S(1)} %collective-permute-done.2, f32[2,64,64]{2,1,0:T(8,128)S(1)} %collective-permute-done.1, f32[2,64,64]{2,1,0:T(8,128)} %get-tuple-element.9, f32[2,64,64]{2,1,0:T(8,128)S(1)} %collective-permute-done), kind=kLoop, calls=%fused_computation.9 | loop fusion | flops 32768 | bytes 147456 | tf_op jit(solution)/shard_map/convert_element_type | solution.py:148
  30.2 0.1 broadcast_in_dim.6
  30.3 0.1 broadcast_in_dim.14
  30.4 9.0 %all_to_all.10 = bf16[8,2,4096]{2,1,0:T(2,128)(2,1)S(1)} all-to-all(bf16[8,2,4096]{2,1,0:T(2,128)(2,1)S(1)} %broadcast_in_dim.14), channel_id=1, replica_groups=mesh['dp'=8,'mp'=4] {'dp'}, dimensions={0} | all-to-all | bytes 262144 | tf_op jit(solution)/shard_map/all_to_all | solution.py:44
  39.4 0.1 reshape.8
  39.5 2.8 %fusion.11 = f32[16,512]{1,0:T(8,128)S(1)} fusion(bf16[16,4096]{1,0:T(8,128)(2,1)S(1)} %reshape.8, bf16[4096,512]{1,0:T(8,128)(2,1)} %param.12), kind=kOutput, calls=%fused_computation.19 | convolution fusion | flops 67108864 | bytes 4358144 | tf_op jit(solution)/shard_map/dot_general | solution.py:151
  42.3 0.7 %broadcast_in_dim.15 = f32[8,16,512]{2,1,0:T(8,128)} broadcast(f32[16,512]{1,0:T(8,128)S(1)} %fusion.11), dimensions={1,2} | broadcast | bytes 294912 | tf_op jit(solution)/shard_map/broadcast_in_dim | solution.py:43
  43.0 3.4 %all-to-all-start.1 = ((f32[8,16,512]{2,1,0:T(8,128)}), f32[8,16,512]{2,1,0:T(8,128)S(1)}, u32[]{:S(2)}, u32[]{:S(2)}) async-start(f32[8,16,512]{2,1,0:T(8,128)} %broadcast_in_dim.15), calls=%async_computation.1 | async-start | bytes 524288 | tf_op jit(solution)/shard_map/all_to_all | solution.py:44
  46.5 6.8 %all-to-all-done.1 = f32[8,16,512]{2,1,0:T(8,128)S(1)} async-done(((f32[8,16,512]{2,1,0:T(8,128)}), f32[8,16,512]{2,1,0:T(8,128)S(1)}, u32[]{:S(2)}, u32[]{:S(2)}) %all-to-all-start.1) | async-done | bytes 262176 | tf_op jit(solution)/shard_map/all_to_all | solution.py:44
  53.3 6.0 %fusion.3 = f32[32,1024]{1,0:T(8,128)S(1)} fusion(bf16[128,8,8,512]{3,2,1,0:T(8,128)(2,1)} %bitcast.10, bf16[8,16,512]{2,1,0:T(8,128)(2,1)S(1)} %subtract_convert_fusion, bf16[8,16,512]{2,1,0:T(8,128)(2,1)S(1)} %convert_element_type.13), kind=kOutput, calls=%fused_computation.3 | convolution fusion | flops 268959744 | bytes 8781824 | tf_op jit(solution)/shard_map/dot_general | solution.py:156
  59.4 1.9 %collective-permute-start.5 = (f32[16,256]{1,0:T(8,128)S(1)}, f32[16,256]{1,0:T(8,128)S(1)}, u32[]{:S(2)}, u32[]{:S(2)}) collective-permute-start(f32[16,256]{1,0:T(8,128)S(1)} %get-tuple-element.14), channel_id=1, source_target_pairs={{0,3},{1,0},{2,1},{3,2},{4,7},{5,4},{6,5},{7,6},{8,11},{9,8},{10,9... | collective-permute-start | bytes 49160 | tf_op jit(solution)/shard_map/ppermute | solution.py:18
  61.3 0.0 collective-permute-start.4
  61.3 1.9 %collective-permute-start.3 = (f32[16,256]{1,0:T(8,128)S(1)}, f32[16,256]{1,0:T(8,128)S(1)}, u32[]{:S(2)}, u32[]{:S(2)}) collective-permute-start(f32[16,256]{1,0:T(8,128)S(1)} %get-tuple-element.13), channel_id=1, source_target_pairs={{0,1},{1,2},{2,3},{3,0},{4,5},{5,6},{6,7},{7,4},{8,9},{9,10},{10,1... | collective-permute-start | bytes 49160 | tf_op jit(solution)/shard_map/ppermute | solution.py:18
  63.2 0.0 collective-permute-done.5
  63.2 2.8 %collective-permute-done.4 = f32[16,256]{1,0:T(8,128)S(1)} collective-permute-done((f32[16,256]{1,0:T(8,128)S(1)}, f32[16,256]{1,0:T(8,128)S(1)}, u32[]{:S(2)}, u32[]{:S(2)}) %collective-permute-start.4) | collective-permute-done | bytes 16416 | tf_op jit(solution)/shard_map/ppermute | solution.py:18
  66.0 0.9 %collective-permute-done.3 = f32[16,256]{1,0:T(8,128)S(1)} collective-permute-done((f32[16,256]{1,0:T(8,128)S(1)}, f32[16,256]{1,0:T(8,128)S(1)}, u32[]{:S(2)}, u32[]{:S(2)}) %collective-permute-start.3) | collective-permute-done | bytes 16416 | tf_op jit(solution)/shard_map/ppermute | solution.py:18
  66.9 0.6 add_add_fusion
  (4 shorter events, 0.1 us)
Async XLA Ops:
  17.5 7.9 %collective-permute-start.2 = (f32[2,64,64]{2,1,0:T(8,128)}, f32[2,64,64]{2,1,0:T(8,128)S(1)}, u32[]{:S(2)}, u32[]{:S(2)}) collective-permute-start(f32[2,64,64]{2,1,0:T(8,128)} %get-tuple-element.12), channel_id=1, source_target_pairs={{0,3},{1,0},{2,1},{3,2},{4,7},{5,4},{6,5},{7,6},{8,11},{9,8},{10,9... | collective-permute-start | bytes 98312 | tf_op jit(solution)/shard_map/ppermute | solution.py:18
  22.6 6.8 %collective-permute-start.1 = (f32[2,64,64]{2,1,0:T(8,128)}, f32[2,64,64]{2,1,0:T(8,128)S(1)}, u32[]{:S(2)}, u32[]{:S(2)}) collective-permute-start(f32[2,64,64]{2,1,0:T(8,128)} %get-tuple-element.11), channel_id=1, source_target_pairs={{0,2},{1,3},{2,0},{3,1},{4,6},{5,7},{6,4},{7,5},{8,10},{9,11},{10,... | collective-permute-start | bytes 98312 | tf_op jit(solution)/shard_map/ppermute | solution.py:18
  22.6 6.8 %collective-permute-start = (f32[2,64,64]{2,1,0:T(8,128)}, f32[2,64,64]{2,1,0:T(8,128)S(1)}, u32[]{:S(2)}, u32[]{:S(2)}) collective-permute-start(f32[2,64,64]{2,1,0:T(8,128)} %get-tuple-element.10), channel_id=1, source_target_pairs={{0,1},{1,2},{2,3},{3,0},{4,5},{5,6},{6,7},{7,4},{8,9},{9,10},{10,1... | collective-permute-start | bytes 98312 | tf_op jit(solution)/shard_map/ppermute | solution.py:18
  43.0 10.3 %all-to-all-start.1 = ((f32[8,16,512]{2,1,0:T(8,128)}), f32[8,16,512]{2,1,0:T(8,128)S(1)}, u32[]{:S(2)}, u32[]{:S(2)}) async-start(f32[8,16,512]{2,1,0:T(8,128)} %broadcast_in_dim.15), calls=%async_computation.1 | async-start | bytes 524288 | tf_op jit(solution)/shard_map/all_to_all | solution.py:44
  59.4 3.8 %collective-permute-start.5 = (f32[16,256]{1,0:T(8,128)S(1)}, f32[16,256]{1,0:T(8,128)S(1)}, u32[]{:S(2)}, u32[]{:S(2)}) collective-permute-start(f32[16,256]{1,0:T(8,128)S(1)} %get-tuple-element.14), channel_id=1, source_target_pairs={{0,3},{1,0},{2,1},{3,2},{4,7},{5,4},{6,5},{7,6},{8,11},{9,8},{10,9... | collective-permute-start | bytes 49160 | tf_op jit(solution)/shard_map/ppermute | solution.py:18
  61.3 4.6 %collective-permute-start.4 = (f32[16,256]{1,0:T(8,128)S(1)}, f32[16,256]{1,0:T(8,128)S(1)}, u32[]{:S(2)}, u32[]{:S(2)}) collective-permute-start(f32[16,256]{1,0:T(8,128)S(1)} %get-tuple-element.15), channel_id=1, source_target_pairs={{0,2},{1,3},{2,0},{3,1},{4,6},{5,7},{6,4},{7,5},{8,10},{9,11},{10,... | collective-permute-start | bytes 49160 | tf_op jit(solution)/shard_map/ppermute | solution.py:18
  61.3 5.5 %collective-permute-start.3 = (f32[16,256]{1,0:T(8,128)S(1)}, f32[16,256]{1,0:T(8,128)S(1)}, u32[]{:S(2)}, u32[]{:S(2)}) collective-permute-start(f32[16,256]{1,0:T(8,128)S(1)} %get-tuple-element.13), channel_id=1, source_target_pairs={{0,1},{1,2},{2,3},{3,0},{4,5},{5,6},{6,7},{7,4},{8,9},{9,10},{10,1... | collective-permute-start | bytes 49160 | tf_op jit(solution)/shard_map/ppermute | solution.py:18

commit v13 on v8

--- a/solution.py
+++ b/solution.py
@@ -44,29 +44,48 @@
     return lax.all_to_all(copies, axis, 0, 0, tiled=True)
 
 
-def gradient_kernel(lengths_ref, act_ref, cot_ref, win_ref, wout_ref, out_ref):
+def gradient_kernel(lengths_ref, act_ref, cot_ref, win_ref, wout_ref, out_ref, left_acc, right_acc):
+    chunk = pl.program_id(1)
     tokens = act_ref.shape[1]
-    offset = lax.axis_index("mp") * tokens
     nt = (((1,), (1,)), ((), ()))
     for example in range(act_ref.shape[0]):
         left = lax.dot_general(
             act_ref[example], win_ref[...], nt, preferred_element_type=jnp.float32
-        ).astype(jnp.bfloat16)
+        )
         right = lax.dot_general(
             cot_ref[example], wout_ref[...], nt, preferred_element_type=jnp.float32
         )
-        rows = lax.broadcasted_iota(jnp.int32, right.shape, 0)
-        right = jnp.where(rows < lengths_ref[example] - offset, right, 0.0).astype(jnp.bfloat16)
-        out_ref[example] = lax.dot_general(
-            right, left, (((0,), (0,)), ((), ())), preferred_element_type=jnp.float32
-        )
+
+        @pl.when(chunk == 0)
+        def _():
+            left_acc[example] = left
+            right_acc[example] = right
+
+        @pl.when(chunk > 0)
+        def _():
+            left_acc[example] += left
+            right_acc[example] += right
+
+    @pl.when(chunk == pl.num_programs(1) - 1)
+    def _():
+        offset = lax.axis_index("mp") * tokens
+        for example in range(act_ref.shape[0]):
+            left = left_acc[example].astype(jnp.bfloat16)
+            right = right_acc[example]
+            rows = lax.broadcasted_iota(jnp.int32, right.shape, 0)
+            right = jnp.where(rows < lengths_ref[example] - offset, right, 0.0).astype(jnp.bfloat16)
+            out_ref[example] = lax.dot_general(
+                right, left, (((0,), (0,)), ((), ())), preferred_element_type=jnp.float32
+            )
 
 
 def layer_gradients(activations, cotangents, lengths, project_in, project_out):
     layers, examples, tokens, width = activations.shape
     factor = project_in.shape[1]
-    data = pl.BlockSpec((None, examples, tokens, width), lambda l, lens: (l, 0, 0, 0))
-    weights = pl.BlockSpec((None, factor, width), lambda l, lens: (l, 0, 0))
+    chunks = 4 if width % 512 == 0 else 1
+    part = width // chunks
+    data = pl.BlockSpec((None, examples, tokens, part), lambda l, k, lens: (l, 0, 0, k))
+    weights = pl.BlockSpec((None, factor, part), lambda l, k, lens: (l, 0, k))
     flops = 4 * layers * examples * tokens * width * factor
     moved = 2 * (activations.size + cotangents.size + project_in.size + project_out.size)
     return pl.pallas_call(
@@ -74,9 +93,15 @@
         out_shape=jax.ShapeDtypeStruct((layers, examples, factor, factor), jnp.float32),
         grid_spec=pltpu.PrefetchScalarGridSpec(
             num_scalar_prefetch=1,
-            grid=(layers,),
+            grid=(layers, chunks),
             in_specs=[data, data, weights, weights],
-            out_specs=pl.BlockSpec((None, examples, factor, factor), lambda l, lens: (l, 0, 0, 0)),
+            out_specs=pl.BlockSpec(
+                (None, examples, factor, factor), lambda l, k, lens: (l, 0, 0, 0)
+            ),
+            scratch_shapes=[
+                pltpu.VMEM((examples, tokens, factor), jnp.float32),
+                pltpu.VMEM((examples, tokens, factor), jnp.float32),
+            ],
         ),
         cost_estimate=pl.CostEstimate(flops=flops, transcendentals=0, bytes_accessed=moved),
     )(lengths, activations, cotangents, project_in, project_out)

time: 66.7 us -> 73.7 us (1.10)
  Pallas kernels: 16.9 us -> 23.6 us
    pallas_call x1, Pallas kernels: 16.9 us -> 23.6 us  [layer_gradients(): pl.pallas_call(gradient_kernel, out_shape=jax.ShapeDtypeStruct((layers, e...]
where the time goes in v13:
time: 73.7 us; the launch traced here: 73 us
  Pallas kernels  23.6 us (32%)
  starting transfers between devices  14.5 us (20%)
  waiting for transfers between devices  13.5 us (18%)
  blocking collectives  9.02 us (12%)
  matrix products  8.81 us (12%)
  local copies, waits for them, and re-layouts  1.9 us (3%)
  other arithmetic  1.54 us (2%)
    pallas_call x1, Pallas kernels, layer_gradients(): pl.pallas_call(gradient_kernel, out_shape=jax.ShapeDtypeStruct((layers, e...  23.6 us
    ppermute x6, starting transfers between devices, shifted(): return lax.ppermute(x, axis, [(i, (i + shift) % n) for i in range(n)])  11.1 us
    all_to_all x1, blocking collectives, all_gather_a2a(): return lax.all_to_all(copies, axis, 0, 0, tiled=True)  9.02 us
    all_to_all x1, waiting for transfers between devices, all_gather_a2a(): return lax.all_to_all(copies, axis, 0, 0, tiled=True)  6.81 us
    ppermute x6, waiting for transfers between devices, shifted(): return lax.ppermute(x, axis, [(i, (i + shift) % n) for i in range(n)])  6.68 us
    dot_general x1, matrix products, body_direct(): lax.dot_general(both_all, query_blocks, (((0, 2), (1, 2)), ((), ())), pre...  5.98 us
    all_to_all x1, starting transfers between devices, all_gather_a2a(): return lax.all_to_all(copies, axis, 0, 0, tiled=True)  3.41 us
    dot_general x1, matrix products, body_direct(): jnp.dot(grad_all, preconditioner, preferred_element_type=jnp.float32)  2.83 us
  transfers between devices with their start and end apart: 7, of which 7 were waited for; matrix products, arithmetic and copies ran while one was open for 0% of the time, Pallas kernels for 0%

profile of v13, /device:TPU:0, one launch (start us, length us, event | category | flops | bytes accessed | tf_op | source)
XLA Modules:
  0.0 73.0 jit_solution(15446692285861684801)
XLA Ops:
  0.0 23.6 %shard_map.73 = f32[4,2,64,64]{3,2,1,0:T(8,128)} custom-call(s32[2]{0:T(128)} %lengths_ref.1, bf16[4,2,256,4096]{3,2,1,0:T(8,128)(2,1)} %act_ref.1, bf16[4,2,256,4096]{3,2,1,0:T(8,128)(2,1)} %cot_ref.1, bf16[4,64,4096]{2,1,0:T(8,128)(2,1)} %win_ref.1, bf16[4,64,4096]{2,1,0:T(8,128)(2,1)} %wout_ref.1), custom_call_target="tpu_custom_call" | custom-call | flops 2147483648 | bytes 37748736 | tf_op jit(solution)/shard_map/pallas_call | solution.py:91
  23.6 0.9 %constant_dynamic-slice_fusion.5 = (f32[1,2,64,64]{3,2,1,0:T(8,128)S(1)}, f32[1,2,64,64]{3,2,1,0:T(8,128)S(1)}, f32[1,2,64,64]{3,2,1,0:T(8,128)S(1)}) fusion(f32[4,2,64,64]{3,2,1,0:T(8,128)} %shard_map.73, s32[]{:T(128)S(6)} %select_n.47, s32[]{:T(128)S(6)} %select_n.51, s32[]{:T(128)S(6)} %select_n.49), kind=kLoop, calls=%fused_computation.16 | loop fusion | bytes 196620 | tf_op jit(solution)/shard_map/dynamic_slice | solution.py:27
  24.5 3.1 %collective-permute-start = (f32[1,2,64,64]{3,2,1,0:T(8,128)S(1)}, f32[1,2,64,64]{3,2,1,0:T(8,128)S(1)}, u32[]{:S(2)}, u32[]{:S(2)}) collective-permute-start(f32[1,2,64,64]{3,2,1,0:T(8,128)S(1)} %get-tuple-element.5), channel_id=1, source_target_pairs={{0,1},{1,2},{2,3},{3,0},{4,5},{5,6},{6,7},{7,4},{8,9},{9,10},{10,1... | collective-permute-start | bytes 98312 | tf_op jit(solution)/shard_map/ppermute | solution.py:18
  27.6 2.6 %collective-permute-start.1 = (f32[1,2,64,64]{3,2,1,0:T(8,128)S(1)}, f32[1,2,64,64]{3,2,1,0:T(8,128)S(1)}, u32[]{:S(2)}, u32[]{:S(2)}) collective-permute-start(f32[1,2,64,64]{3,2,1,0:T(8,128)S(1)} %get-tuple-element.7), channel_id=1, source_target_pairs={{0,2},{1,3},{2,0},{3,1},{4,6},{5,7},{6,4},{7,5},{8,10},{9,11},{10,... | collective-permute-start | bytes 98312 | tf_op jit(solution)/shard_map/ppermute | solution.py:18
  30.2 1.3 %collective-permute-start.2 = (f32[1,2,64,64]{3,2,1,0:T(8,128)S(1)}, f32[1,2,64,64]{3,2,1,0:T(8,128)S(1)}, u32[]{:S(2)}, u32[]{:S(2)}) collective-permute-start(f32[1,2,64,64]{3,2,1,0:T(8,128)S(1)} %get-tuple-element.6), channel_id=1, source_target_pairs={{0,3},{1,0},{2,1},{3,2},{4,7},{5,4},{6,5},{7,6},{8,11},{9,8},{10,9... | collective-permute-start | bytes 98312 | tf_op jit(solution)/shard_map/ppermute | solution.py:18
  31.5 0.5 collective-permute-done
  32.1 2.6 %collective-permute-done.1 = f32[1,2,64,64]{3,2,1,0:T(8,128)S(1)} collective-permute-done((f32[1,2,64,64]{3,2,1,0:T(8,128)S(1)}, f32[1,2,64,64]{3,2,1,0:T(8,128)S(1)}, u32[]{:S(2)}, u32[]{:S(2)}) %collective-permute-start.1) | collective-permute-done | bytes 32800 | tf_op jit(solution)/shard_map/ppermute | solution.py:18
  34.7 0.2 collective-permute-done.2
  34.9 0.9 %add_convert_fusion = bf16[1,2,64,64]{3,2,1,0:T(8,128)(2,1)S(1)} fusion(f32[1,2,64,64]{3,2,1,0:T(8,128)S(1)} %collective-permute-done.2, f32[1,2,64,64]{3,2,1,0:T(8,128)S(1)} %collective-permute-done.1, f32[1,2,64,64]{3,2,1,0:T(8,128)S(1)} %collective-permute-done, f32[4,2,64,64]{3,2,1,0:T(8,128)} %shard_map.73, s32[]{:T(128)S(6)} %select_n.45), kind=kLoop, calls=%fused_computation.9 | loop fusion | flops 32768 | bytes 147460 | tf_op jit(solution)/shard_map/convert_element_type | solution.py:162
  35.8 0.1 convert_element_type.20
  35.9 0.1 broadcast_in_dim.4
  35.9 9.0 %all_to_all.10 = bf16[8,2,4096]{2,1,0:T(2,128)(2,1)S(1)} all-to-all(bf16[8,2,4096]{2,1,0:T(2,128)(2,1)S(1)} %broadcast_in_dim.4), channel_id=1, replica_groups=mesh['dp'=8,'mp'=4] {'dp'}, dimensions={0} | all-to-all | bytes 262144 | tf_op jit(solution)/shard_map/all_to_all | solution.py:44
  45.0 0.1 reshape.13
  45.0 2.8 %fusion.10 = f32[16,512]{1,0:T(8,128)S(1)} fusion(bf16[16,4096]{1,0:T(8,128)(2,1)S(1)} %reshape.13, bf16[4096,512]{1,0:T(8,128)(2,1)} %param.12), kind=kOutput, calls=%fused_computation.18 | convolution fusion | flops 67108864 | bytes 4358144 | tf_op jit(solution)/shard_map/dot_general | solution.py:165
  47.8 0.7 %broadcast_in_dim.5 = f32[8,16,512]{2,1,0:T(8,128)} broadcast(f32[16,512]{1,0:T(8,128)S(1)} %fusion.10), dimensions={1,2} | broadcast | bytes 294912 | tf_op jit(solution)/shard_map/broadcast_in_dim | solution.py:43
  48.6 3.4 %all-to-all-start.1 = ((f32[8,16,512]{2,1,0:T(8,128)}), f32[8,16,512]{2,1,0:T(8,128)S(1)}, u32[]{:S(2)}, u32[]{:S(2)}) async-start(f32[8,16,512]{2,1,0:T(8,128)} %broadcast_in_dim.5), calls=%async_computation.1 | async-start | bytes 524288 | tf_op jit(solution)/shard_map/all_to_all | solution.py:44
  52.0 6.8 %all-to-all-done.1 = f32[8,16,512]{2,1,0:T(8,128)S(1)} async-done(((f32[8,16,512]{2,1,0:T(8,128)}), f32[8,16,512]{2,1,0:T(8,128)S(1)}, u32[]{:S(2)}, u32[]{:S(2)}) %all-to-all-start.1) | async-done | bytes 262176 | tf_op jit(solution)/shard_map/all_to_all | solution.py:44
  58.9 6.0 %fusion.3 = f32[32,1024]{1,0:T(8,128)S(1)} fusion(bf16[128,8,8,512]{3,2,1,0:T(8,128)(2,1)} %bitcast.12, bf16[8,16,512]{2,1,0:T(8,128)(2,1)S(1)} %subtract_convert_fusion, bf16[8,16,512]{2,1,0:T(8,128)(2,1)S(1)} %convert_element_type.21), kind=kOutput, calls=%fused_computation.3 | convolution fusion | flops 268959744 | bytes 8781824 | tf_op jit(solution)/shard_map/dot_general | solution.py:170
  64.9 1.6 %collective-permute-start.3 = (f32[16,256]{1,0:T(8,128)S(1)}, f32[16,256]{1,0:T(8,128)S(1)}, u32[]{:S(2)}, u32[]{:S(2)}) collective-permute-start(f32[16,256]{1,0:T(8,128)S(1)} %get-tuple-element.8), channel_id=1, source_target_pairs={{0,1},{1,2},{2,3},{3,0},{4,5},{5,6},{6,7},{7,4},{8,9},{9,10},{10,1... | collective-permute-start | bytes 49160 | tf_op jit(solution)/shard_map/ppermute | solution.py:18
  66.6 2.0 %collective-permute-start.4 = (f32[16,256]{1,0:T(8,128)S(1)}, f32[16,256]{1,0:T(8,128)S(1)}, u32[]{:S(2)}, u32[]{:S(2)}) collective-permute-start(f32[16,256]{1,0:T(8,128)S(1)} %get-tuple-element.10), channel_id=1, source_target_pairs={{0,2},{1,3},{2,0},{3,1},{4,6},{5,7},{6,4},{7,5},{8,10},{9,11},{10,... | collective-permute-start | bytes 49160 | tf_op jit(solution)/shard_map/ppermute | solution.py:18
  68.6 0.4 collective-permute-start.5
  69.0 1.6 %collective-permute-done.3 = f32[16,256]{1,0:T(8,128)S(1)} collective-permute-done((f32[16,256]{1,0:T(8,128)S(1)}, f32[16,256]{1,0:T(8,128)S(1)}, u32[]{:S(2)}, u32[]{:S(2)}) %collective-permute-start.3) | collective-permute-done | bytes 16416 | tf_op jit(solution)/shard_map/ppermute | solution.py:18
  70.6 0.6 collective-permute-done.4
  71.2 1.1 %collective-permute-done.5 = f32[16,256]{1,0:T(8,128)S(1)} collective-permute-done((f32[16,256]{1,0:T(8,128)S(1)}, f32[16,256]{1,0:T(8,128)S(1)}, u32[]{:S(2)}, u32[]{:S(2)}) %collective-permute-start.5) | collective-permute-done | bytes 16416 | tf_op jit(solution)/shard_map/ppermute | solution.py:18
  72.3 0.6 add_add_fusion
  (4 shorter events, 0.1 us)
Async XLA Ops:
  24.5 7.6 %collective-permute-start = (f32[1,2,64,64]{3,2,1,0:T(8,128)S(1)}, f32[1,2,64,64]{3,2,1,0:T(8,128)S(1)}, u32[]{:S(2)}, u32[]{:S(2)}) collective-permute-start(f32[1,2,64,64]{3,2,1,0:T(8,128)S(1)} %get-tuple-element.5), channel_id=1, source_target_pairs={{0,1},{1,2},{2,3},{3,0},{4,5},{5,6},{6,7},{7,4},{8,9},{9,10},{10,1... | collective-permute-start | bytes 98312 | tf_op jit(solution)/shard_map/ppermute | solution.py:18
  27.6 7.1 %collective-permute-start.1 = (f32[1,2,64,64]{3,2,1,0:T(8,128)S(1)}, f32[1,2,64,64]{3,2,1,0:T(8,128)S(1)}, u32[]{:S(2)}, u32[]{:S(2)}) collective-permute-start(f32[1,2,64,64]{3,2,1,0:T(8,128)S(1)} %get-tuple-element.7), channel_id=1, source_target_pairs={{0,2},{1,3},{2,0},{3,1},{4,6},{5,7},{6,4},{7,5},{8,10},{9,11},{10,... | collective-permute-start | bytes 98312 | tf_op jit(solution)/shard_map/ppermute | solution.py:18
  30.2 4.7 %collective-permute-start.2 = (f32[1,2,64,64]{3,2,1,0:T(8,128)S(1)}, f32[1,2,64,64]{3,2,1,0:T(8,128)S(1)}, u32[]{:S(2)}, u32[]{:S(2)}) collective-permute-start(f32[1,2,64,64]{3,2,1,0:T(8,128)S(1)} %get-tuple-element.6), channel_id=1, source_target_pairs={{0,3},{1,0},{2,1},{3,2},{4,7},{5,4},{6,5},{7,6},{8,11},{9,8},{10,9... | collective-permute-start | bytes 98312 | tf_op jit(solution)/shard_map/ppermute | solution.py:18
  48.6 10.3 %all-to-all-start.1 = ((f32[8,16,512]{2,1,0:T(8,128)}), f32[8,16,512]{2,1,0:T(8,128)S(1)}, u32[]{:S(2)}, u32[]{:S(2)}) async-start(f32[8,16,512]{2,1,0:T(8,128)} %broadcast_in_dim.5), calls=%async_computation.1 | async-start | bytes 524288 | tf_op jit(solution)/shard_map/all_to_all | solution.py:44
  64.9 5.7 %collective-permute-start.3 = (f32[16,256]{1,0:T(8,128)S(1)}, f32[16,256]{1,0:T(8,128)S(1)}, u32[]{:S(2)}, u32[]{:S(2)}) collective-permute-start(f32[16,256]{1,0:T(8,128)S(1)} %get-tuple-element.8), channel_id=1, source_target_pairs={{0,1},{1,2},{2,3},{3,0},{4,5},{5,6},{6,7},{7,4},{8,9},{9,10},{10,1... | collective-permute-start | bytes 49160 | tf_op jit(solution)/shard_map/ppermute | solution.py:18
  66.6 4.6 %collective-permute-start.4 = (f32[16,256]{1,0:T(8,128)S(1)}, f32[16,256]{1,0:T(8,128)S(1)}, u32[]{:S(2)}, u32[]{:S(2)}) collective-permute-start(f32[16,256]{1,0:T(8,128)S(1)} %get-tuple-element.10), channel_id=1, source_target_pairs={{0,2},{1,3},{2,0},{3,1},{4,6},{5,7},{6,4},{7,5},{8,10},{9,11},{10,... | collective-permute-start | bytes 49160 | tf_op jit(solution)/shard_map/ppermute | solution.py:18
  68.6 3.7 %collective-permute-start.5 = (f32[16,256]{1,0:T(8,128)S(1)}, f32[16,256]{1,0:T(8,128)S(1)}, u32[]{:S(2)}, u32[]{:S(2)}) collective-permute-start(f32[16,256]{1,0:T(8,128)S(1)} %get-tuple-element.9), channel_id=1, source_target_pairs={{0,3},{1,0},{2,1},{3,2},{4,7},{5,4},{6,5},{7,6},{8,11},{9,8},{10,9... | collective-permute-start | bytes 49160 | tf_op jit(solution)/shard_map/ppermute | solution.py:18

commit v14 on v8

--- a/solution.py
+++ b/solution.py
@@ -133,7 +133,7 @@
     width_dp = lax.axis_size("dp")
     mp_place = lax.axis_index("mp")
     partial_grad = layer_gradients(activations, cotangents, lengths, project_in, project_out)
-    grad_mine = reduce_scatter_direct(partial_grad, "mp", 0)[0]
+    grad_mine = jnp.sum(lax.all_to_all(partial_grad, "mp", 0, 0, tiled=True), axis=0)
     grad_mine = grad_mine.astype(jnp.bfloat16).reshape(grad_mine.shape[0], block_size)
     grad_all = all_gather_a2a(grad_mine, "dp")
     grad_all = grad_all.reshape(-1, grad_all.shape[-1])

time: 66.7 us -> 70.3 us (1.054)
  blocking collectives: 9.01 us -> 21.2 us
  starting transfers between devices: 14.5 us -> 6.25 us
  waiting for transfers between devices: 13.5 us -> 12.1 us
  local copies, waits for them, and re-layouts: 1.9 us -> 2.8 us
    all_to_all x0 -> x1, blocking collectives: none -> 12.2 us  [body_direct(): lax.all_to_all(partial_grad, 'mp', 0, 0, tiled=True)]
    ppermute x6 -> x3, starting transfers between devices: 11.1 us -> 2.84 us  [shifted(): return lax.ppermute(x, axis, [(i, (i + shift) % n) for i in range(n)])]
    ppermute x6 -> x3, waiting for transfers between devices: 6.68 us -> 5.32 us  [shifted(): return lax.ppermute(x, axis, [(i, (i + shift) % n) for i in range(n)])]
    unnamed x0 -> x2, local copies, waits for them, and re-layouts: none -> 1.31 us
    all_to_all x0 -> x1, other arithmetic: none -> 0.98 us  [body_direct(): lax.all_to_all(partial_grad, 'mp', 0, 0, tiled=True)]
    dynamic_slice x2 -> x1, local copies, waits for them, and re-layouts: 0.93 us -> 0.01 us  [reduce_scatter_direct(): piece = lax.dynamic_slice_in_dim(x, (me + shift) % n * width, width, dim)]
    convert_element_type x1 -> x0, other arithmetic: 0.86 us -> none  [body_direct(): grad_mine.astype(jnp.bfloat16).reshape(grad_mine.shape[0], block_size)]
  transfers between devices with their start and end apart: 7 -> 4, of which waited for: 7 -> 4; matrix products, arithmetic and copies ran while one was open for 0% -> 0% of each run, Pallas kernels for 0% -> 0%
where the time goes in v14:
time: 70.3 us; the launch traced here: 69.9 us
  blocking collectives  21.2 us (30%)
  Pallas kernels  16.9 us (24%)
  waiting for transfers between devices  12.1 us (17%)
  matrix products  8.81 us (13%)
  starting transfers between devices  6.25 us (9%)
  local copies, waits for them, and re-layouts  2.8 us (4%)
  other arithmetic  1.69 us (2%)
    pallas_call x1, Pallas kernels, layer_gradients(): pl.pallas_call(gradient_kernel, out_shape=jax.ShapeDtypeStruct((layers, e...  16.9 us
    all_to_all x1, blocking collectives, body_direct(): lax.all_to_all(partial_grad, 'mp', 0, 0, tiled=True)  12.2 us
    all_to_all x1, blocking collectives, all_gather_a2a(): return lax.all_to_all(copies, axis, 0, 0, tiled=True)  9.02 us
    all_to_all x1, waiting for transfers between devices, all_gather_a2a(): return lax.all_to_all(copies, axis, 0, 0, tiled=True)  6.79 us
    dot_general x1, matrix products, body_direct(): lax.dot_general(both_all, query_blocks, (((0, 2), (1, 2)), ((), ())), pre...  5.98 us
    ppermute x3, waiting for transfers between devices, shifted(): return lax.ppermute(x, axis, [(i, (i + shift) % n) for i in range(n)])  5.32 us
    all_to_all x1, starting transfers between devices, all_gather_a2a(): return lax.all_to_all(copies, axis, 0, 0, tiled=True)  3.41 us
    ppermute x3, starting transfers between devices, shifted(): return lax.ppermute(x, axis, [(i, (i + shift) % n) for i in range(n)])  2.84 us
  transfers between devices with their start and end apart: 4, of which 4 were waited for; matrix products, arithmetic and copies ran while one was open for 0% of the time, Pallas kernels for 0%

profile of v14, /device:TPU:0, one launch (start us, length us, event | category | flops | bytes accessed | tf_op | source)
XLA Modules:
  0.0 69.9 jit_solution(14032433611214270381)
XLA Ops:
  0.0 16.9 %shard_map.73 = f32[4,2,64,64]{3,2,1,0:T(8,128)} custom-call(s32[2]{0:T(128)} %lengths_ref.1, bf16[4,2,256,4096]{3,2,1,0:T(8,128)(2,1)} %act_ref.1, bf16[4,2,256,4096]{3,2,1,0:T(8,128)(2,1)} %cot_ref.1, bf16[4,64,4096]{2,1,0:T(8,128)(2,1)} %win_ref.1, bf16[4,64,4096]{2,1,0:T(8,128)(2,1)} %wout_ref.1), custom_call_target="tpu_custom_call" | custom-call | flops 2147483648 | bytes 37748736 | tf_op jit(solution)/shard_map/pallas_call | solution.py:72
  16.9 1.1 %reshape.16 = f32[4,1,8192]{2,1,0:T(1,128)S(1)} reshape(f32[4,2,64,64]{3,2,1,0:T(8,128)} %shard_map.73) | data formatting | bytes 262144
  18.0 12.2 %all_to_all.15 = f32[4,1,8192]{2,1,0:T(1,128)S(1)} all-to-all(f32[4,1,8192]{2,1,0:T(1,128)S(1)} %reshape.16), channel_id=1, replica_groups=mesh['dp'=8,'mp'=4] {'mp'}, dimensions={0} | all-to-all | bytes 262144 | tf_op jit(solution)/shard_map/all_to_all | solution.py:136
  30.3 0.5 broadcast.4
  30.8 1.0 %reduce = f32[4,8192]{1,0:T(4,128)S(1)} reduce(f32[4,1,8192]{2,1,0:T(1,128)S(1)} %all_to_all.15, f32[]{:T(128)} %broadcast.4), dimensions={1}, to_apply=%all_to_all.9.reduce_sub_computation | reduce | bytes 262148 | tf_op jit(solution)/shard_map/all_to_all | solution.py:136
  31.8 0.2 reshape.17
  32.0 0.1 convert_element_type.20
  32.1 0.1 broadcast_in_dim.4
  32.1 9.0 %all_to_all.16 = bf16[8,2,4096]{2,1,0:T(2,128)(2,1)S(1)} all-to-all(bf16[8,2,4096]{2,1,0:T(2,128)(2,1)S(1)} %broadcast_in_dim.4), channel_id=1, replica_groups=mesh['dp'=8,'mp'=4] {'dp'}, dimensions={0} | all-to-all | bytes 262144 | tf_op jit(solution)/shard_map/all_to_all | solution.py:44
  41.2 0.1 reshape.13
  41.2 2.8 %fusion.10 = f32[16,512]{1,0:T(8,128)S(1)} fusion(bf16[16,4096]{1,0:T(8,128)(2,1)S(1)} %reshape.13, bf16[4096,512]{1,0:T(8,128)(2,1)} %param.12), kind=kOutput, calls=%fused_computation.14 | convolution fusion | flops 67108864 | bytes 4358144 | tf_op jit(solution)/shard_map/dot_general | solution.py:140
  44.1 0.7 %broadcast_in_dim.5 = f32[8,16,512]{2,1,0:T(8,128)} broadcast(f32[16,512]{1,0:T(8,128)S(1)} %fusion.10), dimensions={1,2} | broadcast | bytes 294912 | tf_op jit(solution)/shard_map/broadcast_in_dim | solution.py:43
  44.8 3.4 %all-to-all-start.2 = ((f32[8,16,512]{2,1,0:T(8,128)}), f32[8,16,512]{2,1,0:T(8,128)S(1)}, u32[]{:S(2)}, u32[]{:S(2)}) async-start(f32[8,16,512]{2,1,0:T(8,128)} %broadcast_in_dim.5), calls=%async_computation.2 | async-start | bytes 524288 | tf_op jit(solution)/shard_map/all_to_all | solution.py:44
  48.3 6.8 %all-to-all-done.2 = f32[8,16,512]{2,1,0:T(8,128)S(1)} async-done(((f32[8,16,512]{2,1,0:T(8,128)}), f32[8,16,512]{2,1,0:T(8,128)S(1)}, u32[]{:S(2)}, u32[]{:S(2)}) %all-to-all-start.2) | async-done | bytes 262176 | tf_op jit(solution)/shard_map/all_to_all | solution.py:44
  55.1 6.0 %fusion.3 = f32[32,1024]{1,0:T(8,128)S(1)} fusion(bf16[128,8,8,512]{3,2,1,0:T(8,128)(2,1)} %bitcast.10, bf16[8,16,512]{2,1,0:T(8,128)(2,1)S(1)} %subtract_convert_fusion, bf16[8,16,512]{2,1,0:T(8,128)(2,1)S(1)} %convert_element_type.21), kind=kOutput, calls=%fused_computation.3 | convolution fusion | flops 268959744 | bytes 8781824 | tf_op jit(solution)/shard_map/dot_general | solution.py:145
  61.1 1.5 %collective-permute-start.2 = (f32[16,256]{1,0:T(8,128)S(1)}, f32[16,256]{1,0:T(8,128)S(1)}, u32[]{:S(2)}, u32[]{:S(2)}) collective-permute-start(f32[16,256]{1,0:T(8,128)S(1)} %get-tuple-element.6), channel_id=1, source_target_pairs={{0,3},{1,0},{2,1},{3,2},{4,7},{5,4},{6,5},{7,6},{8,11},{9,8},{10,9... | collective-permute-start | bytes 49160 | tf_op jit(solution)/shard_map/ppermute | solution.py:18
  62.6 1.1 %collective-permute-start.1 = (f32[16,256]{1,0:T(8,128)S(1)}, f32[16,256]{1,0:T(8,128)S(1)}, u32[]{:S(2)}, u32[]{:S(2)}) collective-permute-start(f32[16,256]{1,0:T(8,128)S(1)} %get-tuple-element.7), channel_id=1, source_target_pairs={{0,2},{1,3},{2,0},{3,1},{4,6},{5,7},{6,4},{7,5},{8,10},{9,11},{10,... | collective-permute-start | bytes 49160 | tf_op jit(solution)/shard_map/ppermute | solution.py:18
  63.8 0.2 collective-permute-start
  64.0 1.0 %collective-permute-done.2 = f32[16,256]{1,0:T(8,128)S(1)} collective-permute-done((f32[16,256]{1,0:T(8,128)S(1)}, f32[16,256]{1,0:T(8,128)S(1)}, u32[]{:S(2)}, u32[]{:S(2)}) %collective-permute-start.2) | collective-permute-done | bytes 16416 | tf_op jit(solution)/shard_map/ppermute | solution.py:18
  64.9 2.5 %collective-permute-done.1 = f32[16,256]{1,0:T(8,128)S(1)} collective-permute-done((f32[16,256]{1,0:T(8,128)S(1)}, f32[16,256]{1,0:T(8,128)S(1)}, u32[]{:S(2)}, u32[]{:S(2)}) %collective-permute-start.1) | collective-permute-done | bytes 16416 | tf_op jit(solution)/shard_map/ppermute | solution.py:18
  67.5 1.8 %collective-permute-done = f32[16,256]{1,0:T(8,128)S(1)} collective-permute-done((f32[16,256]{1,0:T(8,128)S(1)}, f32[16,256]{1,0:T(8,128)S(1)}, u32[]{:S(2)}, u32[]{:S(2)}) %collective-permute-start) | collective-permute-done | bytes 16416 | tf_op jit(solution)/shard_map/ppermute | solution.py:18
  69.3 0.6 add_add_fusion
  (5 shorter events, 0.1 us)
Async XLA Ops:
  44.8 10.3 %all-to-all-start.2 = ((f32[8,16,512]{2,1,0:T(8,128)}), f32[8,16,512]{2,1,0:T(8,128)S(1)}, u32[]{:S(2)}, u32[]{:S(2)}) async-start(f32[8,16,512]{2,1,0:T(8,128)} %broadcast_in_dim.5), calls=%async_computation.2 | async-start | bytes 524288 | tf_op jit(solution)/shard_map/all_to_all | solution.py:44
  61.1 3.8 %collective-permute-start.2 = (f32[16,256]{1,0:T(8,128)S(1)}, f32[16,256]{1,0:T(8,128)S(1)}, u32[]{:S(2)}, u32[]{:S(2)}) collective-permute-start(f32[16,256]{1,0:T(8,128)S(1)} %get-tuple-element.6), channel_id=1, source_target_pairs={{0,3},{1,0},{2,1},{3,2},{4,7},{5,4},{6,5},{7,6},{8,11},{9,8},{10,9... | collective-permute-start | bytes 49160 | tf_op jit(solution)/shard_map/ppermute | solution.py:18
  62.6 4.8 %collective-permute-start.1 = (f32[16,256]{1,0:T(8,128)S(1)}, f32[16,256]{1,0:T(8,128)S(1)}, u32[]{:S(2)}, u32[]{:S(2)}) collective-permute-start(f32[16,256]{1,0:T(8,128)S(1)} %get-tuple-element.7), channel_id=1, source_target_pairs={{0,2},{1,3},{2,0},{3,1},{4,6},{5,7},{6,4},{7,5},{8,10},{9,11},{10,... | collective-permute-start | bytes 49160 | tf_op jit(solution)/shard_map/ppermute | solution.py:18
  63.8 5.5 %collective-permute-start = (f32[16,256]{1,0:T(8,128)S(1)}, f32[16,256]{1,0:T(8,128)S(1)}, u32[]{:S(2)}, u32[]{:S(2)}) collective-permute-start(f32[16,256]{1,0:T(8,128)S(1)} %get-tuple-element.5), channel_id=1, source_target_pairs={{0,1},{1,2},{2,3},{3,0},{4,5},{5,6},{6,7},{7,4},{8,9},{9,10},{10,1... | collective-permute-start | bytes 49160 | tf_op jit(solution)/shard_map/ppermute | solution.py:18

commit v15 on v8

--- a/solution.py
+++ b/solution.py
@@ -45,20 +45,24 @@
 
 
 def gradient_kernel(lengths_ref, act_ref, cot_ref, win_ref, wout_ref, out_ref):
-    tokens = act_ref.shape[1]
+    examples, tokens, width = act_ref.shape
     offset = lax.axis_index("mp") * tokens
     nt = (((1,), (1,)), ((), ()))
-    for example in range(act_ref.shape[0]):
-        left = lax.dot_general(
-            act_ref[example], win_ref[...], nt, preferred_element_type=jnp.float32
-        ).astype(jnp.bfloat16)
-        right = lax.dot_general(
-            cot_ref[example], wout_ref[...], nt, preferred_element_type=jnp.float32
-        )
-        rows = lax.broadcasted_iota(jnp.int32, right.shape, 0)
-        right = jnp.where(rows < lengths_ref[example] - offset, right, 0.0).astype(jnp.bfloat16)
+    left = lax.dot_general(
+        act_ref[...].reshape(examples * tokens, width), win_ref[...], nt,
+        preferred_element_type=jnp.float32,
+    ).astype(jnp.bfloat16)
+    right = lax.dot_general(
+        cot_ref[...].reshape(examples * tokens, width), wout_ref[...], nt,
+        preferred_element_type=jnp.float32,
+    )
+    rows = lax.broadcasted_iota(jnp.int32, (tokens, right.shape[1]), 0)
+    for example in range(examples):
+        rows_here = slice(example * tokens, (example + 1) * tokens)
+        right_here = jnp.where(rows < lengths_ref[example] - offset, right[rows_here], 0.0)
         out_ref[example] = lax.dot_general(
-            right, left, (((0,), (0,)), ((), ())), preferred_element_type=jnp.float32
+            right_here.astype(jnp.bfloat16), left[rows_here], (((0,), (0,)), ((), ())),
+            preferred_element_type=jnp.float32,
         )
 
 

time: 66.7 us -> 66.4 us (level)
  no operation moved by 1% of the time
where the time goes in v15:
time: 66.4 us; the launch traced here: 66 us
  Pallas kernels  16.6 us (25%)
  starting transfers between devices  14.5 us (22%)
  waiting for transfers between devices  13.5 us (20%)
  blocking collectives  9.01 us (14%)
  matrix products  8.81 us (13%)
  local copies, waits for them, and re-layouts  1.9 us (3%)
  other arithmetic  1.54 us (2%)
    pallas_call x1, Pallas kernels, layer_gradients(): pl.pallas_call(gradient_kernel, out_shape=jax.ShapeDtypeStruct((layers, e...  16.6 us
    ppermute x6, starting transfers between devices, shifted(): return lax.ppermute(x, axis, [(i, (i + shift) % n) for i in range(n)])  11.1 us
    all_to_all x1, blocking collectives, all_gather_a2a(): return lax.all_to_all(copies, axis, 0, 0, tiled=True)  9.01 us
    all_to_all x1, waiting for transfers between devices, all_gather_a2a(): return lax.all_to_all(copies, axis, 0, 0, tiled=True)  6.81 us
    ppermute x6, waiting for transfers between devices, shifted(): return lax.ppermute(x, axis, [(i, (i + shift) % n) for i in range(n)])  6.69 us
    dot_general x1, matrix products, body_direct(): lax.dot_general(both_all, query_blocks, (((0, 2), (1, 2)), ((), ())), pre...  5.98 us
    all_to_all x1, starting transfers between devices, all_gather_a2a(): return lax.all_to_all(copies, axis, 0, 0, tiled=True)  3.41 us
    dot_general x1, matrix products, body_direct(): jnp.dot(grad_all, preconditioner, preferred_element_type=jnp.float32)  2.83 us
  transfers between devices with their start and end apart: 7, of which 7 were waited for; matrix products, arithmetic and copies ran while one was open for 0% of the time, Pallas kernels for 0%

profile of v15, /device:TPU:0, one launch (start us, length us, event | category | flops | bytes accessed | tf_op | source)
XLA Modules:
  0.0 66.0 jit_solution(15403168569705611227)
XLA Ops:
  0.0 16.6 %shard_map.73 = f32[4,2,64,64]{3,2,1,0:T(8,128)} custom-call(s32[2]{0:T(128)} %lengths_ref.1, bf16[4,2,256,4096]{3,2,1,0:T(8,128)(2,1)} %act_ref.1, bf16[4,2,256,4096]{3,2,1,0:T(8,128)(2,1)} %cot_ref.1, bf16[4,64,4096]{2,1,0:T(8,128)(2,1)} %win_ref.1, bf16[4,64,4096]{2,1,0:T(8,128)(2,1)} %wout_ref.1), custom_call_target="tpu_custom_call" | custom-call | flops 2147483648 | bytes 37748736 | tf_op jit(solution)/shard_map/pallas_call | solution.py:76
  16.6 0.9 %constant_dynamic-slice_fusion.5 = (f32[1,2,64,64]{3,2,1,0:T(8,128)S(1)}, f32[1,2,64,64]{3,2,1,0:T(8,128)S(1)}, f32[1,2,64,64]{3,2,1,0:T(8,128)S(1)}) fusion(f32[4,2,64,64]{3,2,1,0:T(8,128)} %shard_map.73, s32[]{:T(128)S(6)} %select_n.47, s32[]{:T(128)S(6)} %select_n.51, s32[]{:T(128)S(6)} %select_n.49), kind=kLoop, calls=%fused_computation.16 | loop fusion | bytes 196620 | tf_op jit(solution)/shard_map/dynamic_slice | solution.py:27
  17.5 3.1 %collective-permute-start = (f32[1,2,64,64]{3,2,1,0:T(8,128)S(1)}, f32[1,2,64,64]{3,2,1,0:T(8,128)S(1)}, u32[]{:S(2)}, u32[]{:S(2)}) collective-permute-start(f32[1,2,64,64]{3,2,1,0:T(8,128)S(1)} %get-tuple-element.5), channel_id=1, source_target_pairs={{0,1},{1,2},{2,3},{3,0},{4,5},{5,6},{6,7},{7,4},{8,9},{9,10},{10,1... | collective-permute-start | bytes 98312 | tf_op jit(solution)/shard_map/ppermute | solution.py:18
  20.6 2.6 %collective-permute-start.1 = (f32[1,2,64,64]{3,2,1,0:T(8,128)S(1)}, f32[1,2,64,64]{3,2,1,0:T(8,128)S(1)}, u32[]{:S(2)}, u32[]{:S(2)}) collective-permute-start(f32[1,2,64,64]{3,2,1,0:T(8,128)S(1)} %get-tuple-element.7), channel_id=1, source_target_pairs={{0,2},{1,3},{2,0},{3,1},{4,6},{5,7},{6,4},{7,5},{8,10},{9,11},{10,... | collective-permute-start | bytes 98312 | tf_op jit(solution)/shard_map/ppermute | solution.py:18
  23.2 1.3 %collective-permute-start.2 = (f32[1,2,64,64]{3,2,1,0:T(8,128)S(1)}, f32[1,2,64,64]{3,2,1,0:T(8,128)S(1)}, u32[]{:S(2)}, u32[]{:S(2)}) collective-permute-start(f32[1,2,64,64]{3,2,1,0:T(8,128)S(1)} %get-tuple-element.6), channel_id=1, source_target_pairs={{0,3},{1,0},{2,1},{3,2},{4,7},{5,4},{6,5},{7,6},{8,11},{9,8},{10,9... | collective-permute-start | bytes 98312 | tf_op jit(solution)/shard_map/ppermute | solution.py:18
  24.6 0.5 collective-permute-done
  25.1 2.6 %collective-permute-done.1 = f32[1,2,64,64]{3,2,1,0:T(8,128)S(1)} collective-permute-done((f32[1,2,64,64]{3,2,1,0:T(8,128)S(1)}, f32[1,2,64,64]{3,2,1,0:T(8,128)S(1)}, u32[]{:S(2)}, u32[]{:S(2)}) %collective-permute-start.1) | collective-permute-done | bytes 32800 | tf_op jit(solution)/shard_map/ppermute | solution.py:18
  27.7 0.2 collective-permute-done.2
  27.9 0.9 %add_convert_fusion = bf16[1,2,64,64]{3,2,1,0:T(8,128)(2,1)S(1)} fusion(f32[1,2,64,64]{3,2,1,0:T(8,128)S(1)} %collective-permute-done.2, f32[1,2,64,64]{3,2,1,0:T(8,128)S(1)} %collective-permute-done.1, f32[1,2,64,64]{3,2,1,0:T(8,128)S(1)} %collective-permute-done, f32[4,2,64,64]{3,2,1,0:T(8,128)} %shard_map.73, s32[]{:T(128)S(6)} %select_n.45), kind=kLoop, calls=%fused_computation.9 | loop fusion | flops 32768 | bytes 147460 | tf_op jit(solution)/shard_map/convert_element_type | solution.py:141
  28.8 0.1 convert_element_type.20
  28.9 0.1 broadcast_in_dim.4
  29.0 9.0 %all_to_all.10 = bf16[8,2,4096]{2,1,0:T(2,128)(2,1)S(1)} all-to-all(bf16[8,2,4096]{2,1,0:T(2,128)(2,1)S(1)} %broadcast_in_dim.4), channel_id=1, replica_groups=mesh['dp'=8,'mp'=4] {'dp'}, dimensions={0} | all-to-all | bytes 262144 | tf_op jit(solution)/shard_map/all_to_all | solution.py:44
  38.0 0.1 reshape.13
  38.0 2.8 %fusion.10 = f32[16,512]{1,0:T(8,128)S(1)} fusion(bf16[16,4096]{1,0:T(8,128)(2,1)S(1)} %reshape.13, bf16[4096,512]{1,0:T(8,128)(2,1)} %param.12), kind=kOutput, calls=%fused_computation.18 | convolution fusion | flops 67108864 | bytes 4358144 | tf_op jit(solution)/shard_map/dot_general | solution.py:144
  40.9 0.7 %broadcast_in_dim.5 = f32[8,16,512]{2,1,0:T(8,128)} broadcast(f32[16,512]{1,0:T(8,128)S(1)} %fusion.10), dimensions={1,2} | broadcast | bytes 294912 | tf_op jit(solution)/shard_map/broadcast_in_dim | solution.py:43
  41.6 3.4 %all-to-all-start.1 = ((f32[8,16,512]{2,1,0:T(8,128)}), f32[8,16,512]{2,1,0:T(8,128)S(1)}, u32[]{:S(2)}, u32[]{:S(2)}) async-start(f32[8,16,512]{2,1,0:T(8,128)} %broadcast_in_dim.5), calls=%async_computation.1 | async-start | bytes 524288 | tf_op jit(solution)/shard_map/all_to_all | solution.py:44
  45.1 6.8 %all-to-all-done.1 = f32[8,16,512]{2,1,0:T(8,128)S(1)} async-done(((f32[8,16,512]{2,1,0:T(8,128)}), f32[8,16,512]{2,1,0:T(8,128)S(1)}, u32[]{:S(2)}, u32[]{:S(2)}) %all-to-all-start.1) | async-done | bytes 262176 | tf_op jit(solution)/shard_map/all_to_all | solution.py:44
  51.9 6.0 %fusion.3 = f32[32,1024]{1,0:T(8,128)S(1)} fusion(bf16[128,8,8,512]{3,2,1,0:T(8,128)(2,1)} %bitcast.12, bf16[8,16,512]{2,1,0:T(8,128)(2,1)S(1)} %subtract_convert_fusion, bf16[8,16,512]{2,1,0:T(8,128)(2,1)S(1)} %convert_element_type.21), kind=kOutput, calls=%fused_computation.3 | convolution fusion | flops 268959744 | bytes 8781824 | tf_op jit(solution)/shard_map/dot_general | solution.py:149
  58.0 1.6 %collective-permute-start.3 = (f32[16,256]{1,0:T(8,128)S(1)}, f32[16,256]{1,0:T(8,128)S(1)}, u32[]{:S(2)}, u32[]{:S(2)}) collective-permute-start(f32[16,256]{1,0:T(8,128)S(1)} %get-tuple-element.8), channel_id=1, source_target_pairs={{0,1},{1,2},{2,3},{3,0},{4,5},{5,6},{6,7},{7,4},{8,9},{9,10},{10,1... | collective-permute-start | bytes 49160 | tf_op jit(solution)/shard_map/ppermute | solution.py:18
  59.6 2.0 %collective-permute-start.4 = (f32[16,256]{1,0:T(8,128)S(1)}, f32[16,256]{1,0:T(8,128)S(1)}, u32[]{:S(2)}, u32[]{:S(2)}) collective-permute-start(f32[16,256]{1,0:T(8,128)S(1)} %get-tuple-element.10), channel_id=1, source_target_pairs={{0,2},{1,3},{2,0},{3,1},{4,6},{5,7},{6,4},{7,5},{8,10},{9,11},{10,... | collective-permute-start | bytes 49160 | tf_op jit(solution)/shard_map/ppermute | solution.py:18
  61.6 0.4 collective-permute-start.5
  62.0 1.6 %collective-permute-done.3 = f32[16,256]{1,0:T(8,128)S(1)} collective-permute-done((f32[16,256]{1,0:T(8,128)S(1)}, f32[16,256]{1,0:T(8,128)S(1)}, u32[]{:S(2)}, u32[]{:S(2)}) %collective-permute-start.3) | collective-permute-done | bytes 16416 | tf_op jit(solution)/shard_map/ppermute | solution.py:18
  63.6 0.6 collective-permute-done.4
  64.2 1.1 %collective-permute-done.5 = f32[16,256]{1,0:T(8,128)S(1)} collective-permute-done((f32[16,256]{1,0:T(8,128)S(1)}, f32[16,256]{1,0:T(8,128)S(1)}, u32[]{:S(2)}, u32[]{:S(2)}) %collective-permute-start.5) | collective-permute-done | bytes 16416 | tf_op jit(solution)/shard_map/ppermute | solution.py:18
  65.4 0.6 add_add_fusion
  (4 shorter events, 0.1 us)
Async XLA Ops:
  17.5 7.6 %collective-permute-start = (f32[1,2,64,64]{3,2,1,0:T(8,128)S(1)}, f32[1,2,64,64]{3,2,1,0:T(8,128)S(1)}, u32[]{:S(2)}, u32[]{:S(2)}) collective-permute-start(f32[1,2,64,64]{3,2,1,0:T(8,128)S(1)} %get-tuple-element.5), channel_id=1, source_target_pairs={{0,1},{1,2},{2,3},{3,0},{4,5},{5,6},{6,7},{7,4},{8,9},{9,10},{10,1... | collective-permute-start | bytes 98312 | tf_op jit(solution)/shard_map/ppermute | solution.py:18
  20.6 7.1 %collective-permute-start.1 = (f32[1,2,64,64]{3,2,1,0:T(8,128)S(1)}, f32[1,2,64,64]{3,2,1,0:T(8,128)S(1)}, u32[]{:S(2)}, u32[]{:S(2)}) collective-permute-start(f32[1,2,64,64]{3,2,1,0:T(8,128)S(1)} %get-tuple-element.7), channel_id=1, source_target_pairs={{0,2},{1,3},{2,0},{3,1},{4,6},{5,7},{6,4},{7,5},{8,10},{9,11},{10,... | collective-permute-start | bytes 98312 | tf_op jit(solution)/shard_map/ppermute | solution.py:18
  23.2 4.7 %collective-permute-start.2 = (f32[1,2,64,64]{3,2,1,0:T(8,128)S(1)}, f32[1,2,64,64]{3,2,1,0:T(8,128)S(1)}, u32[]{:S(2)}, u32[]{:S(2)}) collective-permute-start(f32[1,2,64,64]{3,2,1,0:T(8,128)S(1)} %get-tuple-element.6), channel_id=1, source_target_pairs={{0,3},{1,0},{2,1},{3,2},{4,7},{5,4},{6,5},{7,6},{8,11},{9,8},{10,9... | collective-permute-start | bytes 98312 | tf_op jit(solution)/shard_map/ppermute | solution.py:18
  41.6 10.3 %all-to-all-start.1 = ((f32[8,16,512]{2,1,0:T(8,128)}), f32[8,16,512]{2,1,0:T(8,128)S(1)}, u32[]{:S(2)}, u32[]{:S(2)}) async-start(f32[8,16,512]{2,1,0:T(8,128)} %broadcast_in_dim.5), calls=%async_computation.1 | async-start | bytes 524288 | tf_op jit(solution)/shard_map/all_to_all | solution.py:44
  58.0 5.7 %collective-permute-start.3 = (f32[16,256]{1,0:T(8,128)S(1)}, f32[16,256]{1,0:T(8,128)S(1)}, u32[]{:S(2)}, u32[]{:S(2)}) collective-permute-start(f32[16,256]{1,0:T(8,128)S(1)} %get-tuple-element.8), channel_id=1, source_target_pairs={{0,1},{1,2},{2,3},{3,0},{4,5},{5,6},{6,7},{7,4},{8,9},{9,10},{10,1... | collective-permute-start | bytes 49160 | tf_op jit(solution)/shard_map/ppermute | solution.py:18
  59.6 4.6 %collective-permute-start.4 = (f32[16,256]{1,0:T(8,128)S(1)}, f32[16,256]{1,0:T(8,128)S(1)}, u32[]{:S(2)}, u32[]{:S(2)}) collective-permute-start(f32[16,256]{1,0:T(8,128)S(1)} %get-tuple-element.10), channel_id=1, source_target_pairs={{0,2},{1,3},{2,0},{3,1},{4,6},{5,7},{6,4},{7,5},{8,10},{9,11},{10,... | collective-permute-start | bytes 49160 | tf_op jit(solution)/shard_map/ppermute | solution.py:18
  61.6 3.7 %collective-permute-start.5 = (f32[16,256]{1,0:T(8,128)S(1)}, f32[16,256]{1,0:T(8,128)S(1)}, u32[]{:S(2)}, u32[]{:S(2)}) collective-permute-start(f32[16,256]{1,0:T(8,128)S(1)} %get-tuple-element.9), channel_id=1, source_target_pairs={{0,3},{1,0},{2,1},{3,2},{4,7},{5,4},{6,5},{7,6},{8,11},{9,8},{10,9... | collective-permute-start | bytes 49160 | tf_op jit(solution)/shard_map/ppermute | solution.py:18

commit v16 on v15

--- a/solution.py
+++ b/solution.py
@@ -86,6 +86,47 @@
     )(lengths, activations, cotangents, project_in, project_out)
 
 
+def precondition_kernel(grad_ref, block_ref, out_ref, total_ref):
+    chunk = pl.program_id(0)
+    term = jnp.dot(grad_ref[...], block_ref[...], preferred_element_type=jnp.float32)
+
+    @pl.when(chunk == 0)
+    def _():
+        total_ref[...] = term
+
+    @pl.when(chunk > 0)
+    def _():
+        total_ref[...] += term
+
+    @pl.when(chunk == pl.num_programs(0) - 1)
+    def _():
+        for copy in range(out_ref.shape[0]):
+            out_ref[copy] = total_ref[...]
+
+
+def precondition(grad_all, preconditioner, copies):
+    rows, depth = grad_all.shape
+    width = preconditioner.shape[1]
+    chunks = 4 if depth % 512 == 0 else 1
+    part = depth // chunks
+    return pl.pallas_call(
+        precondition_kernel,
+        out_shape=jax.ShapeDtypeStruct((copies, rows, width), jnp.float32),
+        grid=(chunks,),
+        in_specs=[
+            pl.BlockSpec((rows, part), lambda k: (0, k)),
+            pl.BlockSpec((part, width), lambda k: (k, 0)),
+        ],
+        out_specs=pl.BlockSpec((copies, rows, width), lambda k: (0, 0, 0)),
+        scratch_shapes=[pltpu.VMEM((rows, width), jnp.float32)],
+        cost_estimate=pl.CostEstimate(
+            flops=2 * rows * depth * width,
+            transcendentals=0,
+            bytes_accessed=2 * (grad_all.size + preconditioner.size) + 4 * copies * rows * width,
+        ),
+    )(grad_all, preconditioner)
+
+
 def body_start(activations, cotangents, lengths, project_in, project_out, preconditioner, queries):
     width_mp = lax.axis_size("mp")
     layer_count = activations.shape[0]
@@ -141,8 +182,8 @@
     grad_mine = grad_mine.astype(jnp.bfloat16).reshape(grad_mine.shape[0], block_size)
     grad_all = all_gather_a2a(grad_mine, "dp")
     grad_all = grad_all.reshape(-1, grad_all.shape[-1])
-    pre_part = jnp.dot(grad_all, preconditioner, preferred_element_type=jnp.float32)
-    upper_grad, lower_grad = split_parts(all_gather_a2a(pre_part, "dp"))
+    copies = precondition(grad_all, preconditioner, width_dp)
+    upper_grad, lower_grad = split_parts(lax.all_to_all(copies, "dp", 0, 0, tiled=True))
     both_all = jnp.concatenate([upper_grad, lower_grad], axis=1)
     blocks, block = both_all.shape[0], both_all.shape[2]
     query_blocks = queries.reshape(queries.shape[0], blocks, block)

time: 66.4 us -> 67.6 us (1.018)
  Pallas kernels: 16.6 us -> 20.7 us
  matrix products: 8.81 us -> 5.98 us
    pallas_call x0 -> x1, Pallas kernels: none -> 4.12 us  [precondition(): pl.pallas_call(precondition_kernel, out_shape=jax.ShapeDtypeStruct((copie...]
    dot_general x1 -> x0, matrix products: 2.83 us -> none  [body_direct(): jnp.dot(grad_all, preconditioner, preferred_element_type=jnp.float32)]
    broadcast_in_dim x2 -> x1, local copies, waits for them, and re-layouts: 0.81 us -> 0.07 us  [all_gather_a2a(): copies = jnp.broadcast_to(x[None], (n,) + x.shape)]
where the time goes in v16:
time: 67.6 us; the launch traced here: 67.2 us
  Pallas kernels  20.7 us (31%)
  starting transfers between devices  14.5 us (21%)
  waiting for transfers between devices  13.5 us (20%)
  blocking collectives  9.01 us (13%)
  matrix products  5.98 us (9%)
  local copies, waits for them, and re-layouts  1.79 us (3%)
  other arithmetic  1.54 us (2%)
    pallas_call x1, Pallas kernels, layer_gradients(): pl.pallas_call(gradient_kernel, out_shape=jax.ShapeDtypeStruct((layers, e...  16.6 us
    ppermute x6, starting transfers between devices, shifted(): return lax.ppermute(x, axis, [(i, (i + shift) % n) for i in range(n)])  11.1 us
    all_to_all x1, blocking collectives, all_gather_a2a(): return lax.all_to_all(copies, axis, 0, 0, tiled=True)  9.01 us
    all_to_all x1, waiting for transfers between devices, body_direct(): lax.all_to_all(copies, 'dp', 0, 0, tiled=True)  6.81 us
    ppermute x6, waiting for transfers between devices, shifted(): return lax.ppermute(x, axis, [(i, (i + shift) % n) for i in range(n)])  6.69 us
    dot_general x1, matrix products, body_direct(): lax.dot_general(both_all, query_blocks, (((0, 2), (1, 2)), ((), ())), pre...  5.98 us
    pallas_call x1, Pallas kernels, precondition(): pl.pallas_call(precondition_kernel, out_shape=jax.ShapeDtypeStruct((copie...  4.12 us
    all_to_all x1, starting transfers between devices, body_direct(): lax.all_to_all(copies, 'dp', 0, 0, tiled=True)  3.41 us
  transfers between devices with their start and end apart: 7, of which 7 were waited for; matrix products, arithmetic and copies ran while one was open for 0% of the time, Pallas kernels for 0%

profile of v16, /device:TPU:0, one launch (start us, length us, event | category | flops | bytes accessed | tf_op | source)
XLA Modules:
  0.0 67.2 jit_solution(17748626626642460301)
XLA Ops:
  0.0 16.6 %shard_map.73 = f32[4,2,64,64]{3,2,1,0:T(8,128)} custom-call(s32[2]{0:T(128)} %lengths_ref.1, bf16[4,2,256,4096]{3,2,1,0:T(8,128)(2,1)} %act_ref.1, bf16[4,2,256,4096]{3,2,1,0:T(8,128)(2,1)} %cot_ref.1, bf16[4,64,4096]{2,1,0:T(8,128)(2,1)} %win_ref.1, bf16[4,64,4096]{2,1,0:T(8,128)(2,1)} %wout_ref.1), custom_call_target="tpu_custom_call" | custom-call | flops 2147483648 | bytes 37748736 | tf_op jit(solution)/shard_map/pallas_call | solution.py:76
  16.6 0.9 %constant_dynamic-slice_fusion.5 = (f32[1,2,64,64]{3,2,1,0:T(8,128)S(1)}, f32[1,2,64,64]{3,2,1,0:T(8,128)S(1)}, f32[1,2,64,64]{3,2,1,0:T(8,128)S(1)}) fusion(f32[4,2,64,64]{3,2,1,0:T(8,128)} %shard_map.73, s32[]{:T(128)S(6)} %select_n.47, s32[]{:T(128)S(6)} %select_n.51, s32[]{:T(128)S(6)} %select_n.49), kind=kLoop, calls=%fused_computation.16 | loop fusion | bytes 196620 | tf_op jit(solution)/shard_map/dynamic_slice | solution.py:27
  17.5 3.1 %collective-permute-start = (f32[1,2,64,64]{3,2,1,0:T(8,128)S(1)}, f32[1,2,64,64]{3,2,1,0:T(8,128)S(1)}, u32[]{:S(2)}, u32[]{:S(2)}) collective-permute-start(f32[1,2,64,64]{3,2,1,0:T(8,128)S(1)} %get-tuple-element.5), channel_id=1, source_target_pairs={{0,1},{1,2},{2,3},{3,0},{4,5},{5,6},{6,7},{7,4},{8,9},{9,10},{10,1... | collective-permute-start | bytes 98312 | tf_op jit(solution)/shard_map/ppermute | solution.py:18
  20.6 2.6 %collective-permute-start.1 = (f32[1,2,64,64]{3,2,1,0:T(8,128)S(1)}, f32[1,2,64,64]{3,2,1,0:T(8,128)S(1)}, u32[]{:S(2)}, u32[]{:S(2)}) collective-permute-start(f32[1,2,64,64]{3,2,1,0:T(8,128)S(1)} %get-tuple-element.7), channel_id=1, source_target_pairs={{0,2},{1,3},{2,0},{3,1},{4,6},{5,7},{6,4},{7,5},{8,10},{9,11},{10,... | collective-permute-start | bytes 98312 | tf_op jit(solution)/shard_map/ppermute | solution.py:18
  23.2 1.3 %collective-permute-start.2 = (f32[1,2,64,64]{3,2,1,0:T(8,128)S(1)}, f32[1,2,64,64]{3,2,1,0:T(8,128)S(1)}, u32[]{:S(2)}, u32[]{:S(2)}) collective-permute-start(f32[1,2,64,64]{3,2,1,0:T(8,128)S(1)} %get-tuple-element.6), channel_id=1, source_target_pairs={{0,3},{1,0},{2,1},{3,2},{4,7},{5,4},{6,5},{7,6},{8,11},{9,8},{10,9... | collective-permute-start | bytes 98312 | tf_op jit(solution)/shard_map/ppermute | solution.py:18
  24.6 0.5 collective-permute-done
  25.1 2.6 %collective-permute-done.1 = f32[1,2,64,64]{3,2,1,0:T(8,128)S(1)} collective-permute-done((f32[1,2,64,64]{3,2,1,0:T(8,128)S(1)}, f32[1,2,64,64]{3,2,1,0:T(8,128)S(1)}, u32[]{:S(2)}, u32[]{:S(2)}) %collective-permute-start.1) | collective-permute-done | bytes 32800 | tf_op jit(solution)/shard_map/ppermute | solution.py:18
  27.7 0.2 collective-permute-done.2
  27.9 0.9 %add_convert_fusion = bf16[1,2,64,64]{3,2,1,0:T(8,128)(2,1)S(1)} fusion(f32[1,2,64,64]{3,2,1,0:T(8,128)S(1)} %collective-permute-done.2, f32[1,2,64,64]{3,2,1,0:T(8,128)S(1)} %collective-permute-done.1, f32[1,2,64,64]{3,2,1,0:T(8,128)S(1)} %collective-permute-done, f32[4,2,64,64]{3,2,1,0:T(8,128)} %shard_map.73, s32[]{:T(128)S(6)} %select_n.45), kind=kLoop, calls=%fused_computation.9 | loop fusion | flops 32768 | bytes 147460 | tf_op jit(solution)/shard_map/convert_element_type | solution.py:182
  28.8 0.1 convert_element_type.20
  28.9 0.1 broadcast_in_dim.2
  29.0 9.0 %all_to_all.10 = bf16[8,2,4096]{2,1,0:T(2,128)(2,1)S(1)} all-to-all(bf16[8,2,4096]{2,1,0:T(2,128)(2,1)S(1)} %broadcast_in_dim.2), channel_id=1, replica_groups=mesh['dp'=8,'mp'=4] {'dp'}, dimensions={0} | all-to-all | bytes 262144 | tf_op jit(solution)/shard_map/all_to_all | solution.py:44
  38.0 0.7 %reshape.12.grad_ref = bf16[16,4096]{1,0:T(8,128)(2,1)} reshape(bf16[8,2,4096]{2,1,0:T(2,128)(2,1)S(1)} %all_to_all.10) | data formatting | bytes 262144 | tf_op jit(solution)/shard_map/reshape | solution.py:184
  38.7 4.1 %shard_map.74 = f32[8,16,512]{2,1,0:T(8,128)} custom-call(bf16[16,4096]{1,0:T(8,128)(2,1)} %reshape.12.grad_ref, bf16[4096,512]{1,0:T(8,128)(2,1)} %block_ref.1), custom_call_target="tpu_custom_call" | custom-call | flops 67108864 | bytes 4587520 | tf_op jit(solution)/shard_map/pallas_call | solution.py:112
  42.8 3.4 %all-to-all-start.1 = ((f32[8,16,512]{2,1,0:T(8,128)}), f32[8,16,512]{2,1,0:T(8,128)S(1)}, u32[]{:S(2)}, u32[]{:S(2)}) async-start(f32[8,16,512]{2,1,0:T(8,128)} %shard_map.74), calls=%async_computation.1 | async-start | bytes 524288 | tf_op jit(solution)/shard_map/all_to_all | solution.py:186
  46.2 6.8 %all-to-all-done.1 = f32[8,16,512]{2,1,0:T(8,128)S(1)} async-done(((f32[8,16,512]{2,1,0:T(8,128)}), f32[8,16,512]{2,1,0:T(8,128)S(1)}, u32[]{:S(2)}, u32[]{:S(2)}) %all-to-all-start.1) | async-done | bytes 262176 | tf_op jit(solution)/shard_map/all_to_all | solution.py:186
  53.1 6.0 %fusion.3 = f32[32,1024]{1,0:T(8,128)S(1)} fusion(bf16[128,8,8,512]{3,2,1,0:T(8,128)(2,1)} %bitcast.10, bf16[8,16,512]{2,1,0:T(8,128)(2,1)S(1)} %subtract_convert_fusion, bf16[8,16,512]{2,1,0:T(8,128)(2,1)S(1)} %convert_element_type.21), kind=kOutput, calls=%fused_computation.3 | convolution fusion | flops 268959744 | bytes 8781824 | tf_op jit(solution)/shard_map/dot_general | solution.py:190
  59.2 1.6 %collective-permute-start.3 = (f32[16,256]{1,0:T(8,128)S(1)}, f32[16,256]{1,0:T(8,128)S(1)}, u32[]{:S(2)}, u32[]{:S(2)}) collective-permute-start(f32[16,256]{1,0:T(8,128)S(1)} %get-tuple-element.8), channel_id=1, source_target_pairs={{0,1},{1,2},{2,3},{3,0},{4,5},{5,6},{6,7},{7,4},{8,9},{9,10},{10,1... | collective-permute-start | bytes 49160 | tf_op jit(solution)/shard_map/ppermute | solution.py:18
  60.8 2.0 %collective-permute-start.4 = (f32[16,256]{1,0:T(8,128)S(1)}, f32[16,256]{1,0:T(8,128)S(1)}, u32[]{:S(2)}, u32[]{:S(2)}) collective-permute-start(f32[16,256]{1,0:T(8,128)S(1)} %get-tuple-element.10), channel_id=1, source_target_pairs={{0,2},{1,3},{2,0},{3,1},{4,6},{5,7},{6,4},{7,5},{8,10},{9,11},{10,... | collective-permute-start | bytes 49160 | tf_op jit(solution)/shard_map/ppermute | solution.py:18
  62.8 0.4 collective-permute-start.5
  63.2 1.6 %collective-permute-done.3 = f32[16,256]{1,0:T(8,128)S(1)} collective-permute-done((f32[16,256]{1,0:T(8,128)S(1)}, f32[16,256]{1,0:T(8,128)S(1)}, u32[]{:S(2)}, u32[]{:S(2)}) %collective-permute-start.3) | collective-permute-done | bytes 16416 | tf_op jit(solution)/shard_map/ppermute | solution.py:18
  64.8 0.6 collective-permute-done.4
  65.4 1.1 %collective-permute-done.5 = f32[16,256]{1,0:T(8,128)S(1)} collective-permute-done((f32[16,256]{1,0:T(8,128)S(1)}, f32[16,256]{1,0:T(8,128)S(1)}, u32[]{:S(2)}, u32[]{:S(2)}) %collective-permute-start.5) | collective-permute-done | bytes 16416 | tf_op jit(solution)/shard_map/ppermute | solution.py:18
  66.6 0.6 add_add_fusion
  (4 shorter events, 0.1 us)
Async XLA Ops:
  17.5 7.6 %collective-permute-start = (f32[1,2,64,64]{3,2,1,0:T(8,128)S(1)}, f32[1,2,64,64]{3,2,1,0:T(8,128)S(1)}, u32[]{:S(2)}, u32[]{:S(2)}) collective-permute-start(f32[1,2,64,64]{3,2,1,0:T(8,128)S(1)} %get-tuple-element.5), channel_id=1, source_target_pairs={{0,1},{1,2},{2,3},{3,0},{4,5},{5,6},{6,7},{7,4},{8,9},{9,10},{10,1... | collective-permute-start | bytes 98312 | tf_op jit(solution)/shard_map/ppermute | solution.py:18
  20.6 7.1 %collective-permute-start.1 = (f32[1,2,64,64]{3,2,1,0:T(8,128)S(1)}, f32[1,2,64,64]{3,2,1,0:T(8,128)S(1)}, u32[]{:S(2)}, u32[]{:S(2)}) collective-permute-start(f32[1,2,64,64]{3,2,1,0:T(8,128)S(1)} %get-tuple-element.7), channel_id=1, source_target_pairs={{0,2},{1,3},{2,0},{3,1},{4,6},{5,7},{6,4},{7,5},{8,10},{9,11},{10,... | collective-permute-start | bytes 98312 | tf_op jit(solution)/shard_map/ppermute | solution.py:18
  23.2 4.7 %collective-permute-start.2 = (f32[1,2,64,64]{3,2,1,0:T(8,128)S(1)}, f32[1,2,64,64]{3,2,1,0:T(8,128)S(1)}, u32[]{:S(2)}, u32[]{:S(2)}) collective-permute-start(f32[1,2,64,64]{3,2,1,0:T(8,128)S(1)} %get-tuple-element.6), channel_id=1, source_target_pairs={{0,3},{1,0},{2,1},{3,2},{4,7},{5,4},{6,5},{7,6},{8,11},{9,8},{10,9... | collective-permute-start | bytes 98312 | tf_op jit(solution)/shard_map/ppermute | solution.py:18
  42.8 10.3 %all-to-all-start.1 = ((f32[8,16,512]{2,1,0:T(8,128)}), f32[8,16,512]{2,1,0:T(8,128)S(1)}, u32[]{:S(2)}, u32[]{:S(2)}) async-start(f32[8,16,512]{2,1,0:T(8,128)} %shard_map.74), calls=%async_computation.1 | async-start | bytes 524288 | tf_op jit(solution)/shard_map/all_to_all | solution.py:186
  59.2 5.7 %collective-permute-start.3 = (f32[16,256]{1,0:T(8,128)S(1)}, f32[16,256]{1,0:T(8,128)S(1)}, u32[]{:S(2)}, u32[]{:S(2)}) collective-permute-start(f32[16,256]{1,0:T(8,128)S(1)} %get-tuple-element.8), channel_id=1, source_target_pairs={{0,1},{1,2},{2,3},{3,0},{4,5},{5,6},{6,7},{7,4},{8,9},{9,10},{10,1... | collective-permute-start | bytes 49160 | tf_op jit(solution)/shard_map/ppermute | solution.py:18
  60.8 4.6 %collective-permute-start.4 = (f32[16,256]{1,0:T(8,128)S(1)}, f32[16,256]{1,0:T(8,128)S(1)}, u32[]{:S(2)}, u32[]{:S(2)}) collective-permute-start(f32[16,256]{1,0:T(8,128)S(1)} %get-tuple-element.10), channel_id=1, source_target_pairs={{0,2},{1,3},{2,0},{3,1},{4,6},{5,7},{6,4},{7,5},{8,10},{9,11},{10,... | collective-permute-start | bytes 49160 | tf_op jit(solution)/shard_map/ppermute | solution.py:18
  62.8 3.7 %collective-permute-start.5 = (f32[16,256]{1,0:T(8,128)S(1)}, f32[16,256]{1,0:T(8,128)S(1)}, u32[]{:S(2)}, u32[]{:S(2)}) collective-permute-start(f32[16,256]{1,0:T(8,128)S(1)} %get-tuple-element.9), channel_id=1, source_target_pairs={{0,3},{1,0},{2,1},{3,2},{4,7},{5,4},{6,5},{7,6},{8,11},{9,8},{10,9... | collective-permute-start | bytes 49160 | tf_op jit(solution)/shard_map/ppermute | solution.py:18

commit v17 on v12

--- a/solution.py
+++ b/solution.py
@@ -44,7 +44,7 @@
     return lax.all_to_all(copies, axis, 0, 0, tiled=True)
 
 
-def gradient_kernel(order_ref, lengths_ref, act_ref, cot_ref, win_ref, wout_ref, *out_refs):
+def gradient_kernel(lengths_ref, act_ref, cot_ref, win_ref, wout_ref, *out_refs):
     step = pl.program_id(0)
     tokens = act_ref.shape[1]
     offset = lax.axis_index("mp") * tokens
@@ -69,25 +69,29 @@
                 out_ref[example] = grad
 
 
-def layer_gradients(order, activations, cotangents, lengths, project_in, project_out):
+def layer_gradients(activations, cotangents, lengths, project_in, project_out):
     layers, examples, tokens, width = activations.shape
     factor = project_in.shape[1]
-    data = pl.BlockSpec((None, examples, tokens, width), lambda t, rank, lens: (rank[t], 0, 0, 0))
-    weights = pl.BlockSpec((None, factor, width), lambda t, rank, lens: (rank[t], 0, 0))
-    result = pl.BlockSpec((examples, factor, factor), lambda t, rank, lens: (0, 0, 0))
+
+    def layer_of(t):
+        return (lax.axis_index("mp") + 1 + t) % layers
+
+    data = pl.BlockSpec((None, examples, tokens, width), lambda t, lens: (layer_of(t), 0, 0, 0))
+    weights = pl.BlockSpec((None, factor, width), lambda t, lens: (layer_of(t), 0, 0))
+    result = pl.BlockSpec((examples, factor, factor), lambda t, lens: (0, 0, 0))
     flops = 4 * layers * examples * tokens * width * factor
     moved = 2 * (activations.size + cotangents.size + project_in.size + project_out.size)
     return pl.pallas_call(
         gradient_kernel,
         out_shape=[jax.ShapeDtypeStruct((examples, factor, factor), jnp.float32)] * layers,
         grid_spec=pltpu.PrefetchScalarGridSpec(
-            num_scalar_prefetch=2,
+            num_scalar_prefetch=1,
             grid=(layers,),
             in_specs=[data, data, weights, weights],
             out_specs=[result] * layers,
         ),
         cost_estimate=pl.CostEstimate(flops=flops, transcendentals=0, bytes_accessed=moved),
-    )(order, lengths, activations, cotangents, project_in, project_out)
+    )(lengths, activations, cotangents, project_in, project_out)
 
 
 def body_start(activations, cotangents, lengths, project_in, project_out, preconditioner, queries):
@@ -140,8 +144,7 @@
     block_size = factor_size * factor_size
     width_dp = lax.axis_size("dp")
     mp_place = lax.axis_index("mp")
-    order = (mp_place + jnp.arange(1, layer_count + 1, dtype=jnp.int32)) % layer_count
-    grads = layer_gradients(order, activations, cotangents, lengths, project_in, project_out)
+    grads = layer_gradients(activations, cotangents, lengths, project_in, project_out)
     grad_mine = grads[-1]
     for shift in range(1, layer_count):
         grad_mine = grad_mine + shifted(grads[shift - 1], "mp", shift)

time: 67.9 us -> 67.4 us (level)
  no operation moved by 1% of the time
where the time goes in v17:
time: 67.4 us; the launch traced here: 67 us
  Pallas kernels  17.1 us (25%)
  waiting for transfers between devices  16.1 us (24%)
  starting transfers between devices  13.4 us (20%)
  blocking collectives  9.02 us (13%)
  matrix products  8.81 us (13%)
  other arithmetic  1.54 us (2%)
  local copies, waits for them, and re-layouts  0.98 us (1%)
    pallas_call x1, Pallas kernels, layer_gradients(): pl.pallas_call(gradient_kernel, out_shape=[jax.ShapeDtypeStruct((examples...  17.1 us
    ppermute x6, starting transfers between devices, shifted(): return lax.ppermute(x, axis, [(i, (i + shift) % n) for i in range(n)])  9.97 us
    ppermute x6, waiting for transfers between devices, shifted(): return lax.ppermute(x, axis, [(i, (i + shift) % n) for i in range(n)])  9.32 us
    all_to_all x1, blocking collectives, all_gather_a2a(): return lax.all_to_all(copies, axis, 0, 0, tiled=True)  9.02 us
    all_to_all x1, waiting for transfers between devices, all_gather_a2a(): return lax.all_to_all(copies, axis, 0, 0, tiled=True)  6.79 us
    dot_general x1, matrix products, body_direct(): lax.dot_general(both_all, query_blocks, (((0, 2), (1, 2)), ((), ())), pre...  5.98 us
    all_to_all x1, starting transfers between devices, all_gather_a2a(): return lax.all_to_all(copies, axis, 0, 0, tiled=True)  3.41 us
    dot_general x1, matrix products, body_direct(): jnp.dot(grad_all, preconditioner, preferred_element_type=jnp.float32)  2.83 us
  transfers between devices with their start and end apart: 7, of which 5 were waited for; matrix products, arithmetic and copies ran while one was open for 0% of the time, Pallas kernels for 0%

profile of v17, /device:TPU:0, one launch (start us, length us, event | category | flops | bytes accessed | tf_op | source)
XLA Modules:
  0.0 67.0 jit_solution(3038773791076947423)
XLA Ops:
  0.0 17.1 %shard_map.73 = (f32[2,64,64]{2,1,0:T(8,128)}, f32[2,64,64]{2,1,0:T(8,128)}, f32[2,64,64]{2,1,0:T(8,128)}, f32[2,64,64]{2,1,0:T(8,128)}) custom-call(s32[2]{0:T(128)} %lengths_ref.1, bf16[4,2,256,4096]{3,2,1,0:T(8,128)(2,1)} %act_ref.1, bf16[4,2,256,4096]{3,2,1,0:T(8,128)(2,1)} %cot_ref.1, bf16[4,64,4096]{2,1,0:T(8,128)(2,1)} %win_ref.1, ...), custom_call_target="tpu_custom_call" | custom-call | flops 2147483648 | bytes 37748736 | tf_op jit(solution)/shard_map/pallas_call | solution.py:84
  17.1 5.1 %collective-permute-start.2 = (f32[2,64,64]{2,1,0:T(8,128)}, f32[2,64,64]{2,1,0:T(8,128)S(1)}, u32[]{:S(2)}, u32[]{:S(2)}) collective-permute-start(f32[2,64,64]{2,1,0:T(8,128)} %get-tuple-element.12), channel_id=1, source_target_pairs={{0,3},{1,0},{2,1},{3,2},{4,7},{5,4},{6,5},{7,6},{8,11},{9,8},{10,9... | collective-permute-start | bytes 98312 | tf_op jit(solution)/shard_map/ppermute | solution.py:18
  22.1 0.0 collective-permute-start.1
  22.1 1.1 %collective-permute-start = (f32[2,64,64]{2,1,0:T(8,128)}, f32[2,64,64]{2,1,0:T(8,128)S(1)}, u32[]{:S(2)}, u32[]{:S(2)}) collective-permute-start(f32[2,64,64]{2,1,0:T(8,128)} %get-tuple-element.10), channel_id=1, source_target_pairs={{0,1},{1,2},{2,3},{3,0},{4,5},{5,6},{6,7},{7,4},{8,9},{9,10},{10,1... | collective-permute-start | bytes 98312 | tf_op jit(solution)/shard_map/ppermute | solution.py:18
  23.2 1.7 %collective-permute-done.2 = f32[2,64,64]{2,1,0:T(8,128)S(1)} collective-permute-done((f32[2,64,64]{2,1,0:T(8,128)}, f32[2,64,64]{2,1,0:T(8,128)S(1)}, u32[]{:S(2)}, u32[]{:S(2)}) %collective-permute-start.2) | collective-permute-done | bytes 32800 | tf_op jit(solution)/shard_map/ppermute | solution.py:18
  24.9 3.9 %collective-permute-done.1 = f32[2,64,64]{2,1,0:T(8,128)S(1)} collective-permute-done((f32[2,64,64]{2,1,0:T(8,128)}, f32[2,64,64]{2,1,0:T(8,128)S(1)}, u32[]{:S(2)}, u32[]{:S(2)}) %collective-permute-start.1) | collective-permute-done | bytes 32800 | tf_op jit(solution)/shard_map/ppermute | solution.py:18
  28.9 0.0 collective-permute-done
  28.9 0.9 %add_convert_fusion = bf16[2,64,64]{2,1,0:T(8,128)(2,1)S(1)} fusion(f32[2,64,64]{2,1,0:T(8,128)S(1)} %collective-permute-done.2, f32[2,64,64]{2,1,0:T(8,128)S(1)} %collective-permute-done.1, f32[2,64,64]{2,1,0:T(8,128)} %get-tuple-element.9, f32[2,64,64]{2,1,0:T(8,128)S(1)} %collective-permute-done), kind=kLoop, calls=%fused_computation.9 | loop fusion | flops 32768 | bytes 147456 | tf_op jit(solution)/shard_map/convert_element_type | solution.py:151
  29.7 0.1 broadcast_in_dim.6
  29.8 0.1 broadcast_in_dim.14
  29.9 9.0 %all_to_all.10 = bf16[8,2,4096]{2,1,0:T(2,128)(2,1)S(1)} all-to-all(bf16[8,2,4096]{2,1,0:T(2,128)(2,1)S(1)} %broadcast_in_dim.14), channel_id=1, replica_groups=mesh['dp'=8,'mp'=4] {'dp'}, dimensions={0} | all-to-all | bytes 262144 | tf_op jit(solution)/shard_map/all_to_all | solution.py:44
  38.9 0.1 reshape.8
  39.0 2.8 %fusion.10 = f32[16,512]{1,0:T(8,128)S(1)} fusion(bf16[16,4096]{1,0:T(8,128)(2,1)S(1)} %reshape.8, bf16[4096,512]{1,0:T(8,128)(2,1)} %param.12), kind=kOutput, calls=%fused_computation.15 | convolution fusion | flops 67108864 | bytes 4358144 | tf_op jit(solution)/shard_map/dot_general | solution.py:154
  41.8 0.7 %broadcast_in_dim.15 = f32[8,16,512]{2,1,0:T(8,128)} broadcast(f32[16,512]{1,0:T(8,128)S(1)} %fusion.10), dimensions={1,2} | broadcast | bytes 294912 | tf_op jit(solution)/shard_map/broadcast_in_dim | solution.py:43
  42.6 3.4 %all-to-all-start.1 = ((f32[8,16,512]{2,1,0:T(8,128)}), f32[8,16,512]{2,1,0:T(8,128)S(1)}, u32[]{:S(2)}, u32[]{:S(2)}) async-start(f32[8,16,512]{2,1,0:T(8,128)} %broadcast_in_dim.15), calls=%async_computation.1 | async-start | bytes 524288 | tf_op jit(solution)/shard_map/all_to_all | solution.py:44
  46.0 6.8 %all-to-all-done.1 = f32[8,16,512]{2,1,0:T(8,128)S(1)} async-done(((f32[8,16,512]{2,1,0:T(8,128)}), f32[8,16,512]{2,1,0:T(8,128)S(1)}, u32[]{:S(2)}, u32[]{:S(2)}) %all-to-all-start.1) | async-done | bytes 262176 | tf_op jit(solution)/shard_map/all_to_all | solution.py:44
  52.9 6.0 %fusion.3 = f32[32,1024]{1,0:T(8,128)S(1)} fusion(bf16[128,8,8,512]{3,2,1,0:T(8,128)(2,1)} %bitcast.10, bf16[8,16,512]{2,1,0:T(8,128)(2,1)S(1)} %subtract_convert_fusion, bf16[8,16,512]{2,1,0:T(8,128)(2,1)S(1)} %convert_element_type.13), kind=kOutput, calls=%fused_computation.3 | convolution fusion | flops 268959744 | bytes 8781824 | tf_op jit(solution)/shard_map/dot_general | solution.py:159
  58.9 1.9 %collective-permute-start.5 = (f32[16,256]{1,0:T(8,128)S(1)}, f32[16,256]{1,0:T(8,128)S(1)}, u32[]{:S(2)}, u32[]{:S(2)}) collective-permute-start(f32[16,256]{1,0:T(8,128)S(1)} %get-tuple-element.14), channel_id=1, source_target_pairs={{0,3},{1,0},{2,1},{3,2},{4,7},{5,4},{6,5},{7,6},{8,11},{9,8},{10,9... | collective-permute-start | bytes 49160 | tf_op jit(solution)/shard_map/ppermute | solution.py:18
  60.8 0.0 collective-permute-start.4
  60.9 1.9 %collective-permute-start.3 = (f32[16,256]{1,0:T(8,128)S(1)}, f32[16,256]{1,0:T(8,128)S(1)}, u32[]{:S(2)}, u32[]{:S(2)}) collective-permute-start(f32[16,256]{1,0:T(8,128)S(1)} %get-tuple-element.13), channel_id=1, source_target_pairs={{0,1},{1,2},{2,3},{3,0},{4,5},{5,6},{6,7},{7,4},{8,9},{9,10},{10,1... | collective-permute-start | bytes 49160 | tf_op jit(solution)/shard_map/ppermute | solution.py:18
  62.7 0.0 collective-permute-done.5
  62.7 2.7 %collective-permute-done.4 = f32[16,256]{1,0:T(8,128)S(1)} collective-permute-done((f32[16,256]{1,0:T(8,128)S(1)}, f32[16,256]{1,0:T(8,128)S(1)}, u32[]{:S(2)}, u32[]{:S(2)}) %collective-permute-start.4) | collective-permute-done | bytes 16416 | tf_op jit(solution)/shard_map/ppermute | solution.py:18
  65.5 0.9 %collective-permute-done.3 = f32[16,256]{1,0:T(8,128)S(1)} collective-permute-done((f32[16,256]{1,0:T(8,128)S(1)}, f32[16,256]{1,0:T(8,128)S(1)}, u32[]{:S(2)}, u32[]{:S(2)}) %collective-permute-start.3) | collective-permute-done | bytes 16416 | tf_op jit(solution)/shard_map/ppermute | solution.py:18
  66.4 0.6 add_add_fusion
  (4 shorter events, 0.1 us)
Async XLA Ops:
  17.1 7.9 %collective-permute-start.2 = (f32[2,64,64]{2,1,0:T(8,128)}, f32[2,64,64]{2,1,0:T(8,128)S(1)}, u32[]{:S(2)}, u32[]{:S(2)}) collective-permute-start(f32[2,64,64]{2,1,0:T(8,128)} %get-tuple-element.12), channel_id=1, source_target_pairs={{0,3},{1,0},{2,1},{3,2},{4,7},{5,4},{6,5},{7,6},{8,11},{9,8},{10,9... | collective-permute-start | bytes 98312 | tf_op jit(solution)/shard_map/ppermute | solution.py:18
  22.1 6.7 %collective-permute-start.1 = (f32[2,64,64]{2,1,0:T(8,128)}, f32[2,64,64]{2,1,0:T(8,128)S(1)}, u32[]{:S(2)}, u32[]{:S(2)}) collective-permute-start(f32[2,64,64]{2,1,0:T(8,128)} %get-tuple-element.11), channel_id=1, source_target_pairs={{0,2},{1,3},{2,0},{3,1},{4,6},{5,7},{6,4},{7,5},{8,10},{9,11},{10,... | collective-permute-start | bytes 98312 | tf_op jit(solution)/shard_map/ppermute | solution.py:18
  22.1 6.7 %collective-permute-start = (f32[2,64,64]{2,1,0:T(8,128)}, f32[2,64,64]{2,1,0:T(8,128)S(1)}, u32[]{:S(2)}, u32[]{:S(2)}) collective-permute-start(f32[2,64,64]{2,1,0:T(8,128)} %get-tuple-element.10), channel_id=1, source_target_pairs={{0,1},{1,2},{2,3},{3,0},{4,5},{5,6},{6,7},{7,4},{8,9},{9,10},{10,1... | collective-permute-start | bytes 98312 | tf_op jit(solution)/shard_map/ppermute | solution.py:18
  42.6 10.3 %all-to-all-start.1 = ((f32[8,16,512]{2,1,0:T(8,128)}), f32[8,16,512]{2,1,0:T(8,128)S(1)}, u32[]{:S(2)}, u32[]{:S(2)}) async-start(f32[8,16,512]{2,1,0:T(8,128)} %broadcast_in_dim.15), calls=%async_computation.1 | async-start | bytes 524288 | tf_op jit(solution)/shard_map/all_to_all | solution.py:44
  58.9 3.8 %collective-permute-start.5 = (f32[16,256]{1,0:T(8,128)S(1)}, f32[16,256]{1,0:T(8,128)S(1)}, u32[]{:S(2)}, u32[]{:S(2)}) collective-permute-start(f32[16,256]{1,0:T(8,128)S(1)} %get-tuple-element.14), channel_id=1, source_target_pairs={{0,3},{1,0},{2,1},{3,2},{4,7},{5,4},{6,5},{7,6},{8,11},{9,8},{10,9... | collective-permute-start | bytes 49160 | tf_op jit(solution)/shard_map/ppermute | solution.py:18
  60.8 4.6 %collective-permute-start.4 = (f32[16,256]{1,0:T(8,128)S(1)}, f32[16,256]{1,0:T(8,128)S(1)}, u32[]{:S(2)}, u32[]{:S(2)}) collective-permute-start(f32[16,256]{1,0:T(8,128)S(1)} %get-tuple-element.15), channel_id=1, source_target_pairs={{0,2},{1,3},{2,0},{3,1},{4,6},{5,7},{6,4},{7,5},{8,10},{9,11},{10,... | collective-permute-start | bytes 49160 | tf_op jit(solution)/shard_map/ppermute | solution.py:18
  60.9 5.5 %collective-permute-start.3 = (f32[16,256]{1,0:T(8,128)S(1)}, f32[16,256]{1,0:T(8,128)S(1)}, u32[]{:S(2)}, u32[]{:S(2)}) collective-permute-start(f32[16,256]{1,0:T(8,128)S(1)} %get-tuple-element.13), channel_id=1, source_target_pairs={{0,1},{1,2},{2,3},{3,0},{4,5},{5,6},{6,7},{7,4},{8,9},{9,10},{10,1... | collective-permute-start | bytes 49160 | tf_op jit(solution)/shard_map/ppermute | solution.py:18

commit v18 on v15

--- a/solution.py
+++ b/solution.py
@@ -141,8 +141,11 @@
     grad_mine = grad_mine.astype(jnp.bfloat16).reshape(grad_mine.shape[0], block_size)
     grad_all = all_gather_a2a(grad_mine, "dp")
     grad_all = grad_all.reshape(-1, grad_all.shape[-1])
-    pre_part = jnp.dot(grad_all, preconditioner, preferred_element_type=jnp.float32)
-    upper_grad, lower_grad = split_parts(all_gather_a2a(pre_part, "dp"))
+    grad_copies = jnp.broadcast_to(grad_all[None], (width_dp,) + grad_all.shape)
+    pre_copies = jnp.einsum(
+        "nej,jc->nec", grad_copies, preconditioner, preferred_element_type=jnp.float32
+    )
+    upper_grad, lower_grad = split_parts(lax.all_to_all(pre_copies, "dp", 0, 0, tiled=True))
     both_all = jnp.concatenate([upper_grad, lower_grad], axis=1)
     blocks, block = both_all.shape[0], both_all.shape[2]
     query_blocks = queries.reshape(queries.shape[0], blocks, block)

time: 66.4 us -> 66.4 us (level)
  matrix products: 8.81 us -> 9.59 us
  local copies, waits for them, and re-layouts: 1.9 us -> 1.15 us
    dot_general x1, matrix products: 2.83 us -> 3.61 us  [body_direct(): jnp.einsum('nej,jc->nec', grad_copies, preconditioner, preferred_element_...]
    broadcast_in_dim x2 -> x1, local copies, waits for them, and re-layouts: 0.81 us -> 0.07 us  [all_gather_a2a(): copies = jnp.broadcast_to(x[None], (n,) + x.shape)]
where the time goes in v18:
time: 66.4 us; the launch traced here: 66 us
  Pallas kernels  16.6 us (25%)
  starting transfers between devices  14.5 us (22%)
  waiting for transfers between devices  13.5 us (20%)
  matrix products  9.59 us (14%)
  blocking collectives  9.01 us (14%)
  other arithmetic  1.54 us (2%)
  local copies, waits for them, and re-layouts  1.15 us (2%)
    pallas_call x1, Pallas kernels, layer_gradients(): pl.pallas_call(gradient_kernel, out_shape=jax.ShapeDtypeStruct((layers, e...  16.6 us
    ppermute x6, starting transfers between devices, shifted(): return lax.ppermute(x, axis, [(i, (i + shift) % n) for i in range(n)])  11.1 us
    all_to_all x1, blocking collectives, all_gather_a2a(): return lax.all_to_all(copies, axis, 0, 0, tiled=True)  9.01 us
    all_to_all x1, waiting for transfers between devices, body_direct(): lax.all_to_all(pre_copies, 'dp', 0, 0, tiled=True)  6.81 us
    ppermute x6, waiting for transfers between devices, shifted(): return lax.ppermute(x, axis, [(i, (i + shift) % n) for i in range(n)])  6.69 us
    dot_general x1, matrix products, body_direct(): lax.dot_general(both_all, query_blocks, (((0, 2), (1, 2)), ((), ())), pre...  5.98 us
    dot_general x1, matrix products, body_direct(): jnp.einsum('nej,jc->nec', grad_copies, preconditioner, preferred_element_...  3.61 us
    all_to_all x1, starting transfers between devices, body_direct(): lax.all_to_all(pre_copies, 'dp', 0, 0, tiled=True)  3.41 us
  transfers between devices with their start and end apart: 7, of which 7 were waited for; matrix products, arithmetic and copies ran while one was open for 0% of the time, Pallas kernels for 0%

profile of v18, /device:TPU:0, one launch (start us, length us, event | category | flops | bytes accessed | tf_op | source)
XLA Modules:
  0.0 66.0 jit_solution(16091282507546773100)
XLA Ops:
  0.0 16.6 %shard_map.73 = f32[4,2,64,64]{3,2,1,0:T(8,128)} custom-call(s32[2]{0:T(128)} %lengths_ref.1, bf16[4,2,256,4096]{3,2,1,0:T(8,128)(2,1)} %act_ref.1, bf16[4,2,256,4096]{3,2,1,0:T(8,128)(2,1)} %cot_ref.1, bf16[4,64,4096]{2,1,0:T(8,128)(2,1)} %win_ref.1, bf16[4,64,4096]{2,1,0:T(8,128)(2,1)} %wout_ref.1), custom_call_target="tpu_custom_call" | custom-call | flops 2147483648 | bytes 37748736 | tf_op jit(solution)/shard_map/pallas_call | solution.py:76
  16.6 0.9 %constant_dynamic-slice_fusion.5 = (f32[1,2,64,64]{3,2,1,0:T(8,128)S(1)}, f32[1,2,64,64]{3,2,1,0:T(8,128)S(1)}, f32[1,2,64,64]{3,2,1,0:T(8,128)S(1)}) fusion(f32[4,2,64,64]{3,2,1,0:T(8,128)} %shard_map.73, s32[]{:T(128)S(6)} %select_n.47, s32[]{:T(128)S(6)} %select_n.51, s32[]{:T(128)S(6)} %select_n.49), kind=kLoop, calls=%fused_computation.19 | loop fusion | bytes 196620 | tf_op jit(solution)/shard_map/dynamic_slice | solution.py:27
  17.5 3.1 %collective-permute-start = (f32[1,2,64,64]{3,2,1,0:T(8,128)S(1)}, f32[1,2,64,64]{3,2,1,0:T(8,128)S(1)}, u32[]{:S(2)}, u32[]{:S(2)}) collective-permute-start(f32[1,2,64,64]{3,2,1,0:T(8,128)S(1)} %get-tuple-element.5), channel_id=1, source_target_pairs={{0,1},{1,2},{2,3},{3,0},{4,5},{5,6},{6,7},{7,4},{8,9},{9,10},{10,1... | collective-permute-start | bytes 98312 | tf_op jit(solution)/shard_map/ppermute | solution.py:18
  20.6 2.6 %collective-permute-start.1 = (f32[1,2,64,64]{3,2,1,0:T(8,128)S(1)}, f32[1,2,64,64]{3,2,1,0:T(8,128)S(1)}, u32[]{:S(2)}, u32[]{:S(2)}) collective-permute-start(f32[1,2,64,64]{3,2,1,0:T(8,128)S(1)} %get-tuple-element.7), channel_id=1, source_target_pairs={{0,2},{1,3},{2,0},{3,1},{4,6},{5,7},{6,4},{7,5},{8,10},{9,11},{10,... | collective-permute-start | bytes 98312 | tf_op jit(solution)/shard_map/ppermute | solution.py:18
  23.2 1.3 %collective-permute-start.2 = (f32[1,2,64,64]{3,2,1,0:T(8,128)S(1)}, f32[1,2,64,64]{3,2,1,0:T(8,128)S(1)}, u32[]{:S(2)}, u32[]{:S(2)}) collective-permute-start(f32[1,2,64,64]{3,2,1,0:T(8,128)S(1)} %get-tuple-element.6), channel_id=1, source_target_pairs={{0,3},{1,0},{2,1},{3,2},{4,7},{5,4},{6,5},{7,6},{8,11},{9,8},{10,9... | collective-permute-start | bytes 98312 | tf_op jit(solution)/shard_map/ppermute | solution.py:18
  24.6 0.5 collective-permute-done
  25.1 2.6 %collective-permute-done.1 = f32[1,2,64,64]{3,2,1,0:T(8,128)S(1)} collective-permute-done((f32[1,2,64,64]{3,2,1,0:T(8,128)S(1)}, f32[1,2,64,64]{3,2,1,0:T(8,128)S(1)}, u32[]{:S(2)}, u32[]{:S(2)}) %collective-permute-start.1) | collective-permute-done | bytes 32800 | tf_op jit(solution)/shard_map/ppermute | solution.py:18
  27.7 0.2 collective-permute-done.2
  27.9 0.9 %add_convert_fusion = bf16[1,2,64,64]{3,2,1,0:T(8,128)(2,1)S(1)} fusion(f32[1,2,64,64]{3,2,1,0:T(8,128)S(1)} %collective-permute-done.2, f32[1,2,64,64]{3,2,1,0:T(8,128)S(1)} %collective-permute-done.1, f32[1,2,64,64]{3,2,1,0:T(8,128)S(1)} %collective-permute-done, f32[4,2,64,64]{3,2,1,0:T(8,128)} %shard_map.73, s32[]{:T(128)S(6)} %select_n.45), kind=kLoop, calls=%fused_computation.12 | loop fusion | flops 32768 | bytes 147460 | tf_op jit(solution)/shard_map/convert_element_type | solution.py:141
  28.8 0.1 convert_element_type.20
  28.9 0.1 broadcast_in_dim.12
  29.0 9.0 %all_to_all.10 = bf16[8,2,4096]{2,1,0:T(2,128)(2,1)S(1)} all-to-all(bf16[8,2,4096]{2,1,0:T(2,128)(2,1)S(1)} %broadcast_in_dim.12), channel_id=1, replica_groups=mesh['dp'=8,'mp'=4] {'dp'}, dimensions={0} | all-to-all | bytes 262144 | tf_op jit(solution)/shard_map/all_to_all | solution.py:44
  38.0 0.1 broadcast_in_dim.13
  38.0 3.6 %fusion.3 = f32[8,16,512]{2,1,0:T(8,128)} fusion(bf16[4096,512]{1,0:T(8,128)(2,1)} %param.12, bf16[16,4096]{1,0:T(8,128)(2,1)S(1)} %broadcast_in_dim.13), kind=kOutput, calls=%fused_computation.3 | convolution fusion | flops 536870912 | bytes 4587520 | tf_op jit(solution)/shard_map/nej,jc->nec/dot_general | solution.py:145
  41.7 3.4 %all-to-all-start.1 = ((f32[8,16,512]{2,1,0:T(8,128)}), f32[8,16,512]{2,1,0:T(8,128)S(1)}, u32[]{:S(2)}, u32[]{:S(2)}) async-start(f32[8,16,512]{2,1,0:T(8,128)} %fusion.3), calls=%async_computation.1 | async-start | bytes 524288 | tf_op jit(solution)/shard_map/all_to_all | solution.py:148
  45.1 6.8 %all-to-all-done.1 = f32[8,16,512]{2,1,0:T(8,128)S(1)} async-done(((f32[8,16,512]{2,1,0:T(8,128)}), f32[8,16,512]{2,1,0:T(8,128)S(1)}, u32[]{:S(2)}, u32[]{:S(2)}) %all-to-all-start.1) | async-done | bytes 262176 | tf_op jit(solution)/shard_map/all_to_all | solution.py:148
  52.0 6.0 %fusion.5 = f32[32,1024]{1,0:T(8,128)S(1)} fusion(bf16[128,8,8,512]{3,2,1,0:T(8,128)(2,1)} %bitcast.13, bf16[8,16,512]{2,1,0:T(8,128)(2,1)S(1)} %subtract_convert_fusion, bf16[8,16,512]{2,1,0:T(8,128)(2,1)S(1)} %convert_element_type.21), kind=kOutput, calls=%fused_computation.5 | convolution fusion | flops 268959744 | bytes 8781824 | tf_op jit(solution)/shard_map/dot_general | solution.py:152
  58.0 1.6 %collective-permute-start.3 = (f32[16,256]{1,0:T(8,128)S(1)}, f32[16,256]{1,0:T(8,128)S(1)}, u32[]{:S(2)}, u32[]{:S(2)}) collective-permute-start(f32[16,256]{1,0:T(8,128)S(1)} %get-tuple-element.8), channel_id=1, source_target_pairs={{0,1},{1,2},{2,3},{3,0},{4,5},{5,6},{6,7},{7,4},{8,9},{9,10},{10,1... | collective-permute-start | bytes 49160 | tf_op jit(solution)/shard_map/ppermute | solution.py:18
  59.6 2.0 %collective-permute-start.4 = (f32[16,256]{1,0:T(8,128)S(1)}, f32[16,256]{1,0:T(8,128)S(1)}, u32[]{:S(2)}, u32[]{:S(2)}) collective-permute-start(f32[16,256]{1,0:T(8,128)S(1)} %get-tuple-element.10), channel_id=1, source_target_pairs={{0,2},{1,3},{2,0},{3,1},{4,6},{5,7},{6,4},{7,5},{8,10},{9,11},{10,... | collective-permute-start | bytes 49160 | tf_op jit(solution)/shard_map/ppermute | solution.py:18
  61.7 0.4 collective-permute-start.5
  62.1 1.6 %collective-permute-done.3 = f32[16,256]{1,0:T(8,128)S(1)} collective-permute-done((f32[16,256]{1,0:T(8,128)S(1)}, f32[16,256]{1,0:T(8,128)S(1)}, u32[]{:S(2)}, u32[]{:S(2)}) %collective-permute-start.3) | collective-permute-done | bytes 16416 | tf_op jit(solution)/shard_map/ppermute | solution.py:18
  63.7 0.6 collective-permute-done.4
  64.3 1.1 %collective-permute-done.5 = f32[16,256]{1,0:T(8,128)S(1)} collective-permute-done((f32[16,256]{1,0:T(8,128)S(1)}, f32[16,256]{1,0:T(8,128)S(1)}, u32[]{:S(2)}, u32[]{:S(2)}) %collective-permute-start.5) | collective-permute-done | bytes 16416 | tf_op jit(solution)/shard_map/ppermute | solution.py:18
  65.4 0.6 add_add_fusion
  (4 shorter events, 0.1 us)
Async XLA Ops:
  17.5 7.6 %collective-permute-start = (f32[1,2,64,64]{3,2,1,0:T(8,128)S(1)}, f32[1,2,64,64]{3,2,1,0:T(8,128)S(1)}, u32[]{:S(2)}, u32[]{:S(2)}) collective-permute-start(f32[1,2,64,64]{3,2,1,0:T(8,128)S(1)} %get-tuple-element.5), channel_id=1, source_target_pairs={{0,1},{1,2},{2,3},{3,0},{4,5},{5,6},{6,7},{7,4},{8,9},{9,10},{10,1... | collective-permute-start | bytes 98312 | tf_op jit(solution)/shard_map/ppermute | solution.py:18
  20.6 7.1 %collective-permute-start.1 = (f32[1,2,64,64]{3,2,1,0:T(8,128)S(1)}, f32[1,2,64,64]{3,2,1,0:T(8,128)S(1)}, u32[]{:S(2)}, u32[]{:S(2)}) collective-permute-start(f32[1,2,64,64]{3,2,1,0:T(8,128)S(1)} %get-tuple-element.7), channel_id=1, source_target_pairs={{0,2},{1,3},{2,0},{3,1},{4,6},{5,7},{6,4},{7,5},{8,10},{9,11},{10,... | collective-permute-start | bytes 98312 | tf_op jit(solution)/shard_map/ppermute | solution.py:18
  23.2 4.7 %collective-permute-start.2 = (f32[1,2,64,64]{3,2,1,0:T(8,128)S(1)}, f32[1,2,64,64]{3,2,1,0:T(8,128)S(1)}, u32[]{:S(2)}, u32[]{:S(2)}) collective-permute-start(f32[1,2,64,64]{3,2,1,0:T(8,128)S(1)} %get-tuple-element.6), channel_id=1, source_target_pairs={{0,3},{1,0},{2,1},{3,2},{4,7},{5,4},{6,5},{7,6},{8,11},{9,8},{10,9... | collective-permute-start | bytes 98312 | tf_op jit(solution)/shard_map/ppermute | solution.py:18
  41.7 10.3 %all-to-all-start.1 = ((f32[8,16,512]{2,1,0:T(8,128)}), f32[8,16,512]{2,1,0:T(8,128)S(1)}, u32[]{:S(2)}, u32[]{:S(2)}) async-start(f32[8,16,512]{2,1,0:T(8,128)} %fusion.3), calls=%async_computation.1 | async-start | bytes 524288 | tf_op jit(solution)/shard_map/all_to_all | solution.py:148
  58.0 5.7 %collective-permute-start.3 = (f32[16,256]{1,0:T(8,128)S(1)}, f32[16,256]{1,0:T(8,128)S(1)}, u32[]{:S(2)}, u32[]{:S(2)}) collective-permute-start(f32[16,256]{1,0:T(8,128)S(1)} %get-tuple-element.8), channel_id=1, source_target_pairs={{0,1},{1,2},{2,3},{3,0},{4,5},{5,6},{6,7},{7,4},{8,9},{9,10},{10,1... | collective-permute-start | bytes 49160 | tf_op jit(solution)/shard_map/ppermute | solution.py:18
  59.6 4.6 %collective-permute-start.4 = (f32[16,256]{1,0:T(8,128)S(1)}, f32[16,256]{1,0:T(8,128)S(1)}, u32[]{:S(2)}, u32[]{:S(2)}) collective-permute-start(f32[16,256]{1,0:T(8,128)S(1)} %get-tuple-element.10), channel_id=1, source_target_pairs={{0,2},{1,3},{2,0},{3,1},{4,6},{5,7},{6,4},{7,5},{8,10},{9,11},{10,... | collective-permute-start | bytes 49160 | tf_op jit(solution)/shard_map/ppermute | solution.py:18
  61.7 3.7 %collective-permute-start.5 = (f32[16,256]{1,0:T(8,128)S(1)}, f32[16,256]{1,0:T(8,128)S(1)}, u32[]{:S(2)}, u32[]{:S(2)}) collective-permute-start(f32[16,256]{1,0:T(8,128)S(1)} %get-tuple-element.9), channel_id=1, source_target_pairs={{0,3},{1,0},{2,1},{3,2},{4,7},{5,4},{6,5},{7,6},{8,11},{9,8},{10,9... | collective-permute-start | bytes 49160 | tf_op jit(solution)/shard_map/ppermute | solution.py:18

commit v19 on v18

--- a/solution.py
+++ b/solution.py
@@ -23,7 +23,7 @@
     me = lax.axis_index(axis)
     width = x.shape[dim] // n
     total = lax.dynamic_slice_in_dim(x, me * width, width, dim)
-    for shift in range(1, n):
+    for shift in reversed(range(1, n)):
         piece = lax.dynamic_slice_in_dim(x, ((me + shift) % n) * width, width, dim)
         total = total + shifted(piece, axis, shift)
     return total

time: 66.4 us -> 67.7 us (1.020)
  waiting for transfers between devices: 13.5 us -> 15.9 us
  starting transfers between devices: 14.5 us -> 13.4 us
    ppermute x6, waiting for transfers between devices: 6.69 us -> 9.1 us  [shifted(): return lax.ppermute(x, axis, [(i, (i + shift) % n) for i in range(n)])]
    ppermute x6, starting transfers between devices: 11.1 us -> 9.99 us  [shifted(): return lax.ppermute(x, axis, [(i, (i + shift) % n) for i in range(n)])]
  transfers between devices with their start and end apart: 7 -> 7, of which waited for: 7 -> 5; matrix products, arithmetic and copies ran while one was open for 0% -> 0% of each run, Pallas kernels for 0% -> 0%
where the time goes in v19:
time: 67.7 us; the launch traced here: 67.3 us
  Pallas kernels  16.6 us (25%)
  waiting for transfers between devices  15.9 us (23%)
  starting transfers between devices  13.4 us (20%)
  matrix products  9.59 us (14%)
  blocking collectives  9.01 us (13%)
  other arithmetic  1.54 us (2%)
  local copies, waits for them, and re-layouts  1.15 us (2%)
    pallas_call x1, Pallas kernels, layer_gradients(): pl.pallas_call(gradient_kernel, out_shape=jax.ShapeDtypeStruct((layers, e...  16.6 us
    ppermute x6, starting transfers between devices, shifted(): return lax.ppermute(x, axis, [(i, (i + shift) % n) for i in range(n)])  9.99 us
    ppermute x6, waiting for transfers between devices, shifted(): return lax.ppermute(x, axis, [(i, (i + shift) % n) for i in range(n)])  9.1 us
    all_to_all x1, blocking collectives, all_gather_a2a(): return lax.all_to_all(copies, axis, 0, 0, tiled=True)  9.01 us
    all_to_all x1, waiting for transfers between devices, body_direct(): lax.all_to_all(pre_copies, 'dp', 0, 0, tiled=True)  6.81 us
    dot_general x1, matrix products, body_direct(): lax.dot_general(both_all, query_blocks, (((0, 2), (1, 2)), ((), ())), pre...  5.98 us
    dot_general x1, matrix products, body_direct(): jnp.einsum('nej,jc->nec', grad_copies, preconditioner, preferred_element_...  3.61 us
    all_to_all x1, starting transfers between devices, body_direct(): lax.all_to_all(pre_copies, 'dp', 0, 0, tiled=True)  3.41 us
  transfers between devices with their start and end apart: 7, of which 5 were waited for; matrix products, arithmetic and copies ran while one was open for 0% of the time, Pallas kernels for 0%

profile of v19, /device:TPU:0, one launch (start us, length us, event | category | flops | bytes accessed | tf_op | source)
XLA Modules:
  0.0 67.3 jit_solution(8480880829406350737)
XLA Ops:
  0.0 16.6 %shard_map.73 = f32[4,2,64,64]{3,2,1,0:T(8,128)} custom-call(s32[2]{0:T(128)} %lengths_ref.1, bf16[4,2,256,4096]{3,2,1,0:T(8,128)(2,1)} %act_ref.1, bf16[4,2,256,4096]{3,2,1,0:T(8,128)(2,1)} %cot_ref.1, bf16[4,64,4096]{2,1,0:T(8,128)(2,1)} %win_ref.1, bf16[4,64,4096]{2,1,0:T(8,128)(2,1)} %wout_ref.1), custom_call_target="tpu_custom_call" | custom-call | flops 2147483648 | bytes 37748736 | tf_op jit(solution)/shard_map/pallas_call | solution.py:76
  16.6 0.9 %constant_dynamic-slice_fusion.5 = (f32[1,2,64,64]{3,2,1,0:T(8,128)S(1)}, f32[1,2,64,64]{3,2,1,0:T(8,128)S(1)}, f32[1,2,64,64]{3,2,1,0:T(8,128)S(1)}) fusion(f32[4,2,64,64]{3,2,1,0:T(8,128)} %shard_map.73, s32[]{:T(128)S(6)} %select_n.47, s32[]{:T(128)S(6)} %select_n.51, s32[]{:T(128)S(6)} %select_n.49), kind=kLoop, calls=%fused_computation.19 | loop fusion | bytes 196620 | tf_op jit(solution)/shard_map/dynamic_slice | solution.py:27
  17.5 5.1 %collective-permute-start = (f32[1,2,64,64]{3,2,1,0:T(8,128)S(1)}, f32[1,2,64,64]{3,2,1,0:T(8,128)S(1)}, u32[]{:S(2)}, u32[]{:S(2)}) collective-permute-start(f32[1,2,64,64]{3,2,1,0:T(8,128)S(1)} %get-tuple-element.5), channel_id=1, source_target_pairs={{0,3},{1,0},{2,1},{3,2},{4,7},{5,4},{6,5},{7,6},{8,11},{9,8},{10,9... | collective-permute-start | bytes 98312 | tf_op jit(solution)/shard_map/ppermute | solution.py:18
  22.7 0.0 collective-permute-start.1
  22.7 1.0 %collective-permute-start.2 = (f32[1,2,64,64]{3,2,1,0:T(8,128)S(1)}, f32[1,2,64,64]{3,2,1,0:T(8,128)S(1)}, u32[]{:S(2)}, u32[]{:S(2)}) collective-permute-start(f32[1,2,64,64]{3,2,1,0:T(8,128)S(1)} %get-tuple-element.6), channel_id=1, source_target_pairs={{0,1},{1,2},{2,3},{3,0},{4,5},{5,6},{6,7},{7,4},{8,9},{9,10},{10,1... | collective-permute-start | bytes 98312 | tf_op jit(solution)/shard_map/ppermute | solution.py:18
  23.7 1.5 %collective-permute-done = f32[1,2,64,64]{3,2,1,0:T(8,128)S(1)} collective-permute-done((f32[1,2,64,64]{3,2,1,0:T(8,128)S(1)}, f32[1,2,64,64]{3,2,1,0:T(8,128)S(1)}, u32[]{:S(2)}, u32[]{:S(2)}) %collective-permute-start) | collective-permute-done | bytes 32800 | tf_op jit(solution)/shard_map/ppermute | solution.py:18
  25.1 4.0 %collective-permute-done.1 = f32[1,2,64,64]{3,2,1,0:T(8,128)S(1)} collective-permute-done((f32[1,2,64,64]{3,2,1,0:T(8,128)S(1)}, f32[1,2,64,64]{3,2,1,0:T(8,128)S(1)}, u32[]{:S(2)}, u32[]{:S(2)}) %collective-permute-start.1) | collective-permute-done | bytes 32800 | tf_op jit(solution)/shard_map/ppermute | solution.py:18
  29.1 0.0 collective-permute-done.2
  29.1 0.9 %add_convert_fusion = bf16[1,2,64,64]{3,2,1,0:T(8,128)(2,1)S(1)} fusion(f32[1,2,64,64]{3,2,1,0:T(8,128)S(1)} %collective-permute-done.2, f32[1,2,64,64]{3,2,1,0:T(8,128)S(1)} %collective-permute-done.1, f32[1,2,64,64]{3,2,1,0:T(8,128)S(1)} %collective-permute-done, f32[4,2,64,64]{3,2,1,0:T(8,128)} %shard_map.73, s32[]{:T(128)S(6)} %select_n.45), kind=kLoop, calls=%fused_computation.12 | loop fusion | flops 32768 | bytes 147460 | tf_op jit(solution)/shard_map/convert_element_type | solution.py:141
  30.0 0.1 convert_element_type.20
  30.1 0.1 broadcast_in_dim.12
  30.2 9.0 %all_to_all.10 = bf16[8,2,4096]{2,1,0:T(2,128)(2,1)S(1)} all-to-all(bf16[8,2,4096]{2,1,0:T(2,128)(2,1)S(1)} %broadcast_in_dim.12), channel_id=1, replica_groups=mesh['dp'=8,'mp'=4] {'dp'}, dimensions={0} | all-to-all | bytes 262144 | tf_op jit(solution)/shard_map/all_to_all | solution.py:44
  39.2 0.1 broadcast_in_dim.13
  39.2 3.6 %fusion.3 = f32[8,16,512]{2,1,0:T(8,128)} fusion(bf16[4096,512]{1,0:T(8,128)(2,1)} %param.12, bf16[16,4096]{1,0:T(8,128)(2,1)S(1)} %broadcast_in_dim.13), kind=kOutput, calls=%fused_computation.3 | convolution fusion | flops 536870912 | bytes 4587520 | tf_op jit(solution)/shard_map/nej,jc->nec/dot_general | solution.py:145
  42.8 3.4 %all-to-all-start.1 = ((f32[8,16,512]{2,1,0:T(8,128)}), f32[8,16,512]{2,1,0:T(8,128)S(1)}, u32[]{:S(2)}, u32[]{:S(2)}) async-start(f32[8,16,512]{2,1,0:T(8,128)} %fusion.3), calls=%async_computation.1 | async-start | bytes 524288 | tf_op jit(solution)/shard_map/all_to_all | solution.py:148
  46.3 6.8 %all-to-all-done.1 = f32[8,16,512]{2,1,0:T(8,128)S(1)} async-done(((f32[8,16,512]{2,1,0:T(8,128)}), f32[8,16,512]{2,1,0:T(8,128)S(1)}, u32[]{:S(2)}, u32[]{:S(2)}) %all-to-all-start.1) | async-done | bytes 262176 | tf_op jit(solution)/shard_map/all_to_all | solution.py:148
  53.2 6.0 %fusion.5 = f32[32,1024]{1,0:T(8,128)S(1)} fusion(bf16[128,8,8,512]{3,2,1,0:T(8,128)(2,1)} %bitcast.13, bf16[8,16,512]{2,1,0:T(8,128)(2,1)S(1)} %subtract_convert_fusion, bf16[8,16,512]{2,1,0:T(8,128)(2,1)S(1)} %convert_element_type.21), kind=kOutput, calls=%fused_computation.5 | convolution fusion | flops 268959744 | bytes 8781824 | tf_op jit(solution)/shard_map/dot_general | solution.py:152
  59.2 2.0 %collective-permute-start.3 = (f32[16,256]{1,0:T(8,128)S(1)}, f32[16,256]{1,0:T(8,128)S(1)}, u32[]{:S(2)}, u32[]{:S(2)}) collective-permute-start(f32[16,256]{1,0:T(8,128)S(1)} %get-tuple-element.8), channel_id=1, source_target_pairs={{0,3},{1,0},{2,1},{3,2},{4,7},{5,4},{6,5},{7,6},{8,11},{9,8},{10,9... | collective-permute-start | bytes 49160 | tf_op jit(solution)/shard_map/ppermute | solution.py:18
  61.1 0.0 collective-permute-start.4
  61.1 1.9 %collective-permute-start.5 = (f32[16,256]{1,0:T(8,128)S(1)}, f32[16,256]{1,0:T(8,128)S(1)}, u32[]{:S(2)}, u32[]{:S(2)}) collective-permute-start(f32[16,256]{1,0:T(8,128)S(1)} %get-tuple-element.9), channel_id=1, source_target_pairs={{0,1},{1,2},{2,3},{3,0},{4,5},{5,6},{6,7},{7,4},{8,9},{9,10},{10,1... | collective-permute-start | bytes 49160 | tf_op jit(solution)/shard_map/ppermute | solution.py:18
  63.0 0.0 collective-permute-done.3
  63.0 2.7 %collective-permute-done.4 = f32[16,256]{1,0:T(8,128)S(1)} collective-permute-done((f32[16,256]{1,0:T(8,128)S(1)}, f32[16,256]{1,0:T(8,128)S(1)}, u32[]{:S(2)}, u32[]{:S(2)}) %collective-permute-start.4) | collective-permute-done | bytes 16416 | tf_op jit(solution)/shard_map/ppermute | solution.py:18
  65.8 0.9 %collective-permute-done.5 = f32[16,256]{1,0:T(8,128)S(1)} collective-permute-done((f32[16,256]{1,0:T(8,128)S(1)}, f32[16,256]{1,0:T(8,128)S(1)}, u32[]{:S(2)}, u32[]{:S(2)}) %collective-permute-start.5) | collective-permute-done | bytes 16416 | tf_op jit(solution)/shard_map/ppermute | solution.py:18
  66.7 0.6 add_add_fusion
  (4 shorter events, 0.1 us)
Async XLA Ops:
  17.5 7.6 %collective-permute-start = (f32[1,2,64,64]{3,2,1,0:T(8,128)S(1)}, f32[1,2,64,64]{3,2,1,0:T(8,128)S(1)}, u32[]{:S(2)}, u32[]{:S(2)}) collective-permute-start(f32[1,2,64,64]{3,2,1,0:T(8,128)S(1)} %get-tuple-element.5), channel_id=1, source_target_pairs={{0,3},{1,0},{2,1},{3,2},{4,7},{5,4},{6,5},{7,6},{8,11},{9,8},{10,9... | collective-permute-start | bytes 98312 | tf_op jit(solution)/shard_map/ppermute | solution.py:18
  22.7 6.5 %collective-permute-start.1 = (f32[1,2,64,64]{3,2,1,0:T(8,128)S(1)}, f32[1,2,64,64]{3,2,1,0:T(8,128)S(1)}, u32[]{:S(2)}, u32[]{:S(2)}) collective-permute-start(f32[1,2,64,64]{3,2,1,0:T(8,128)S(1)} %get-tuple-element.7), channel_id=1, source_target_pairs={{0,2},{1,3},{2,0},{3,1},{4,6},{5,7},{6,4},{7,5},{8,10},{9,11},{10,... | collective-permute-start | bytes 98312 | tf_op jit(solution)/shard_map/ppermute | solution.py:18
  22.7 6.5 %collective-permute-start.2 = (f32[1,2,64,64]{3,2,1,0:T(8,128)S(1)}, f32[1,2,64,64]{3,2,1,0:T(8,128)S(1)}, u32[]{:S(2)}, u32[]{:S(2)}) collective-permute-start(f32[1,2,64,64]{3,2,1,0:T(8,128)S(1)} %get-tuple-element.6), channel_id=1, source_target_pairs={{0,1},{1,2},{2,3},{3,0},{4,5},{5,6},{6,7},{7,4},{8,9},{9,10},{10,1... | collective-permute-start | bytes 98312 | tf_op jit(solution)/shard_map/ppermute | solution.py:18
  42.8 10.3 %all-to-all-start.1 = ((f32[8,16,512]{2,1,0:T(8,128)}), f32[8,16,512]{2,1,0:T(8,128)S(1)}, u32[]{:S(2)}, u32[]{:S(2)}) async-start(f32[8,16,512]{2,1,0:T(8,128)} %fusion.3), calls=%async_computation.1 | async-start | bytes 524288 | tf_op jit(solution)/shard_map/all_to_all | solution.py:148
  59.2 3.9 %collective-permute-start.3 = (f32[16,256]{1,0:T(8,128)S(1)}, f32[16,256]{1,0:T(8,128)S(1)}, u32[]{:S(2)}, u32[]{:S(2)}) collective-permute-start(f32[16,256]{1,0:T(8,128)S(1)} %get-tuple-element.8), channel_id=1, source_target_pairs={{0,3},{1,0},{2,1},{3,2},{4,7},{5,4},{6,5},{7,6},{8,11},{9,8},{10,9... | collective-permute-start | bytes 49160 | tf_op jit(solution)/shard_map/ppermute | solution.py:18
  61.1 4.6 %collective-permute-start.4 = (f32[16,256]{1,0:T(8,128)S(1)}, f32[16,256]{1,0:T(8,128)S(1)}, u32[]{:S(2)}, u32[]{:S(2)}) collective-permute-start(f32[16,256]{1,0:T(8,128)S(1)} %get-tuple-element.10), channel_id=1, source_target_pairs={{0,2},{1,3},{2,0},{3,1},{4,6},{5,7},{6,4},{7,5},{8,10},{9,11},{10,... | collective-permute-start | bytes 49160 | tf_op jit(solution)/shard_map/ppermute | solution.py:18
  61.1 5.5 %collective-permute-start.5 = (f32[16,256]{1,0:T(8,128)S(1)}, f32[16,256]{1,0:T(8,128)S(1)}, u32[]{:S(2)}, u32[]{:S(2)}) collective-permute-start(f32[16,256]{1,0:T(8,128)S(1)} %get-tuple-element.9), channel_id=1, source_target_pairs={{0,1},{1,2},{2,3},{3,0},{4,5},{5,6},{6,7},{7,4},{8,9},{9,10},{10,1... | collective-permute-start | bytes 49160 | tf_op jit(solution)/shard_map/ppermute | solution.py:18
